TPU v7x, 512 devices: a whole 4x8x8 slice. The times are simulated.
512 devices in a mesh: req: 64 (over x, y, core), tp: 8 (over z).
Axes of the slice: x: 4, y: 8, z: 8, core: 2. Of those that a mesh axis runs over, the one named last changes fastest.
Arguments:
- queries: bfloat16 [16384, 2048], P('req', 'tp'), may hold values from -10 to 10
- new_kv: bfloat16 [16384, 2048], P('req', 'tp'), may hold values from -4 to 4
- kv_pool: bfloat16 [512, 4, 256, 2048], P('req', None, None, 'tp'), may hold values from -4 to 4
- cache_lens: int32 [512], P('req'), may hold values from 2 to 1024, as said below
- parents: int32 [512, 32], P('req'), may hold values from 0 to 31, as said below
- accepted: int32 [512], P('req'), may hold values from 0 to 31, as said below
- residual: bfloat16 [16384, 4096], P(('req', 'tp')), may hold values from -3 to 3
- w_out: bfloat16 [2048, 4096], P('tp'), may hold values from -0.125 to 0.125
- norm_gain: float32 [4096], replicated, may hold values from 0.25 to 1.75
Outputs:
- hidden_out: bfloat16 [16384, 4096], P(('req', 'tp'))
- normed: bfloat16 [16384, 4096], P(('req', 'tp'))
- accepted_kv: bfloat16 [512, 8, 2048], P('req', None, 'tp')
Inputs may be any that keep to these rules, and one draw needn't show every extreme that they name: parents[r, 0] = 0 and parents[r, i] < i for i >= 1; every node lies at depth 7 or less; nodes 1 to 7 form a chain below the root. Some request's accepted node lies at depth 7. `cache_lens`: some request holds 1024 cached rows and some holds 2.
All inputs are finite; a program needn't handle non-finite values.
Results may differ from a plain program's by a relative error of at most 0.015.
Values may be sent and summed in bfloat16 or wider, within the bound.
No kernel may reach another device: no remote copies, remote signals or barrier semaphores. Data moves between devices by JAX's collectives and lax.ppermute only.
A program may use at most 64 MiB of HBM per device.

v0:
```python
from functools import reduce

import jax
import jax.numpy as jnp
from jax import lax
from jax.sharding import PartitionSpec as P

HD = 128
TREE = 32
MAXD = 7
PATH = 8


NEGATIVE = -1e30


def shifted(value, axis, steps):
    count = lax.axis_size(axis)
    pairs = [(source, (source + steps) % count) for source in range(count)]
    return lax.ppermute(value, axis, pairs)


def ancestors(parents):
    node_ids = jnp.arange(TREE, dtype=jnp.int32)
    current = jnp.broadcast_to(node_ids, parents.shape)
    marked = jnp.zeros(parents.shape + (TREE,), jnp.int32)
    for depth_step in range(MAXD + 1):
        onehot_rows = (current[..., None] == node_ids).astype(jnp.int32)
        marked = jnp.maximum(marked, onehot_rows)
        current = jnp.sum(onehot_rows * parents[..., None, :], axis=-1, dtype=jnp.int32)
    return marked


def block_partial(query_rows, key_rows, value_rows, allowed):
    scale_factor = HD ** (-0.5)
    scores = (
        jnp.einsum("rtkgd,rckd->rtkgc", query_rows, key_rows, preferred_element_type=jnp.float32)
        * scale_factor
    )
    visible = allowed[:, :, None, None, :]
    largest = jnp.max(jnp.where(visible, scores, NEGATIVE), axis=-1)
    weights = jnp.where(visible, jnp.exp(scores - largest[..., None]), 0.0)
    totals = jnp.sum(weights, axis=-1)
    weighted = jnp.einsum(
        "rtkgc,rckd->rtkgd",
        weights.astype(jnp.bfloat16),
        value_rows,
        preferred_element_type=jnp.float32,
    )
    return (largest, totals, weighted)


def page_term(query_rows, page_rows, lengths, page_index):
    req_count, row_count, row_width = page_rows.shape
    kv_local = row_width // (2 * HD)
    split_rows = page_rows.reshape(req_count, row_count, kv_local, 2, HD)
    positions = page_index * row_count + jnp.arange(row_count, dtype=jnp.int32)
    allowed = positions[None, None, :] < lengths[:, None, None]
    return block_partial(query_rows, split_rows[:, :, :, 0], split_rows[:, :, :, 1], allowed)


def merge_blocks(block_list):
    largest = reduce(jnp.maximum, [block_part[0] for block_part in block_list])
    factors = [jnp.exp(block_part[0] - largest) for block_part in block_list]
    denominator = reduce(
        jnp.add, [factor * block_part[1] for factor, block_part in zip(factors, block_list)]
    )
    numerator = reduce(
        jnp.add,
        [factor[..., None] * block_part[2] for factor, block_part in zip(factors, block_list)],
    )
    return (denominator, numerator)


def per_device(queries, new_kv, kv_pool, cache_lens, parents, accepted, residual, w_out, norm_gain):
    req_count, page_count, page_size, row_width = kv_pool.shape
    kv_local = row_width // (2 * HD)
    q_local = queries.shape[1] // HD
    group = q_local // kv_local
    query_rows = queries.reshape(req_count, TREE, kv_local, group, HD)
    fresh = new_kv.reshape(req_count, TREE, kv_local, 2, HD)
    marked = ancestors(parents)
    block_list = [block_partial(query_rows, fresh[:, :, :, 0], fresh[:, :, :, 1], marked > 0)]
    for page_index in range(page_count):
        page_rows = kv_pool[:, page_index]
        if page_index > 0:
            page_rows = shifted(page_rows, "req", -page_index)
        block_list.append(page_term(query_rows, page_rows, cache_lens, page_index))
    denominator, numerator = merge_blocks(block_list)
    attention = (
        (numerator / denominator[..., None])
        .astype(jnp.bfloat16)
        .reshape(req_count * TREE, q_local * HD)
    )
    product = jnp.dot(attention, w_out, preferred_element_type=jnp.float32)
    summed = lax.psum_scatter(
        lax.optimization_barrier(product.astype(jnp.bfloat16))
        .astype(jnp.float32)
        .astype(jnp.bfloat16),
        "tp",
        scatter_dimension=0,
        tiled=True,
    ).astype(jnp.float32)
    hidden_out = (residual.astype(jnp.float32) + summed).astype(jnp.bfloat16)
    widened = hidden_out.astype(jnp.float32)
    normed = (
        widened * lax.rsqrt(jnp.mean(widened * widened, axis=-1, keepdims=True) + 1e-05) * norm_gain
    ).astype(jnp.bfloat16)
    node_ids = jnp.arange(TREE, dtype=jnp.int32)
    chosen = (accepted[:, None] == node_ids[None, :]).astype(jnp.int32)
    on_path = jnp.sum(chosen[:, :, None] * marked, axis=1, dtype=jnp.int32)
    path_rank = jnp.cumsum(on_path, axis=1, dtype=jnp.int32) - 1
    path_slots = jnp.arange(PATH, dtype=jnp.int32)
    selector = (
        (path_rank[:, None, :] == path_slots[None, :, None]) & (on_path[:, None, :] > 0)
    ).astype(jnp.bfloat16)
    fresh_rows = new_kv.reshape(req_count, TREE, row_width)
    accepted_kv = jnp.einsum(
        "rku,ruc->rkc", selector, fresh_rows, preferred_element_type=jnp.float32
    ).astype(jnp.bfloat16)
    return (hidden_out, normed, accepted_kv)


def solution(mesh):
    placed = (
        P("req", "tp"),
        P("req", "tp"),
        P("req", None, None, "tp"),
        P("req"),
        P("req", None),
        P("req"),
        P(("req", "tp"), None),
        P("tp", None),
        P(),
    )
    return jax.shard_map(
        per_device,
        mesh=mesh,
        in_specs=placed,
        out_specs=(P(("req", "tp"), None), P(("req", "tp"), None), P("req", None, "tp")),
        check_vma=False,
    )
```

profile of v0, /device:TPU:6, one launch (start us, length us, event | category | flops | bytes accessed | tf_op | source)
XLA Modules:
  0.0 155.2 jit_solution(3436846767245971140)
XLA Ops:
  7.2 0.0 reduce-scatter.2.cloned.1.call-start
  7.2 4.0 %fusion.65 = (bf16[8,1,256,256]{3,2,1,0:T(8,128)(2,1)S(1)}, bf16[8,1,256,256]{3,2,1,0:T(8,128)(2,1)}, bf16[8,1,256,256]{3,2,1,0:T(8,128)(2,1)}, bf16[8,1,256,256]{3,2,1,0:T(8,128)(2,1)}) fusion(bf16[8,4,256,256]{3,2,1,0:T(8,128)(2,1)} %param.11), kind=kLoop, calls=%fused_computation.138 | loop fusion | bytes 8388608 | tf_op jit(solution)/shard_map/slice | solution.py:85
  11.3 2.3 %copy.57 = bf16[8,1,256,256]{2,3,0,1:T(8,128)(2,1)} copy(bf16[8,1,256,256]{3,2,1,0:T(8,128)(2,1)} %get-tuple-element.14) | data formatting | bytes 2097152
  13.5 5.9 %collective-permute-start.2 = (bf16[8,256,256]{1,2,0:T(8,128)(2,1)}, bf16[8,256,256]{1,2,0:T(8,128)(2,1)}, u32[]{:S(2)}, u32[]{:S(2)}) collective-permute-start(bf16[8,256,256]{1,2,0:T(8,128)(2,1)} %bitcast.221), channel_id=1, source_target_pairs={{0,488},{8,496},{16,504},{24,0},{32,8},{40,16},{48,24},{56,32},{64... | collective-permute-start | bytes 3145736 | tf_op jit(solution)/shard_map/ppermute | solution.py:20
  19.4 2.3 %copy.55 = bf16[8,1,256,256]{2,3,0,1:T(8,128)(2,1)} copy(bf16[8,1,256,256]{3,2,1,0:T(8,128)(2,1)} %get-tuple-element.12) | data formatting | bytes 2097152
  21.7 3.2 %collective-permute-start.1 = (bf16[8,256,256]{1,2,0:T(8,128)(2,1)}, bf16[8,256,256]{1,2,0:T(8,128)(2,1)}, u32[]{:S(2)}, u32[]{:S(2)}) collective-permute-start(bf16[8,256,256]{1,2,0:T(8,128)(2,1)} %bitcast.220), channel_id=1, source_target_pairs={{0,496},{8,504},{16,0},{24,8},{32,16},{40,24},{48,32},{56,40},{64,... | collective-permute-start | bytes 3145736 | tf_op jit(solution)/shard_map/ppermute | solution.py:20
  25.0 2.3 %copy.53 = bf16[8,1,256,256]{2,3,0,1:T(8,128)(2,1)} copy(bf16[8,1,256,256]{3,2,1,0:T(8,128)(2,1)} %get-tuple-element.13) | data formatting | bytes 2097152
  27.3 2.5 %collective-permute-start = (bf16[8,256,256]{1,2,0:T(8,128)(2,1)}, bf16[8,256,256]{1,2,0:T(8,128)(2,1)}, u32[]{:S(2)}, u32[]{:S(2)}) collective-permute-start(bf16[8,256,256]{1,2,0:T(8,128)(2,1)} %bitcast.219), channel_id=1, source_target_pairs={{0,504},{8,0},{16,8},{24,16},{32,24},{40,32},{48,40},{56,48},{64,5... | collective-permute-start | bytes 3145736 | tf_op jit(solution)/shard_map/ppermute | solution.py:20
  29.8 0.1 select_reduce_fusion.11
  29.9 0.1 select_reduce_fusion.10
  30.0 0.1 select_reduce_fusion.9
  30.1 0.1 select_reduce_fusion.8
  30.2 0.2 copy-done.9
  30.5 0.1 select_reduce_fusion.7
  30.6 0.1 select_reduce_fusion.6
  30.7 0.6 copy-done.7
  31.3 0.7 select_reduce_fusion.5
  32.0 0.9 fusion.66
  32.9 0.9 fusion.49
  33.8 1.6 %reshape.524 = bf16[8,32,2,128]{3,2,1,0:T(2,128)(2,1)} reshape(bf16[256,256]{1,0:T(8,128)(2,1)} %param.9) | data formatting | bytes 262144 | tf_op jit(solution)/shard_map/reshape.2
  35.4 1.3 copy.51
  36.8 1.3 select_reduce_fusion.4
  38.1 0.1 fusion.40
  38.2 0.7 iota_compare_fusion.9
  38.9 1.4 select_reduce_fusion.3
  40.3 14.0 %collective-permute-done.2 = bf16[8,256,256]{1,2,0:T(8,128)(2,1)} collective-permute-done((bf16[8,256,256]{1,2,0:T(8,128)(2,1)}, bf16[8,256,256]{1,2,0:T(8,128)(2,1)}, u32[]{:S(2)}, u32[]{:S(2)}) %collective-permute-start.2) | collective-permute-done | bytes 1048608 | tf_op jit(solution)/shard_map/ppermute | solution.py:20
  54.3 1.4 select_reduce_fusion
  55.7 20.5 %collective-permute-done.1 = bf16[8,256,256]{1,2,0:T(8,128)(2,1)} collective-permute-done((bf16[8,256,256]{1,2,0:T(8,128)(2,1)}, bf16[8,256,256]{1,2,0:T(8,128)(2,1)}, u32[]{:S(2)}, u32[]{:S(2)}) %collective-permute-start.1) | collective-permute-done | bytes 1048608 | tf_op jit(solution)/shard_map/ppermute | solution.py:20
  76.2 1.4 select_reduce_fusion.1
  77.5 9.9 %collective-permute-done = bf16[8,256,256]{1,2,0:T(8,128)(2,1)} collective-permute-done((bf16[8,256,256]{1,2,0:T(8,128)(2,1)}, bf16[8,256,256]{1,2,0:T(8,128)(2,1)}, u32[]{:S(2)}, u32[]{:S(2)}) %collective-permute-start) | collective-permute-done | bytes 1048608 | tf_op jit(solution)/shard_map/ppermute | solution.py:20
  87.4 1.4 select_reduce_fusion.2
  88.8 0.4 bitcast_reduce_fusion
  89.2 0.4 bitcast_reduce_fusion.2
  89.7 1.5 fusion.4
  91.2 1.4 fusion.5
  92.6 0.2 fusion.14
  92.8 0.3 fusion.9
  93.2 1.4 fusion.16
  94.6 0.1 copy.38
  94.7 2.1 %convolution_convert_fusion = bf16[256,4096]{1,0:T(8,128)(2,1)} fusion(bf16[256,4096]{1,0:T(8,128)(2,1)S(1)} %copy-done, bf16[32,8,2,128]{3,2,1,0:T(2,128)(2,1)S(1)} %bitcast.222), kind=kOutput, calls=%fused_computation | convolution fusion | flops 537919488 | bytes 4325376 | tf_op jit(solution)/shard_map/dot_general | solution.py:95
  96.8 0.6 copy-done.13
  97.4 0.1 fusion.59
  97.5 0.2 multiply_reduce_fusion
  97.8 0.2 reduce_window_sum.11
  98.0 0.8 convolution_convert_fusion.1
  98.7 47.6 %reduce-scatter.2.cloned.1.call-done = bf16[32,4096]{1,0:T(8,128)(2,1)} async-done(((bf16[256,4096]{1,0:T(8,128)(2,1)}), bf16[32,4096]{1,0:T(8,128)(2,1)}) %reduce-scatter.2.cloned.1.call-update) | async-done | bytes 262160 | tf_op jit(solution)/shard_map/reduce_scatter | solution.py:96
  146.3 1.2 fusion.17
  147.5 0.8 fusion.19
  (34 shorter events, 0.2 us)
Async XLA Ops:
  7.2 87.5 %copy-start = (bf16[256,4096]{1,0:T(8,128)(2,1)S(1)}, bf16[256,4096]{1,0:T(8,128)(2,1)}, u32[]{:S(2)}) copy-start(bf16[256,4096]{1,0:T(8,128)(2,1)} %param.16) | copy-start | bytes 6291460
  7.2 139.1 %reduce-scatter.2.cloned.1.call-start = ((), (), s32[]{:S(2)}) async-start(), calls=%async_computation.1 | async-start | bytes 2359296 | tf_op jit(solution)/shard_map/reduce_scatter | solution.py:96
  13.5 40.8 %collective-permute-start.2 = (bf16[8,256,256]{1,2,0:T(8,128)(2,1)}, bf16[8,256,256]{1,2,0:T(8,128)(2,1)}, u32[]{:S(2)}, u32[]{:S(2)}) collective-permute-start(bf16[8,256,256]{1,2,0:T(8,128)(2,1)} %bitcast.221), channel_id=1, source_target_pairs={{0,488},{8,496},{16,504},{24,0},{32,8},{40,16},{48,24},{56,32},{64... | collective-permute-start | bytes 3145736 | tf_op jit(solution)/shard_map/ppermute | solution.py:20
  19.4 10.3 %copy-start.5 = (s32[8,32]{1,0:T(8,128)S(1)}, s32[8,32]{1,0:T(8,128)}, u32[]{:S(2)}) copy-start(s32[8,32]{1,0:T(8,128)} %param.13) | copy-start | bytes 3076
  19.4 12.6 %copy-start.3 = (bf16[256,256]{1,0:T(8,128)(2,1)S(1)}, bf16[256,256]{1,0:T(8,128)(2,1)}, u32[]{:S(2)}) copy-start(bf16[256,256]{1,0:T(8,128)(2,1)} %param.10) | copy-start | bytes 393220
  21.7 54.4 %collective-permute-start.1 = (bf16[8,256,256]{1,2,0:T(8,128)(2,1)}, bf16[8,256,256]{1,2,0:T(8,128)(2,1)}, u32[]{:S(2)}, u32[]{:S(2)}) collective-permute-start(bf16[8,256,256]{1,2,0:T(8,128)(2,1)} %bitcast.220), channel_id=1, source_target_pairs={{0,496},{8,504},{16,0},{24,8},{32,16},{40,24},{48,32},{56,40},{64,... | collective-permute-start | bytes 3145736 | tf_op jit(solution)/shard_map/ppermute | solution.py:20
  27.3 60.1 %collective-permute-start = (bf16[8,256,256]{1,2,0:T(8,128)(2,1)}, bf16[8,256,256]{1,2,0:T(8,128)(2,1)}, u32[]{:S(2)}, u32[]{:S(2)}) collective-permute-start(bf16[8,256,256]{1,2,0:T(8,128)(2,1)} %bitcast.219), channel_id=1, source_target_pairs={{0,504},{8,0},{16,8},{24,16},{32,24},{40,32},{48,40},{56,48},{64,5... | collective-permute-start | bytes 3145736 | tf_op jit(solution)/shard_map/ppermute | solution.py:20
  29.9 0.6 copy-start.9
  30.7 0.6 copy-start.7
  36.7 17.6 %copy-start.6 = (bf16[8,32,2,128]{3,2,1,0:T(2,128)(2,1)S(1)}, bf16[8,32,2,128]{3,2,1,0:T(2,128)(2,1)}, u32[]{:S(2)}) copy-start(bf16[8,32,2,128]{3,2,1,0:T(2,128)(2,1)} %reshape.524) | copy-start | bytes 393220
  89.6 3.2 %copy-start.1 = (bf16[8,1,256,256]{2,3,0,1:T(8,128)(2,1)S(1)}, bf16[8,1,256,256]{2,3,0,1:T(8,128)(2,1)}, u32[]{:S(2)}) copy-start(bf16[8,1,256,256]{2,3,0,1:T(8,128)(2,1)} %copy.51) | copy-start | bytes 3145732
  96.8 0.7 copy-start.13
  96.8 0.7 copy-start.8
  96.8 0.7 copy-start.10
  96.8 0.7 copy-start.11
  96.8 49.5 %copy-start.4 = (bf16[32,4096]{1,0:T(8,128)(2,1)S(1)}, bf16[32,4096]{1,0:T(8,128)(2,1)}, u32[]{:S(2)}) copy-start(bf16[32,4096]{1,0:T(8,128)(2,1)} %param.15) | copy-start | bytes 786436
  96.8 50.7 %copy-start.12 = (f32[4096]{0:T(1024)S(1)}, f32[4096]{0:T(1024)}, u32[]{:S(2)}) copy-start(f32[4096]{0:T(1024)} %param.17) | copy-start | bytes 49156
  147.5 0.9 copy-start.2
Sparse Core Ops, SparseCore 0:
  97.0 49.2 reduce-scatter.1
where the time goes:
time: 156 us; the launch traced here: 155 us
  waiting for transfers between devices  92 us (59%)
  local copies, waits for them, and re-layouts  16.4 us (11%)
  matrix products  14.5 us (9%)
  between operations  14.3 us (9%)
  starting transfers between devices  11.6 us (7%)
  other arithmetic  6.49 us (4%)
    reduce_scatter x1, waiting for transfers between devices, per_device(): lax.psum_scatter(lax.optimization_barrier(product.astype(jnp.bfloat16)).a...  47.6 us
    ppermute x3, waiting for transfers between devices, shifted(): return lax.ppermute(value, axis, pairs)  44.4 us
    ppermute x3, starting transfers between devices, shifted(): return lax.ppermute(value, axis, pairs)  11.6 us
    unnamed x32, local copies, waits for them, and re-layouts  9.68 us
    dot_general x5, matrix products, block_partial(): jnp.einsum('rtkgd,rckd->rtkgc', query_rows, key_rows, preferred_element_t...  6.77 us
    dot_general x5, matrix products, block_partial(): jnp.einsum('rtkgc,rckd->rtkgd', weights.astype(jnp.bfloat16), value_rows,...  4.86 us
    slice x1, local copies, waits for them, and re-layouts, per_device(): page_rows = kv_pool[:, page_index]  4.03 us
  transfers between devices with their start and end apart: 4, of which 4 were waited for; matrix products, arithmetic and copies ran while one was open for 12% of the time, Pallas kernels for 0%

commit v1 on v0

--- a/solution.py
+++ b/solution.py
@@ -9,6 +9,7 @@
 TREE = 32
 MAXD = 7
 PATH = 8
+EXTRA = 16
 
 
 NEGATIVE = -1e30
@@ -31,7 +32,7 @@
     return marked
 
 
-def block_partial(query_rows, key_rows, value_rows, allowed):
+def block_partial(query_rows, key_rows, value_rows, allowed, round_max=False):
     scale_factor = HD ** (-0.5)
     scores = (
         jnp.einsum("rtkgd,rckd->rtkgc", query_rows, key_rows, preferred_element_type=jnp.float32)
@@ -39,6 +40,8 @@
     )
     visible = allowed[:, :, None, None, :]
     largest = jnp.max(jnp.where(visible, scores, NEGATIVE), axis=-1)
+    if round_max:
+        largest = largest.astype(jnp.bfloat16).astype(jnp.float32)
     weights = jnp.where(visible, jnp.exp(scores - largest[..., None]), 0.0)
     totals = jnp.sum(weights, axis=-1)
     weighted = jnp.einsum(
@@ -50,13 +53,15 @@
     return (largest, totals, weighted)
 
 
-def page_term(query_rows, page_rows, lengths, page_index):
+def page_term(query_rows, page_rows, lengths, page_index, round_max=False):
     req_count, row_count, row_width = page_rows.shape
     kv_local = row_width // (2 * HD)
     split_rows = page_rows.reshape(req_count, row_count, kv_local, 2, HD)
     positions = page_index * row_count + jnp.arange(row_count, dtype=jnp.int32)
     allowed = positions[None, None, :] < lengths[:, None, None]
-    return block_partial(query_rows, split_rows[:, :, :, 0], split_rows[:, :, :, 1], allowed)
+    return block_partial(
+        query_rows, split_rows[:, :, :, 0], split_rows[:, :, :, 1], allowed, round_max
+    )
 
 
 def merge_blocks(block_list):
@@ -70,6 +75,54 @@
         [factor[..., None] * block_part[2] for factor, block_part in zip(factors, block_list)],
     )
     return (denominator, numerator)
+
+
+def pack_queries(queries, lengths):
+    width = queries.shape[1]
+    count = lengths.shape[0]
+    hi = (lengths // 16).astype(jnp.bfloat16)
+    lo = (lengths % 16).astype(jnp.bfloat16)
+    extra = jnp.zeros((EXTRA, width), jnp.bfloat16)
+    extra = extra.at[0, :count].set(hi).at[1, :count].set(lo)
+    return jnp.concatenate([queries, extra], axis=0)
+
+
+def unpack_queries(packed, count):
+    rows = packed.shape[0] - EXTRA
+    extra = packed[rows:]
+    hi = extra[0, :count].astype(jnp.int32)
+    lo = extra[1, :count].astype(jnp.int32)
+    return packed[:rows], hi * 16 + lo
+
+
+def pack_partial(part):
+    largest, totals, weighted = part
+    req_count, tree, kv_local, group = largest.shape
+    tokens = req_count * tree
+    heads = kv_local * group
+    body = weighted.reshape(tokens, heads * HD).astype(jnp.bfloat16)
+    total_hi = totals.astype(jnp.bfloat16)
+    total_lo = (totals - total_hi.astype(jnp.float32)).astype(jnp.bfloat16)
+    stats = jnp.stack(
+        [largest.astype(jnp.bfloat16), total_hi, total_lo], axis=0
+    ).reshape(3, tokens, heads)
+    stats = jnp.transpose(stats, (0, 2, 1)).reshape(3 * heads, tokens)
+    width = heads * HD
+    extra = jnp.zeros((EXTRA, width), jnp.bfloat16)
+    extra = extra.at[: 3 * heads, :tokens].set(stats)
+    return jnp.concatenate([body, extra], axis=0)
+
+
+def unpack_partial(packed, shape):
+    req_count, tree, kv_local, group = shape
+    tokens = req_count * tree
+    heads = kv_local * group
+    body = packed[:tokens].astype(jnp.float32).reshape(req_count, tree, kv_local, group, HD)
+    stats = packed[tokens : tokens + 3 * heads, :tokens].astype(jnp.float32)
+    stats = jnp.transpose(stats.reshape(3, heads, tokens), (0, 2, 1)).reshape(
+        3, req_count, tree, kv_local, group
+    )
+    return (stats[0], stats[1] + stats[2], body)
 
 
 def per_device(queries, new_kv, kv_pool, cache_lens, parents, accepted, residual, w_out, norm_gain):
@@ -80,12 +133,23 @@
     query_rows = queries.reshape(req_count, TREE, kv_local, group, HD)
     fresh = new_kv.reshape(req_count, TREE, kv_local, 2, HD)
     marked = ancestors(parents)
+
+    packed_queries = pack_queries(queries, cache_lens)
+    arrived = [shifted(packed_queries, "req", page_index) for page_index in range(1, page_count)]
+
     block_list = [block_partial(query_rows, fresh[:, :, :, 0], fresh[:, :, :, 1], marked > 0)]
-    for page_index in range(page_count):
-        page_rows = kv_pool[:, page_index]
-        if page_index > 0:
-            page_rows = shifted(page_rows, "req", -page_index)
-        block_list.append(page_term(query_rows, page_rows, cache_lens, page_index))
+    block_list.append(page_term(query_rows, kv_pool[:, 0], cache_lens, 0))
+
+    returned = []
+    for page_index in range(1, page_count):
+        guest_queries, guest_lengths = unpack_queries(arrived[page_index - 1], req_count)
+        guest_rows = guest_queries.reshape(req_count, TREE, kv_local, group, HD)
+        part = page_term(guest_rows, kv_pool[:, page_index], guest_lengths, page_index, True)
+        returned.append(shifted(pack_partial(part), "req", -page_index))
+    stat_shape = (req_count, TREE, kv_local, group)
+    for packed in returned:
+        block_list.append(unpack_partial(packed, stat_shape))
+
     denominator, numerator = merge_blocks(block_list)
     attention = (
         (numerator / denominator[..., None])

time: 156 us -> 187 us (1.20)
  waiting for transfers between devices: 92 us -> 47.9 us
  local copies, waits for them, and re-layouts: 16.4 us -> 53.1 us
  other arithmetic: 6.49 us -> 35.2 us
  starting transfers between devices: 11.6 us -> 18.4 us
  matrix products: 14.5 us -> 16.5 us
    ppermute x3 -> x6, waiting for transfers between devices: 44.4 us -> 0.02 us  [shifted(): return lax.ppermute(value, axis, pairs)]
    convert_element_type x0 -> x9, local copies, waits for them, and re-layouts: none -> 7.1 us  [the longest x6 4.07 us: block_partial(): largest = largest.astype(jnp.bfloat16).astype(jnp.float32)]
    ppermute x3 -> x6, starting transfers between devices: 11.6 us -> 18.4 us  [shifted(): return lax.ppermute(value, axis, pairs)]
    another operation x1 -> x7, local copies, waits for them, and re-layouts: 1.6 us -> 7.01 us
    reshape x0 -> x3, local copies, waits for them, and re-layouts: none -> 5.37 us  [unpack_partial(): packed[:tokens].astype(jnp.float32)]
    reshape x0 -> x3, other arithmetic: none -> 4.87 us  [unpack_partial(): packed[:tokens].astype(jnp.float32)]
    slice x1 -> x4, local copies, waits for them, and re-layouts: 4.03 us -> 8.69 us  [the longest x3 4.78 us: unpack_queries(): return (packed[:rows], hi * 16 + lo)]
    concatenate x0 -> x4, other arithmetic: none -> 4.35 us  [the longest x3 2.78 us: pack_partial(): return jnp.concatenate([body, extra], axis=0)]
  transfers between devices with their start and end apart: 4 -> 7, of which waited for: 4 -> 1; matrix products, arithmetic and copies ran while one was open for 12% -> 32% of each run, Pallas kernels for 0% -> 0%
where the time goes in v1:
time: 187 us; the launch traced here: 186 us
  local copies, waits for them, and re-layouts  53.1 us (28%)
  waiting for transfers between devices  47.9 us (26%)
  other arithmetic  35.2 us (19%)
  starting transfers between devices  18.4 us (10%)
  matrix products  16.5 us (9%)
  between operations  14.5 us (8%)
    reduce_scatter x1, waiting for transfers between devices, per_device(): lax.psum_scatter(lax.optimization_barrier(product.astype(jnp.bfloat16)).a...  47.8 us
    ppermute x6, starting transfers between devices, shifted(): return lax.ppermute(value, axis, pairs)  18.4 us
    unnamed x55, local copies, waits for them, and re-layouts  10 us
    dot_general x5, matrix products, block_partial(): jnp.einsum('rtkgc,rckd->rtkgd', weights.astype(jnp.bfloat16), value_rows,...  7.02 us
    another operation x7, local copies, waits for them, and re-layouts  7.01 us
    dot_general x5, matrix products, block_partial(): jnp.einsum('rtkgd,rckd->rtkgc', query_rows, key_rows, preferred_element_t...  6.63 us
    reshape x3, local copies, waits for them, and re-layouts, unpack_partial(): packed[:tokens].astype(jnp.float32)  5.37 us
    reduce_sum x5, other arithmetic, block_partial(): totals = jnp.sum(weights, axis=-1)  5.01 us
  transfers between devices with their start and end apart: 7, of which 1 were waited for; matrix products, arithmetic and copies ran while one was open for 32% of the time, Pallas kernels for 0%

profile of v1, /device:TPU:6, one launch (start us, length us, event | category | flops | bytes accessed | tf_op | source)
XLA Modules:
  0.0 185.5 jit_solution(18265161466212239014)
XLA Ops:
  8.2 1.6 pad_maximum_fusion
  9.8 2.9 %collective-permute-start.4 = (bf16[272,256]{1,0:T(8,128)(2,1)}, bf16[272,256]{1,0:T(8,128)(2,1)}, u32[]{:S(2)}, u32[]{:S(2)}) collective-permute-start(bf16[272,256]{1,0:T(8,128)(2,1)} %pad_maximum_fusion), channel_id=1, source_target_pairs={{0,24},{8,32},{16,40},{24,48},{32,56},{40,64},{48,72},{56,80},{64,... | collective-permute-start | bytes 417800 | tf_op jit(solution)/shard_map/ppermute | solution.py:21
  12.7 3.5 %collective-permute-start.2 = (bf16[272,256]{1,0:T(8,128)(2,1)}, bf16[272,256]{1,0:T(8,128)(2,1)}, u32[]{:S(2)}, u32[]{:S(2)}) collective-permute-start(bf16[272,256]{1,0:T(8,128)(2,1)} %pad_maximum_fusion), channel_id=1, source_target_pairs={{0,16},{8,24},{16,32},{24,40},{32,48},{40,56},{48,64},{56,72},{64,... | collective-permute-start | bytes 417800 | tf_op jit(solution)/shard_map/ppermute | solution.py:21
  16.2 3.3 %collective-permute-start = (bf16[272,256]{1,0:T(8,128)(2,1)}, bf16[272,256]{1,0:T(8,128)(2,1)}, u32[]{:S(2)}, u32[]{:S(2)}) collective-permute-start(bf16[272,256]{1,0:T(8,128)(2,1)} %pad_maximum_fusion), channel_id=1, source_target_pairs={{0,8},{8,16},{16,24},{24,32},{32,40},{40,48},{48,56},{56,64},{64,7... | collective-permute-start | bytes 417800 | tf_op jit(solution)/shard_map/ppermute | solution.py:21
  21.3 1.6 reshape.1089
  22.9 1.3 iota_compare_fusion.10
  24.2 3.9 %fusion.90 = (bf16[8,1,256,256]{3,2,1,0:T(8,128)(2,1)S(1)}, bf16[8,1,256,256]{3,2,1,0:T(8,128)(2,1)}, bf16[8,1,256,256]{3,2,1,0:T(8,128)(2,1)}, bf16[8,1,256,256]{3,2,1,0:T(8,128)(2,1)}) fusion(bf16[8,4,256,256]{3,2,1,0:T(8,128)(2,1)} %param.21), kind=kLoop, calls=%fused_computation.195 | loop fusion | bytes 8388608 | tf_op jit(solution)/shard_map/slice | solution.py:141
  28.1 2.3 %copy.199 = bf16[8,1,256,256]{2,3,0,1:T(8,128)(2,1)} copy(bf16[8,1,256,256]{3,2,1,0:T(8,128)(2,1)} %get-tuple-element.80) | data formatting | bytes 2097152
  30.4 2.3 %copy.196 = bf16[8,1,256,256]{2,3,0,1:T(8,128)(2,1)} copy(bf16[8,1,256,256]{3,2,1,0:T(8,128)(2,1)} %get-tuple-element.78) | data formatting | bytes 2097152
  32.7 2.3 %copy.193 = bf16[8,1,256,256]{2,3,0,1:T(8,128)(2,1)} copy(bf16[8,1,256,256]{3,2,1,0:T(8,128)(2,1)} %get-tuple-element.79) | data formatting | bytes 2097152
  38.7 1.3 copy.191
  40.0 1.4 select_reduce_fusion.4
  41.4 1.4 select_reduce_fusion.3
  42.8 1.5 fusion.47
  45.2 1.6 slice.271
  46.8 1.6 reshape.1105
  53.6 1.6 slice.264
  55.2 1.6 reshape.1099
  58.3 1.4 select_reduce_fusion.1
  60.3 2.0 %fusion.10 = bf16[8,32,1,2,128]{4,1,3,0,2:T(8,128)(2,1)} fusion(bf16[8,256,1,2,128]{1,4,3,0,2:T(8,128)(2,1)} %bitcast.280, f32[8,1,256,32,2]{2,3,4,0,1:T(8,128)S(1)} %get-tuple-element.94, f32[8,32,2]{1,2,0:T(2,128)S(1)} %convert_element_type.466, pred[8,256]{1,0:T(8,128)(4,1)S(1)} %broadcast_compare_fusion.1), kind=kOutput, calls=%fused_computation.21 | convolution fusion | flops 34013184 | bytes 1183744 | tf_op jit(solution)/shard_map/rtkgc,rckd->rtkgd/dot_general | solution.py:47
  63.3 1.6 slice.257
  64.8 1.6 reshape.1093
  74.2 4.2 %collective-permute-start.5 = (bf16[272,256]{1,0:T(8,128)(2,1)}, bf16[272,256]{1,0:T(8,128)(2,1)}, u32[]{:S(2)}, u32[]{:S(2)}) collective-permute-start(bf16[272,256]{1,0:T(8,128)(2,1)} %fusion.51), channel_id=1, source_target_pairs={{0,488},{8,496},{16,504},{24,0},{32,8},{40,16},{48,24},{56,32},{64... | collective-permute-start | bytes 417800 | tf_op jit(solution)/shard_map/ppermute | solution.py:21
  81.8 2.5 %collective-permute-start.3 = (bf16[272,256]{1,0:T(8,128)(2,1)}, bf16[272,256]{1,0:T(8,128)(2,1)}, u32[]{:S(2)}, u32[]{:S(2)}) collective-permute-start(bf16[272,256]{1,0:T(8,128)(2,1)} %fusion.50), channel_id=1, source_target_pairs={{0,496},{8,504},{16,0},{24,8},{32,16},{40,24},{48,32},{56,40},{64,... | collective-permute-start | bytes 417800 | tf_op jit(solution)/shard_map/ppermute | solution.py:21
  87.5 1.4 fusion.49
  88.9 1.9 %collective-permute-start.1 = (bf16[272,256]{1,0:T(8,128)(2,1)}, bf16[272,256]{1,0:T(8,128)(2,1)}, u32[]{:S(2)}, u32[]{:S(2)}) collective-permute-start(bf16[272,256]{1,0:T(8,128)(2,1)} %fusion.49), channel_id=1, source_target_pairs={{0,504},{8,0},{16,8},{24,16},{32,24},{40,32},{48,40},{56,48},{64,5... | collective-permute-start | bytes 417800 | tf_op jit(solution)/shard_map/ppermute | solution.py:21
  90.9 1.6 slice_convert_fusion
  92.5 1.8 reshape.1128
  94.3 1.6 slice_convert_fusion.1
  95.9 1.8 reshape.1126
  97.7 1.6 slice_convert_fusion.2
  99.3 1.8 reshape.1124
  101.1 1.3 slice_convert_fusion.3
  102.4 1.3 reshape.1131
  103.7 1.3 fusion.93
  105.0 1.4 add.219
  107.6 1.3 reshape.1130
  108.9 1.3 fusion.92
  110.2 1.3 add.216
  112.8 1.3 reshape.1129
  114.1 1.3 fusion.94
  115.4 1.3 add.213
  116.7 1.3 squeeze.6
  118.0 1.3 squeeze.7
  119.4 1.3 squeeze.8
  122.9 1.8 fusion.33
  124.8 2.1 %convolution_convert_fusion = bf16[256,4096]{1,0:T(8,128)(2,1)} fusion(bf16[256,4096]{1,0:T(8,128)(2,1)S(1)} %copy-done, bf16[32,8,2,128]{3,2,1,0:T(2,128)(2,1)S(1)} %bitcast.283), kind=kOutput, calls=%fused_computation | convolution fusion | flops 537919488 | bytes 4325376 | tf_op jit(solution)/shard_map/dot_general | solution.py:159
  128.8 47.8 %reduce-scatter.2.cloned.1.call-done = bf16[32,4096]{1,0:T(8,128)(2,1)} async-done(((bf16[256,4096]{1,0:T(8,128)(2,1)}), bf16[32,4096]{1,0:T(8,128)(2,1)}) %reduce-scatter.2.cloned.1.call-update) | async-done | bytes 262160 | tf_op jit(solution)/shard_map/reduce_scatter | solution.py:160
  (138 shorter events, 38.3 us)
Async XLA Ops:
  7.2 117.6 %copy-start = (bf16[256,4096]{1,0:T(8,128)(2,1)S(1)}, bf16[256,4096]{1,0:T(8,128)(2,1)}, u32[]{:S(2)}) copy-start(bf16[256,4096]{1,0:T(8,128)(2,1)} %param.26) | copy-start | bytes 6291460
  7.2 169.5 %reduce-scatter.2.cloned.1.call-start = ((), (), s32[]{:S(2)}) async-start(), calls=%async_computation.1 | async-start | bytes 2359296 | tf_op jit(solution)/shard_map/reduce_scatter | solution.py:160
  9.8 35.4 %collective-permute-start.4 = (bf16[272,256]{1,0:T(8,128)(2,1)}, bf16[272,256]{1,0:T(8,128)(2,1)}, u32[]{:S(2)}, u32[]{:S(2)}) collective-permute-start(bf16[272,256]{1,0:T(8,128)(2,1)} %pad_maximum_fusion), channel_id=1, source_target_pairs={{0,24},{8,32},{16,40},{24,48},{32,56},{40,64},{48,72},{56,80},{64,... | collective-permute-start | bytes 417800 | tf_op jit(solution)/shard_map/ppermute | solution.py:21
  12.7 40.8 %collective-permute-start.2 = (bf16[272,256]{1,0:T(8,128)(2,1)}, bf16[272,256]{1,0:T(8,128)(2,1)}, u32[]{:S(2)}, u32[]{:S(2)}) collective-permute-start(bf16[272,256]{1,0:T(8,128)(2,1)} %pad_maximum_fusion), channel_id=1, source_target_pairs={{0,16},{8,24},{16,32},{24,40},{32,48},{40,56},{48,64},{56,72},{64,... | collective-permute-start | bytes 417800 | tf_op jit(solution)/shard_map/ppermute | solution.py:21
  16.2 47.1 %collective-permute-start = (bf16[272,256]{1,0:T(8,128)(2,1)}, bf16[272,256]{1,0:T(8,128)(2,1)}, u32[]{:S(2)}, u32[]{:S(2)}) collective-permute-start(bf16[272,256]{1,0:T(8,128)(2,1)} %pad_maximum_fusion), channel_id=1, source_target_pairs={{0,8},{8,16},{16,24},{24,32},{32,40},{40,48},{48,56},{56,64},{64,7... | collective-permute-start | bytes 417800 | tf_op jit(solution)/shard_map/ppermute | solution.py:21
  30.4 4.6 %copy-start.8 = (s32[8,32]{1,0:T(8,128)S(1)}, s32[8,32]{1,0:T(8,128)}, u32[]{:S(2)}) copy-start(s32[8,32]{1,0:T(8,128)} %param.23) | copy-start | bytes 3076
  30.4 7.3 %copy-start.6 = (bf16[256,256]{1,0:T(8,128)(2,1)S(1)}, bf16[256,256]{1,0:T(8,128)(2,1)}, u32[]{:S(2)}) copy-start(bf16[256,256]{1,0:T(8,128)(2,1)} %param.20) | copy-start | bytes 393220
  35.1 0.7 copy-start.15
  35.5 4.5 %copy-start.9 = (s32[8,32]{1,0:T(8,128)}, s32[8,32]{1,0:T(8,128)S(1)}, u32[]{:S(2)}) copy-start(s32[8,32]{1,0:T(8,128)S(1)} %select_reduce_fusion.8) | copy-start | bytes 3076
  35.6 4.4 %copy-start.11 = (s32[8,32]{1,0:T(8,128)}, s32[8,32]{1,0:T(8,128)S(1)}, u32[]{:S(2)}) copy-start(s32[8,32]{1,0:T(8,128)S(1)} %select_reduce_fusion.7) | copy-start | bytes 3076
  35.7 0.6 copy-start.13
  36.3 0.6 copy-start.17
  40.0 4.3 %copy-start.22 = (pred[8,256]{1,0:T(8,128)(4,1)S(1)}, pred[8,256]{1,0:T(8,128)(4,1)}, u32[]{:S(2)}) copy-start(pred[8,256]{1,0:T(8,128)(4,1)} %iota_compare_fusion.10) | copy-start | bytes 6148
  40.0 9.8 %copy-start.3 = (bf16[8,1,256,256]{2,3,0,1:T(8,128)(2,1)S(1)}, bf16[8,1,256,256]{2,3,0,1:T(8,128)(2,1)}, u32[]{:S(2)}) copy-start(bf16[8,1,256,256]{2,3,0,1:T(8,128)(2,1)} %copy.199) | copy-start | bytes 3145732
  42.8 1.5 copy-start.5
  42.8 2.4 %copy-start.19 = (f32[8,32,2]{1,2,0:T(2,128)}, f32[8,32,2]{1,2,0:T(2,128)S(1)}, u32[]{:S(2)}) copy-start(f32[8,32,2]{1,2,0:T(2,128)S(1)} %get-tuple-element.99) | copy-start | bytes 6148
  53.6 14.3 %copy-start.2 = (bf16[8,1,256,256]{2,3,0,1:T(8,128)(2,1)S(1)}, bf16[8,1,256,256]{2,3,0,1:T(8,128)(2,1)}, u32[]{:S(2)}) copy-start(bf16[8,1,256,256]{2,3,0,1:T(8,128)(2,1)} %copy.193) | copy-start | bytes 3145732
  66.4 5.2 %copy-start.20 = (f32[8,32,2]{1,2,0:T(2,128)S(1)}, f32[8,32,2]{1,2,0:T(2,128)}, u32[]{:S(2)}) copy-start(f32[8,32,2]{1,2,0:T(2,128)} %bitcast_reduce_fusion.1) | copy-start | bytes 6148
  74.2 16.6 %collective-permute-start.5 = (bf16[272,256]{1,0:T(8,128)(2,1)}, bf16[272,256]{1,0:T(8,128)(2,1)}, u32[]{:S(2)}, u32[]{:S(2)}) collective-permute-start(bf16[272,256]{1,0:T(8,128)(2,1)} %fusion.51), channel_id=1, source_target_pairs={{0,488},{8,496},{16,504},{24,0},{32,8},{40,16},{48,24},{56,32},{64... | collective-permute-start | bytes 417800 | tf_op jit(solution)/shard_map/ppermute | solution.py:21
  81.8 12.5 %collective-permute-start.3 = (bf16[272,256]{1,0:T(8,128)(2,1)}, bf16[272,256]{1,0:T(8,128)(2,1)}, u32[]{:S(2)}, u32[]{:S(2)}) collective-permute-start(bf16[272,256]{1,0:T(8,128)(2,1)} %fusion.50), channel_id=1, source_target_pairs={{0,496},{8,504},{16,0},{24,8},{32,16},{40,24},{48,32},{56,40},{64,... | collective-permute-start | bytes 417800 | tf_op jit(solution)/shard_map/ppermute | solution.py:21
  87.5 35.4 %copy-start.1 = (bf16[8,1,256,256]{2,3,0,1:T(8,128)(2,1)S(1)}, bf16[8,1,256,256]{2,3,0,1:T(8,128)(2,1)}, u32[]{:S(2)}) copy-start(bf16[8,1,256,256]{2,3,0,1:T(8,128)(2,1)} %copy.191) | copy-start | bytes 3145732
  88.9 8.8 %collective-permute-start.1 = (bf16[272,256]{1,0:T(8,128)(2,1)}, bf16[272,256]{1,0:T(8,128)(2,1)}, u32[]{:S(2)}, u32[]{:S(2)}) collective-permute-start(bf16[272,256]{1,0:T(8,128)(2,1)} %fusion.49), channel_id=1, source_target_pairs={{0,504},{8,0},{16,8},{24,16},{32,24},{40,32},{48,40},{56,48},{64,5... | collective-permute-start | bytes 417800 | tf_op jit(solution)/shard_map/ppermute | solution.py:21
  126.9 0.7 copy-start.23
  126.9 0.7 copy-start.10
  126.9 0.7 copy-start.12
  126.9 0.7 copy-start.14
  126.9 0.7 copy-start.16
  126.9 0.7 copy-start.18
  126.9 49.8 %copy-start.7 = (bf16[32,4096]{1,0:T(8,128)(2,1)S(1)}, bf16[32,4096]{1,0:T(8,128)(2,1)}, u32[]{:S(2)}) copy-start(bf16[32,4096]{1,0:T(8,128)(2,1)} %param.25) | copy-start | bytes 786436
  126.9 50.9 %copy-start.21 = (f32[4096]{0:T(1024)S(1)}, f32[4096]{0:T(1024)}, u32[]{:S(2)}) copy-start(f32[4096]{0:T(1024)} %param.27) | copy-start | bytes 49156
  177.8 0.9 copy-start.4
Sparse Core Ops, SparseCore 0:
  127.1 49.5 reduce-scatter.1

commit v2 on v0

v2 whole, which is shorter than its diff:
```python
import functools

import jax
import jax.numpy as jnp
from jax import lax
from jax.experimental import pallas as pl
from jax.experimental.pallas import tpu as pltpu
from jax.sharding import PartitionSpec as P

HD = 128
TREE = 32
MAXD = 7
PATH = 8
EXTRA = 16
STAT_LANES = 128


NEGATIVE = -1e30


def shifted(value, axis, steps):
    count = lax.axis_size(axis)
    pairs = [(source, (source + steps) % count) for source in range(count)]
    return lax.ppermute(value, axis, pairs)


def ancestors(parents):
    node_ids = jnp.arange(TREE, dtype=jnp.int32)
    current = jnp.broadcast_to(node_ids, parents.shape)
    marked = jnp.zeros(parents.shape + (TREE,), jnp.int32)
    for depth_step in range(MAXD + 1):
        onehot_rows = (current[..., None] == node_ids).astype(jnp.int32)
        marked = jnp.maximum(marked, onehot_rows)
        current = jnp.sum(onehot_rows * parents[..., None, :], axis=-1, dtype=jnp.int32)
    return marked


def attend(query, key, value, valid, round_max):
    scores = lax.dot_general(
        query, key, (((1,), (1,)), ((), ())), preferred_element_type=jnp.float32
    ) * (HD ** (-0.5))
    scores = jnp.where(valid, scores, NEGATIVE)
    largest = jnp.max(scores, axis=1, keepdims=True)
    if round_max:
        largest = largest.astype(jnp.bfloat16).astype(jnp.float32)
    weights = jnp.where(valid, jnp.exp(scores - largest), 0.0)
    totals = jnp.sum(weights, axis=1, keepdims=True)
    weighted = jnp.dot(
        weights.astype(jnp.bfloat16), value, preferred_element_type=jnp.float32
    )
    return largest, totals, weighted


def lane_pick(block, lane):
    lanes = lax.broadcasted_iota(jnp.int32, block.shape, 1)
    return jnp.sum(jnp.where(lanes == lane, block, 0.0), axis=1, keepdims=True)


def holder_kernel(page_index, group, q_ref, qx_ref, kv_ref, out_ref):
    request = pl.program_id(0)
    page_size = kv_ref.shape[0]
    extra = qx_ref[...].astype(jnp.float32)
    length_row = extra[0:1, :] * 16.0 + extra[1:2, :]
    length = lane_pick(length_row, request)
    positions = (
        lax.broadcasted_iota(jnp.int32, (1, page_size), 1) + page_index * page_size
    ).astype(jnp.float32)
    valid = positions < length
    key = kv_ref[:, 0:HD]
    value = kv_ref[:, HD : 2 * HD]
    rows = q_ref.shape[0]
    lanes = lax.broadcasted_iota(jnp.int32, (rows, STAT_LANES), 1)
    stats = jnp.zeros((rows, STAT_LANES), jnp.float32)
    for head in range(group):
        query = q_ref[:, head * HD : (head + 1) * HD]
        largest, totals, weighted = attend(query, key, value, valid, True)
        out_ref[:, head * HD : (head + 1) * HD] = weighted.astype(jnp.bfloat16)
        total_hi = totals.astype(jnp.bfloat16).astype(jnp.float32)
        total_lo = totals - total_hi
        stats = jnp.where(lanes == head, largest, stats)
        stats = jnp.where(lanes == group + head, total_hi, stats)
        stats = jnp.where(lanes == 2 * group + head, total_lo, stats)
    out_ref[:, group * HD : group * HD + STAT_LANES] = stats.astype(jnp.bfloat16)


def holder_partial(packed_queries, kv_pool, page_index, group):
    req_count, page_count, page_size, row_width = kv_pool.shape
    width = packed_queries.shape[1]
    rows = req_count * TREE
    return pl.pallas_call(
        functools.partial(holder_kernel, page_index, group),
        out_shape=jax.ShapeDtypeStruct((rows, width + STAT_LANES), jnp.bfloat16),
        grid=(req_count,),
        in_specs=[
            pl.BlockSpec((TREE, width), lambda r: (r, 0)),
            pl.BlockSpec((EXTRA, width), lambda r: (rows // EXTRA, 0)),
            pl.BlockSpec((None, None, page_size, row_width), lambda r: (r, page_index, 0, 0)),
        ],
        out_specs=pl.BlockSpec((TREE, width + STAT_LANES), lambda r: (r, 0)),
    )(packed_queries, packed_queries, kv_pool)


def home_kernel(group, lens_ref, q_ref, fresh_ref, kv_ref, marked_ref, *rest):
    returned = rest[:-1]
    out_ref = rest[-1]
    request = pl.program_id(0)
    page_size = kv_ref.shape[0]
    length = lens_ref[request]
    page_valid = lax.broadcasted_iota(jnp.int32, (1, page_size), 1) < length
    tree_valid = marked_ref[...] > 0
    for head in range(group):
        query = q_ref[:, head * HD : (head + 1) * HD]
        blocks = [
            attend(query, fresh_ref[:, 0:HD], fresh_ref[:, HD : 2 * HD], tree_valid, False),
            attend(query, kv_ref[:, 0:HD], kv_ref[:, HD : 2 * HD], page_valid, False),
        ]
        for part_ref in returned:
            stats = part_ref[:, group * HD : group * HD + STAT_LANES].astype(jnp.float32)
            largest = lane_pick(stats, head)
            totals = lane_pick(stats, group + head) + lane_pick(stats, 2 * group + head)
            weighted = part_ref[:, head * HD : (head + 1) * HD].astype(jnp.float32)
            blocks.append((largest, totals, weighted))
        top = blocks[0][0]
        for block in blocks[1:]:
            top = jnp.maximum(top, block[0])
        denominator = jnp.zeros_like(top)
        numerator = jnp.zeros(blocks[0][2].shape, jnp.float32)
        for largest, totals, weighted in blocks:
            factor = jnp.exp(largest - top)
            denominator = denominator + factor * totals
            numerator = numerator + factor * weighted
        out_ref[:, head * HD : (head + 1) * HD] = (numerator / denominator).astype(jnp.bfloat16)


def home_attention(cache_lens, queries, new_kv, kv_pool, marked, returned, group):
    req_count, page_count, page_size, row_width = kv_pool.shape
    rows, width = queries.shape
    part_width = returned[0].shape[1]
    in_specs = [
        pl.BlockSpec((TREE, width), lambda r, lens: (r, 0)),
        pl.BlockSpec((TREE, row_width), lambda r, lens: (r, 0)),
        pl.BlockSpec((None, None, page_size, row_width), lambda r, lens: (r, 0, 0, 0)),
        pl.BlockSpec((None, TREE, TREE), lambda r, lens: (r, 0, 0)),
    ] + [pl.BlockSpec((TREE, part_width), lambda r, lens: (r, 0)) for _ in returned]
    return pl.pallas_call(
        functools.partial(home_kernel, group),
        out_shape=jax.ShapeDtypeStruct((rows, width), jnp.bfloat16),
        grid_spec=pltpu.PrefetchScalarGridSpec(
            num_scalar_prefetch=1,
            grid=(req_count,),
            in_specs=in_specs,
            out_specs=pl.BlockSpec((TREE, width), lambda r, lens: (r, 0)),
        ),
    )(cache_lens, queries, new_kv, kv_pool, marked, *returned)


def pack_queries(queries, lengths):
    width = queries.shape[1]
    count = lengths.shape[0]
    pair = jnp.stack([lengths // 16, lengths % 16]).astype(jnp.bfloat16)
    extra = jnp.pad(pair, ((0, EXTRA - 2), (0, width - count)))
    return jnp.concatenate([queries, extra], axis=0)


def per_device(queries, new_kv, kv_pool, cache_lens, parents, accepted, residual, w_out, norm_gain):
    req_count, page_count, page_size, row_width = kv_pool.shape
    kv_local = row_width // (2 * HD)
    q_local = queries.shape[1] // HD
    group = q_local // kv_local
    marked = ancestors(parents)

    packed_queries = pack_queries(queries, cache_lens)
    returned = []
    for page_index in range(1, page_count):
        guest = shifted(packed_queries, "req", page_index)
        part = holder_partial(guest, kv_pool, page_index, group)
        returned.append(shifted(part, "req", -page_index))

    attention = home_attention(cache_lens, queries, new_kv, kv_pool, marked, returned, group)
    product = jnp.dot(attention, w_out, preferred_element_type=jnp.float32)
    summed = lax.psum_scatter(
        lax.optimization_barrier(product.astype(jnp.bfloat16))
        .astype(jnp.float32)
        .astype(jnp.bfloat16),
        "tp",
        scatter_dimension=0,
        tiled=True,
    ).astype(jnp.float32)
    hidden_out = (residual.astype(jnp.float32) + summed).astype(jnp.bfloat16)
    widened = hidden_out.astype(jnp.float32)
    normed = (
        widened * lax.rsqrt(jnp.mean(widened * widened, axis=-1, keepdims=True) + 1e-05) * norm_gain
    ).astype(jnp.bfloat16)
    node_ids = jnp.arange(TREE, dtype=jnp.int32)
    chosen = (accepted[:, None] == node_ids[None, :]).astype(jnp.int32)
    on_path = jnp.sum(chosen[:, :, None] * marked, axis=1, dtype=jnp.int32)
    path_rank = jnp.cumsum(on_path, axis=1, dtype=jnp.int32) - 1
    path_slots = jnp.arange(PATH, dtype=jnp.int32)
    selector = (
        (path_rank[:, None, :] == path_slots[None, :, None]) & (on_path[:, None, :] > 0)
    ).astype(jnp.bfloat16)
    fresh_rows = new_kv.reshape(req_count, TREE, row_width)
    accepted_kv = jnp.einsum(
        "rku,ruc->rkc", selector, fresh_rows, preferred_element_type=jnp.float32
    ).astype(jnp.bfloat16)
    return (hidden_out, normed, accepted_kv)


def solution(mesh):
    placed = (
        P("req", "tp"),
        P("req", "tp"),
        P("req", None, None, "tp"),
        P("req"),
        P("req", None),
        P("req"),
        P(("req", "tp"), None),
        P("tp", None),
        P(),
    )
    return jax.shard_map(
        per_device,
        mesh=mesh,
        in_specs=placed,
        out_specs=(P(("req", "tp"), None), P(("req", "tp"), None), P("req", None, "tp")),
        check_vma=False,
    )
```

time: 156 us -> 141 us (0.904)
  waiting for transfers between devices: 92 us -> 55.5 us
  Pallas kernels: 0 us -> 32.8 us
  local copies, waits for them, and re-layouts: 16.4 us -> 3.3 us
  matrix products: 14.5 us -> 3.72 us
  starting transfers between devices: 11.6 us -> 18.4 us
  other arithmetic: 6.49 us -> 12.4 us
    ppermute x3 -> x6, waiting for transfers between devices: 44.4 us -> 7.45 us  [shifted(): return lax.ppermute(value, axis, pairs)]
    pallas_call x0 -> x4, Pallas kernels: none -> 32.8 us  [the longest x3 22.1 us: holder_partial(): pl.pallas_call(functools.partial(holder_kernel, page_index, group), out_s...]
    dot_general x10 -> x0, matrix products: 11.6 us -> none  [the longest x5 6.77 us: block_partial(): jnp.einsum('rtkgd,rckd->rtkgc', query_rows, key_rows, preferred_element_t...]
    ppermute x3 -> x6, starting transfers between devices: 11.6 us -> 18.3 us  [shifted(): return lax.ppermute(value, axis, pairs)]
    unnamed x32 -> x22, local copies, waits for them, and re-layouts: 9.68 us -> 3.3 us
    reduce_sum x7, other arithmetic: 1.35 us -> 6.8 us  [ancestors(): jnp.sum(onehot_rows * parents[..., None, :], axis=-1, dtype=jnp.int32)]
    slice x2 -> x0, local copies, waits for them, and re-layouts: 4.93 us -> none  [the longest x1 4.03 us: per_device(): page_rows = kv_pool[:, page_index]]
    another operation x1 -> x0, local copies, waits for them, and re-layouts: 1.6 us -> none
  transfers between devices with their start and end apart: 4 -> 7, of which waited for: 4 -> 2; matrix products, arithmetic and copies ran while one was open for 12% -> 7% of each run, Pallas kernels for 0% -> 16%
where the time goes in v2:
time: 141 us; the launch traced here: 140 us
  waiting for transfers between devices  55.5 us (39%)
  Pallas kernels  32.8 us (23%)
  starting transfers between devices  18.4 us (13%)
  between operations  14.2 us (10%)
  other arithmetic  12.4 us (9%)
  matrix products  3.72 us (3%)
  local copies, waits for them, and re-layouts  3.3 us (2%)
    reduce_scatter x1, waiting for transfers between devices, per_device(): lax.psum_scatter(lax.optimization_barrier(product.astype(jnp.bfloat16)).a...  48 us
    pallas_call x3, Pallas kernels, holder_partial(): pl.pallas_call(functools.partial(holder_kernel, page_index, group), out_s...  22.1 us
    ppermute x6, starting transfers between devices, shifted(): return lax.ppermute(value, axis, pairs)  18.3 us
    pallas_call x1, Pallas kernels, home_attention(): pl.pallas_call(functools.partial(home_kernel, group), out_shape=jax.Shape...  10.7 us
    ppermute x6, waiting for transfers between devices, shifted(): return lax.ppermute(value, axis, pairs)  7.45 us
    reduce_sum x7, other arithmetic, ancestors(): jnp.sum(onehot_rows * parents[..., None, :], axis=-1, dtype=jnp.int32)  6.8 us
    unnamed x22, local copies, waits for them, and re-layouts  3.3 us
    dot_general x1, matrix products, per_device(): product = jnp.dot(attention, w_out, preferred_element_type=jnp.float32)  2.97 us
  transfers between devices with their start and end apart: 7, of which 2 were waited for; matrix products, arithmetic and copies ran while one was open for 7% of the time, Pallas kernels for 16%

profile of v2, /device:TPU:6, one launch (start us, length us, event | category | flops | bytes accessed | tf_op | source)
XLA Modules:
  0.0 140.3 jit_solution(1080730586215491209)
XLA Ops:
  7.2 0.0 copy-start
  7.2 0.0 reduce-scatter.2.cloned.1.call-start
  7.2 0.8 convert_bitcast_fusion
  8.0 0.9 pad_maximum_fusion
  9.0 1.9 %collective-permute-start = (bf16[272,256]{1,0:T(8,128)(2,1)S(1)}, bf16[272,256]{1,0:T(8,128)(2,1)S(1)}, u32[]{:S(2)}, u32[]{:S(2)}) collective-permute-start(bf16[272,256]{1,0:T(8,128)(2,1)S(1)} %pad_maximum_fusion), channel_id=1, source_target_pairs={{0,8},{8,16},{16,24},{24,32},{32,40},{40,48},{48,56},{56,64},{64,7... | collective-permute-start | bytes 417800 | tf_op jit(solution)/shard_map/ppermute | solution.py:24
  10.9 3.5 %collective-permute-start.2 = (bf16[272,256]{1,0:T(8,128)(2,1)S(1)}, bf16[272,256]{1,0:T(8,128)(2,1)S(1)}, u32[]{:S(2)}, u32[]{:S(2)}) collective-permute-start(bf16[272,256]{1,0:T(8,128)(2,1)S(1)} %pad_maximum_fusion), channel_id=1, source_target_pairs={{0,16},{8,24},{16,32},{24,40},{32,48},{40,56},{48,64},{56,72},{64,... | collective-permute-start | bytes 417800 | tf_op jit(solution)/shard_map/ppermute | solution.py:24
  14.4 4.5 %collective-permute-start.4 = (bf16[272,256]{1,0:T(8,128)(2,1)S(1)}, bf16[272,256]{1,0:T(8,128)(2,1)S(1)}, u32[]{:S(2)}, u32[]{:S(2)}) collective-permute-start(bf16[272,256]{1,0:T(8,128)(2,1)S(1)} %pad_maximum_fusion), channel_id=1, source_target_pairs={{0,24},{8,32},{16,40},{24,48},{32,56},{40,64},{48,72},{56,80},{64,... | collective-permute-start | bytes 417800 | tf_op jit(solution)/shard_map/ppermute | solution.py:24
  18.9 0.9 select_reduce_fusion.6
  19.8 1.0 select_reduce_fusion.5
  20.8 1.0 select_reduce_fusion.4
  21.8 1.0 select_reduce_fusion.3
  22.8 1.0 select_reduce_fusion.2
  23.7 0.7 fusion.13
  24.5 1.0 select_reduce_fusion.1
  25.5 1.0 select_reduce_fusion
  26.4 0.0 collective-permute-done.q_ref.qx_ref
  26.5 0.0 copy-start.4
  26.5 0.6 copy-done.4
  27.1 7.4 %shard_map.112 = bf16[256,384]{1,0:T(8,128)(2,1)} custom-call(bf16[272,256]{1,0:T(8,128)(2,1)} %copy-done.4, bf16[272,256]{1,0:T(8,128)(2,1)} %copy-done.4, bf16[8,4,256,256]{3,2,1,0:T(8,128)(2,1)} %kv_ref.7), custom_call_target="tpu_custom_call" | custom-call | tf_op jit(solution)/shard_map/pallas_call | solution.py:90
  34.5 4.2 %collective-permute-start.1 = (bf16[256,384]{1,0:T(8,128)(2,1)}, bf16[256,384]{1,0:T(8,128)(2,1)S(1)}, u32[]{:S(2)}, u32[]{:S(2)}) collective-permute-start(bf16[256,384]{1,0:T(8,128)(2,1)} %shard_map.112), channel_id=1, source_target_pairs={{0,504},{8,0},{16,8},{24,16},{32,24},{40,32},{48,40},{56,48},{64,5... | collective-permute-start | bytes 589832 | tf_op jit(solution)/shard_map/ppermute | solution.py:24
  38.7 0.0 collective-permute-done.2.q_ref.qx_ref
  38.7 0.0 copy-start.3
  38.7 0.6 copy-done.3
  39.3 7.4 %shard_map.113 = bf16[256,384]{1,0:T(8,128)(2,1)} custom-call(bf16[272,256]{1,0:T(8,128)(2,1)} %copy-done.3, bf16[272,256]{1,0:T(8,128)(2,1)} %copy-done.3, bf16[8,4,256,256]{3,2,1,0:T(8,128)(2,1)} %kv_ref.7), custom_call_target="tpu_custom_call" | custom-call | tf_op jit(solution)/shard_map/pallas_call | solution.py:90
  46.7 2.3 %collective-permute-start.3 = (bf16[256,384]{1,0:T(8,128)(2,1)}, bf16[256,384]{1,0:T(8,128)(2,1)S(1)}, u32[]{:S(2)}, u32[]{:S(2)}) collective-permute-start(bf16[256,384]{1,0:T(8,128)(2,1)} %shard_map.113), channel_id=1, source_target_pairs={{0,496},{8,504},{16,0},{24,8},{32,16},{40,24},{48,32},{56,40},{64,... | collective-permute-start | bytes 589832 | tf_op jit(solution)/shard_map/ppermute | solution.py:24
  49.1 0.0 collective-permute-done.4.q_ref.qx_ref
  49.1 0.0 copy-start.2
  49.1 0.6 copy-done.2
  49.7 7.4 %shard_map.114 = bf16[256,384]{1,0:T(8,128)(2,1)} custom-call(bf16[272,256]{1,0:T(8,128)(2,1)} %copy-done.2, bf16[272,256]{1,0:T(8,128)(2,1)} %copy-done.2, bf16[8,4,256,256]{3,2,1,0:T(8,128)(2,1)} %kv_ref.7), custom_call_target="tpu_custom_call" | custom-call | tf_op jit(solution)/shard_map/pallas_call | solution.py:90
  57.1 1.9 %collective-permute-start.5 = (bf16[256,384]{1,0:T(8,128)(2,1)}, bf16[256,384]{1,0:T(8,128)(2,1)S(1)}, u32[]{:S(2)}, u32[]{:S(2)}) collective-permute-start(bf16[256,384]{1,0:T(8,128)(2,1)} %shard_map.114), channel_id=1, source_target_pairs={{0,488},{8,496},{16,504},{24,0},{32,8},{40,16},{48,24},{56,32},{64... | collective-permute-start | bytes 589832 | tf_op jit(solution)/shard_map/ppermute | solution.py:24
  59.0 1.0 multiply_reduce_fusion
  60.0 0.0 collective-permute-done.1.rest_0_
  60.0 0.0 collective-permute-done.3.rest_1_
  60.0 0.0 copy-start.8
  60.0 7.4 %collective-permute-done.5.rest_2_ = bf16[256,384]{1,0:T(8,128)(2,1)S(1)} collective-permute-done((bf16[256,384]{1,0:T(8,128)(2,1)}, bf16[256,384]{1,0:T(8,128)(2,1)S(1)}, u32[]{:S(2)}, u32[]{:S(2)}) %collective-permute-start.5) | collective-permute-done | bytes 196640 | tf_op jit(solution)/shard_map/ppermute | solution.py:24
  67.5 0.0 copy-done.7
  67.5 0.0 copy-done.8
  67.5 0.7 copy-done.9
  68.1 10.7 %shard_map.115 = bf16[256,256]{1,0:T(8,128)(2,1)} custom-call(s32[8]{0:T(128)} %lens_ref.1, bf16[256,256]{1,0:T(8,128)(2,1)} %q_ref.1, bf16[256,256]{1,0:T(8,128)(2,1)} %fresh_ref.1, bf16[8,4,256,256]{3,2,1,0:T(8,128)(2,1)} %kv_ref.7, s32[8,32,32]{2,1,0:T(8,128)} %get-tuple-element.6.marked_ref, bf16[256,384]{1,0:T(8,128)(2,1)} %copy-done.7, ...), custom_call_target="tpu_custom_call" | custom-call | tf_op jit(solution)/shard_map/pallas_call | solution.py:145
  78.8 0.0 copy-done
  78.8 3.0 %convolution_convert_fusion = bf16[256,4096]{1,0:T(8,128)(2,1)} fusion(bf16[256,256]{1,0:T(8,128)(2,1)} %shard_map.115, bf16[256,4096]{1,0:T(8,128)(2,1)S(1)} %copy-done), kind=kOutput, calls=%fused_computation | convolution fusion | flops 537919488 | bytes 4325376 | tf_op jit(solution)/shard_map/dot_general | solution.py:180
  81.8 0.0 reduce-scatter.2.cloned.1.call-update
  81.8 0.2 reduce_window_sum.11
  82.0 0.7 copy-done.5
  82.7 0.8 convolution_convert_fusion.1
  83.4 48.0 %reduce-scatter.2.cloned.1.call-done = bf16[32,4096]{1,0:T(8,128)(2,1)} async-done(((bf16[256,4096]{1,0:T(8,128)(2,1)}), bf16[32,4096]{1,0:T(8,128)(2,1)}) %reduce-scatter.2.cloned.1.call-update) | async-done | bytes 262160 | tf_op jit(solution)/shard_map/reduce_scatter | solution.py:181
  131.5 1.2 fusion
  132.7 0.8 fusion.2
  (13 shorter events, 0.0 us)
Async XLA Ops:
  7.2 71.7 %copy-start = (bf16[256,4096]{1,0:T(8,128)(2,1)S(1)}, bf16[256,4096]{1,0:T(8,128)(2,1)}, u32[]{:S(2)}) copy-start(bf16[256,4096]{1,0:T(8,128)(2,1)} %param.16) | copy-start | bytes 6291460
  7.2 124.3 %reduce-scatter.2.cloned.1.call-start = ((), (), s32[]{:S(2)}) async-start(), calls=%async_computation.1 | async-start | bytes 2359296 | tf_op jit(solution)/shard_map/reduce_scatter | solution.py:181
  9.0 17.5 %collective-permute-start = (bf16[272,256]{1,0:T(8,128)(2,1)S(1)}, bf16[272,256]{1,0:T(8,128)(2,1)S(1)}, u32[]{:S(2)}, u32[]{:S(2)}) collective-permute-start(bf16[272,256]{1,0:T(8,128)(2,1)S(1)} %pad_maximum_fusion), channel_id=1, source_target_pairs={{0,8},{8,16},{16,24},{24,32},{32,40},{40,48},{48,56},{56,64},{64,7... | collective-permute-start | bytes 417800 | tf_op jit(solution)/shard_map/ppermute | solution.py:24
  10.9 27.8 %collective-permute-start.2 = (bf16[272,256]{1,0:T(8,128)(2,1)S(1)}, bf16[272,256]{1,0:T(8,128)(2,1)S(1)}, u32[]{:S(2)}, u32[]{:S(2)}) collective-permute-start(bf16[272,256]{1,0:T(8,128)(2,1)S(1)} %pad_maximum_fusion), channel_id=1, source_target_pairs={{0,16},{8,24},{16,32},{24,40},{32,48},{40,56},{48,64},{56,72},{64,... | collective-permute-start | bytes 417800 | tf_op jit(solution)/shard_map/ppermute | solution.py:24
  14.4 34.7 %collective-permute-start.4 = (bf16[272,256]{1,0:T(8,128)(2,1)S(1)}, bf16[272,256]{1,0:T(8,128)(2,1)S(1)}, u32[]{:S(2)}, u32[]{:S(2)}) collective-permute-start(bf16[272,256]{1,0:T(8,128)(2,1)S(1)} %pad_maximum_fusion), channel_id=1, source_target_pairs={{0,24},{8,32},{16,40},{24,48},{32,56},{40,64},{48,72},{56,80},{64,... | collective-permute-start | bytes 417800 | tf_op jit(solution)/shard_map/ppermute | solution.py:24
  26.5 0.7 copy-start.4
  34.5 25.5 %collective-permute-start.1 = (bf16[256,384]{1,0:T(8,128)(2,1)}, bf16[256,384]{1,0:T(8,128)(2,1)S(1)}, u32[]{:S(2)}, u32[]{:S(2)}) collective-permute-start(bf16[256,384]{1,0:T(8,128)(2,1)} %shard_map.112), channel_id=1, source_target_pairs={{0,504},{8,0},{16,8},{24,16},{32,24},{40,32},{48,40},{56,48},{64,5... | collective-permute-start | bytes 589832 | tf_op jit(solution)/shard_map/ppermute | solution.py:24
  38.7 0.6 copy-start.3
  46.7 13.3 %collective-permute-start.3 = (bf16[256,384]{1,0:T(8,128)(2,1)}, bf16[256,384]{1,0:T(8,128)(2,1)S(1)}, u32[]{:S(2)}, u32[]{:S(2)}) collective-permute-start(bf16[256,384]{1,0:T(8,128)(2,1)} %shard_map.113), channel_id=1, source_target_pairs={{0,496},{8,504},{16,0},{24,8},{32,16},{40,24},{48,32},{56,40},{64,... | collective-permute-start | bytes 589832 | tf_op jit(solution)/shard_map/ppermute | solution.py:24
  49.1 0.6 copy-start.2
  57.1 10.4 %collective-permute-start.5 = (bf16[256,384]{1,0:T(8,128)(2,1)}, bf16[256,384]{1,0:T(8,128)(2,1)S(1)}, u32[]{:S(2)}, u32[]{:S(2)}) collective-permute-start(bf16[256,384]{1,0:T(8,128)(2,1)} %shard_map.114), channel_id=1, source_target_pairs={{0,488},{8,496},{16,504},{24,0},{32,8},{40,16},{48,24},{56,32},{64... | collective-permute-start | bytes 589832 | tf_op jit(solution)/shard_map/ppermute | solution.py:24
  60.0 7.5 %copy-start.7 = (bf16[256,384]{1,0:T(8,128)(2,1)}, bf16[256,384]{1,0:T(8,128)(2,1)S(1)}, u32[]{:S(2)}) copy-start(bf16[256,384]{1,0:T(8,128)(2,1)S(1)} %collective-permute-done.1.rest_0_) | copy-start | bytes 589828
  60.0 7.5 %copy-start.8 = (bf16[256,384]{1,0:T(8,128)(2,1)}, bf16[256,384]{1,0:T(8,128)(2,1)S(1)}, u32[]{:S(2)}) copy-start(bf16[256,384]{1,0:T(8,128)(2,1)S(1)} %collective-permute-done.3.rest_1_) | copy-start | bytes 589828
  67.5 0.7 copy-start.9
  81.8 0.9 copy-start.5
  81.8 49.7 %copy-start.6 = (bf16[32,4096]{1,0:T(8,128)(2,1)S(1)}, bf16[32,4096]{1,0:T(8,128)(2,1)}, u32[]{:S(2)}) copy-start(bf16[32,4096]{1,0:T(8,128)(2,1)} %param.15) | copy-start | bytes 786436
  81.8 50.9 %copy-start.10 = (f32[4096]{0:T(1024)S(1)}, f32[4096]{0:T(1024)}, u32[]{:S(2)}) copy-start(f32[4096]{0:T(1024)} %param.17) | copy-start | bytes 49156
  132.6 0.9 copy-start.1
Sparse Core Ops, SparseCore 0:
  81.9 49.4 reduce-scatter.1

commit v3 on v2

v3 whole, which is shorter than its diff:
```python
import functools

import jax
import jax.numpy as jnp
from jax import lax
from jax.experimental import pallas as pl
from jax.experimental.pallas import tpu as pltpu
from jax.sharding import PartitionSpec as P

HD = 128
TREE = 32
MAXD = 7
PATH = 8
EXTRA = 16
STAT_LANES = 128


NEGATIVE = -1e30


def shifted(value, axis, steps):
    count = lax.axis_size(axis)
    pairs = [(source, (source + steps) % count) for source in range(count)]
    return lax.ppermute(value, axis, pairs)


def attend(query, key, value, valid, round_max):
    scores = lax.dot_general(
        query, key, (((1,), (1,)), ((), ())), preferred_element_type=jnp.float32
    ) * (HD ** (-0.5))
    scores = jnp.where(valid, scores, NEGATIVE)
    largest = jnp.max(scores, axis=1, keepdims=True)
    if round_max:
        largest = largest.astype(jnp.bfloat16).astype(jnp.float32)
    weights = jnp.where(valid, jnp.exp(scores - largest), 0.0)
    totals = jnp.sum(weights, axis=1, keepdims=True)
    weighted = jnp.dot(
        weights.astype(jnp.bfloat16), value, preferred_element_type=jnp.float32
    )
    return largest, totals, weighted


def lane_pick(block, lane):
    lanes = lax.broadcasted_iota(jnp.int32, block.shape, 1)
    return jnp.sum(jnp.where(lanes == lane, block, 0.0), axis=1, keepdims=True)


def stacked_heads(rows_ref, row0, group):
    parts = [rows_ref[row0 : row0 + TREE, g * HD : (g + 1) * HD] for g in range(group)]
    return jnp.concatenate(parts, axis=0)


def local_kernel(group, lens_ref, acc_ref, q_ref, fresh_ref, kv_ref, parents_ref,
                 sum_ref, stat_ref, path_ref):
    req_count, page_size = kv_ref.shape[0], kv_ref.shape[1]
    sub = lax.broadcasted_iota(jnp.int32, (TREE, TREE), 0)
    lane = lax.broadcasted_iota(jnp.int32, (TREE, TREE), 1)
    identity = (sub == lane).astype(jnp.float32)
    inclusive = (sub <= lane).astype(jnp.bfloat16)
    parent_cols = parents_ref[...].astype(jnp.float32)
    stat_lanes = lax.broadcasted_iota(jnp.int32, (TREE, STAT_LANES), 1)
    for r in range(req_count):
        row0 = r * TREE
        parent = lane_pick(parent_cols, r)
        reach = jnp.maximum((parent == lane.astype(jnp.float32)).astype(jnp.float32), identity)
        for _ in range(3):
            square = jnp.dot(reach.astype(jnp.bfloat16), reach.astype(jnp.bfloat16),
                             preferred_element_type=jnp.float32)
            reach = jnp.minimum(square, 1.0)
        on_path = jnp.sum(jnp.where(sub == acc_ref[r], reach, 0.0), axis=0, keepdims=True)
        rank = jnp.dot(jnp.broadcast_to(on_path, (8, TREE)).astype(jnp.bfloat16), inclusive,
                       preferred_element_type=jnp.float32)[0:1]
        slot = lax.broadcasted_iota(jnp.int32, (PATH, TREE), 0).astype(jnp.float32)
        selector = jnp.where((rank - 1.0 == slot) & (on_path > 0.5), 1.0, 0.0)
        fresh = fresh_ref[row0 : row0 + TREE, :]
        path_ref[r] = jnp.dot(selector.astype(jnp.bfloat16), fresh,
                              preferred_element_type=jnp.float32).astype(path_ref.dtype)

        query = stacked_heads(q_ref, row0, group)
        tree_valid = jnp.concatenate([reach] * group, axis=0) > 0.5
        length = lens_ref[r]
        page_valid = lax.broadcasted_iota(jnp.int32, (1, page_size), 1) < length
        m1, l1, a1 = attend(query, fresh[:, 0:HD], fresh[:, HD : 2 * HD], tree_valid, False)
        m2, l2, a2 = attend(query, kv_ref[r, :, 0:HD], kv_ref[r, :, HD : 2 * HD], page_valid, False)
        top = jnp.maximum(m1, m2)
        f1 = jnp.exp(m1 - top)
        f2 = jnp.exp(m2 - top)
        totals = f1 * l1 + f2 * l2
        weighted = f1 * a1 + f2 * a2
        stats = jnp.zeros((TREE, STAT_LANES), jnp.float32)
        for g in range(group):
            rows = slice(g * TREE, (g + 1) * TREE)
            sum_ref[row0 : row0 + TREE, g * HD : (g + 1) * HD] = weighted[rows]
            stats = jnp.where(stat_lanes == g, top[rows], stats)
            stats = jnp.where(stat_lanes == group + g, totals[rows], stats)
        stat_ref[row0 : row0 + TREE, :] = stats


def local_partial(cache_lens, accepted, queries, new_kv, kv_pool, parents, group):
    req_count, page_count, page_size, row_width = kv_pool.shape
    rows, width = queries.shape
    vmem = pltpu.MemorySpace.VMEM
    return pl.pallas_call(
        functools.partial(local_kernel, group),
        out_shape=(
            jax.ShapeDtypeStruct((rows, width), jnp.float32),
            jax.ShapeDtypeStruct((rows, STAT_LANES), jnp.float32),
            jax.ShapeDtypeStruct((req_count, PATH, row_width), jnp.bfloat16),
        ),
        grid_spec=pltpu.PrefetchScalarGridSpec(
            num_scalar_prefetch=2,
            grid=(1,),
            in_specs=[
                pl.BlockSpec((rows, width), lambda i, a, b: (0, 0)),
                pl.BlockSpec((rows, row_width), lambda i, a, b: (0, 0)),
                pl.BlockSpec((req_count, None, page_size, row_width), lambda i, a, b: (0, 0, 0, 0)),
                pl.BlockSpec((TREE, req_count), lambda i, a, b: (0, 0)),
            ],
            out_specs=(
                pl.BlockSpec((rows, width), lambda i, a, b: (0, 0)),
                pl.BlockSpec((rows, STAT_LANES), lambda i, a, b: (0, 0)),
                pl.BlockSpec((req_count, PATH, row_width), lambda i, a, b: (0, 0, 0)),
            ),
        ),
    )(cache_lens, accepted, queries, new_kv, kv_pool, parents.T)


def holder_kernel(page_index, group, q_ref, kv_ref, out_ref):
    req_count, page_size = kv_ref.shape[0], kv_ref.shape[1]
    rows = req_count * TREE
    extra = q_ref[rows : rows + EXTRA, :].astype(jnp.float32)
    length_row = extra[0:1, :] * 16.0 + extra[1:2, :]
    positions = (
        lax.broadcasted_iota(jnp.int32, (1, page_size), 1) + page_index * page_size
    ).astype(jnp.float32)
    stat_lanes = lax.broadcasted_iota(jnp.int32, (TREE, STAT_LANES), 1)
    for r in range(req_count):
        row0 = r * TREE
        valid = positions < lane_pick(length_row, r)
        query = stacked_heads(q_ref, row0, group)
        largest, totals, weighted = attend(
            query, kv_ref[r, :, 0:HD], kv_ref[r, :, HD : 2 * HD], valid, True
        )
        total_hi = totals.astype(jnp.bfloat16).astype(jnp.float32)
        total_lo = totals - total_hi
        stats = jnp.zeros((TREE, STAT_LANES), jnp.float32)
        for g in range(group):
            part = slice(g * TREE, (g + 1) * TREE)
            out_ref[row0 : row0 + TREE, g * HD : (g + 1) * HD] = weighted[part].astype(jnp.bfloat16)
            stats = jnp.where(stat_lanes == g, largest[part], stats)
            stats = jnp.where(stat_lanes == group + g, total_hi[part], stats)
            stats = jnp.where(stat_lanes == 2 * group + g, total_lo[part], stats)
        out_ref[row0 : row0 + TREE, group * HD : group * HD + STAT_LANES] = stats.astype(jnp.bfloat16)


def holder_partial(packed_queries, kv_pool, page_index, group):
    req_count, page_count, page_size, row_width = kv_pool.shape
    packed_rows, width = packed_queries.shape
    rows = req_count * TREE
    return pl.pallas_call(
        functools.partial(holder_kernel, page_index, group),
        out_shape=jax.ShapeDtypeStruct((rows, width + STAT_LANES), jnp.bfloat16),
        grid=(1,),
        in_specs=[
            pl.BlockSpec((packed_rows, width), lambda i: (0, 0)),
            pl.BlockSpec((req_count, None, page_size, row_width), lambda i: (0, page_index, 0, 0)),
        ],
        out_specs=pl.BlockSpec((rows, width + STAT_LANES), lambda i: (0, 0)),
    )(packed_queries, kv_pool)


def merge_kernel(group, sum_ref, stat_ref, *rest):
    returned = rest[:-2]
    w_ref = rest[-2]
    out_ref = rest[-1]
    rows = sum_ref.shape[0]
    for r in range(rows // TREE):
        row0 = r * TREE
        local_stats = stat_ref[row0 : row0 + TREE, :]
        heads = []
        for g in range(group):
            cols = slice(g * HD, (g + 1) * HD)
            blocks = [(lane_pick(local_stats, g), lane_pick(local_stats, group + g),
                       sum_ref[row0 : row0 + TREE, cols])]
            for part_ref in returned:
                stats = part_ref[row0 : row0 + TREE, group * HD : group * HD + STAT_LANES].astype(jnp.float32)
                totals = lane_pick(stats, group + g) + lane_pick(stats, 2 * group + g)
                blocks.append((lane_pick(stats, g), totals,
                               part_ref[row0 : row0 + TREE, cols].astype(jnp.float32)))
            top = blocks[0][0]
            for block in blocks[1:]:
                top = jnp.maximum(top, block[0])
            denominator = jnp.zeros_like(top)
            numerator = jnp.zeros((TREE, HD), jnp.float32)
            for largest, totals, weighted in blocks:
                factor = jnp.exp(largest - top)
                denominator = denominator + factor * totals
                numerator = numerator + factor * weighted
            heads.append((numerator / denominator).astype(jnp.bfloat16))
        attention = jnp.concatenate(heads, axis=1)
        out_ref[row0 : row0 + TREE, :] = jnp.dot(
            attention, w_ref[...], preferred_element_type=jnp.float32
        ).astype(out_ref.dtype)


def merge_project(sums, stats, returned, w_out, group):
    rows, width = sums.shape
    part_width = returned[0].shape[1]
    model = w_out.shape[1]
    full = lambda shape: pl.BlockSpec(shape, lambda i: (0, 0))
    return pl.pallas_call(
        functools.partial(merge_kernel, group),
        out_shape=jax.ShapeDtypeStruct((rows, model), jnp.bfloat16),
        grid=(1,),
        in_specs=[full((rows, width)), full((rows, STAT_LANES))]
        + [full((rows, part_width)) for _ in returned]
        + [full(w_out.shape)],
        out_specs=full((rows, model)),
        compiler_params=pltpu.CompilerParams(vmem_limit_bytes=48 * 1024 * 1024),
    )(sums, stats, *returned, w_out)


def pack_queries(queries, lengths):
    width = queries.shape[1]
    count = lengths.shape[0]
    pair = jnp.stack([lengths // 16, lengths % 16]).astype(jnp.bfloat16)
    extra = jnp.pad(pair, ((0, EXTRA - 2), (0, width - count)))
    return jnp.concatenate([queries, extra], axis=0)


def per_device(queries, new_kv, kv_pool, cache_lens, parents, accepted, residual, w_out, norm_gain):
    req_count, page_count, page_size, row_width = kv_pool.shape
    kv_local = row_width // (2 * HD)
    q_local = queries.shape[1] // HD
    group = q_local // kv_local

    packed_queries = pack_queries(queries, cache_lens)
    guests = [shifted(packed_queries, "req", p) for p in range(1, page_count)]
    sums, stats, accepted_kv = local_partial(
        cache_lens, accepted, queries, new_kv, kv_pool, parents, group
    )
    returned = []
    for page_index in range(1, page_count):
        part = holder_partial(guests[page_index - 1], kv_pool, page_index, group)
        returned.append(shifted(part, "req", -page_index))

    product = merge_project(sums, stats, returned, w_out, group)
    summed = lax.psum_scatter(product, "tp", scatter_dimension=0, tiled=True).astype(jnp.float32)
    hidden_out = (residual.astype(jnp.float32) + summed).astype(jnp.bfloat16)
    widened = hidden_out.astype(jnp.float32)
    normed = (
        widened * lax.rsqrt(jnp.mean(widened * widened, axis=-1, keepdims=True) + 1e-05) * norm_gain
    ).astype(jnp.bfloat16)
    return (hidden_out, normed, accepted_kv)


def solution(mesh):
    placed = (
        P("req", "tp"),
        P("req", "tp"),
        P("req", None, None, "tp"),
        P("req"),
        P("req", None),
        P("req"),
        P(("req", "tp"), None),
        P("tp", None),
        P(),
    )
    return jax.shard_map(
        per_device,
        mesh=mesh,
        in_specs=placed,
        out_specs=(P(("req", "tp"), None), P(("req", "tp"), None), P("req", None, "tp")),
        check_vma=False,
    )
```

time: 141 us -> 118 us (0.84)
  other arithmetic: 12.4 us -> 3.59 us
  Pallas kernels: 32.8 us -> 26.4 us
  waiting for transfers between devices: 55.5 us -> 49.5 us
  matrix products: 3.72 us -> 0 us
    pallas_call x3, Pallas kernels: 22.1 us -> 12.1 us  [holder_partial(): pl.pallas_call(functools.partial(holder_kernel, page_index, group), out_s...]
    reduce_sum x8 -> x0, other arithmetic: 7.77 us -> none  [the longest x7 6.8 us: ancestors(): jnp.sum(onehot_rows * parents[..., None, :], axis=-1, dtype=jnp.int32)]
    ppermute x6, waiting for transfers between devices: 7.45 us -> 0.02 us  [shifted(): return lax.ppermute(value, axis, pairs)]
    dot_general x2 -> x0, matrix products: 3.72 us -> none  [the longest x1 2.97 us: per_device(): product = jnp.dot(attention, w_out, preferred_element_type=jnp.float32)]
    pallas_call x1 -> x2, Pallas kernels: 10.7 us -> 14.3 us  [the longest x1 9.81 us: local_partial(): pl.pallas_call(functools.partial(local_kernel, group), out_shape=(jax.Sha...]
    unnamed x22 -> x21, local copies, waits for them, and re-layouts: 3.3 us -> 4.5 us
  transfers between devices with their start and end apart: 7 -> 7, of which waited for: 2 -> 1; matrix products, arithmetic and copies ran while one was open for 7% -> 1% of each run, Pallas kernels for 16% -> 19%
where the time goes in v3:
time: 118 us; the launch traced here: 117 us
  waiting for transfers between devices  49.5 us (42%)
  Pallas kernels  26.4 us (22%)
  starting transfers between devices  18.5 us (16%)
  between operations  14.2 us (12%)
  local copies, waits for them, and re-layouts  4.5 us (4%)
  other arithmetic  3.59 us (3%)
    reduce_scatter x1, waiting for transfers between devices, per_device(): lax.psum_scatter(product, 'tp', scatter_dimension=0, tiled=True)  49.4 us
    ppermute x6, starting transfers between devices, shifted(): return lax.ppermute(value, axis, pairs)  18.5 us
    pallas_call x3, Pallas kernels, holder_partial(): pl.pallas_call(functools.partial(holder_kernel, page_index, group), out_s...  12.1 us
    pallas_call x1, Pallas kernels, local_partial(): pl.pallas_call(functools.partial(local_kernel, group), out_shape=(jax.Sha...  9.81 us
    unnamed x21, local copies, waits for them, and re-layouts  4.5 us
    pallas_call x1, Pallas kernels, merge_project(): pl.pallas_call(functools.partial(merge_kernel, group), out_shape=jax.Shap...  4.49 us
  transfers between devices with their start and end apart: 7, of which 1 were waited for; matrix products, arithmetic and copies ran while one was open for 1% of the time, Pallas kernels for 19%

profile of v3, /device:TPU:6, one launch (start us, length us, event | category | flops | bytes accessed | tf_op | source)
XLA Modules:
  0.0 116.7 jit_solution(4319187859752518689)
XLA Ops:
  7.2 0.0 reduce-scatter.2.cloned.1.call-start
  7.2 0.7 convert_bitcast_fusion
  7.9 0.9 pad_maximum_fusion
  8.8 1.9 %collective-permute-start = (bf16[272,256]{1,0:T(8,128)(2,1)S(1)}, bf16[272,256]{1,0:T(8,128)(2,1)S(1)}, u32[]{:S(2)}, u32[]{:S(2)}) collective-permute-start(bf16[272,256]{1,0:T(8,128)(2,1)S(1)} %pad_maximum_fusion), channel_id=1, source_target_pairs={{0,8},{8,16},{16,24},{24,32},{32,40},{40,48},{48,56},{56,64},{64,7... | collective-permute-start | bytes 417800 | tf_op jit(solution)/shard_map/ppermute | solution.py:24
  10.7 3.5 %collective-permute-start.2 = (bf16[272,256]{1,0:T(8,128)(2,1)S(1)}, bf16[272,256]{1,0:T(8,128)(2,1)S(1)}, u32[]{:S(2)}, u32[]{:S(2)}) collective-permute-start(bf16[272,256]{1,0:T(8,128)(2,1)S(1)} %pad_maximum_fusion), channel_id=1, source_target_pairs={{0,16},{8,24},{16,32},{24,40},{32,48},{40,56},{48,64},{56,72},{64,... | collective-permute-start | bytes 417800 | tf_op jit(solution)/shard_map/ppermute | solution.py:24
  14.2 4.5 %collective-permute-start.4 = (bf16[272,256]{1,0:T(8,128)(2,1)S(1)}, bf16[272,256]{1,0:T(8,128)(2,1)S(1)}, u32[]{:S(2)}, u32[]{:S(2)}) collective-permute-start(bf16[272,256]{1,0:T(8,128)(2,1)S(1)} %pad_maximum_fusion), channel_id=1, source_target_pairs={{0,24},{8,32},{16,40},{24,48},{32,56},{40,64},{48,72},{56,80},{64,... | collective-permute-start | bytes 417800 | tf_op jit(solution)/shard_map/ppermute | solution.py:24
  18.7 0.0 collective-permute-done.q_ref
  18.7 0.0 copy-start.7
  18.8 0.6 copy-done.7
  19.4 4.0 %shard_map.113 = bf16[256,384]{1,0:T(8,128)(2,1)} custom-call(bf16[272,256]{1,0:T(8,128)(2,1)} %copy-done.7, bf16[8,4,256,256]{3,2,1,0:T(8,128)(2,1)} %kv_ref.7), custom_call_target="tpu_custom_call" | custom-call | tf_op jit(solution)/shard_map/pallas_call | solution.py:160
  23.4 4.2 %collective-permute-start.1 = (bf16[256,384]{1,0:T(8,128)(2,1)}, bf16[256,384]{1,0:T(8,128)(2,1)S(1)}, u32[]{:S(2)}, u32[]{:S(2)}) collective-permute-start(bf16[256,384]{1,0:T(8,128)(2,1)} %shard_map.113), channel_id=1, source_target_pairs={{0,504},{8,0},{16,8},{24,16},{32,24},{40,32},{48,40},{56,48},{64,5... | collective-permute-start | bytes 589832 | tf_op jit(solution)/shard_map/ppermute | solution.py:24
  27.6 0.0 collective-permute-done.2.q_ref
  27.6 0.0 copy-start.6
  27.6 0.6 copy-done.6
  28.3 4.0 %shard_map.114 = bf16[256,384]{1,0:T(8,128)(2,1)} custom-call(bf16[272,256]{1,0:T(8,128)(2,1)} %copy-done.6, bf16[8,4,256,256]{3,2,1,0:T(8,128)(2,1)} %kv_ref.7), custom_call_target="tpu_custom_call" | custom-call | tf_op jit(solution)/shard_map/pallas_call | solution.py:160
  32.3 0.0 copy-start.9
  32.3 2.5 %collective-permute-start.3 = (bf16[256,384]{1,0:T(8,128)(2,1)}, bf16[256,384]{1,0:T(8,128)(2,1)S(1)}, u32[]{:S(2)}, u32[]{:S(2)}) collective-permute-start(bf16[256,384]{1,0:T(8,128)(2,1)} %shard_map.114), channel_id=1, source_target_pairs={{0,496},{8,504},{16,0},{24,8},{32,16},{40,24},{48,32},{56,40},{64,... | collective-permute-start | bytes 589832 | tf_op jit(solution)/shard_map/ppermute | solution.py:24
  34.8 0.0 collective-permute-done.4.q_ref
  34.8 0.0 copy-start.5
  34.9 0.6 copy-done.5
  35.5 4.1 %shard_map.115 = bf16[256,384]{1,0:T(8,128)(2,1)} custom-call(bf16[272,256]{1,0:T(8,128)(2,1)} %copy-done.5, bf16[8,4,256,256]{3,2,1,0:T(8,128)(2,1)} %kv_ref.7), custom_call_target="tpu_custom_call" | custom-call | tf_op jit(solution)/shard_map/pallas_call | solution.py:160
  39.6 1.9 %collective-permute-start.5 = (bf16[256,384]{1,0:T(8,128)(2,1)}, bf16[256,384]{1,0:T(8,128)(2,1)S(1)}, u32[]{:S(2)}, u32[]{:S(2)}) collective-permute-start(bf16[256,384]{1,0:T(8,128)(2,1)} %shard_map.115), channel_id=1, source_target_pairs={{0,488},{8,496},{16,504},{24,0},{32,8},{40,16},{48,24},{56,32},{64... | collective-permute-start | bytes 589832 | tf_op jit(solution)/shard_map/ppermute | solution.py:24
  41.5 0.0 copy-done.9
  41.5 0.7 copy.12
  42.2 0.0 copy-start
  42.2 9.8 %shard_map.112 = (f32[256,256]{1,0:T(8,128)}, f32[256,128]{1,0:T(8,128)}, bf16[8,8,256]{2,1,0:T(8,128)(2,1)}) custom-call(s32[8]{0:T(128)} %lens_ref.1, s32[8]{0:T(128)} %acc_ref.1, bf16[256,256]{1,0:T(8,128)(2,1)} %q_ref.1, bf16[256,256]{1,0:T(8,128)(2,1)} %fresh_ref.1, bf16[8,4,256,256]{3,2,1,0:T(8,128)(2,1)} %kv_ref.7, s32[32,8]{1,0:T(8,128)} %bitcast.5), custom_call_target="tpu_custom_call" | custom-call | tf_op jit(solution)/shard_map/pallas_call | solution.py:103
  52.0 0.0 collective-permute-done.1.rest_0_
  52.0 0.0 collective-permute-done.3.rest_1_
  52.0 0.0 collective-permute-done.5.rest_2_
  52.0 0.0 copy-done
  52.0 0.0 copy-start.1
  52.0 0.9 copy-done.1
  52.9 0.0 copy-start.2
  52.9 0.9 copy-done.2
  53.8 4.5 %shard_map.116 = bf16[256,4096]{1,0:T(8,128)(2,1)} custom-call(f32[256,256]{1,0:T(8,128)S(1)} %copy-done.1, f32[256,128]{1,0:T(8,128)S(1)} %copy-done.2, bf16[256,384]{1,0:T(8,128)(2,1)S(1)} %collective-permute-done.1.rest_0_, bf16[256,384]{1,0:T(8,128)(2,1)S(1)} %collective-permute-done.3.rest_1_, bf16[256,384]{1,0:T(8,128)(2,1)S(1)} %collective-permute-done.5.rest_2_, ...), custom_call_target="tpu_custom_call" | custom-call | tf_op jit(solution)/shard_map/pallas_call | solution.py:211
  58.3 0.0 copy-start.4
  58.3 0.0 copy-start.8
  58.3 0.0 reduce-scatter.2.cloned.1.call-update
  58.4 49.4 %reduce-scatter.2.cloned.1.call-done = bf16[32,4096]{1,0:T(8,128)(2,1)} async-done(((bf16[256,4096]{1,0:T(8,128)(2,1)}), bf16[32,4096]{1,0:T(8,128)(2,1)}) %reduce-scatter.2.cloned.1.call-update) | async-done | bytes 262160 | tf_op jit(solution)/shard_map/reduce_scatter | solution.py:248
  107.8 0.0 copy-done.4
  107.8 1.2 fusion
  108.9 0.0 copy-start.3
  109.0 0.0 copy-done.8
  109.0 0.8 fusion.2
  109.8 0.0 copy-done.3
  (2 shorter events, 0.0 us)
Async XLA Ops:
  7.2 100.6 %reduce-scatter.2.cloned.1.call-start = ((), (), s32[]{:S(2)}) async-start(), calls=%async_computation.1 | async-start | bytes 2359296 | tf_op jit(solution)/shard_map/reduce_scatter | solution.py:248
  8.8 9.9 %collective-permute-start = (bf16[272,256]{1,0:T(8,128)(2,1)S(1)}, bf16[272,256]{1,0:T(8,128)(2,1)S(1)}, u32[]{:S(2)}, u32[]{:S(2)}) collective-permute-start(bf16[272,256]{1,0:T(8,128)(2,1)S(1)} %pad_maximum_fusion), channel_id=1, source_target_pairs={{0,8},{8,16},{16,24},{24,32},{32,40},{40,48},{48,56},{56,64},{64,7... | collective-permute-start | bytes 417800 | tf_op jit(solution)/shard_map/ppermute | solution.py:24
  10.7 16.9 %collective-permute-start.2 = (bf16[272,256]{1,0:T(8,128)(2,1)S(1)}, bf16[272,256]{1,0:T(8,128)(2,1)S(1)}, u32[]{:S(2)}, u32[]{:S(2)}) collective-permute-start(bf16[272,256]{1,0:T(8,128)(2,1)S(1)} %pad_maximum_fusion), channel_id=1, source_target_pairs={{0,16},{8,24},{16,32},{24,40},{32,48},{40,56},{48,64},{56,72},{64,... | collective-permute-start | bytes 417800 | tf_op jit(solution)/shard_map/ppermute | solution.py:24
  14.2 20.6 %collective-permute-start.4 = (bf16[272,256]{1,0:T(8,128)(2,1)S(1)}, bf16[272,256]{1,0:T(8,128)(2,1)S(1)}, u32[]{:S(2)}, u32[]{:S(2)}) collective-permute-start(bf16[272,256]{1,0:T(8,128)(2,1)S(1)} %pad_maximum_fusion), channel_id=1, source_target_pairs={{0,24},{8,32},{16,40},{24,48},{32,56},{40,64},{48,72},{56,80},{64,... | collective-permute-start | bytes 417800 | tf_op jit(solution)/shard_map/ppermute | solution.py:24
  18.7 0.7 copy-start.7
  23.4 28.5 %collective-permute-start.1 = (bf16[256,384]{1,0:T(8,128)(2,1)}, bf16[256,384]{1,0:T(8,128)(2,1)S(1)}, u32[]{:S(2)}, u32[]{:S(2)}) collective-permute-start(bf16[256,384]{1,0:T(8,128)(2,1)} %shard_map.113), channel_id=1, source_target_pairs={{0,504},{8,0},{16,8},{24,16},{32,24},{40,32},{48,40},{56,48},{64,5... | collective-permute-start | bytes 589832 | tf_op jit(solution)/shard_map/ppermute | solution.py:24
  27.6 0.7 copy-start.6
  32.3 9.1 %copy-start.9 = (s32[8,32]{1,0:T(8,128)S(1)}, s32[8,32]{1,0:T(8,128)}, u32[]{:S(2)}) copy-start(s32[8,32]{1,0:T(8,128)} %param.13) | copy-start | bytes 3076
  32.3 19.6 %collective-permute-start.3 = (bf16[256,384]{1,0:T(8,128)(2,1)}, bf16[256,384]{1,0:T(8,128)(2,1)S(1)}, u32[]{:S(2)}, u32[]{:S(2)}) collective-permute-start(bf16[256,384]{1,0:T(8,128)(2,1)} %shard_map.114), channel_id=1, source_target_pairs={{0,496},{8,504},{16,0},{24,8},{32,16},{40,24},{48,32},{56,40},{64,... | collective-permute-start | bytes 589832 | tf_op jit(solution)/shard_map/ppermute | solution.py:24
  34.8 0.7 copy-start.5
  39.6 12.4 %collective-permute-start.5 = (bf16[256,384]{1,0:T(8,128)(2,1)}, bf16[256,384]{1,0:T(8,128)(2,1)S(1)}, u32[]{:S(2)}, u32[]{:S(2)}) collective-permute-start(bf16[256,384]{1,0:T(8,128)(2,1)} %shard_map.115), channel_id=1, source_target_pairs={{0,488},{8,496},{16,504},{24,0},{32,8},{40,16},{48,24},{56,32},{64... | collective-permute-start | bytes 589832 | tf_op jit(solution)/shard_map/ppermute | solution.py:24
  42.2 9.8 %copy-start = (bf16[256,4096]{1,0:T(8,128)(2,1)S(1)}, bf16[256,4096]{1,0:T(8,128)(2,1)}, u32[]{:S(2)}) copy-start(bf16[256,4096]{1,0:T(8,128)(2,1)} %rest_3_.1) | copy-start | bytes 6291460
  52.0 1.0 copy-start.1
  52.9 0.9 copy-start.2
  58.3 49.5 %copy-start.4 = (bf16[32,4096]{1,0:T(8,128)(2,1)S(1)}, bf16[32,4096]{1,0:T(8,128)(2,1)}, u32[]{:S(2)}) copy-start(bf16[32,4096]{1,0:T(8,128)(2,1)} %param.15) | copy-start | bytes 786436
  58.3 50.6 %copy-start.8 = (f32[4096]{0:T(1024)S(1)}, f32[4096]{0:T(1024)}, u32[]{:S(2)}) copy-start(f32[4096]{0:T(1024)} %param.17) | copy-start | bytes 49156
  108.9 0.9 copy-start.3
Sparse Core Ops, SparseCore 0:
  58.5 49.2 reduce-scatter.1

commit v4 on v3

--- a/solution.py
+++ b/solution.py
@@ -245,7 +245,10 @@
         returned.append(shifted(part, "req", -page_index))
 
     product = merge_project(sums, stats, returned, w_out, group)
-    summed = lax.psum_scatter(product, "tp", scatter_dimension=0, tiled=True).astype(jnp.float32)
+    tp_count = lax.axis_size("tp")
+    pieces = product.reshape(tp_count, product.shape[0] // tp_count, product.shape[1])
+    gathered = lax.all_to_all(pieces, "tp", 0, 0, tiled=False)
+    summed = jnp.sum(gathered.astype(jnp.float32), axis=0)
     hidden_out = (residual.astype(jnp.float32) + summed).astype(jnp.bfloat16)
     widened = hidden_out.astype(jnp.float32)
     normed = (

time: 118 us -> 118 us (level)
  the two profiles are of different devices: /device:TPU:6 before, /device:TPU:1 now
where the time goes in v4:
time: 118 us; the launch traced here: 117 us
  blocking collectives  56.8 us (48%)
  starting transfers between devices  26.6 us (23%)
  Pallas kernels  25.1 us (21%)
  local copies, waits for them, and re-layouts  5.14 us (4%)
  other arithmetic  2.92 us (2%)
    all_to_all x1, blocking collectives, per_device(): gathered = lax.all_to_all(pieces, 'tp', 0, 0, tiled=False)  56.8 us
    ppermute x6, starting transfers between devices, shifted(): return lax.ppermute(value, axis, pairs)  26.6 us
    pallas_call x3, Pallas kernels, holder_partial(): pl.pallas_call(functools.partial(holder_kernel, page_index, group), out_s...  12.1 us
    pallas_call x1, Pallas kernels, local_partial(): pl.pallas_call(functools.partial(local_kernel, group), out_shape=(jax.Sha...  9.81 us
    unnamed x21, local copies, waits for them, and re-layouts  5.14 us
    pallas_call x1, Pallas kernels, merge_project(): pl.pallas_call(functools.partial(merge_kernel, group), out_shape=jax.Shap...  3.14 us
  transfers between devices with their start and end apart: 6, of which 0 were waited for; matrix products, arithmetic and copies ran while one was open for 1% of the time, Pallas kernels for 19%

profile of v4, /device:TPU:1, one launch (start us, length us, event | category | flops | bytes accessed | tf_op | source)
XLA Modules:
  0.0 117.3 jit_solution(4725873127280744722)
XLA Ops:
  0.6 0.7 convert_bitcast_fusion
  1.3 0.9 pad_maximum_fusion
  2.2 4.6 %collective-permute-start = (bf16[272,256]{1,0:T(8,128)(2,1)S(1)}, bf16[272,256]{1,0:T(8,128)(2,1)S(1)}, u32[]{:S(2)}, u32[]{:S(2)}) collective-permute-start(bf16[272,256]{1,0:T(8,128)(2,1)S(1)} %pad_maximum_fusion), channel_id=1, source_target_pairs={{0,8},{8,16},{16,24},{24,32},{32,40},{40,48},{48,56},{56,64},{64,7... | collective-permute-start | bytes 417800 | tf_op jit(solution)/shard_map/ppermute | solution.py:24
  6.8 3.2 %collective-permute-start.2 = (bf16[272,256]{1,0:T(8,128)(2,1)S(1)}, bf16[272,256]{1,0:T(8,128)(2,1)S(1)}, u32[]{:S(2)}, u32[]{:S(2)}) collective-permute-start(bf16[272,256]{1,0:T(8,128)(2,1)S(1)} %pad_maximum_fusion), channel_id=1, source_target_pairs={{0,16},{8,24},{16,32},{24,40},{32,48},{40,56},{48,64},{56,72},{64,... | collective-permute-start | bytes 417800 | tf_op jit(solution)/shard_map/ppermute | solution.py:24
  10.0 3.2 %collective-permute-start.4 = (bf16[272,256]{1,0:T(8,128)(2,1)S(1)}, bf16[272,256]{1,0:T(8,128)(2,1)S(1)}, u32[]{:S(2)}, u32[]{:S(2)}) collective-permute-start(bf16[272,256]{1,0:T(8,128)(2,1)S(1)} %pad_maximum_fusion), channel_id=1, source_target_pairs={{0,24},{8,32},{16,40},{24,48},{32,56},{40,64},{48,72},{56,80},{64,... | collective-permute-start | bytes 417800 | tf_op jit(solution)/shard_map/ppermute | solution.py:24
  13.3 0.0 collective-permute-done.q_ref
  13.3 0.0 copy-start.7
  13.3 0.6 copy-done.7
  13.9 4.0 %shard_map.113 = bf16[256,384]{1,0:T(8,128)(2,1)} custom-call(bf16[272,256]{1,0:T(8,128)(2,1)} %copy-done.7, bf16[8,4,256,256]{3,2,1,0:T(8,128)(2,1)} %kv_ref.7), custom_call_target="tpu_custom_call" | custom-call | tf_op jit(solution)/shard_map/pallas_call | solution.py:160
  18.0 7.4 %collective-permute-start.1 = (bf16[256,384]{1,0:T(8,128)(2,1)}, bf16[256,384]{1,0:T(8,128)(2,1)S(1)}, u32[]{:S(2)}, u32[]{:S(2)}) collective-permute-start(bf16[256,384]{1,0:T(8,128)(2,1)} %shard_map.113), channel_id=1, source_target_pairs={{0,504},{8,0},{16,8},{24,16},{32,24},{40,32},{48,40},{56,48},{64,5... | collective-permute-start | bytes 589832 | tf_op jit(solution)/shard_map/ppermute | solution.py:24
  25.4 0.0 collective-permute-done.2.q_ref
  25.4 0.0 copy-start.6
  25.4 0.6 copy-done.6
  26.1 4.0 %shard_map.114 = bf16[256,384]{1,0:T(8,128)(2,1)} custom-call(bf16[272,256]{1,0:T(8,128)(2,1)} %copy-done.6, bf16[8,4,256,256]{3,2,1,0:T(8,128)(2,1)} %kv_ref.7), custom_call_target="tpu_custom_call" | custom-call | tf_op jit(solution)/shard_map/pallas_call | solution.py:160
  30.1 0.0 copy-start.9
  30.1 3.2 %collective-permute-start.3 = (bf16[256,384]{1,0:T(8,128)(2,1)}, bf16[256,384]{1,0:T(8,128)(2,1)S(1)}, u32[]{:S(2)}, u32[]{:S(2)}) collective-permute-start(bf16[256,384]{1,0:T(8,128)(2,1)} %shard_map.114), channel_id=1, source_target_pairs={{0,496},{8,504},{16,0},{24,8},{32,16},{40,24},{48,32},{56,40},{64,... | collective-permute-start | bytes 589832 | tf_op jit(solution)/shard_map/ppermute | solution.py:24
  33.3 0.0 collective-permute-done.4.q_ref
  33.3 0.0 copy-start.5
  33.3 0.6 copy-done.5
  34.0 4.0 %shard_map.115 = bf16[256,384]{1,0:T(8,128)(2,1)} custom-call(bf16[272,256]{1,0:T(8,128)(2,1)} %copy-done.5, bf16[8,4,256,256]{3,2,1,0:T(8,128)(2,1)} %kv_ref.7), custom_call_target="tpu_custom_call" | custom-call | tf_op jit(solution)/shard_map/pallas_call | solution.py:160
  38.0 5.0 %collective-permute-start.5 = (bf16[256,384]{1,0:T(8,128)(2,1)}, bf16[256,384]{1,0:T(8,128)(2,1)S(1)}, u32[]{:S(2)}, u32[]{:S(2)}) collective-permute-start(bf16[256,384]{1,0:T(8,128)(2,1)} %shard_map.115), channel_id=1, source_target_pairs={{0,488},{8,496},{16,504},{24,0},{32,8},{40,16},{48,24},{56,32},{64... | collective-permute-start | bytes 589832 | tf_op jit(solution)/shard_map/ppermute | solution.py:24
  43.0 0.0 copy-done.9
  43.0 0.7 copy.12
  43.7 0.0 copy-start
  43.7 9.8 %shard_map.112 = (f32[256,256]{1,0:T(8,128)}, f32[256,128]{1,0:T(8,128)}, bf16[8,8,256]{2,1,0:T(8,128)(2,1)}) custom-call(s32[8]{0:T(128)} %lens_ref.1, s32[8]{0:T(128)} %acc_ref.1, bf16[256,256]{1,0:T(8,128)(2,1)} %q_ref.1, bf16[256,256]{1,0:T(8,128)(2,1)} %fresh_ref.1, bf16[8,4,256,256]{3,2,1,0:T(8,128)(2,1)} %kv_ref.7, s32[32,8]{1,0:T(8,128)} %bitcast.7), custom_call_target="tpu_custom_call" | custom-call | tf_op jit(solution)/shard_map/pallas_call | solution.py:103
  53.5 0.0 collective-permute-done.1.rest_0_
  53.5 0.0 collective-permute-done.3.rest_1_
  53.5 0.0 collective-permute-done.5.rest_2_
  53.5 0.0 copy-done
  53.5 0.0 copy-start.1
  53.5 0.9 copy-done.1
  54.5 0.0 copy-start.2
  54.5 0.9 copy-done.2
  55.4 3.1 %shard_map.116 = bf16[256,4096]{1,0:T(8,128)(2,1)S(1)} custom-call(f32[256,256]{1,0:T(8,128)S(1)} %copy-done.1, f32[256,128]{1,0:T(8,128)S(1)} %copy-done.2, bf16[256,384]{1,0:T(8,128)(2,1)S(1)} %collective-permute-done.1.rest_0_, bf16[256,384]{1,0:T(8,128)(2,1)S(1)} %collective-permute-done.3.rest_1_, bf16[256,384]{1,0:T(8,128)(2,1)S(1)} %collective-permute-done.5.rest_2_, ...), custom_call_target="tpu_custom_call" | custom-call | tf_op jit(solution)/shard_map/pallas_call | solution.py:211
  58.5 56.8 %all_to_all.5 = bf16[8,32,4096]{2,1,0:T(8,128)(2,1)S(1)} all-to-all(bf16[8,32,4096]{2,1,0:T(8,128)(2,1)S(1)} %bitcast.6), channel_id=1, replica_groups=mesh['req'=64,'tp'=8] {'tp'}, dimensions={0} | all-to-all | bytes 4194304 | tf_op jit(solution)/shard_map/all_to_all | solution.py:250
  115.3 0.0 copy-start.4
  115.3 0.0 copy-start.8
  115.3 0.3 convert_reduce_fusion
  115.6 0.6 copy-done.4
  116.2 0.2 fusion
  116.4 0.0 copy-start.3
  116.4 0.0 copy-done.8
  116.5 0.8 fusion.2
  117.3 0.0 copy-done.3
  (2 shorter events, 0.0 us)
Async XLA Ops:
  2.2 11.0 %collective-permute-start = (bf16[272,256]{1,0:T(8,128)(2,1)S(1)}, bf16[272,256]{1,0:T(8,128)(2,1)S(1)}, u32[]{:S(2)}, u32[]{:S(2)}) collective-permute-start(bf16[272,256]{1,0:T(8,128)(2,1)S(1)} %pad_maximum_fusion), channel_id=1, source_target_pairs={{0,8},{8,16},{16,24},{24,32},{32,40},{40,48},{48,56},{56,64},{64,7... | collective-permute-start | bytes 417800 | tf_op jit(solution)/shard_map/ppermute | solution.py:24
  6.8 18.6 %collective-permute-start.2 = (bf16[272,256]{1,0:T(8,128)(2,1)S(1)}, bf16[272,256]{1,0:T(8,128)(2,1)S(1)}, u32[]{:S(2)}, u32[]{:S(2)}) collective-permute-start(bf16[272,256]{1,0:T(8,128)(2,1)S(1)} %pad_maximum_fusion), channel_id=1, source_target_pairs={{0,16},{8,24},{16,32},{24,40},{32,48},{40,56},{48,64},{56,72},{64,... | collective-permute-start | bytes 417800 | tf_op jit(solution)/shard_map/ppermute | solution.py:24
  10.0 23.3 %collective-permute-start.4 = (bf16[272,256]{1,0:T(8,128)(2,1)S(1)}, bf16[272,256]{1,0:T(8,128)(2,1)S(1)}, u32[]{:S(2)}, u32[]{:S(2)}) collective-permute-start(bf16[272,256]{1,0:T(8,128)(2,1)S(1)} %pad_maximum_fusion), channel_id=1, source_target_pairs={{0,24},{8,32},{16,40},{24,48},{32,56},{40,64},{48,72},{56,80},{64,... | collective-permute-start | bytes 417800 | tf_op jit(solution)/shard_map/ppermute | solution.py:24
  13.3 0.7 copy-start.7
  18.0 35.5 %collective-permute-start.1 = (bf16[256,384]{1,0:T(8,128)(2,1)}, bf16[256,384]{1,0:T(8,128)(2,1)S(1)}, u32[]{:S(2)}, u32[]{:S(2)}) collective-permute-start(bf16[256,384]{1,0:T(8,128)(2,1)} %shard_map.113), channel_id=1, source_target_pairs={{0,504},{8,0},{16,8},{24,16},{32,24},{40,32},{48,40},{56,48},{64,5... | collective-permute-start | bytes 589832 | tf_op jit(solution)/shard_map/ppermute | solution.py:24
  25.4 0.7 copy-start.6
  30.1 12.9 %copy-start.9 = (s32[8,32]{1,0:T(8,128)S(1)}, s32[8,32]{1,0:T(8,128)}, u32[]{:S(2)}) copy-start(s32[8,32]{1,0:T(8,128)} %param.13) | copy-start | bytes 3076
  30.1 23.4 %collective-permute-start.3 = (bf16[256,384]{1,0:T(8,128)(2,1)}, bf16[256,384]{1,0:T(8,128)(2,1)S(1)}, u32[]{:S(2)}, u32[]{:S(2)}) collective-permute-start(bf16[256,384]{1,0:T(8,128)(2,1)} %shard_map.114), channel_id=1, source_target_pairs={{0,496},{8,504},{16,0},{24,8},{32,16},{40,24},{48,32},{56,40},{64,... | collective-permute-start | bytes 589832 | tf_op jit(solution)/shard_map/ppermute | solution.py:24
  33.3 0.7 copy-start.5
  38.0 15.5 %collective-permute-start.5 = (bf16[256,384]{1,0:T(8,128)(2,1)}, bf16[256,384]{1,0:T(8,128)(2,1)S(1)}, u32[]{:S(2)}, u32[]{:S(2)}) collective-permute-start(bf16[256,384]{1,0:T(8,128)(2,1)} %shard_map.115), channel_id=1, source_target_pairs={{0,488},{8,496},{16,504},{24,0},{32,8},{40,16},{48,24},{56,32},{64... | collective-permute-start | bytes 589832 | tf_op jit(solution)/shard_map/ppermute | solution.py:24
  43.7 9.8 %copy-start = (bf16[256,4096]{1,0:T(8,128)(2,1)S(1)}, bf16[256,4096]{1,0:T(8,128)(2,1)}, u32[]{:S(2)}) copy-start(bf16[256,4096]{1,0:T(8,128)(2,1)} %rest_3_.1) | copy-start | bytes 6291460
  53.5 1.0 copy-start.1
  54.5 0.9 copy-start.2
  115.3 1.0 copy-start.4
  115.3 1.2 copy-start.8
  116.4 0.9 copy-start.3

commit v5 on v4

--- a/solution.py
+++ b/solution.py
@@ -50,38 +50,82 @@
     return jnp.concatenate(parts, axis=0)
 
 
-def local_kernel(group, lens_ref, acc_ref, q_ref, fresh_ref, kv_ref, parents_ref,
-                 sum_ref, stat_ref, path_ref):
+def tree_kernel(group, acc_ref, q_ref, fresh_ref, parent_ref, part_ref, path_ref):
+    rows = fresh_ref.shape[0]
+    req_count = rows // TREE
+    sub = lax.broadcasted_iota(jnp.int32, (rows, rows), 0)
+    lane = lax.broadcasted_iota(jnp.int32, (rows, rows), 1)
+    same_block = (sub // TREE) == (lane // TREE)
+    reach = jnp.where((parent_ref[...] == lane) | (sub == lane), 1.0, 0.0)
+    for _ in range(3):
+        square = jnp.dot(reach.astype(jnp.bfloat16), reach.astype(jnp.bfloat16),
+                         preferred_element_type=jnp.float32)
+        reach = jnp.minimum(square, 1.0)
+    inclusive = jnp.where(same_block & (sub <= lane), 1.0, 0.0).astype(jnp.bfloat16)
+    sel_sub = lax.broadcasted_iota(jnp.int32, (req_count * PATH, rows), 0)
+    sel_lane = lax.broadcasted_iota(jnp.int32, (req_count * PATH, rows), 1)
+    chosen = jnp.zeros((req_count * PATH, rows), jnp.float32)
+    for r in range(req_count):
+        target = r * TREE + acc_ref[r]
+        chosen = jnp.where((sel_sub // PATH == r) & (sel_lane == target), 1.0, chosen)
+    on_path = jnp.dot(chosen.astype(jnp.bfloat16), reach.astype(jnp.bfloat16),
+                      preferred_element_type=jnp.float32)
+    rank = jnp.dot(on_path.astype(jnp.bfloat16), inclusive, preferred_element_type=jnp.float32)
+    slot = (sel_sub % PATH).astype(jnp.float32)
+    selector = jnp.where((rank - 1.0 == slot) & (on_path > 0.5), 1.0, 0.0)
+    path = jnp.dot(selector.astype(jnp.bfloat16), fresh_ref[...],
+                   preferred_element_type=jnp.float32).astype(path_ref.dtype)
+    for r in range(req_count):
+        path_ref[r] = path[r * PATH : (r + 1) * PATH]
+
+    valid = jnp.concatenate([reach > 0.5] * group, axis=0)
+    query = jnp.concatenate([q_ref[:, g * HD : (g + 1) * HD] for g in range(group)], axis=0)
+    largest, totals, weighted = attend(query, fresh_ref[:, 0:HD], fresh_ref[:, HD : 2 * HD], valid, False)
+    stat_lanes = lax.broadcasted_iota(jnp.int32, (rows, STAT_LANES), 1)
+    stats = jnp.zeros((rows, STAT_LANES), jnp.float32)
+    for g in range(group):
+        part = slice(g * rows, (g + 1) * rows)
+        stats = jnp.where(stat_lanes == g, largest[part], stats)
+        stats = jnp.where(stat_lanes == group + g, totals[part], stats)
+        part_ref[:, g * HD : (g + 1) * HD] = weighted[part]
+    part_ref[:, group * HD : group * HD + STAT_LANES] = stats
+
+
+def tree_partial(accepted, queries, new_kv, parents, group):
+    rows, width = queries.shape
+    req_count = parents.shape[0]
+    row_width = new_kv.shape[1]
+    offsets = TREE * jnp.arange(req_count, dtype=jnp.int32)[:, None]
+    parent_rows = (parents + offsets).reshape(rows, 1)
+    full = lambda shape: pl.BlockSpec(shape, lambda i, a: (0,) * len(shape))
+    return pl.pallas_call(
+        functools.partial(tree_kernel, group),
+        out_shape=(
+            jax.ShapeDtypeStruct((rows, width + STAT_LANES), jnp.float32),
+            jax.ShapeDtypeStruct((req_count, PATH, row_width), jnp.bfloat16),
+        ),
+        grid_spec=pltpu.PrefetchScalarGridSpec(
+            num_scalar_prefetch=1,
+            grid=(1,),
+            in_specs=[full((rows, width)), full((rows, row_width)), full((rows, 1))],
+            out_specs=(full((rows, width + STAT_LANES)), full((req_count, PATH, row_width))),
+        ),
+    )(accepted, queries, new_kv, parent_rows)
+
+
+def local_kernel(group, lens_ref, q_ref, kv_ref, tree_ref, sum_ref, stat_ref):
     req_count, page_size = kv_ref.shape[0], kv_ref.shape[1]
-    sub = lax.broadcasted_iota(jnp.int32, (TREE, TREE), 0)
-    lane = lax.broadcasted_iota(jnp.int32, (TREE, TREE), 1)
-    identity = (sub == lane).astype(jnp.float32)
-    inclusive = (sub <= lane).astype(jnp.bfloat16)
-    parent_cols = parents_ref[...].astype(jnp.float32)
     stat_lanes = lax.broadcasted_iota(jnp.int32, (TREE, STAT_LANES), 1)
     for r in range(req_count):
         row0 = r * TREE
-        parent = lane_pick(parent_cols, r)
-        reach = jnp.maximum((parent == lane.astype(jnp.float32)).astype(jnp.float32), identity)
-        for _ in range(3):
-            square = jnp.dot(reach.astype(jnp.bfloat16), reach.astype(jnp.bfloat16),
-                             preferred_element_type=jnp.float32)
-            reach = jnp.minimum(square, 1.0)
-        on_path = jnp.sum(jnp.where(sub == acc_ref[r], reach, 0.0), axis=0, keepdims=True)
-        rank = jnp.dot(jnp.broadcast_to(on_path, (8, TREE)).astype(jnp.bfloat16), inclusive,
-                       preferred_element_type=jnp.float32)[0:1]
-        slot = lax.broadcasted_iota(jnp.int32, (PATH, TREE), 0).astype(jnp.float32)
-        selector = jnp.where((rank - 1.0 == slot) & (on_path > 0.5), 1.0, 0.0)
-        fresh = fresh_ref[row0 : row0 + TREE, :]
-        path_ref[r] = jnp.dot(selector.astype(jnp.bfloat16), fresh,
-                              preferred_element_type=jnp.float32).astype(path_ref.dtype)
-
         query = stacked_heads(q_ref, row0, group)
-        tree_valid = jnp.concatenate([reach] * group, axis=0) > 0.5
         length = lens_ref[r]
         page_valid = lax.broadcasted_iota(jnp.int32, (1, page_size), 1) < length
-        m1, l1, a1 = attend(query, fresh[:, 0:HD], fresh[:, HD : 2 * HD], tree_valid, False)
         m2, l2, a2 = attend(query, kv_ref[r, :, 0:HD], kv_ref[r, :, HD : 2 * HD], page_valid, False)
+        tree_stats = tree_ref[row0 : row0 + TREE, group * HD : group * HD + STAT_LANES]
+        m1 = jnp.concatenate([lane_pick(tree_stats, g) for g in range(group)], axis=0)
+        l1 = jnp.concatenate([lane_pick(tree_stats, group + g) for g in range(group)], axis=0)
+        a1 = stacked_heads(tree_ref, row0, group)
         top = jnp.maximum(m1, m2)
         f1 = jnp.exp(m1 - top)
         f2 = jnp.exp(m2 - top)
@@ -96,36 +140,32 @@
         stat_ref[row0 : row0 + TREE, :] = stats
 
 
-def local_partial(cache_lens, accepted, queries, new_kv, kv_pool, parents, group):
+def local_partial(cache_lens, queries, kv_pool, tree_part, group):
     req_count, page_count, page_size, row_width = kv_pool.shape
     rows, width = queries.shape
-    vmem = pltpu.MemorySpace.VMEM
     return pl.pallas_call(
         functools.partial(local_kernel, group),
         out_shape=(
             jax.ShapeDtypeStruct((rows, width), jnp.float32),
             jax.ShapeDtypeStruct((rows, STAT_LANES), jnp.float32),
-            jax.ShapeDtypeStruct((req_count, PATH, row_width), jnp.bfloat16),
         ),
         grid_spec=pltpu.PrefetchScalarGridSpec(
-            num_scalar_prefetch=2,
+            num_scalar_prefetch=1,
             grid=(1,),
             in_specs=[
-                pl.BlockSpec((rows, width), lambda i, a, b: (0, 0)),
-                pl.BlockSpec((rows, row_width), lambda i, a, b: (0, 0)),
-                pl.BlockSpec((req_count, None, page_size, row_width), lambda i, a, b: (0, 0, 0, 0)),
-                pl.BlockSpec((TREE, req_count), lambda i, a, b: (0, 0)),
+                pl.BlockSpec((rows, width), lambda i, a: (0, 0)),
+                pl.BlockSpec((req_count, None, page_size, row_width), lambda i, a: (0, 0, 0, 0)),
+                pl.BlockSpec(tree_part.shape, lambda i, a: (0, 0)),
             ],
             out_specs=(
-                pl.BlockSpec((rows, width), lambda i, a, b: (0, 0)),
-                pl.BlockSpec((rows, STAT_LANES), lambda i, a, b: (0, 0)),
-                pl.BlockSpec((req_count, PATH, row_width), lambda i, a, b: (0, 0, 0)),
+                pl.BlockSpec((rows, width), lambda i, a: (0, 0)),
+                pl.BlockSpec((rows, STAT_LANES), lambda i, a: (0, 0)),
             ),
         ),
-    )(cache_lens, accepted, queries, new_kv, kv_pool, parents.T)
-
-
-def holder_kernel(page_index, group, q_ref, kv_ref, out_ref):
+    )(cache_lens, queries, kv_pool, tree_part)
+
+
+def holder_kernel(page_index, group, q_ref, kv_ref, order_ref, out_ref):
     req_count, page_size = kv_ref.shape[0], kv_ref.shape[1]
     rows = req_count * TREE
     extra = q_ref[rows : rows + EXTRA, :].astype(jnp.float32)
@@ -153,7 +193,7 @@
         out_ref[row0 : row0 + TREE, group * HD : group * HD + STAT_LANES] = stats.astype(jnp.bfloat16)
 
 
-def holder_partial(packed_queries, kv_pool, page_index, group):
+def holder_partial(packed_queries, kv_pool, page_index, group, order_after):
     req_count, page_count, page_size, row_width = kv_pool.shape
     packed_rows, width = packed_queries.shape
     rows = req_count * TREE
@@ -164,9 +204,10 @@
         in_specs=[
             pl.BlockSpec((packed_rows, width), lambda i: (0, 0)),
             pl.BlockSpec((req_count, None, page_size, row_width), lambda i: (0, page_index, 0, 0)),
+            pl.BlockSpec((8, STAT_LANES), lambda i: (0, 0)),
         ],
         out_specs=pl.BlockSpec((rows, width + STAT_LANES), lambda i: (0, 0)),
-    )(packed_queries, kv_pool)
+    )(packed_queries, kv_pool, order_after)
 
 
 def merge_kernel(group, sum_ref, stat_ref, *rest):
@@ -236,13 +277,12 @@
 
     packed_queries = pack_queries(queries, cache_lens)
     guests = [shifted(packed_queries, "req", p) for p in range(1, page_count)]
-    sums, stats, accepted_kv = local_partial(
-        cache_lens, accepted, queries, new_kv, kv_pool, parents, group
-    )
+    tree_part, accepted_kv = tree_partial(accepted, queries, new_kv, parents, group)
     returned = []
     for page_index in range(1, page_count):
-        part = holder_partial(guests[page_index - 1], kv_pool, page_index, group)
+        part = holder_partial(guests[page_index - 1], kv_pool, page_index, group, tree_part)
         returned.append(shifted(part, "req", -page_index))
+    sums, stats = local_partial(cache_lens, queries, kv_pool, tree_part, group)
 
     product = merge_project(sums, stats, returned, w_out, group)
     tp_count = lax.axis_size("tp")

time: 118 us -> 122 us (1.034)
  blocking collectives: 56.8 us -> 59 us
  waiting for transfers between devices: 0.02 us -> 1.94 us
    pallas_call x1, Pallas kernels: 9.81 us -> 5.13 us  [local_partial(): pl.pallas_call(functools.partial(local_kernel, group), out_shape=(jax.Sha...]
    pallas_call x0 -> x1, Pallas kernels: none -> 3.71 us  [tree_partial(): pl.pallas_call(functools.partial(tree_kernel, group), out_shape=(jax.Shap...]
    all_to_all x1, blocking collectives: 56.8 us -> 59 us  [per_device(): gathered = lax.all_to_all(pieces, 'tp', 0, 0, tiled=False)]
    ppermute x6, waiting for transfers between devices: 0.02 us -> 1.94 us  [shifted(): return lax.ppermute(value, axis, pairs)]
    unnamed x21 -> x18, local copies, waits for them, and re-layouts: 5.14 us -> 4.48 us
  transfers between devices with their start and end apart: 6 -> 6, of which waited for: 0 -> 1; matrix products, arithmetic and copies ran while one was open for 1% -> 1% of each run, Pallas kernels for 19% -> 17%
where the time goes in v5:
time: 122 us; the launch traced here: 121 us
  blocking collectives  59 us (48%)
  starting transfers between devices  26.3 us (22%)
  Pallas kernels  24.1 us (20%)
  local copies, waits for them, and re-layouts  5.27 us (4%)
  other arithmetic  3.69 us (3%)
  waiting for transfers between devices  1.94 us (2%)
    all_to_all x1, blocking collectives, per_device(): gathered = lax.all_to_all(pieces, 'tp', 0, 0, tiled=False)  59 us
    ppermute x6, starting transfers between devices, shifted(): return lax.ppermute(value, axis, pairs)  26.3 us
    pallas_call x3, Pallas kernels, holder_partial(): pl.pallas_call(functools.partial(holder_kernel, page_index, group), out_s...  12.1 us
    pallas_call x1, Pallas kernels, local_partial(): pl.pallas_call(functools.partial(local_kernel, group), out_shape=(jax.Sha...  5.13 us
    unnamed x18, local copies, waits for them, and re-layouts  4.48 us
    pallas_call x1, Pallas kernels, tree_partial(): pl.pallas_call(functools.partial(tree_kernel, group), out_shape=(jax.Shap...  3.71 us
    pallas_call x1, Pallas kernels, merge_project(): pl.pallas_call(functools.partial(merge_kernel, group), out_shape=jax.Shap...  3.15 us
  transfers between devices with their start and end apart: 6, of which 1 were waited for; matrix products, arithmetic and copies ran while one was open for 1% of the time, Pallas kernels for 17%

profile of v5, /device:TPU:1, one launch (start us, length us, event | category | flops | bytes accessed | tf_op | source)
XLA Modules:
  0.0 121.1 jit_solution(6543762095930205445)
XLA Ops:
  0.6 0.7 convert_bitcast_fusion
  1.3 0.9 pad_maximum_fusion
  2.2 5.6 %collective-permute-start.4 = (bf16[272,256]{1,0:T(8,128)(2,1)S(1)}, bf16[272,256]{1,0:T(8,128)(2,1)S(1)}, u32[]{:S(2)}, u32[]{:S(2)}) collective-permute-start(bf16[272,256]{1,0:T(8,128)(2,1)S(1)} %pad_maximum_fusion), channel_id=1, source_target_pairs={{0,24},{8,32},{16,40},{24,48},{32,56},{40,64},{48,72},{56,80},{64,... | collective-permute-start | bytes 417800 | tf_op jit(solution)/shard_map/ppermute | solution.py:24
  7.8 3.2 %collective-permute-start.2 = (bf16[272,256]{1,0:T(8,128)(2,1)S(1)}, bf16[272,256]{1,0:T(8,128)(2,1)S(1)}, u32[]{:S(2)}, u32[]{:S(2)}) collective-permute-start(bf16[272,256]{1,0:T(8,128)(2,1)S(1)} %pad_maximum_fusion), channel_id=1, source_target_pairs={{0,16},{8,24},{16,32},{24,40},{32,48},{40,56},{48,64},{56,72},{64,... | collective-permute-start | bytes 417800 | tf_op jit(solution)/shard_map/ppermute | solution.py:24
  11.1 2.2 %collective-permute-start = (bf16[272,256]{1,0:T(8,128)(2,1)S(1)}, bf16[272,256]{1,0:T(8,128)(2,1)S(1)}, u32[]{:S(2)}, u32[]{:S(2)}) collective-permute-start(bf16[272,256]{1,0:T(8,128)(2,1)S(1)} %pad_maximum_fusion), channel_id=1, source_target_pairs={{0,8},{8,16},{16,24},{24,32},{32,40},{40,48},{48,56},{56,64},{64,7... | collective-permute-start | bytes 417800 | tf_op jit(solution)/shard_map/ppermute | solution.py:24
  13.3 0.8 broadcast_add_fusion
  14.0 0.8 reshape.28.parent_ref
  14.8 3.7 %shard_map.112 = (f32[256,384]{1,0:T(8,128)}, bf16[8,8,256]{2,1,0:T(8,128)(2,1)}) custom-call(s32[8]{0:T(128)} %acc_ref.1, bf16[256,256]{1,0:T(8,128)(2,1)} %q_ref.3, bf16[256,256]{1,0:T(8,128)(2,1)} %fresh_ref.1, s32[256,1]{1,0:T(8,128)} %reshape.28.parent_ref), custom_call_target="tpu_custom_call" | custom-call | tf_op jit(solution)/shard_map/pallas_call | solution.py:101
  18.5 0.0 collective-permute-done.q_ref
  18.5 0.0 copy-start.7
  18.5 0.7 copy-done.7
  19.2 4.0 %shard_map.114 = bf16[256,384]{1,0:T(8,128)(2,1)} custom-call(bf16[272,256]{1,0:T(8,128)(2,1)} %copy-done.7, bf16[8,4,256,256]{3,2,1,0:T(8,128)(2,1)} %kv_ref.7, f32[256,384]{1,0:T(8,128)} %get-tuple-element.7.tree_ref.order_ref), custom_call_target="tpu_custom_call" | custom-call | tf_op jit(solution)/shard_map/pallas_call | solution.py:200
  23.2 6.4 %collective-permute-start.1 = (bf16[256,384]{1,0:T(8,128)(2,1)}, bf16[256,384]{1,0:T(8,128)(2,1)S(1)}, u32[]{:S(2)}, u32[]{:S(2)}) collective-permute-start(bf16[256,384]{1,0:T(8,128)(2,1)} %shard_map.114), channel_id=1, source_target_pairs={{0,504},{8,0},{16,8},{24,16},{32,24},{40,32},{48,40},{56,48},{64,5... | collective-permute-start | bytes 589832 | tf_op jit(solution)/shard_map/ppermute | solution.py:24
  29.7 0.0 collective-permute-done.2.q_ref
  29.7 0.0 copy-start.6
  29.7 0.6 copy-done.6
  30.4 4.0 %shard_map.115 = bf16[256,384]{1,0:T(8,128)(2,1)} custom-call(bf16[272,256]{1,0:T(8,128)(2,1)} %copy-done.6, bf16[8,4,256,256]{3,2,1,0:T(8,128)(2,1)} %kv_ref.7, f32[256,384]{1,0:T(8,128)} %get-tuple-element.7.tree_ref.order_ref), custom_call_target="tpu_custom_call" | custom-call | tf_op jit(solution)/shard_map/pallas_call | solution.py:200
  34.4 4.0 %collective-permute-start.3 = (bf16[256,384]{1,0:T(8,128)(2,1)}, bf16[256,384]{1,0:T(8,128)(2,1)S(1)}, u32[]{:S(2)}, u32[]{:S(2)}) collective-permute-start(bf16[256,384]{1,0:T(8,128)(2,1)} %shard_map.115), channel_id=1, source_target_pairs={{0,496},{8,504},{16,0},{24,8},{32,16},{40,24},{48,32},{56,40},{64,... | collective-permute-start | bytes 589832 | tf_op jit(solution)/shard_map/ppermute | solution.py:24
  38.4 0.0 collective-permute-done.4.q_ref
  38.4 0.0 copy-start.5
  38.4 0.6 copy-done.5
  39.1 4.0 %shard_map.116 = bf16[256,384]{1,0:T(8,128)(2,1)} custom-call(bf16[272,256]{1,0:T(8,128)(2,1)} %copy-done.5, bf16[8,4,256,256]{3,2,1,0:T(8,128)(2,1)} %kv_ref.7, f32[256,384]{1,0:T(8,128)} %get-tuple-element.7.tree_ref.order_ref), custom_call_target="tpu_custom_call" | custom-call | tf_op jit(solution)/shard_map/pallas_call | solution.py:200
  43.1 0.0 copy-start
  43.1 4.8 %collective-permute-start.5 = (bf16[256,384]{1,0:T(8,128)(2,1)}, bf16[256,384]{1,0:T(8,128)(2,1)S(1)}, u32[]{:S(2)}, u32[]{:S(2)}) collective-permute-start(bf16[256,384]{1,0:T(8,128)(2,1)} %shard_map.116), channel_id=1, source_target_pairs={{0,488},{8,496},{16,504},{24,0},{32,8},{40,16},{48,24},{56,32},{64... | collective-permute-start | bytes 589832 | tf_op jit(solution)/shard_map/ppermute | solution.py:24
  48.0 5.1 %shard_map.113 = (f32[256,256]{1,0:T(8,128)}, f32[256,128]{1,0:T(8,128)}) custom-call(s32[8]{0:T(128)} %lens_ref.1, bf16[256,256]{1,0:T(8,128)(2,1)} %q_ref.3, bf16[8,4,256,256]{3,2,1,0:T(8,128)(2,1)} %kv_ref.7, f32[256,384]{1,0:T(8,128)} %get-tuple-element.7.tree_ref.order_ref), custom_call_target="tpu_custom_call" | custom-call | tf_op jit(solution)/shard_map/pallas_call | solution.py:146
  53.1 0.0 collective-permute-done.1.rest_0_
  53.1 0.0 collective-permute-done.3.rest_1_
  53.1 1.9 %collective-permute-done.5.rest_2_ = bf16[256,384]{1,0:T(8,128)(2,1)S(1)} collective-permute-done((bf16[256,384]{1,0:T(8,128)(2,1)}, bf16[256,384]{1,0:T(8,128)(2,1)S(1)}, u32[]{:S(2)}, u32[]{:S(2)}) %collective-permute-start.5) | collective-permute-done | bytes 196640 | tf_op jit(solution)/shard_map/ppermute | solution.py:24
  55.0 0.0 copy-done
  55.0 0.0 copy-start.1
  55.0 0.9 copy-done.1
  56.0 0.0 copy-start.2
  56.0 0.9 copy-done.2
  56.9 3.1 %shard_map.117 = bf16[256,4096]{1,0:T(8,128)(2,1)S(1)} custom-call(f32[256,256]{1,0:T(8,128)S(1)} %copy-done.1, f32[256,128]{1,0:T(8,128)S(1)} %copy-done.2, bf16[256,384]{1,0:T(8,128)(2,1)S(1)} %collective-permute-done.1.rest_0_, bf16[256,384]{1,0:T(8,128)(2,1)S(1)} %collective-permute-done.3.rest_1_, bf16[256,384]{1,0:T(8,128)(2,1)S(1)} %collective-permute-done.5.rest_2_, ...), custom_call_target="tpu_custom_call" | custom-call | tf_op jit(solution)/shard_map/pallas_call | solution.py:252
  60.0 59.0 %all_to_all.5 = bf16[8,32,4096]{2,1,0:T(8,128)(2,1)S(1)} all-to-all(bf16[8,32,4096]{2,1,0:T(8,128)(2,1)S(1)} %bitcast.5), channel_id=1, replica_groups=mesh['req'=64,'tp'=8] {'tp'}, dimensions={0} | all-to-all | bytes 4194304 | tf_op jit(solution)/shard_map/all_to_all | solution.py:290
  119.0 0.0 copy-start.4
  119.1 0.0 copy-start.8
  119.1 0.3 convert_reduce_fusion
  119.4 0.6 copy-done.4
  120.0 0.2 fusion
  120.2 0.0 copy-start.3
  120.2 0.0 copy-done.8
  120.2 0.8 fusion.2
  121.1 0.0 copy-done.3
  (3 shorter events, 0.0 us)
Async XLA Ops:
  2.2 36.2 %collective-permute-start.4 = (bf16[272,256]{1,0:T(8,128)(2,1)S(1)}, bf16[272,256]{1,0:T(8,128)(2,1)S(1)}, u32[]{:S(2)}, u32[]{:S(2)}) collective-permute-start(bf16[272,256]{1,0:T(8,128)(2,1)S(1)} %pad_maximum_fusion), channel_id=1, source_target_pairs={{0,24},{8,32},{16,40},{24,48},{32,56},{40,64},{48,72},{56,80},{64,... | collective-permute-start | bytes 417800 | tf_op jit(solution)/shard_map/ppermute | solution.py:24
  7.8 21.8 %collective-permute-start.2 = (bf16[272,256]{1,0:T(8,128)(2,1)S(1)}, bf16[272,256]{1,0:T(8,128)(2,1)S(1)}, u32[]{:S(2)}, u32[]{:S(2)}) collective-permute-start(bf16[272,256]{1,0:T(8,128)(2,1)S(1)} %pad_maximum_fusion), channel_id=1, source_target_pairs={{0,16},{8,24},{16,32},{24,40},{32,48},{40,56},{48,64},{56,72},{64,... | collective-permute-start | bytes 417800 | tf_op jit(solution)/shard_map/ppermute | solution.py:24
  11.1 7.5 %collective-permute-start = (bf16[272,256]{1,0:T(8,128)(2,1)S(1)}, bf16[272,256]{1,0:T(8,128)(2,1)S(1)}, u32[]{:S(2)}, u32[]{:S(2)}) collective-permute-start(bf16[272,256]{1,0:T(8,128)(2,1)S(1)} %pad_maximum_fusion), channel_id=1, source_target_pairs={{0,8},{8,16},{16,24},{24,32},{32,40},{40,48},{48,56},{56,64},{64,7... | collective-permute-start | bytes 417800 | tf_op jit(solution)/shard_map/ppermute | solution.py:24
  18.5 0.7 copy-start.7
  23.2 29.9 %collective-permute-start.1 = (bf16[256,384]{1,0:T(8,128)(2,1)}, bf16[256,384]{1,0:T(8,128)(2,1)S(1)}, u32[]{:S(2)}, u32[]{:S(2)}) collective-permute-start(bf16[256,384]{1,0:T(8,128)(2,1)} %shard_map.114), channel_id=1, source_target_pairs={{0,504},{8,0},{16,8},{24,16},{32,24},{40,32},{48,40},{56,48},{64,5... | collective-permute-start | bytes 589832 | tf_op jit(solution)/shard_map/ppermute | solution.py:24
  29.7 0.7 copy-start.6
  34.4 18.7 %collective-permute-start.3 = (bf16[256,384]{1,0:T(8,128)(2,1)}, bf16[256,384]{1,0:T(8,128)(2,1)S(1)}, u32[]{:S(2)}, u32[]{:S(2)}) collective-permute-start(bf16[256,384]{1,0:T(8,128)(2,1)} %shard_map.115), channel_id=1, source_target_pairs={{0,496},{8,504},{16,0},{24,8},{32,16},{40,24},{48,32},{56,40},{64,... | collective-permute-start | bytes 589832 | tf_op jit(solution)/shard_map/ppermute | solution.py:24
  38.4 0.7 copy-start.5
  43.1 11.9 %copy-start = (bf16[256,4096]{1,0:T(8,128)(2,1)S(1)}, bf16[256,4096]{1,0:T(8,128)(2,1)}, u32[]{:S(2)}) copy-start(bf16[256,4096]{1,0:T(8,128)(2,1)} %rest_3_.1) | copy-start | bytes 6291460
  43.1 11.9 %collective-permute-start.5 = (bf16[256,384]{1,0:T(8,128)(2,1)}, bf16[256,384]{1,0:T(8,128)(2,1)S(1)}, u32[]{:S(2)}, u32[]{:S(2)}) collective-permute-start(bf16[256,384]{1,0:T(8,128)(2,1)} %shard_map.116), channel_id=1, source_target_pairs={{0,488},{8,496},{16,504},{24,0},{32,8},{40,16},{48,24},{56,32},{64... | collective-permute-start | bytes 589832 | tf_op jit(solution)/shard_map/ppermute | solution.py:24
  55.0 1.0 copy-start.1
  56.0 0.9 copy-start.2
  119.0 1.0 copy-start.4
  119.1 1.2 copy-start.8
  120.2 0.9 copy-start.3

commit v6 on v5

--- a/solution.py
+++ b/solution.py
@@ -13,6 +13,7 @@
 PATH = 8
 EXTRA = 16
 STAT_LANES = 128
+SHIPPED_PAGES = (1, 2)
 
 
 NEGATIVE = -1e30
@@ -113,24 +114,34 @@
     )(accepted, queries, new_kv, parent_rows)
 
 
-def local_kernel(group, lens_ref, q_ref, kv_ref, tree_ref, sum_ref, stat_ref):
+def local_kernel(group, page_ids, lens_ref, q_ref, kv_ref, tree_ref, *rest):
+    pages = rest[: len(page_ids) - 1]
+    sum_ref, stat_ref = rest[-2:]
     req_count, page_size = kv_ref.shape[0], kv_ref.shape[1]
     stat_lanes = lax.broadcasted_iota(jnp.int32, (TREE, STAT_LANES), 1)
     for r in range(req_count):
         row0 = r * TREE
         query = stacked_heads(q_ref, row0, group)
         length = lens_ref[r]
-        page_valid = lax.broadcasted_iota(jnp.int32, (1, page_size), 1) < length
-        m2, l2, a2 = attend(query, kv_ref[r, :, 0:HD], kv_ref[r, :, HD : 2 * HD], page_valid, False)
         tree_stats = tree_ref[row0 : row0 + TREE, group * HD : group * HD + STAT_LANES]
-        m1 = jnp.concatenate([lane_pick(tree_stats, g) for g in range(group)], axis=0)
-        l1 = jnp.concatenate([lane_pick(tree_stats, group + g) for g in range(group)], axis=0)
-        a1 = stacked_heads(tree_ref, row0, group)
-        top = jnp.maximum(m1, m2)
-        f1 = jnp.exp(m1 - top)
-        f2 = jnp.exp(m2 - top)
-        totals = f1 * l1 + f2 * l2
-        weighted = f1 * a1 + f2 * a2
+        blocks = [(
+            jnp.concatenate([lane_pick(tree_stats, g) for g in range(group)], axis=0),
+            jnp.concatenate([lane_pick(tree_stats, group + g) for g in range(group)], axis=0),
+            stacked_heads(tree_ref, row0, group),
+        )]
+        for page_index, page_ref in zip(page_ids, (kv_ref,) + tuple(pages)):
+            positions = lax.broadcasted_iota(jnp.int32, (1, page_size), 1) + page_index * page_size
+            blocks.append(attend(query, page_ref[r, :, 0:HD], page_ref[r, :, HD : 2 * HD],
+                                 positions < length, False))
+        top = blocks[0][0]
+        for block in blocks[1:]:
+            top = jnp.maximum(top, block[0])
+        totals = jnp.zeros_like(top)
+        weighted = jnp.zeros(blocks[0][2].shape, jnp.float32)
+        for largest, part_totals, part_weighted in blocks:
+            factor = jnp.exp(largest - top)
+            totals = totals + factor * part_totals
+            weighted = weighted + factor * part_weighted
         stats = jnp.zeros((TREE, STAT_LANES), jnp.float32)
         for g in range(group):
             rows = slice(g * TREE, (g + 1) * TREE)
@@ -140,11 +151,13 @@
         stat_ref[row0 : row0 + TREE, :] = stats
 
 
-def local_partial(cache_lens, queries, kv_pool, tree_part, group):
+def local_partial(cache_lens, queries, kv_pool, tree_part, shipped, group):
     req_count, page_count, page_size, row_width = kv_pool.shape
     rows, width = queries.shape
+    page_ids = (0,) + tuple(index for index, _ in shipped)
+    page_spec = pl.BlockSpec((req_count, page_size, row_width), lambda i, a: (0, 0, 0))
     return pl.pallas_call(
-        functools.partial(local_kernel, group),
+        functools.partial(local_kernel, group, page_ids),
         out_shape=(
             jax.ShapeDtypeStruct((rows, width), jnp.float32),
             jax.ShapeDtypeStruct((rows, STAT_LANES), jnp.float32),
@@ -156,13 +169,13 @@
                 pl.BlockSpec((rows, width), lambda i, a: (0, 0)),
                 pl.BlockSpec((req_count, None, page_size, row_width), lambda i, a: (0, 0, 0, 0)),
                 pl.BlockSpec(tree_part.shape, lambda i, a: (0, 0)),
-            ],
+            ] + [page_spec for _ in shipped],
             out_specs=(
                 pl.BlockSpec((rows, width), lambda i, a: (0, 0)),
                 pl.BlockSpec((rows, STAT_LANES), lambda i, a: (0, 0)),
             ),
         ),
-    )(cache_lens, queries, kv_pool, tree_part)
+    )(cache_lens, queries, kv_pool, tree_part, *[page for _, page in shipped])
 
 
 def holder_kernel(page_index, group, q_ref, kv_ref, order_ref, out_ref):
@@ -275,14 +288,16 @@
     q_local = queries.shape[1] // HD
     group = q_local // kv_local
 
+    shipped = [(p, shifted(kv_pool[:, p], "req", -p)) for p in SHIPPED_PAGES]
+    visited = [p for p in range(1, page_count) if p not in SHIPPED_PAGES]
     packed_queries = pack_queries(queries, cache_lens)
-    guests = [shifted(packed_queries, "req", p) for p in range(1, page_count)]
+    guests = [shifted(packed_queries, "req", p) for p in visited]
     tree_part, accepted_kv = tree_partial(accepted, queries, new_kv, parents, group)
     returned = []
-    for page_index in range(1, page_count):
-        part = holder_partial(guests[page_index - 1], kv_pool, page_index, group, tree_part)
+    for page_index, guest in zip(visited, guests):
+        part = holder_partial(guest, kv_pool, page_index, group, tree_part)
         returned.append(shifted(part, "req", -page_index))
-    sums, stats = local_partial(cache_lens, queries, kv_pool, tree_part, group)
+    sums, stats = local_partial(cache_lens, queries, kv_pool, tree_part, shipped, group)
 
     product = merge_project(sums, stats, returned, w_out, group)
     tp_count = lax.axis_size("tp")

time: 122 us -> 123 us (level)
  the two profiles are of different devices: /device:TPU:1 before, /device:TPU:6 now
where the time goes in v6:
time: 123 us; the launch traced here: 122 us
  blocking collectives  57.9 us (47%)
  waiting for transfers between devices  21.1 us (17%)
  Pallas kernels  20.3 us (17%)
  starting transfers between devices  13.3 us (11%)
  local copies, waits for them, and re-layouts  7.09 us (6%)
  other arithmetic  1.44 us (1%)
    all_to_all x1, blocking collectives, per_device(): gathered = lax.all_to_all(pieces, 'tp', 0, 0, tiled=False)  57.9 us
    ppermute x4, waiting for transfers between devices, shifted(): return lax.ppermute(value, axis, pairs)  21.1 us
    ppermute x4, starting transfers between devices, shifted(): return lax.ppermute(value, axis, pairs)  13.3 us
    pallas_call x1, Pallas kernels, local_partial(): pl.pallas_call(functools.partial(local_kernel, group, page_ids), out_shap...  9.5 us
    pallas_call x1, Pallas kernels, holder_partial(): pl.pallas_call(functools.partial(holder_kernel, page_index, group), out_s...  4.04 us
    pallas_call x1, Pallas kernels, tree_partial(): pl.pallas_call(functools.partial(tree_kernel, group), out_shape=(jax.Shap...  3.72 us
    unnamed x22, local copies, waits for them, and re-layouts  3.19 us
    squeeze x1, local copies, waits for them, and re-layouts, per_device(): shipped = [(p, shifted(kv_pool[:, p], 'req', -p)) for p in SHIPPED_PAGES]  3.11 us
  transfers between devices with their start and end apart: 4, of which 3 were waited for; matrix products, arithmetic and copies ran while one was open for 1% of the time, Pallas kernels for 14%

profile of v6, /device:TPU:6, one launch (start us, length us, event | category | flops | bytes accessed | tf_op | source)
XLA Modules:
  0.0 122.0 jit_solution(5301458607177804503)
XLA Ops:
  0.6 0.0 copy-start.10
  0.6 0.0 copy-start.3
  0.7 0.0 copy-start.9
  0.7 3.1 %slice_bitcast_fusion = (bf16[8,256,256]{2,1,0:T(8,128)(2,1)}, bf16[8,256,256]{2,1,0:T(8,128)(2,1)}) fusion(bf16[8,4,256,256]{3,2,1,0:T(8,128)(2,1)} %kv_ref.3), kind=kLoop, calls=%fused_computation.1 | loop fusion | bytes 4194304 | tf_op jit(solution)/shard_map/squeeze | solution.py:291
  3.8 5.6 %collective-permute-start.1 = (bf16[8,256,256]{2,1,0:T(8,128)(2,1)}, bf16[8,256,256]{2,1,0:T(8,128)(2,1)S(1)}, u32[]{:S(2)}, u32[]{:S(2)}) collective-permute-start(bf16[8,256,256]{2,1,0:T(8,128)(2,1)} %get-tuple-element.13), channel_id=1, source_target_pairs={{0,496},{8,504},{16,0},{24,8},{32,16},{40,24},{48,32},{56,40},{64,... | collective-permute-start | bytes 3145736 | tf_op jit(solution)/shard_map/ppermute | solution.py:25
  9.4 2.4 %collective-permute-start = (bf16[8,256,256]{2,1,0:T(8,128)(2,1)}, bf16[8,256,256]{2,1,0:T(8,128)(2,1)}, u32[]{:S(2)}, u32[]{:S(2)}) collective-permute-start(bf16[8,256,256]{2,1,0:T(8,128)(2,1)} %get-tuple-element.14), channel_id=1, source_target_pairs={{0,504},{8,0},{16,8},{24,16},{32,24},{40,32},{48,40},{56,48},{64,5... | collective-permute-start | bytes 3145736 | tf_op jit(solution)/shard_map/ppermute | solution.py:25
  11.8 0.0 copy-done.10
  11.9 0.0 copy-done.3
  11.9 1.9 %collective-permute-start.2 = (bf16[272,256]{1,0:T(8,128)(2,1)S(1)}, bf16[272,256]{1,0:T(8,128)(2,1)S(1)}, u32[]{:S(2)}, u32[]{:S(2)}) collective-permute-start(bf16[272,256]{1,0:T(8,128)(2,1)S(1)} %pad_maximum_fusion), channel_id=1, source_target_pairs={{0,24},{8,32},{16,40},{24,48},{32,56},{40,64},{48,72},{56,80},{64,... | collective-permute-start | bytes 417800 | tf_op jit(solution)/shard_map/ppermute | solution.py:25
  13.9 0.0 copy-done.9
  13.9 0.1 broadcast_add_fusion
  13.9 0.8 reshape.28.parent_ref
  14.7 3.7 %shard_map.112 = (f32[256,384]{1,0:T(8,128)}, bf16[8,8,256]{2,1,0:T(8,128)(2,1)}) custom-call(s32[8]{0:T(128)} %acc_ref.1, bf16[256,256]{1,0:T(8,128)(2,1)} %q_ref.3, bf16[256,256]{1,0:T(8,128)(2,1)} %fresh_ref.1, s32[256,1]{1,0:T(8,128)} %reshape.28.parent_ref), custom_call_target="tpu_custom_call" | custom-call | tf_op jit(solution)/shard_map/pallas_call | solution.py:102
  18.4 3.5 %collective-permute-done.2.q_ref = bf16[272,256]{1,0:T(8,128)(2,1)S(1)} collective-permute-done((bf16[272,256]{1,0:T(8,128)(2,1)S(1)}, bf16[272,256]{1,0:T(8,128)(2,1)S(1)}, u32[]{:S(2)}, u32[]{:S(2)}) %collective-permute-start.2) | collective-permute-done | bytes 139296 | tf_op jit(solution)/shard_map/ppermute | solution.py:25
  21.9 0.0 copy-start.7
  21.9 0.7 copy-done.7
  22.6 4.0 %shard_map.114 = bf16[256,384]{1,0:T(8,128)(2,1)} custom-call(bf16[272,256]{1,0:T(8,128)(2,1)} %copy-done.7, bf16[8,4,256,256]{3,2,1,0:T(8,128)(2,1)} %kv_ref.3, f32[256,384]{1,0:T(8,128)} %get-tuple-element.7.tree_ref.order_ref), custom_call_target="tpu_custom_call" | custom-call | tf_op jit(solution)/shard_map/pallas_call | solution.py:213
  26.6 0.0 copy-start
  26.6 3.4 %collective-permute-start.3 = (bf16[256,384]{1,0:T(8,128)(2,1)}, bf16[256,384]{1,0:T(8,128)(2,1)S(1)}, u32[]{:S(2)}, u32[]{:S(2)}) collective-permute-start(bf16[256,384]{1,0:T(8,128)(2,1)} %shard_map.114), channel_id=1, source_target_pairs={{0,488},{8,496},{16,504},{24,0},{32,8},{40,16},{48,24},{56,32},{64... | collective-permute-start | bytes 589832 | tf_op jit(solution)/shard_map/ppermute | solution.py:25
  30.0 3.2 %collective-permute-done.1.rest_1_ = bf16[8,256,256]{2,1,0:T(8,128)(2,1)S(1)} collective-permute-done((bf16[8,256,256]{2,1,0:T(8,128)(2,1)}, bf16[8,256,256]{2,1,0:T(8,128)(2,1)S(1)}, u32[]{:S(2)}, u32[]{:S(2)}) %collective-permute-start.1) | collective-permute-done | bytes 1048608 | tf_op jit(solution)/shard_map/ppermute | solution.py:25
  33.2 0.0 copy-start.5
  33.2 14.4 %collective-permute-done.rest_0_ = bf16[8,256,256]{2,1,0:T(8,128)(2,1)} collective-permute-done((bf16[8,256,256]{2,1,0:T(8,128)(2,1)}, bf16[8,256,256]{2,1,0:T(8,128)(2,1)}, u32[]{:S(2)}, u32[]{:S(2)}) %collective-permute-start) | collective-permute-done | bytes 1048608 | tf_op jit(solution)/shard_map/ppermute | solution.py:25
  47.6 0.0 copy-done.5
  47.6 9.5 %shard_map.113 = (f32[256,256]{1,0:T(8,128)}, f32[256,128]{1,0:T(8,128)}) custom-call(s32[8]{0:T(128)} %lens_ref.1, bf16[256,256]{1,0:T(8,128)(2,1)} %q_ref.3, bf16[8,4,256,256]{3,2,1,0:T(8,128)(2,1)} %kv_ref.3, f32[256,384]{1,0:T(8,128)} %get-tuple-element.7.tree_ref.order_ref, bf16[8,256,256]{2,1,0:T(8,128)(2,1)} %collective-permute-done.rest_0_, ...), custom_call_target="tpu_custom_call" | custom-call | tf_op jit(solution)/shard_map/pallas_call | solution.py:159
  57.1 0.0 collective-permute-done.3.rest_0_
  57.1 0.0 copy-done
  57.1 0.0 copy-start.1
  57.1 0.9 copy-done.1
  58.1 0.0 copy-start.2
  58.1 0.9 copy-done.2
  59.0 3.1 %shard_map.115 = bf16[256,4096]{1,0:T(8,128)(2,1)S(1)} custom-call(f32[256,256]{1,0:T(8,128)S(1)} %copy-done.1, f32[256,128]{1,0:T(8,128)S(1)} %copy-done.2, bf16[256,384]{1,0:T(8,128)(2,1)S(1)} %collective-permute-done.3.rest_0_, bf16[256,4096]{1,0:T(8,128)(2,1)S(1)} %copy-done), custom_call_target="tpu_custom_call" | custom-call | tf_op jit(solution)/shard_map/pallas_call | solution.py:265
  62.0 57.9 %all_to_all.5 = bf16[8,32,4096]{2,1,0:T(8,128)(2,1)S(1)} all-to-all(bf16[8,32,4096]{2,1,0:T(8,128)(2,1)S(1)} %bitcast.13), channel_id=1, replica_groups=mesh['req'=64,'tp'=8] {'tp'}, dimensions={0} | all-to-all | bytes 4194304 | tf_op jit(solution)/shard_map/all_to_all | solution.py:305
  119.9 0.0 copy-start.6
  119.9 0.0 copy-start.8
  119.9 0.3 convert_reduce_fusion
  120.2 0.6 copy-done.6
  120.9 0.2 fusion
  121.1 0.0 copy-start.4
  121.1 0.0 copy-done.8
  121.1 0.8 fusion.2
  122.0 0.0 copy-done.4
  (5 shorter events, 0.0 us)
Async XLA Ops:
  0.6 11.2 %copy-start.10 = (s32[8]{0:T(128)S(1)}, s32[8]{0:T(128)}, u32[]{:S(2)}) copy-start(s32[8]{0:T(128)} %lens_ref.1) | copy-start | bytes 100
  0.6 11.2 %copy-start.3 = (bf16[256,256]{1,0:T(8,128)(2,1)S(1)}, bf16[256,256]{1,0:T(8,128)(2,1)}, u32[]{:S(2)}) copy-start(bf16[256,256]{1,0:T(8,128)(2,1)} %q_ref.3) | copy-start | bytes 393220
  0.7 13.2 %copy-start.9 = (s32[8,32]{1,0:T(8,128)S(1)}, s32[8,32]{1,0:T(8,128)}, u32[]{:S(2)}) copy-start(s32[8,32]{1,0:T(8,128)} %param.13) | copy-start | bytes 3076
  3.8 29.4 %collective-permute-start.1 = (bf16[8,256,256]{2,1,0:T(8,128)(2,1)}, bf16[8,256,256]{2,1,0:T(8,128)(2,1)S(1)}, u32[]{:S(2)}, u32[]{:S(2)}) collective-permute-start(bf16[8,256,256]{2,1,0:T(8,128)(2,1)} %get-tuple-element.13), channel_id=1, source_target_pairs={{0,496},{8,504},{16,0},{24,8},{32,16},{40,24},{48,32},{56,40},{64,... | collective-permute-start | bytes 3145736 | tf_op jit(solution)/shard_map/ppermute | solution.py:25
  9.4 38.2 %collective-permute-start = (bf16[8,256,256]{2,1,0:T(8,128)(2,1)}, bf16[8,256,256]{2,1,0:T(8,128)(2,1)}, u32[]{:S(2)}, u32[]{:S(2)}) collective-permute-start(bf16[8,256,256]{2,1,0:T(8,128)(2,1)} %get-tuple-element.14), channel_id=1, source_target_pairs={{0,504},{8,0},{16,8},{24,16},{32,24},{40,32},{48,40},{56,48},{64,5... | collective-permute-start | bytes 3145736 | tf_op jit(solution)/shard_map/ppermute | solution.py:25
  11.9 10.0 %collective-permute-start.2 = (bf16[272,256]{1,0:T(8,128)(2,1)S(1)}, bf16[272,256]{1,0:T(8,128)(2,1)S(1)}, u32[]{:S(2)}, u32[]{:S(2)}) collective-permute-start(bf16[272,256]{1,0:T(8,128)(2,1)S(1)} %pad_maximum_fusion), channel_id=1, source_target_pairs={{0,24},{8,32},{16,40},{24,48},{32,56},{40,64},{48,72},{56,80},{64,... | collective-permute-start | bytes 417800 | tf_op jit(solution)/shard_map/ppermute | solution.py:25
  21.9 0.7 copy-start.7
  26.6 30.5 %copy-start = (bf16[256,4096]{1,0:T(8,128)(2,1)S(1)}, bf16[256,4096]{1,0:T(8,128)(2,1)}, u32[]{:S(2)}) copy-start(bf16[256,4096]{1,0:T(8,128)(2,1)} %rest_1_.1) | copy-start | bytes 6291460
  26.6 30.5 %collective-permute-start.3 = (bf16[256,384]{1,0:T(8,128)(2,1)}, bf16[256,384]{1,0:T(8,128)(2,1)S(1)}, u32[]{:S(2)}, u32[]{:S(2)}) collective-permute-start(bf16[256,384]{1,0:T(8,128)(2,1)} %shard_map.114), channel_id=1, source_target_pairs={{0,488},{8,496},{16,504},{24,0},{32,8},{40,16},{48,24},{56,32},{64... | collective-permute-start | bytes 589832 | tf_op jit(solution)/shard_map/ppermute | solution.py:25
  33.2 14.4 %copy-start.5 = (bf16[8,256,256]{2,1,0:T(8,128)(2,1)}, bf16[8,256,256]{2,1,0:T(8,128)(2,1)S(1)}, u32[]{:S(2)}) copy-start(bf16[8,256,256]{2,1,0:T(8,128)(2,1)S(1)} %collective-permute-done.1.rest_1_) | copy-start | bytes 3145732
  57.1 1.0 copy-start.1
  58.1 0.9 copy-start.2
  119.9 1.0 copy-start.6
  119.9 1.2 copy-start.8
  121.1 0.9 copy-start.4

commit v7 on v6

--- a/solution.py
+++ b/solution.py
@@ -13,7 +13,7 @@
 PATH = 8
 EXTRA = 16
 STAT_LANES = 128
-SHIPPED_PAGES = (1, 2)
+SHIPPED_PAGES = (1,)
 
 
 NEGATIVE = -1e30

time: 123 us -> 114 us (0.927)
  waiting for transfers between devices: 21.1 us -> 3.89 us
  blocking collectives: 57.9 us -> 62.3 us
  starting transfers between devices: 13.3 us -> 15.5 us
  Pallas kernels: 20.3 us -> 22.2 us
    ppermute x4 -> x5, waiting for transfers between devices: 21.1 us -> 3.89 us  [shifted(): return lax.ppermute(value, axis, pairs)]
    all_to_all x1, blocking collectives: 57.9 us -> 62.3 us  [per_device(): gathered = lax.all_to_all(pieces, 'tp', 0, 0, tiled=False)]
    pallas_call x1 -> x2, Pallas kernels: 4.04 us -> 8.07 us  [holder_partial(): pl.pallas_call(functools.partial(holder_kernel, page_index, group), out_s...]
    pallas_call x1, Pallas kernels: 9.5 us -> 7.3 us  [local_partial(): pl.pallas_call(functools.partial(local_kernel, group, page_ids), out_shap...]
    ppermute x4 -> x5, starting transfers between devices: 13.3 us -> 15.5 us  [shifted(): return lax.ppermute(value, axis, pairs)]
  transfers between devices with their start and end apart: 4 -> 5, of which waited for: 3 -> 1; matrix products, arithmetic and copies ran while one was open for 1% -> 1% of each run, Pallas kernels for 14% -> 17%
where the time goes in v7:
time: 114 us; the launch traced here: 113 us
  blocking collectives  62.3 us (55%)
  Pallas kernels  22.2 us (19%)
  starting transfers between devices  15.5 us (14%)
  local copies, waits for them, and re-layouts  6.98 us (6%)
  waiting for transfers between devices  3.89 us (3%)
  other arithmetic  1.44 us (1%)
    all_to_all x1, blocking collectives, per_device(): gathered = lax.all_to_all(pieces, 'tp', 0, 0, tiled=False)  62.3 us
    ppermute x5, starting transfers between devices, shifted(): return lax.ppermute(value, axis, pairs)  15.5 us
    pallas_call x2, Pallas kernels, holder_partial(): pl.pallas_call(functools.partial(holder_kernel, page_index, group), out_s...  8.07 us
    pallas_call x1, Pallas kernels, local_partial(): pl.pallas_call(functools.partial(local_kernel, group, page_ids), out_shap...  7.3 us
    ppermute x5, waiting for transfers between devices, shifted(): return lax.ppermute(value, axis, pairs)  3.89 us
    unnamed x22, local copies, waits for them, and re-layouts  3.84 us
    pallas_call x1, Pallas kernels, tree_partial(): pl.pallas_call(functools.partial(tree_kernel, group), out_shape=(jax.Shap...  3.72 us
    pallas_call x1, Pallas kernels, merge_project(): pl.pallas_call(functools.partial(merge_kernel, group), out_shape=jax.Shap...  3.11 us
  transfers between devices with their start and end apart: 5, of which 1 were waited for; matrix products, arithmetic and copies ran while one was open for 1% of the time, Pallas kernels for 17%

profile of v7, /device:TPU:6, one launch (start us, length us, event | category | flops | bytes accessed | tf_op | source)
XLA Modules:
  0.0 113.1 jit_solution(12394249169168502743)
XLA Ops:
  0.6 0.0 copy-start.10
  0.6 0.0 copy-start.3
  0.7 0.0 copy-start.9
  0.7 2.4 %slice_bitcast_fusion = bf16[8,256,256]{2,1,0:T(8,128)(2,1)} fusion(bf16[8,4,256,256]{3,2,1,0:T(8,128)(2,1)} %kv_ref.5), kind=kLoop, calls=%fused_computation.1 | loop fusion | bytes 2097152 | tf_op jit(solution)/shard_map/squeeze | solution.py:291
  3.0 5.1 %collective-permute-start = (bf16[8,256,256]{2,1,0:T(8,128)(2,1)}, bf16[8,256,256]{2,1,0:T(8,128)(2,1)}, u32[]{:S(2)}, u32[]{:S(2)}) collective-permute-start(bf16[8,256,256]{2,1,0:T(8,128)(2,1)} %slice_bitcast_fusion), channel_id=1, source_target_pairs={{0,504},{8,0},{16,8},{24,16},{32,24},{40,32},{48,40},{56,48},{64,5... | collective-permute-start | bytes 3145736 | tf_op jit(solution)/shard_map/ppermute | solution.py:25
  8.1 0.0 copy-done.10
  8.1 0.0 copy-done.3
  8.2 1.9 %collective-permute-start.3 = (bf16[272,256]{1,0:T(8,128)(2,1)S(1)}, bf16[272,256]{1,0:T(8,128)(2,1)S(1)}, u32[]{:S(2)}, u32[]{:S(2)}) collective-permute-start(bf16[272,256]{1,0:T(8,128)(2,1)S(1)} %pad_maximum_fusion), channel_id=1, source_target_pairs={{0,24},{8,32},{16,40},{24,48},{32,56},{40,64},{48,72},{56,80},{64,... | collective-permute-start | bytes 417800 | tf_op jit(solution)/shard_map/ppermute | solution.py:25
  10.1 2.0 %collective-permute-start.1 = (bf16[272,256]{1,0:T(8,128)(2,1)S(1)}, bf16[272,256]{1,0:T(8,128)(2,1)S(1)}, u32[]{:S(2)}, u32[]{:S(2)}) collective-permute-start(bf16[272,256]{1,0:T(8,128)(2,1)S(1)} %pad_maximum_fusion), channel_id=1, source_target_pairs={{0,16},{8,24},{16,32},{24,40},{32,48},{40,56},{48,64},{56,72},{64,... | collective-permute-start | bytes 417800 | tf_op jit(solution)/shard_map/ppermute | solution.py:25
  12.1 0.0 copy-done.9
  12.1 0.1 broadcast_add_fusion
  12.2 0.8 reshape.28.parent_ref
  13.0 3.7 %shard_map.112 = (f32[256,384]{1,0:T(8,128)}, bf16[8,8,256]{2,1,0:T(8,128)(2,1)}) custom-call(s32[8]{0:T(128)} %acc_ref.1, bf16[256,256]{1,0:T(8,128)(2,1)} %q_ref.3, bf16[256,256]{1,0:T(8,128)(2,1)} %fresh_ref.1, s32[256,1]{1,0:T(8,128)} %reshape.28.parent_ref), custom_call_target="tpu_custom_call" | custom-call | tf_op jit(solution)/shard_map/pallas_call | solution.py:102
  16.7 3.9 %collective-permute-done.1.q_ref = bf16[272,256]{1,0:T(8,128)(2,1)S(1)} collective-permute-done((bf16[272,256]{1,0:T(8,128)(2,1)S(1)}, bf16[272,256]{1,0:T(8,128)(2,1)S(1)}, u32[]{:S(2)}, u32[]{:S(2)}) %collective-permute-start.1) | collective-permute-done | bytes 139296 | tf_op jit(solution)/shard_map/ppermute | solution.py:25
  20.6 0.0 copy-start.7
  20.6 0.7 copy-done.7
  21.2 4.0 %shard_map.114 = bf16[256,384]{1,0:T(8,128)(2,1)} custom-call(bf16[272,256]{1,0:T(8,128)(2,1)} %copy-done.7, bf16[8,4,256,256]{3,2,1,0:T(8,128)(2,1)} %kv_ref.5, f32[256,384]{1,0:T(8,128)} %get-tuple-element.7.tree_ref.order_ref), custom_call_target="tpu_custom_call" | custom-call | tf_op jit(solution)/shard_map/pallas_call | solution.py:213
  25.3 2.1 %collective-permute-start.2 = (bf16[256,384]{1,0:T(8,128)(2,1)}, bf16[256,384]{1,0:T(8,128)(2,1)S(1)}, u32[]{:S(2)}, u32[]{:S(2)}) collective-permute-start(bf16[256,384]{1,0:T(8,128)(2,1)} %shard_map.114), channel_id=1, source_target_pairs={{0,496},{8,504},{16,0},{24,8},{32,16},{40,24},{48,32},{56,40},{64,... | collective-permute-start | bytes 589832 | tf_op jit(solution)/shard_map/ppermute | solution.py:25
  27.4 0.0 collective-permute-done.3.q_ref
  27.4 0.0 copy-start.6
  27.4 0.6 copy-done.6
  28.1 4.0 %shard_map.115 = bf16[256,384]{1,0:T(8,128)(2,1)} custom-call(bf16[272,256]{1,0:T(8,128)(2,1)} %copy-done.6, bf16[8,4,256,256]{3,2,1,0:T(8,128)(2,1)} %kv_ref.5, f32[256,384]{1,0:T(8,128)} %get-tuple-element.7.tree_ref.order_ref), custom_call_target="tpu_custom_call" | custom-call | tf_op jit(solution)/shard_map/pallas_call | solution.py:213
  32.1 0.0 copy-start
  32.1 4.4 %collective-permute-start.4 = (bf16[256,384]{1,0:T(8,128)(2,1)}, bf16[256,384]{1,0:T(8,128)(2,1)S(1)}, u32[]{:S(2)}, u32[]{:S(2)}) collective-permute-start(bf16[256,384]{1,0:T(8,128)(2,1)} %shard_map.115), channel_id=1, source_target_pairs={{0,488},{8,496},{16,504},{24,0},{32,8},{40,16},{48,24},{56,32},{64... | collective-permute-start | bytes 589832 | tf_op jit(solution)/shard_map/ppermute | solution.py:25
  36.5 0.0 collective-permute-done.rest_0_
  36.5 7.3 %shard_map.113 = (f32[256,256]{1,0:T(8,128)}, f32[256,128]{1,0:T(8,128)}) custom-call(s32[8]{0:T(128)} %lens_ref.1, bf16[256,256]{1,0:T(8,128)(2,1)} %q_ref.3, bf16[8,4,256,256]{3,2,1,0:T(8,128)(2,1)} %kv_ref.5, f32[256,384]{1,0:T(8,128)} %get-tuple-element.7.tree_ref.order_ref, bf16[8,256,256]{2,1,0:T(8,128)(2,1)} %collective-permute-done.rest_0_), custom_call_target="tpu_custom_call" | custom-call | tf_op jit(solution)/shard_map/pallas_call | solution.py:159
  43.8 0.0 collective-permute-done.2.rest_0_
  43.8 0.0 collective-permute-done.4.rest_1_
  43.8 0.0 copy-done
  43.8 0.0 copy-start.1
  43.8 0.9 copy-done.1
  44.8 0.0 copy-start.2
  44.8 0.9 copy-done.2
  45.7 3.1 %shard_map.116 = bf16[256,4096]{1,0:T(8,128)(2,1)S(1)} custom-call(f32[256,256]{1,0:T(8,128)S(1)} %copy-done.1, f32[256,128]{1,0:T(8,128)S(1)} %copy-done.2, bf16[256,384]{1,0:T(8,128)(2,1)S(1)} %collective-permute-done.2.rest_0_, bf16[256,384]{1,0:T(8,128)(2,1)S(1)} %collective-permute-done.4.rest_1_, bf16[256,4096]{1,0:T(8,128)(2,1)S(1)} %copy-done), custom_call_target="tpu_custom_call" | custom-call | tf_op jit(solution)/shard_map/pallas_call | solution.py:265
  48.8 62.3 %all_to_all.5 = bf16[8,32,4096]{2,1,0:T(8,128)(2,1)S(1)} all-to-all(bf16[8,32,4096]{2,1,0:T(8,128)(2,1)S(1)} %bitcast.9), channel_id=1, replica_groups=mesh['req'=64,'tp'=8] {'tp'}, dimensions={0} | all-to-all | bytes 4194304 | tf_op jit(solution)/shard_map/all_to_all | solution.py:305
  111.1 0.0 copy-start.5
  111.1 0.0 copy-start.8
  111.1 0.3 convert_reduce_fusion
  111.4 0.6 copy-done.5
  112.0 0.2 fusion
  112.2 0.0 copy-start.4
  112.2 0.0 copy-done.8
  112.3 0.8 fusion.2
  113.1 0.0 copy-done.4
  (5 shorter events, 0.0 us)
Async XLA Ops:
  0.6 7.5 %copy-start.10 = (s32[8]{0:T(128)S(1)}, s32[8]{0:T(128)}, u32[]{:S(2)}) copy-start(s32[8]{0:T(128)} %lens_ref.1) | copy-start | bytes 100
  0.6 7.5 %copy-start.3 = (bf16[256,256]{1,0:T(8,128)(2,1)S(1)}, bf16[256,256]{1,0:T(8,128)(2,1)}, u32[]{:S(2)}) copy-start(bf16[256,256]{1,0:T(8,128)(2,1)} %q_ref.3) | copy-start | bytes 393220
  0.7 11.5 %copy-start.9 = (s32[8,32]{1,0:T(8,128)S(1)}, s32[8,32]{1,0:T(8,128)}, u32[]{:S(2)}) copy-start(s32[8,32]{1,0:T(8,128)} %param.13) | copy-start | bytes 3076
  3.0 33.5 %collective-permute-start = (bf16[8,256,256]{2,1,0:T(8,128)(2,1)}, bf16[8,256,256]{2,1,0:T(8,128)(2,1)}, u32[]{:S(2)}, u32[]{:S(2)}) collective-permute-start(bf16[8,256,256]{2,1,0:T(8,128)(2,1)} %slice_bitcast_fusion), channel_id=1, source_target_pairs={{0,504},{8,0},{16,8},{24,16},{32,24},{40,32},{48,40},{56,48},{64,5... | collective-permute-start | bytes 3145736 | tf_op jit(solution)/shard_map/ppermute | solution.py:25
  8.2 19.2 %collective-permute-start.3 = (bf16[272,256]{1,0:T(8,128)(2,1)S(1)}, bf16[272,256]{1,0:T(8,128)(2,1)S(1)}, u32[]{:S(2)}, u32[]{:S(2)}) collective-permute-start(bf16[272,256]{1,0:T(8,128)(2,1)S(1)} %pad_maximum_fusion), channel_id=1, source_target_pairs={{0,24},{8,32},{16,40},{24,48},{32,56},{40,64},{48,72},{56,80},{64,... | collective-permute-start | bytes 417800 | tf_op jit(solution)/shard_map/ppermute | solution.py:25
  10.1 10.5 %collective-permute-start.1 = (bf16[272,256]{1,0:T(8,128)(2,1)S(1)}, bf16[272,256]{1,0:T(8,128)(2,1)S(1)}, u32[]{:S(2)}, u32[]{:S(2)}) collective-permute-start(bf16[272,256]{1,0:T(8,128)(2,1)S(1)} %pad_maximum_fusion), channel_id=1, source_target_pairs={{0,16},{8,24},{16,32},{24,40},{32,48},{40,56},{48,64},{56,72},{64,... | collective-permute-start | bytes 417800 | tf_op jit(solution)/shard_map/ppermute | solution.py:25
  20.6 0.7 copy-start.7
  25.3 18.5 %collective-permute-start.2 = (bf16[256,384]{1,0:T(8,128)(2,1)}, bf16[256,384]{1,0:T(8,128)(2,1)S(1)}, u32[]{:S(2)}, u32[]{:S(2)}) collective-permute-start(bf16[256,384]{1,0:T(8,128)(2,1)} %shard_map.114), channel_id=1, source_target_pairs={{0,496},{8,504},{16,0},{24,8},{32,16},{40,24},{48,32},{56,40},{64,... | collective-permute-start | bytes 589832 | tf_op jit(solution)/shard_map/ppermute | solution.py:25
  27.4 0.7 copy-start.6
  32.1 11.7 %copy-start = (bf16[256,4096]{1,0:T(8,128)(2,1)S(1)}, bf16[256,4096]{1,0:T(8,128)(2,1)}, u32[]{:S(2)}) copy-start(bf16[256,4096]{1,0:T(8,128)(2,1)} %rest_2_.1) | copy-start | bytes 6291460
  32.1 11.7 %collective-permute-start.4 = (bf16[256,384]{1,0:T(8,128)(2,1)}, bf16[256,384]{1,0:T(8,128)(2,1)S(1)}, u32[]{:S(2)}, u32[]{:S(2)}) collective-permute-start(bf16[256,384]{1,0:T(8,128)(2,1)} %shard_map.115), channel_id=1, source_target_pairs={{0,488},{8,496},{16,504},{24,0},{32,8},{40,16},{48,24},{56,32},{64... | collective-permute-start | bytes 589832 | tf_op jit(solution)/shard_map/ppermute | solution.py:25
  43.8 1.0 copy-start.1
  44.8 0.9 copy-start.2
  111.1 1.0 copy-start.5
  111.1 1.2 %copy-start.8 = (f32[4096]{0:T(1024)S(1)}, f32[4096]{0:T(1024)}, u32[]{:S(2)}) copy-start(f32[4096]{0:T(1024)} %param.17) | copy-start | bytes 49156
  112.2 0.9 copy-start.4

commit v8 on v7

--- a/solution.py
+++ b/solution.py
@@ -274,6 +274,35 @@
     )(sums, stats, *returned, w_out)
 
 
+def chain_reduce_scatter(product, axis):
+    count = lax.axis_size(axis)
+    me = lax.axis_index(axis)
+    chunk = product.shape[0] // count
+    pieces = product.reshape(count, chunk, product.shape[1])
+
+    def piece(offset):
+        return lax.dynamic_index_in_dim(pieces, (me + offset) % count, 0, keepdims=False)
+
+    forward_hops = count // 2
+    backward_hops = count - 1 - forward_hops
+    forward = piece(forward_hops)
+    backward = piece(-backward_hops) if backward_hops > 0 else None
+    for step in range(1, forward_hops + 1):
+        forward = shifted(forward, axis, 1)
+        if backward is not None and step <= backward_hops:
+            backward = shifted(backward, axis, -1)
+        if step < forward_hops:
+            forward = (forward.astype(jnp.float32)
+                       + piece(forward_hops - step).astype(jnp.float32)).astype(jnp.bfloat16)
+        if backward is not None and step < backward_hops:
+            backward = (backward.astype(jnp.float32)
+                        + piece(step - backward_hops).astype(jnp.float32)).astype(jnp.bfloat16)
+    total = piece(0).astype(jnp.float32) + forward.astype(jnp.float32)
+    if backward is not None:
+        total = total + backward.astype(jnp.float32)
+    return total
+
+
 def pack_queries(queries, lengths):
     width = queries.shape[1]
     count = lengths.shape[0]
@@ -300,10 +329,7 @@
     sums, stats = local_partial(cache_lens, queries, kv_pool, tree_part, shipped, group)
 
     product = merge_project(sums, stats, returned, w_out, group)
-    tp_count = lax.axis_size("tp")
-    pieces = product.reshape(tp_count, product.shape[0] // tp_count, product.shape[1])
-    gathered = lax.all_to_all(pieces, "tp", 0, 0, tiled=False)
-    summed = jnp.sum(gathered.astype(jnp.float32), axis=0)
+    summed = chain_reduce_scatter(product, "tp")
     hidden_out = (residual.astype(jnp.float32) + summed).astype(jnp.bfloat16)
     widened = hidden_out.astype(jnp.float32)
     normed = (

time: 114 us -> 106 us (0.930)
  the two profiles are of different devices: /device:TPU:6 before, /device:TPU:62 now
where the time goes in v8:
time: 106 us
  starting transfers between devices  41.3 us (39%)
  waiting for transfers between devices  30.7 us (29%)
  Pallas kernels  22.2 us (21%)
  local copies, waits for them, and re-layouts  7.98 us (8%)
  other arithmetic  2.48 us (2%)
    ppermute x12, starting transfers between devices, shifted(): return lax.ppermute(value, axis, pairs)  41.3 us
    ppermute x12, waiting for transfers between devices, shifted(): return lax.ppermute(value, axis, pairs)  30.7 us
    pallas_call x2, Pallas kernels, holder_partial(): pl.pallas_call(functools.partial(holder_kernel, page_index, group), out_s...  8.07 us
    pallas_call x1, Pallas kernels, local_partial(): pl.pallas_call(functools.partial(local_kernel, group, page_ids), out_shap...  7.32 us
    unnamed x24, local copies, waits for them, and re-layouts  5.79 us
    pallas_call x1, Pallas kernels, tree_partial(): pl.pallas_call(functools.partial(tree_kernel, group), out_shape=(jax.Shap...  3.7 us
    pallas_call x1, Pallas kernels, merge_project(): pl.pallas_call(functools.partial(merge_kernel, group), out_shape=jax.Shap...  3.11 us
  transfers between devices with their start and end apart: 12, of which 7 were waited for; matrix products, arithmetic and copies ran while one was open for 2% of the time, Pallas kernels for 18%

profile of v8, /device:TPU:62, one launch (start us, length us, event | category | flops | bytes accessed | tf_op | source)
XLA Modules:
  0.0 105.7 jit_solution(3747864611506024820)
XLA Ops:
  0.6 0.0 copy-start.11
  0.6 0.0 copy-start.3
  0.7 1.3 %slice_bitcast_fusion = bf16[8,256,256]{2,1,0:T(8,128)(2,1)S(1)} fusion(bf16[8,4,256,256]{3,2,1,0:T(8,128)(2,1)} %kv_ref.5), kind=kLoop, calls=%fused_computation | loop fusion | bytes 2097152 | tf_op jit(solution)/shard_map/squeeze | solution.py:320
  2.0 2.7 %collective-permute-start = (bf16[8,256,256]{2,1,0:T(8,128)(2,1)S(1)}, bf16[8,256,256]{2,1,0:T(8,128)(2,1)S(1)}, u32[]{:S(2)}, u32[]{:S(2)}) collective-permute-start(bf16[8,256,256]{2,1,0:T(8,128)(2,1)S(1)} %slice_bitcast_fusion), channel_id=1, source_target_pairs={{0,504},{8,0},{16,8},{24,16},{32,24},{40,32},{48,40},{56,48},{64,5... | collective-permute-start | bytes 3145736 | tf_op jit(solution)/shard_map/ppermute | solution.py:25
  4.8 6.2 %collective-permute-start.1 = (bf16[272,256]{1,0:T(8,128)(2,1)S(1)}, bf16[272,256]{1,0:T(8,128)(2,1)S(1)}, u32[]{:S(2)}, u32[]{:S(2)}) collective-permute-start(bf16[272,256]{1,0:T(8,128)(2,1)S(1)} %pad_maximum_fusion), channel_id=1, source_target_pairs={{0,16},{8,24},{16,32},{24,40},{32,48},{40,56},{48,64},{56,72},{64,... | collective-permute-start | bytes 417800 | tf_op jit(solution)/shard_map/ppermute | solution.py:25
  11.0 2.0 %collective-permute-start.3 = (bf16[272,256]{1,0:T(8,128)(2,1)S(1)}, bf16[272,256]{1,0:T(8,128)(2,1)S(1)}, u32[]{:S(2)}, u32[]{:S(2)}) collective-permute-start(bf16[272,256]{1,0:T(8,128)(2,1)S(1)} %pad_maximum_fusion), channel_id=1, source_target_pairs={{0,24},{8,32},{16,40},{24,48},{32,56},{40,64},{48,72},{56,80},{64,... | collective-permute-start | bytes 417800 | tf_op jit(solution)/shard_map/ppermute | solution.py:25
  13.0 0.1 broadcast_add_fusion
  13.1 0.8 reshape.46.parent_ref
  13.9 3.7 %shard_map.112 = (f32[256,384]{1,0:T(8,128)}, bf16[8,8,256]{2,1,0:T(8,128)(2,1)}) custom-call(s32[8]{0:T(128)} %acc_ref.1, bf16[256,256]{1,0:T(8,128)(2,1)} %q_ref.3, bf16[256,256]{1,0:T(8,128)(2,1)} %fresh_ref.1, s32[256,1]{1,0:T(8,128)} %reshape.46.parent_ref), custom_call_target="tpu_custom_call" | custom-call | tf_op jit(solution)/shard_map/pallas_call | solution.py:102
  17.6 0.0 collective-permute-done.1.q_ref
  17.6 0.7 copy-done.8
  18.3 4.0 %shard_map.114 = bf16[256,384]{1,0:T(8,128)(2,1)} custom-call(bf16[272,256]{1,0:T(8,128)(2,1)} %copy-done.8, bf16[8,4,256,256]{3,2,1,0:T(8,128)(2,1)} %kv_ref.5, f32[256,384]{1,0:T(8,128)} %get-tuple-element.7.tree_ref.order_ref), custom_call_target="tpu_custom_call" | custom-call | tf_op jit(solution)/shard_map/pallas_call | solution.py:213
  22.3 3.6 %collective-permute-start.2 = (bf16[256,384]{1,0:T(8,128)(2,1)}, bf16[256,384]{1,0:T(8,128)(2,1)S(1)}, u32[]{:S(2)}, u32[]{:S(2)}) collective-permute-start(bf16[256,384]{1,0:T(8,128)(2,1)} %shard_map.114), channel_id=1, source_target_pairs={{0,496},{8,504},{16,0},{24,8},{32,16},{40,24},{48,32},{56,40},{64,... | collective-permute-start | bytes 589832 | tf_op jit(solution)/shard_map/ppermute | solution.py:25
  26.0 0.0 copy-start.7
  26.0 0.6 copy-done.7
  26.6 4.0 %shard_map.115 = bf16[256,384]{1,0:T(8,128)(2,1)} custom-call(bf16[272,256]{1,0:T(8,128)(2,1)} %copy-done.7, bf16[8,4,256,256]{3,2,1,0:T(8,128)(2,1)} %kv_ref.5, f32[256,384]{1,0:T(8,128)} %get-tuple-element.7.tree_ref.order_ref), custom_call_target="tpu_custom_call" | custom-call | tf_op jit(solution)/shard_map/pallas_call | solution.py:213
  30.7 2.7 %collective-permute-start.4 = (bf16[256,384]{1,0:T(8,128)(2,1)}, bf16[256,384]{1,0:T(8,128)(2,1)S(1)}, u32[]{:S(2)}, u32[]{:S(2)}) collective-permute-start(bf16[256,384]{1,0:T(8,128)(2,1)} %shard_map.115), channel_id=1, source_target_pairs={{0,488},{8,496},{16,504},{24,0},{32,8},{40,16},{48,24},{56,32},{64... | collective-permute-start | bytes 589832 | tf_op jit(solution)/shard_map/ppermute | solution.py:25
  33.4 0.0 collective-permute-done.rest_0_
  33.4 1.0 copy-done.5
  34.4 7.3 %shard_map.113 = (f32[256,256]{1,0:T(8,128)}, f32[256,128]{1,0:T(8,128)}) custom-call(s32[8]{0:T(128)} %lens_ref.1, bf16[256,256]{1,0:T(8,128)(2,1)} %q_ref.3, bf16[8,4,256,256]{3,2,1,0:T(8,128)(2,1)} %kv_ref.5, f32[256,384]{1,0:T(8,128)} %get-tuple-element.7.tree_ref.order_ref, bf16[8,256,256]{2,1,0:T(8,128)(2,1)} %copy-done.5), custom_call_target="tpu_custom_call" | custom-call | tf_op jit(solution)/shard_map/pallas_call | solution.py:159
  41.7 0.0 collective-permute-done.2.rest_0_
  41.7 2.3 %collective-permute-done.4.rest_1_ = bf16[256,384]{1,0:T(8,128)(2,1)S(1)} collective-permute-done((bf16[256,384]{1,0:T(8,128)(2,1)}, bf16[256,384]{1,0:T(8,128)(2,1)S(1)}, u32[]{:S(2)}, u32[]{:S(2)}) %collective-permute-start.4) | collective-permute-done | bytes 196640 | tf_op jit(solution)/shard_map/ppermute | solution.py:25
  44.0 1.6 %copy-done = bf16[256,4096]{1,0:T(8,128)(2,1)S(1)} copy-done((bf16[256,4096]{1,0:T(8,128)(2,1)S(1)}, bf16[256,4096]{1,0:T(8,128)(2,1)}, u32[]{:S(2)}) %copy-start) | copy-done | bytes 2097176
  45.6 0.9 copy-done.1
  46.6 0.9 copy-done.2
  47.5 3.1 %shard_map.116 = bf16[256,4096]{1,0:T(8,128)(2,1)S(1)} custom-call(f32[256,256]{1,0:T(8,128)S(1)} %copy-done.1, f32[256,128]{1,0:T(8,128)S(1)} %copy-done.2, bf16[256,384]{1,0:T(8,128)(2,1)S(1)} %collective-permute-done.2.rest_0_, bf16[256,384]{1,0:T(8,128)(2,1)S(1)} %collective-permute-done.4.rest_1_, bf16[256,4096]{1,0:T(8,128)(2,1)S(1)} %copy-done), custom_call_target="tpu_custom_call" | custom-call | tf_op jit(solution)/shard_map/pallas_call | solution.py:265
  50.6 0.1 dynamic-slice_bitcast_fusion.1
  50.6 0.0 copy-start.6
  50.7 2.1 %collective-permute-start.5 = (bf16[32,4096]{1,0:T(8,128)(2,1)S(1)}, bf16[32,4096]{1,0:T(8,128)(2,1)}, u32[]{:S(2)}, u32[]{:S(2)}) collective-permute-start(bf16[32,4096]{1,0:T(8,128)(2,1)S(1)} %get-tuple-element.17), channel_id=1, source_target_pairs={{0,1},{1,2},{2,3},{3,4},{4,5},{5,6},{6,7},{7,0},{8,9},{9,10},{10,1... | collective-permute-start | bytes 786440 | tf_op jit(solution)/shard_map/ppermute | solution.py:25
  52.7 8.4 %collective-permute-start.9 = (bf16[32,4096]{1,0:T(8,128)(2,1)S(1)}, bf16[32,4096]{1,0:T(8,128)(2,1)S(1)}, u32[]{:S(2)}, u32[]{:S(2)}) collective-permute-start(bf16[32,4096]{1,0:T(8,128)(2,1)S(1)} %get-tuple-element.18), channel_id=1, source_target_pairs={{0,7},{1,0},{2,1},{3,2},{4,3},{5,4},{6,5},{7,6},{8,15},{9,8},{10,9... | collective-permute-start | bytes 786440 | tf_op jit(solution)/shard_map/ppermute | solution.py:25
  61.1 3.3 %collective-permute-done.5 = bf16[32,4096]{1,0:T(8,128)(2,1)} collective-permute-done((bf16[32,4096]{1,0:T(8,128)(2,1)S(1)}, bf16[32,4096]{1,0:T(8,128)(2,1)}, u32[]{:S(2)}, u32[]{:S(2)}) %collective-permute-start.5) | collective-permute-done | bytes 262176 | tf_op jit(solution)/shard_map/ppermute | solution.py:25
  64.4 1.0 fusion.7
  65.5 1.9 %collective-permute-start.6 = (bf16[32,4096]{1,0:T(8,128)(2,1)S(1)}, bf16[32,4096]{1,0:T(8,128)(2,1)S(1)}, u32[]{:S(2)}, u32[]{:S(2)}) collective-permute-start(bf16[32,4096]{1,0:T(8,128)(2,1)S(1)} %fusion.7), channel_id=1, source_target_pairs={{0,1},{1,2},{2,3},{3,4},{4,5},{5,6},{6,7},{7,0},{8,9},{9,10},{10,1... | collective-permute-start | bytes 786440 | tf_op jit(solution)/shard_map/ppermute | solution.py:25
  67.4 0.0 copy-start.9
  67.4 0.0 collective-permute-done.9
  67.4 9.5 %collective-permute-done.6 = bf16[32,4096]{1,0:T(8,128)(2,1)S(1)} collective-permute-done((bf16[32,4096]{1,0:T(8,128)(2,1)S(1)}, bf16[32,4096]{1,0:T(8,128)(2,1)S(1)}, u32[]{:S(2)}, u32[]{:S(2)}) %collective-permute-start.6) | collective-permute-done | bytes 262176 | tf_op jit(solution)/shard_map/ppermute | solution.py:25
  76.9 0.1 fusion.6
  77.1 3.1 %collective-permute-start.10 = (bf16[32,4096]{1,0:T(8,128)(2,1)S(1)}, bf16[32,4096]{1,0:T(8,128)(2,1)S(1)}, u32[]{:S(2)}, u32[]{:S(2)}) collective-permute-start(bf16[32,4096]{1,0:T(8,128)(2,1)S(1)} %get-tuple-element.16), channel_id=1, source_target_pairs={{0,7},{1,0},{2,1},{3,2},{4,3},{5,4},{6,5},{7,6},{8,15},{9,8},{10,9... | collective-permute-start | bytes 786440 | tf_op jit(solution)/shard_map/ppermute | solution.py:25
  80.2 2.8 %collective-permute-start.7 = (bf16[32,4096]{1,0:T(8,128)(2,1)S(1)}, bf16[32,4096]{1,0:T(8,128)(2,1)S(1)}, u32[]{:S(2)}, u32[]{:S(2)}) collective-permute-start(bf16[32,4096]{1,0:T(8,128)(2,1)S(1)} %get-tuple-element.15), channel_id=1, source_target_pairs={{0,1},{1,2},{2,3},{3,4},{4,5},{5,6},{6,7},{7,0},{8,9},{9,10},{10,1... | collective-permute-start | bytes 786440 | tf_op jit(solution)/shard_map/ppermute | solution.py:25
  83.0 4.8 %collective-permute-done.10 = bf16[32,4096]{1,0:T(8,128)(2,1)S(1)} collective-permute-done((bf16[32,4096]{1,0:T(8,128)(2,1)S(1)}, bf16[32,4096]{1,0:T(8,128)(2,1)S(1)}, u32[]{:S(2)}, u32[]{:S(2)}) %collective-permute-start.10) | collective-permute-done | bytes 262176 | tf_op jit(solution)/shard_map/ppermute | solution.py:25
  87.8 3.9 %collective-permute-done.7 = bf16[32,4096]{1,0:T(8,128)(2,1)S(1)} collective-permute-done((bf16[32,4096]{1,0:T(8,128)(2,1)S(1)}, bf16[32,4096]{1,0:T(8,128)(2,1)S(1)}, u32[]{:S(2)}, u32[]{:S(2)}) %collective-permute-start.7) | collective-permute-done | bytes 262176 | tf_op jit(solution)/shard_map/ppermute | solution.py:25
  91.7 0.1 fusion.5
  91.9 1.9 %collective-permute-start.11 = (bf16[32,4096]{1,0:T(8,128)(2,1)S(1)}, bf16[32,4096]{1,0:T(8,128)(2,1)S(1)}, u32[]{:S(2)}, u32[]{:S(2)}) collective-permute-start(bf16[32,4096]{1,0:T(8,128)(2,1)S(1)} %get-tuple-element.14), channel_id=1, source_target_pairs={{0,7},{1,0},{2,1},{3,2},{4,3},{5,4},{6,5},{7,6},{8,15},{9,8},{10,9... | collective-permute-start | bytes 786440 | tf_op jit(solution)/shard_map/ppermute | solution.py:25
  93.8 3.9 %collective-permute-start.8 = (bf16[32,4096]{1,0:T(8,128)(2,1)S(1)}, bf16[32,4096]{1,0:T(8,128)(2,1)S(1)}, u32[]{:S(2)}, u32[]{:S(2)}) collective-permute-start(bf16[32,4096]{1,0:T(8,128)(2,1)S(1)} %get-tuple-element.13), channel_id=1, source_target_pairs={{0,1},{1,2},{2,3},{3,4},{4,5},{5,6},{6,7},{7,0},{8,9},{9,10},{10,1... | collective-permute-start | bytes 786440 | tf_op jit(solution)/shard_map/ppermute | solution.py:25
  97.7 3.7 %collective-permute-done.11 = bf16[32,4096]{1,0:T(8,128)(2,1)S(1)} collective-permute-done((bf16[32,4096]{1,0:T(8,128)(2,1)S(1)}, bf16[32,4096]{1,0:T(8,128)(2,1)S(1)}, u32[]{:S(2)}, u32[]{:S(2)}) %collective-permute-start.11) | collective-permute-done | bytes 262176 | tf_op jit(solution)/shard_map/ppermute | solution.py:25
  101.4 3.1 %collective-permute-done.8 = bf16[32,4096]{1,0:T(8,128)(2,1)S(1)} collective-permute-done((bf16[32,4096]{1,0:T(8,128)(2,1)S(1)}, bf16[32,4096]{1,0:T(8,128)(2,1)S(1)}, u32[]{:S(2)}, u32[]{:S(2)}) %collective-permute-start.8) | collective-permute-done | bytes 262176 | tf_op jit(solution)/shard_map/ppermute | solution.py:25
  104.5 0.3 fusion
  104.8 0.8 fusion.2
  (19 shorter events, 0.1 us)
Async XLA Ops:
  0.6 4.1 %copy-start.11 = (s32[8]{0:T(128)S(1)}, s32[8]{0:T(128)}, u32[]{:S(2)}) copy-start(s32[8]{0:T(128)} %lens_ref.1) | copy-start | bytes 100
  0.6 4.1 %copy-start.3 = (bf16[256,256]{1,0:T(8,128)(2,1)S(1)}, bf16[256,256]{1,0:T(8,128)(2,1)}, u32[]{:S(2)}) copy-start(bf16[256,256]{1,0:T(8,128)(2,1)} %q_ref.3) | copy-start | bytes 393220
  0.7 12.4 %copy-start.10 = (s32[8,32]{1,0:T(8,128)S(1)}, s32[8,32]{1,0:T(8,128)}, u32[]{:S(2)}) copy-start(s32[8,32]{1,0:T(8,128)} %param.13) | copy-start | bytes 3076
  2.0 31.4 %collective-permute-start = (bf16[8,256,256]{2,1,0:T(8,128)(2,1)S(1)}, bf16[8,256,256]{2,1,0:T(8,128)(2,1)S(1)}, u32[]{:S(2)}, u32[]{:S(2)}) collective-permute-start(bf16[8,256,256]{2,1,0:T(8,128)(2,1)S(1)} %slice_bitcast_fusion), channel_id=1, source_target_pairs={{0,504},{8,0},{16,8},{24,16},{32,24},{40,32},{48,40},{56,48},{64,5... | collective-permute-start | bytes 3145736 | tf_op jit(solution)/shard_map/ppermute | solution.py:25
  4.8 12.8 %collective-permute-start.1 = (bf16[272,256]{1,0:T(8,128)(2,1)S(1)}, bf16[272,256]{1,0:T(8,128)(2,1)S(1)}, u32[]{:S(2)}, u32[]{:S(2)}) collective-permute-start(bf16[272,256]{1,0:T(8,128)(2,1)S(1)} %pad_maximum_fusion), channel_id=1, source_target_pairs={{0,16},{8,24},{16,32},{24,40},{32,48},{40,56},{48,64},{56,72},{64,... | collective-permute-start | bytes 417800 | tf_op jit(solution)/shard_map/ppermute | solution.py:25
  11.0 15.0 %collective-permute-start.3 = (bf16[272,256]{1,0:T(8,128)(2,1)S(1)}, bf16[272,256]{1,0:T(8,128)(2,1)S(1)}, u32[]{:S(2)}, u32[]{:S(2)}) collective-permute-start(bf16[272,256]{1,0:T(8,128)(2,1)S(1)} %pad_maximum_fusion), channel_id=1, source_target_pairs={{0,24},{8,32},{16,40},{24,48},{32,56},{40,64},{48,72},{56,80},{64,... | collective-permute-start | bytes 417800 | tf_op jit(solution)/shard_map/ppermute | solution.py:25
  17.6 0.7 copy-start.8
  22.3 19.4 %collective-permute-start.2 = (bf16[256,384]{1,0:T(8,128)(2,1)}, bf16[256,384]{1,0:T(8,128)(2,1)S(1)}, u32[]{:S(2)}, u32[]{:S(2)}) collective-permute-start(bf16[256,384]{1,0:T(8,128)(2,1)} %shard_map.114), channel_id=1, source_target_pairs={{0,496},{8,504},{16,0},{24,8},{32,16},{40,24},{48,32},{56,40},{64,... | collective-permute-start | bytes 589832 | tf_op jit(solution)/shard_map/ppermute | solution.py:25
  26.0 0.7 copy-start.7
  30.7 13.4 %collective-permute-start.4 = (bf16[256,384]{1,0:T(8,128)(2,1)}, bf16[256,384]{1,0:T(8,128)(2,1)S(1)}, u32[]{:S(2)}, u32[]{:S(2)}) collective-permute-start(bf16[256,384]{1,0:T(8,128)(2,1)} %shard_map.115), channel_id=1, source_target_pairs={{0,488},{8,496},{16,504},{24,0},{32,8},{40,16},{48,24},{56,32},{64... | collective-permute-start | bytes 589832 | tf_op jit(solution)/shard_map/ppermute | solution.py:25
  33.4 1.0 copy-start.5
  44.0 1.6 %copy-start = (bf16[256,4096]{1,0:T(8,128)(2,1)S(1)}, bf16[256,4096]{1,0:T(8,128)(2,1)}, u32[]{:S(2)}) copy-start(bf16[256,4096]{1,0:T(8,128)(2,1)} %rest_2_.1) | copy-start | bytes 6291460
  45.6 0.9 copy-start.1
  46.6 0.9 copy-start.2
  50.6 53.9 %copy-start.6 = (bf16[32,4096]{1,0:T(8,128)(2,1)S(1)}, bf16[32,4096]{1,0:T(8,128)(2,1)}, u32[]{:S(2)}) copy-start(bf16[32,4096]{1,0:T(8,128)(2,1)} %param.15) | copy-start | bytes 786436
  50.7 13.8 %collective-permute-start.5 = (bf16[32,4096]{1,0:T(8,128)(2,1)S(1)}, bf16[32,4096]{1,0:T(8,128)(2,1)}, u32[]{:S(2)}, u32[]{:S(2)}) collective-permute-start(bf16[32,4096]{1,0:T(8,128)(2,1)S(1)} %get-tuple-element.17), channel_id=1, source_target_pairs={{0,1},{1,2},{2,3},{3,4},{4,5},{5,6},{6,7},{7,0},{8,9},{9,10},{10,1... | collective-permute-start | bytes 786440 | tf_op jit(solution)/shard_map/ppermute | solution.py:25
  52.7 14.7 %collective-permute-start.9 = (bf16[32,4096]{1,0:T(8,128)(2,1)S(1)}, bf16[32,4096]{1,0:T(8,128)(2,1)S(1)}, u32[]{:S(2)}, u32[]{:S(2)}) collective-permute-start(bf16[32,4096]{1,0:T(8,128)(2,1)S(1)} %get-tuple-element.18), channel_id=1, source_target_pairs={{0,7},{1,0},{2,1},{3,2},{4,3},{5,4},{6,5},{7,6},{8,15},{9,8},{10,9... | collective-permute-start | bytes 786440 | tf_op jit(solution)/shard_map/ppermute | solution.py:25
  65.5 11.5 %collective-permute-start.6 = (bf16[32,4096]{1,0:T(8,128)(2,1)S(1)}, bf16[32,4096]{1,0:T(8,128)(2,1)S(1)}, u32[]{:S(2)}, u32[]{:S(2)}) collective-permute-start(bf16[32,4096]{1,0:T(8,128)(2,1)S(1)} %fusion.7), channel_id=1, source_target_pairs={{0,1},{1,2},{2,3},{3,4},{4,5},{5,6},{6,7},{7,0},{8,9},{9,10},{10,1... | collective-permute-start | bytes 786440 | tf_op jit(solution)/shard_map/ppermute | solution.py:25
  67.4 37.4 %copy-start.9 = (f32[4096]{0:T(1024)S(1)}, f32[4096]{0:T(1024)}, u32[]{:S(2)}) copy-start(f32[4096]{0:T(1024)} %param.17) | copy-start | bytes 49156
  77.1 10.7 %collective-permute-start.10 = (bf16[32,4096]{1,0:T(8,128)(2,1)S(1)}, bf16[32,4096]{1,0:T(8,128)(2,1)S(1)}, u32[]{:S(2)}, u32[]{:S(2)}) collective-permute-start(bf16[32,4096]{1,0:T(8,128)(2,1)S(1)} %get-tuple-element.16), channel_id=1, source_target_pairs={{0,7},{1,0},{2,1},{3,2},{4,3},{5,4},{6,5},{7,6},{8,15},{9,8},{10,9... | collective-permute-start | bytes 786440 | tf_op jit(solution)/shard_map/ppermute | solution.py:25
  80.2 11.6 %collective-permute-start.7 = (bf16[32,4096]{1,0:T(8,128)(2,1)S(1)}, bf16[32,4096]{1,0:T(8,128)(2,1)S(1)}, u32[]{:S(2)}, u32[]{:S(2)}) collective-permute-start(bf16[32,4096]{1,0:T(8,128)(2,1)S(1)} %get-tuple-element.15), channel_id=1, source_target_pairs={{0,1},{1,2},{2,3},{3,4},{4,5},{5,6},{6,7},{7,0},{8,9},{9,10},{10,1... | collective-permute-start | bytes 786440 | tf_op jit(solution)/shard_map/ppermute | solution.py:25
  91.9 9.5 %collective-permute-start.11 = (bf16[32,4096]{1,0:T(8,128)(2,1)S(1)}, bf16[32,4096]{1,0:T(8,128)(2,1)S(1)}, u32[]{:S(2)}, u32[]{:S(2)}) collective-permute-start(bf16[32,4096]{1,0:T(8,128)(2,1)S(1)} %get-tuple-element.14), channel_id=1, source_target_pairs={{0,7},{1,0},{2,1},{3,2},{4,3},{5,4},{6,5},{7,6},{8,15},{9,8},{10,9... | collective-permute-start | bytes 786440 | tf_op jit(solution)/shard_map/ppermute | solution.py:25
  93.8 10.8 %collective-permute-start.8 = (bf16[32,4096]{1,0:T(8,128)(2,1)S(1)}, bf16[32,4096]{1,0:T(8,128)(2,1)S(1)}, u32[]{:S(2)}, u32[]{:S(2)}) collective-permute-start(bf16[32,4096]{1,0:T(8,128)(2,1)S(1)} %get-tuple-element.13), channel_id=1, source_target_pairs={{0,1},{1,2},{2,3},{3,4},{4,5},{5,6},{6,7},{7,0},{8,9},{9,10},{10,1... | collective-permute-start | bytes 786440 | tf_op jit(solution)/shard_map/ppermute | solution.py:25
  104.8 0.9 copy-start.4

commit v9 on v8

--- a/solution.py
+++ b/solution.py
@@ -283,23 +283,25 @@
     def piece(offset):
         return lax.dynamic_index_in_dim(pieces, (me + offset) % count, 0, keepdims=False)
 
-    forward_hops = count // 2
-    backward_hops = count - 1 - forward_hops
-    forward = piece(forward_hops)
-    backward = piece(-backward_hops) if backward_hops > 0 else None
-    for step in range(1, forward_hops + 1):
+    hops = (count - 1) // 2
+    opposite = None
+    if count % 2 == 0:
+        opposite = shifted(piece(count // 2), axis, count // 2)
+    forward = piece(hops) if hops > 0 else None
+    backward = piece(-hops) if hops > 0 else None
+    for step in range(1, hops + 1):
         forward = shifted(forward, axis, 1)
-        if backward is not None and step <= backward_hops:
-            backward = shifted(backward, axis, -1)
-        if step < forward_hops:
+        backward = shifted(backward, axis, -1)
+        if step < hops:
             forward = (forward.astype(jnp.float32)
-                       + piece(forward_hops - step).astype(jnp.float32)).astype(jnp.bfloat16)
-        if backward is not None and step < backward_hops:
+                       + piece(hops - step).astype(jnp.float32)).astype(jnp.bfloat16)
             backward = (backward.astype(jnp.float32)
-                        + piece(step - backward_hops).astype(jnp.float32)).astype(jnp.bfloat16)
-    total = piece(0).astype(jnp.float32) + forward.astype(jnp.float32)
-    if backward is not None:
-        total = total + backward.astype(jnp.float32)
+                        + piece(step - hops).astype(jnp.float32)).astype(jnp.bfloat16)
+    total = piece(0).astype(jnp.float32)
+    if hops > 0:
+        total = total + forward.astype(jnp.float32) + backward.astype(jnp.float32)
+    if opposite is not None:
+        total = total + opposite.astype(jnp.float32)
     return total
 
 

time: 106 us -> 112 us (1.057)
  the two profiles are of different devices: /device:TPU:62 before, /device:TPU:8 now
where the time goes in v9:
time: 112 us; the launch traced here: 111 us
  starting transfers between devices  53.2 us (48%)
  Pallas kernels  22.2 us (20%)
  waiting for transfers between devices  21 us (19%)
  local copies, waits for them, and re-layouts  8.68 us (8%)
  other arithmetic  5.13 us (5%)
    ppermute x12, starting transfers between devices, shifted(): return lax.ppermute(value, axis, pairs)  53.2 us
    ppermute x12, waiting for transfers between devices, shifted(): return lax.ppermute(value, axis, pairs)  21 us
    pallas_call x2, Pallas kernels, holder_partial(): pl.pallas_call(functools.partial(holder_kernel, page_index, group), out_s...  8.06 us
    pallas_call x1, Pallas kernels, local_partial(): pl.pallas_call(functools.partial(local_kernel, group, page_ids), out_shap...  7.31 us
    unnamed x26, local copies, waits for them, and re-layouts  6.47 us
    pallas_call x1, Pallas kernels, tree_partial(): pl.pallas_call(functools.partial(tree_kernel, group), out_shape=(jax.Shap...  3.7 us
    pallas_call x1, Pallas kernels, merge_project(): pl.pallas_call(functools.partial(merge_kernel, group), out_shape=jax.Shap...  3.11 us
    convert_element_type x2, other arithmetic, chain_reduce_scatter(): forward = (forward.astype(jnp.float32) + piece(hops - step).astype(jnp.fl...  2.93 us
  transfers between devices with their start and end apart: 12, of which 6 were waited for; matrix products, arithmetic and copies ran while one was open for 2% of the time, Pallas kernels for 17%

profile of v9, /device:TPU:8, one launch (start us, length us, event | category | flops | bytes accessed | tf_op | source)
XLA Modules:
  0.0 111.3 jit_solution(3837515761054323798)
XLA Ops:
  0.6 0.0 copy-start.12
  0.6 0.0 copy-start.3
  0.7 1.3 %slice_bitcast_fusion = bf16[8,256,256]{2,1,0:T(8,128)(2,1)S(1)} fusion(bf16[8,4,256,256]{3,2,1,0:T(8,128)(2,1)} %kv_ref.5), kind=kLoop, calls=%fused_computation | loop fusion | bytes 2097152 | tf_op jit(solution)/shard_map/squeeze | solution.py:322
  2.0 1.9 %collective-permute-start = (bf16[8,256,256]{2,1,0:T(8,128)(2,1)S(1)}, bf16[8,256,256]{2,1,0:T(8,128)(2,1)S(1)}, u32[]{:S(2)}, u32[]{:S(2)}) collective-permute-start(bf16[8,256,256]{2,1,0:T(8,128)(2,1)S(1)} %slice_bitcast_fusion), channel_id=1, source_target_pairs={{0,504},{8,0},{16,8},{24,16},{32,24},{40,32},{48,40},{56,48},{64,5... | collective-permute-start | bytes 3145736 | tf_op jit(solution)/shard_map/ppermute | solution.py:25
  4.0 3.5 %collective-permute-start.1 = (bf16[272,256]{1,0:T(8,128)(2,1)S(1)}, bf16[272,256]{1,0:T(8,128)(2,1)S(1)}, u32[]{:S(2)}, u32[]{:S(2)}) collective-permute-start(bf16[272,256]{1,0:T(8,128)(2,1)S(1)} %pad_maximum_fusion), channel_id=1, source_target_pairs={{0,16},{8,24},{16,32},{24,40},{32,48},{40,56},{48,64},{56,72},{64,... | collective-permute-start | bytes 417800 | tf_op jit(solution)/shard_map/ppermute | solution.py:25
  7.5 3.3 %collective-permute-start.3 = (bf16[272,256]{1,0:T(8,128)(2,1)S(1)}, bf16[272,256]{1,0:T(8,128)(2,1)S(1)}, u32[]{:S(2)}, u32[]{:S(2)}) collective-permute-start(bf16[272,256]{1,0:T(8,128)(2,1)S(1)} %pad_maximum_fusion), channel_id=1, source_target_pairs={{0,24},{8,32},{16,40},{24,48},{32,56},{40,64},{48,72},{56,80},{64,... | collective-permute-start | bytes 417800 | tf_op jit(solution)/shard_map/ppermute | solution.py:25
  10.8 0.1 broadcast_add_fusion
  10.9 0.8 reshape.43.parent_ref
  11.7 3.7 %shard_map.112 = (f32[256,384]{1,0:T(8,128)}, bf16[8,8,256]{2,1,0:T(8,128)(2,1)}) custom-call(s32[8]{0:T(128)} %acc_ref.1, bf16[256,256]{1,0:T(8,128)(2,1)} %q_ref.3, bf16[256,256]{1,0:T(8,128)(2,1)} %fresh_ref.1, s32[256,1]{1,0:T(8,128)} %reshape.43.parent_ref), custom_call_target="tpu_custom_call" | custom-call | tf_op jit(solution)/shard_map/pallas_call | solution.py:102
  15.4 1.5 %collective-permute-done.1.q_ref = bf16[272,256]{1,0:T(8,128)(2,1)S(1)} collective-permute-done((bf16[272,256]{1,0:T(8,128)(2,1)S(1)}, bf16[272,256]{1,0:T(8,128)(2,1)S(1)}, u32[]{:S(2)}, u32[]{:S(2)}) %collective-permute-start.1) | collective-permute-done | bytes 139296 | tf_op jit(solution)/shard_map/ppermute | solution.py:25
  16.9 0.7 copy-done.9
  17.6 4.0 %shard_map.114 = bf16[256,384]{1,0:T(8,128)(2,1)} custom-call(bf16[272,256]{1,0:T(8,128)(2,1)} %copy-done.9, bf16[8,4,256,256]{3,2,1,0:T(8,128)(2,1)} %kv_ref.5, f32[256,384]{1,0:T(8,128)} %get-tuple-element.7.tree_ref.order_ref), custom_call_target="tpu_custom_call" | custom-call | tf_op jit(solution)/shard_map/pallas_call | solution.py:213
  21.6 7.8 %collective-permute-start.2 = (bf16[256,384]{1,0:T(8,128)(2,1)}, bf16[256,384]{1,0:T(8,128)(2,1)S(1)}, u32[]{:S(2)}, u32[]{:S(2)}) collective-permute-start(bf16[256,384]{1,0:T(8,128)(2,1)} %shard_map.114), channel_id=1, source_target_pairs={{0,496},{8,504},{16,0},{24,8},{32,16},{40,24},{48,32},{56,40},{64,... | collective-permute-start | bytes 589832 | tf_op jit(solution)/shard_map/ppermute | solution.py:25
  29.4 0.0 collective-permute-done.3.q_ref
  29.5 0.0 copy-start.8
  29.5 0.6 copy-done.8
  30.1 4.0 %shard_map.115 = bf16[256,384]{1,0:T(8,128)(2,1)} custom-call(bf16[272,256]{1,0:T(8,128)(2,1)} %copy-done.8, bf16[8,4,256,256]{3,2,1,0:T(8,128)(2,1)} %kv_ref.5, f32[256,384]{1,0:T(8,128)} %get-tuple-element.7.tree_ref.order_ref), custom_call_target="tpu_custom_call" | custom-call | tf_op jit(solution)/shard_map/pallas_call | solution.py:213
  34.1 3.0 %collective-permute-start.4 = (bf16[256,384]{1,0:T(8,128)(2,1)}, bf16[256,384]{1,0:T(8,128)(2,1)S(1)}, u32[]{:S(2)}, u32[]{:S(2)}) collective-permute-start(bf16[256,384]{1,0:T(8,128)(2,1)} %shard_map.115), channel_id=1, source_target_pairs={{0,488},{8,496},{16,504},{24,0},{32,8},{40,16},{48,24},{56,32},{64... | collective-permute-start | bytes 589832 | tf_op jit(solution)/shard_map/ppermute | solution.py:25
  37.2 0.0 collective-permute-done.rest_0_
  37.2 1.0 copy-done.5
  38.2 7.3 %shard_map.113 = (f32[256,256]{1,0:T(8,128)}, f32[256,128]{1,0:T(8,128)}) custom-call(s32[8]{0:T(128)} %lens_ref.1, bf16[256,256]{1,0:T(8,128)(2,1)} %q_ref.3, bf16[8,4,256,256]{3,2,1,0:T(8,128)(2,1)} %kv_ref.5, f32[256,384]{1,0:T(8,128)} %get-tuple-element.7.tree_ref.order_ref, bf16[8,256,256]{2,1,0:T(8,128)(2,1)} %copy-done.5), custom_call_target="tpu_custom_call" | custom-call | tf_op jit(solution)/shard_map/pallas_call | solution.py:159
  45.5 0.0 collective-permute-done.2.rest_0_
  45.5 0.0 collective-permute-done.4.rest_1_
  45.5 0.0 copy-start
  45.5 1.6 %copy-done = bf16[256,4096]{1,0:T(8,128)(2,1)S(1)} copy-done((bf16[256,4096]{1,0:T(8,128)(2,1)S(1)}, bf16[256,4096]{1,0:T(8,128)(2,1)}, u32[]{:S(2)}) %copy-start) | copy-done | bytes 2097176
  47.1 0.9 copy-done.1
  48.1 0.9 copy-done.2
  49.0 3.1 %shard_map.116 = bf16[256,4096]{1,0:T(8,128)(2,1)S(1)} custom-call(f32[256,256]{1,0:T(8,128)S(1)} %copy-done.1, f32[256,128]{1,0:T(8,128)S(1)} %copy-done.2, bf16[256,384]{1,0:T(8,128)(2,1)S(1)} %collective-permute-done.2.rest_0_, bf16[256,384]{1,0:T(8,128)(2,1)S(1)} %collective-permute-done.4.rest_1_, bf16[256,4096]{1,0:T(8,128)(2,1)S(1)} %copy-done), custom_call_target="tpu_custom_call" | custom-call | tf_op jit(solution)/shard_map/pallas_call | solution.py:265
  52.1 0.1 dynamic-slice_bitcast_fusion.2
  52.2 4.1 %collective-permute-start.5 = (bf16[32,4096]{1,0:T(8,128)(2,1)S(1)}, bf16[32,4096]{1,0:T(8,128)(2,1)S(1)}, u32[]{:S(2)}, u32[]{:S(2)}) collective-permute-start(bf16[32,4096]{1,0:T(8,128)(2,1)S(1)} %get-tuple-element.17), channel_id=1, source_target_pairs={{0,1},{1,2},{2,3},{3,4},{4,5},{5,6},{6,7},{7,0},{8,9},{9,10},{10,1... | collective-permute-start | bytes 786440 | tf_op jit(solution)/shard_map/ppermute | solution.py:25
  56.3 8.6 %collective-permute-start.8 = (bf16[32,4096]{1,0:T(8,128)(2,1)S(1)}, bf16[32,4096]{1,0:T(8,128)(2,1)}, u32[]{:S(2)}, u32[]{:S(2)}) collective-permute-start(bf16[32,4096]{1,0:T(8,128)(2,1)S(1)} %get-tuple-element.19), channel_id=1, source_target_pairs={{0,7},{1,0},{2,1},{3,2},{4,3},{5,4},{6,5},{7,6},{8,15},{9,8},{10,9... | collective-permute-start | bytes 786440 | tf_op jit(solution)/shard_map/ppermute | solution.py:25
  64.9 0.0 copy-start.10
  65.0 4.3 %collective-permute-done.5 = bf16[32,4096]{1,0:T(8,128)(2,1)S(1)} collective-permute-done((bf16[32,4096]{1,0:T(8,128)(2,1)S(1)}, bf16[32,4096]{1,0:T(8,128)(2,1)S(1)}, u32[]{:S(2)}, u32[]{:S(2)}) %collective-permute-start.5) | collective-permute-done | bytes 262176 | tf_op jit(solution)/shard_map/ppermute | solution.py:25
  69.2 0.7 copy-done.7
  69.9 0.5 collective-permute-done.8
  70.4 1.2 %fusion.6 = (bf16[32,4096]{1,0:T(8,128)(2,1)S(1)}, bf16[32,4096]{1,0:T(8,128)(2,1)S(1)}) fusion(bf16[32,4096]{1,0:T(8,128)(2,1)} %copy-done.7, bf16[8,32,4096]{2,1,0:T(8,128)(2,1)S(1)} %bitcast.32, s32[]{:T(128)S(6)} %select_n.78, s32[]{:T(128)S(6)} %select_n.84, bf16[32,4096]{1,0:T(8,128)(2,1)} %collective-permute-done.8), kind=kLoop, calls=%fused_computation.13 | loop fusion | flops 1048576 | bytes 1572872 | tf_op jit(solution)/shard_map/convert_element_type | solution.py:297
  71.6 1.9 %collective-permute-start.6 = (bf16[32,4096]{1,0:T(8,128)(2,1)S(1)}, bf16[32,4096]{1,0:T(8,128)(2,1)S(1)}, u32[]{:S(2)}, u32[]{:S(2)}) collective-permute-start(bf16[32,4096]{1,0:T(8,128)(2,1)S(1)} %get-tuple-element.15), channel_id=1, source_target_pairs={{0,1},{1,2},{2,3},{3,4},{4,5},{5,6},{6,7},{7,0},{8,9},{9,10},{10,1... | collective-permute-start | bytes 786440 | tf_op jit(solution)/shard_map/ppermute | solution.py:25
  73.5 5.7 %collective-permute-start.9 = (bf16[32,4096]{1,0:T(8,128)(2,1)S(1)}, bf16[32,4096]{1,0:T(8,128)(2,1)}, u32[]{:S(2)}, u32[]{:S(2)}) collective-permute-start(bf16[32,4096]{1,0:T(8,128)(2,1)S(1)} %get-tuple-element.16), channel_id=1, source_target_pairs={{0,7},{1,0},{2,1},{3,2},{4,3},{5,4},{6,5},{7,6},{8,15},{9,8},{10,9... | collective-permute-start | bytes 786440 | tf_op jit(solution)/shard_map/ppermute | solution.py:25
  79.2 5.1 %collective-permute-start.11 = (bf16[32,4096]{1,0:T(8,128)(2,1)S(1)}, bf16[32,4096]{1,0:T(8,128)(2,1)}, u32[]{:S(2)}, u32[]{:S(2)}) collective-permute-start(bf16[32,4096]{1,0:T(8,128)(2,1)S(1)} %get-tuple-element.18), channel_id=1, source_target_pairs={{0,4},{1,5},{2,6},{3,7},{4,0},{5,1},{6,2},{7,3},{8,12},{9,13},{10,... | collective-permute-start | bytes 786440 | tf_op jit(solution)/shard_map/ppermute | solution.py:25
  84.3 0.0 collective-permute-done.6
  84.3 7.3 %collective-permute-done.9 = bf16[32,4096]{1,0:T(8,128)(2,1)} collective-permute-done((bf16[32,4096]{1,0:T(8,128)(2,1)S(1)}, bf16[32,4096]{1,0:T(8,128)(2,1)}, u32[]{:S(2)}, u32[]{:S(2)}) %collective-permute-start.9) | collective-permute-done | bytes 262176 | tf_op jit(solution)/shard_map/ppermute | solution.py:25
  91.6 1.8 %fusion.5 = (bf16[32,4096]{1,0:T(8,128)(2,1)S(1)}, bf16[32,4096]{1,0:T(8,128)(2,1)}) fusion(bf16[32,4096]{1,0:T(8,128)(2,1)S(1)} %collective-permute-done.6, bf16[8,32,4096]{2,1,0:T(8,128)(2,1)S(1)} %bitcast.33, s32[]{:T(128)S(6)} %select_n.80, s32[]{:T(128)S(6)} %select_n.86, bf16[32,4096]{1,0:T(8,128)(2,1)} %collective-permute-done.9), kind=kLoop, calls=%fused_computation.11 | loop fusion | flops 1048576 | bytes 1572872 | tf_op jit(solution)/shard_map/convert_element_type | solution.py:297
  93.3 6.3 %collective-permute-start.10 = (bf16[32,4096]{1,0:T(8,128)(2,1)}, bf16[32,4096]{1,0:T(8,128)(2,1)S(1)}, u32[]{:S(2)}, u32[]{:S(2)}) collective-permute-start(bf16[32,4096]{1,0:T(8,128)(2,1)} %get-tuple-element.14), channel_id=1, source_target_pairs={{0,7},{1,0},{2,1},{3,2},{4,3},{5,4},{6,5},{7,6},{8,15},{9,8},{10,9... | collective-permute-start | bytes 786440 | tf_op jit(solution)/shard_map/ppermute | solution.py:25
  99.7 1.9 %collective-permute-start.7 = (bf16[32,4096]{1,0:T(8,128)(2,1)S(1)}, bf16[32,4096]{1,0:T(8,128)(2,1)S(1)}, u32[]{:S(2)}, u32[]{:S(2)}) collective-permute-start(bf16[32,4096]{1,0:T(8,128)(2,1)S(1)} %get-tuple-element.13), channel_id=1, source_target_pairs={{0,1},{1,2},{2,3},{3,4},{4,5},{5,6},{6,7},{7,0},{8,9},{9,10},{10,1... | collective-permute-start | bytes 786440 | tf_op jit(solution)/shard_map/ppermute | solution.py:25
  101.6 2.2 %collective-permute-done.10 = bf16[32,4096]{1,0:T(8,128)(2,1)S(1)} collective-permute-done((bf16[32,4096]{1,0:T(8,128)(2,1)}, bf16[32,4096]{1,0:T(8,128)(2,1)S(1)}, u32[]{:S(2)}, u32[]{:S(2)}) %collective-permute-start.10) | collective-permute-done | bytes 262176 | tf_op jit(solution)/shard_map/ppermute | solution.py:25
  103.9 5.3 %collective-permute-done.7 = bf16[32,4096]{1,0:T(8,128)(2,1)S(1)} collective-permute-done((bf16[32,4096]{1,0:T(8,128)(2,1)S(1)}, bf16[32,4096]{1,0:T(8,128)(2,1)S(1)}, u32[]{:S(2)}, u32[]{:S(2)}) %collective-permute-start.7) | collective-permute-done | bytes 262176 | tf_op jit(solution)/shard_map/ppermute | solution.py:25
  109.2 1.3 %fusion = (f32[32]{0:T(128)S(1)}, bf16[32,4096]{1,0:T(8,128)(2,1)S(1)}) fusion(bf16[32,4096]{1,0:T(8,128)(2,1)} %collective-permute-done.11, bf16[32,4096]{1,0:T(8,128)(2,1)S(1)} %collective-permute-done.10, bf16[32,4096]{1,0:T(8,128)(2,1)S(1)} %collective-permute-done.7, bf16[8,32,4096]{2,1,0:T(8,128)(2,1)S(1)} %bitcast.34, s32[]{:T(128)S(6)} %select_n.74, ...), kind=kLoop, calls=%fused_computation.3 | loop fusion | flops 1703904 | bytes 1572996 | tf_op jit(solution)/shard_map/reduce_sum | solution.py:338
  110.4 0.8 fusion.2
  (20 shorter events, 0.1 us)
Async XLA Ops:
  0.6 3.3 %copy-start.12 = (s32[8]{0:T(128)S(1)}, s32[8]{0:T(128)}, u32[]{:S(2)}) copy-start(s32[8]{0:T(128)} %lens_ref.1) | copy-start | bytes 100
  0.6 3.3 %copy-start.3 = (bf16[256,256]{1,0:T(8,128)(2,1)S(1)}, bf16[256,256]{1,0:T(8,128)(2,1)}, u32[]{:S(2)}) copy-start(bf16[256,256]{1,0:T(8,128)(2,1)} %q_ref.3) | copy-start | bytes 393220
  0.7 10.2 %copy-start.11 = (s32[8,32]{1,0:T(8,128)S(1)}, s32[8,32]{1,0:T(8,128)}, u32[]{:S(2)}) copy-start(s32[8,32]{1,0:T(8,128)} %param.13) | copy-start | bytes 3076
  2.0 35.2 %collective-permute-start = (bf16[8,256,256]{2,1,0:T(8,128)(2,1)S(1)}, bf16[8,256,256]{2,1,0:T(8,128)(2,1)S(1)}, u32[]{:S(2)}, u32[]{:S(2)}) collective-permute-start(bf16[8,256,256]{2,1,0:T(8,128)(2,1)S(1)} %slice_bitcast_fusion), channel_id=1, source_target_pairs={{0,504},{8,0},{16,8},{24,16},{32,24},{40,32},{48,40},{56,48},{64,5... | collective-permute-start | bytes 3145736 | tf_op jit(solution)/shard_map/ppermute | solution.py:25
  4.0 12.9 %collective-permute-start.1 = (bf16[272,256]{1,0:T(8,128)(2,1)S(1)}, bf16[272,256]{1,0:T(8,128)(2,1)S(1)}, u32[]{:S(2)}, u32[]{:S(2)}) collective-permute-start(bf16[272,256]{1,0:T(8,128)(2,1)S(1)} %pad_maximum_fusion), channel_id=1, source_target_pairs={{0,16},{8,24},{16,32},{24,40},{32,48},{40,56},{48,64},{56,72},{64,... | collective-permute-start | bytes 417800 | tf_op jit(solution)/shard_map/ppermute | solution.py:25
  7.5 21.9 %collective-permute-start.3 = (bf16[272,256]{1,0:T(8,128)(2,1)S(1)}, bf16[272,256]{1,0:T(8,128)(2,1)S(1)}, u32[]{:S(2)}, u32[]{:S(2)}) collective-permute-start(bf16[272,256]{1,0:T(8,128)(2,1)S(1)} %pad_maximum_fusion), channel_id=1, source_target_pairs={{0,24},{8,32},{16,40},{24,48},{32,56},{40,64},{48,72},{56,80},{64,... | collective-permute-start | bytes 417800 | tf_op jit(solution)/shard_map/ppermute | solution.py:25
  16.9 0.7 copy-start.9
  21.6 23.9 %collective-permute-start.2 = (bf16[256,384]{1,0:T(8,128)(2,1)}, bf16[256,384]{1,0:T(8,128)(2,1)S(1)}, u32[]{:S(2)}, u32[]{:S(2)}) collective-permute-start(bf16[256,384]{1,0:T(8,128)(2,1)} %shard_map.114), channel_id=1, source_target_pairs={{0,496},{8,504},{16,0},{24,8},{32,16},{40,24},{48,32},{56,40},{64,... | collective-permute-start | bytes 589832 | tf_op jit(solution)/shard_map/ppermute | solution.py:25
  29.5 0.7 copy-start.8
  34.1 11.4 %collective-permute-start.4 = (bf16[256,384]{1,0:T(8,128)(2,1)}, bf16[256,384]{1,0:T(8,128)(2,1)S(1)}, u32[]{:S(2)}, u32[]{:S(2)}) collective-permute-start(bf16[256,384]{1,0:T(8,128)(2,1)} %shard_map.115), channel_id=1, source_target_pairs={{0,488},{8,496},{16,504},{24,0},{32,8},{40,16},{48,24},{56,32},{64... | collective-permute-start | bytes 589832 | tf_op jit(solution)/shard_map/ppermute | solution.py:25
  37.2 1.0 copy-start.5
  45.5 1.6 %copy-start = (bf16[256,4096]{1,0:T(8,128)(2,1)S(1)}, bf16[256,4096]{1,0:T(8,128)(2,1)}, u32[]{:S(2)}) copy-start(bf16[256,4096]{1,0:T(8,128)(2,1)} %rest_2_.1) | copy-start | bytes 6291460
  47.1 0.9 copy-start.1
  48.1 0.9 copy-start.2
  52.1 57.1 %copy-start.6 = (bf16[32,4096]{1,0:T(8,128)(2,1)S(1)}, bf16[32,4096]{1,0:T(8,128)(2,1)}, u32[]{:S(2)}) copy-start(bf16[32,4096]{1,0:T(8,128)(2,1)} %param.15) | copy-start | bytes 786436
  52.2 17.0 %collective-permute-start.5 = (bf16[32,4096]{1,0:T(8,128)(2,1)S(1)}, bf16[32,4096]{1,0:T(8,128)(2,1)S(1)}, u32[]{:S(2)}, u32[]{:S(2)}) collective-permute-start(bf16[32,4096]{1,0:T(8,128)(2,1)S(1)} %get-tuple-element.17), channel_id=1, source_target_pairs={{0,1},{1,2},{2,3},{3,4},{4,5},{5,6},{6,7},{7,0},{8,9},{9,10},{10,1... | collective-permute-start | bytes 786440 | tf_op jit(solution)/shard_map/ppermute | solution.py:25
  56.3 14.1 %collective-permute-start.8 = (bf16[32,4096]{1,0:T(8,128)(2,1)S(1)}, bf16[32,4096]{1,0:T(8,128)(2,1)}, u32[]{:S(2)}, u32[]{:S(2)}) collective-permute-start(bf16[32,4096]{1,0:T(8,128)(2,1)S(1)} %get-tuple-element.19), channel_id=1, source_target_pairs={{0,7},{1,0},{2,1},{3,2},{4,3},{5,4},{6,5},{7,6},{8,15},{9,8},{10,9... | collective-permute-start | bytes 786440 | tf_op jit(solution)/shard_map/ppermute | solution.py:25
  64.9 45.5 %copy-start.10 = (f32[4096]{0:T(1024)S(1)}, f32[4096]{0:T(1024)}, u32[]{:S(2)}) copy-start(f32[4096]{0:T(1024)} %param.17) | copy-start | bytes 49156
  69.2 0.7 copy-start.7
  71.6 12.8 %collective-permute-start.6 = (bf16[32,4096]{1,0:T(8,128)(2,1)S(1)}, bf16[32,4096]{1,0:T(8,128)(2,1)S(1)}, u32[]{:S(2)}, u32[]{:S(2)}) collective-permute-start(bf16[32,4096]{1,0:T(8,128)(2,1)S(1)} %get-tuple-element.15), channel_id=1, source_target_pairs={{0,1},{1,2},{2,3},{3,4},{4,5},{5,6},{6,7},{7,0},{8,9},{9,10},{10,1... | collective-permute-start | bytes 786440 | tf_op jit(solution)/shard_map/ppermute | solution.py:25
  73.5 18.1 %collective-permute-start.9 = (bf16[32,4096]{1,0:T(8,128)(2,1)S(1)}, bf16[32,4096]{1,0:T(8,128)(2,1)}, u32[]{:S(2)}, u32[]{:S(2)}) collective-permute-start(bf16[32,4096]{1,0:T(8,128)(2,1)S(1)} %get-tuple-element.16), channel_id=1, source_target_pairs={{0,7},{1,0},{2,1},{3,2},{4,3},{5,4},{6,5},{7,6},{8,15},{9,8},{10,9... | collective-permute-start | bytes 786440 | tf_op jit(solution)/shard_map/ppermute | solution.py:25
  79.2 22.4 %collective-permute-start.11 = (bf16[32,4096]{1,0:T(8,128)(2,1)S(1)}, bf16[32,4096]{1,0:T(8,128)(2,1)}, u32[]{:S(2)}, u32[]{:S(2)}) collective-permute-start(bf16[32,4096]{1,0:T(8,128)(2,1)S(1)} %get-tuple-element.18), channel_id=1, source_target_pairs={{0,4},{1,5},{2,6},{3,7},{4,0},{5,1},{6,2},{7,3},{8,12},{9,13},{10,... | collective-permute-start | bytes 786440 | tf_op jit(solution)/shard_map/ppermute | solution.py:25
  93.3 10.5 %collective-permute-start.10 = (bf16[32,4096]{1,0:T(8,128)(2,1)}, bf16[32,4096]{1,0:T(8,128)(2,1)S(1)}, u32[]{:S(2)}, u32[]{:S(2)}) collective-permute-start(bf16[32,4096]{1,0:T(8,128)(2,1)} %get-tuple-element.14), channel_id=1, source_target_pairs={{0,7},{1,0},{2,1},{3,2},{4,3},{5,4},{6,5},{7,6},{8,15},{9,8},{10,9... | collective-permute-start | bytes 786440 | tf_op jit(solution)/shard_map/ppermute | solution.py:25
  99.7 9.5 %collective-permute-start.7 = (bf16[32,4096]{1,0:T(8,128)(2,1)S(1)}, bf16[32,4096]{1,0:T(8,128)(2,1)S(1)}, u32[]{:S(2)}, u32[]{:S(2)}) collective-permute-start(bf16[32,4096]{1,0:T(8,128)(2,1)S(1)} %get-tuple-element.13), channel_id=1, source_target_pairs={{0,1},{1,2},{2,3},{3,4},{4,5},{5,6},{6,7},{7,0},{8,9},{9,10},{10,1... | collective-permute-start | bytes 786440 | tf_op jit(solution)/shard_map/ppermute | solution.py:25
  110.4 0.9 copy-start.4

commit v10 on v8

--- a/solution.py
+++ b/solution.py
@@ -223,15 +223,22 @@
     )(packed_queries, kv_pool, order_after)
 
 
-def merge_kernel(group, sum_ref, stat_ref, *rest):
-    returned = rest[:-2]
-    w_ref = rest[-2]
-    out_ref = rest[-1]
+def merge_kernel(group, count, sum_hbm, stat_hbm, *rest):
+    returned = rest[:count]
+    w_hbm, out_ref, sum_ref, stat_ref, w_ref, att_ref, sems = rest[count:]
+    copies = [
+        pltpu.make_async_copy(sum_hbm, sum_ref, sems.at[0]),
+        pltpu.make_async_copy(stat_hbm, stat_ref, sems.at[1]),
+        pltpu.make_async_copy(w_hbm, w_ref, sems.at[2]),
+    ]
+    for copy in copies:
+        copy.start()
+    copies[0].wait()
+    copies[1].wait()
     rows = sum_ref.shape[0]
     for r in range(rows // TREE):
         row0 = r * TREE
         local_stats = stat_ref[row0 : row0 + TREE, :]
-        heads = []
         for g in range(group):
             cols = slice(g * HD, (g + 1) * HD)
             blocks = [(lane_pick(local_stats, g), lane_pick(local_stats, group + g),
@@ -250,11 +257,11 @@
                 factor = jnp.exp(largest - top)
                 denominator = denominator + factor * totals
                 numerator = numerator + factor * weighted
-            heads.append((numerator / denominator).astype(jnp.bfloat16))
-        attention = jnp.concatenate(heads, axis=1)
-        out_ref[row0 : row0 + TREE, :] = jnp.dot(
-            attention, w_ref[...], preferred_element_type=jnp.float32
-        ).astype(out_ref.dtype)
+            att_ref[row0 : row0 + TREE, cols] = (numerator / denominator).astype(jnp.bfloat16)
+    copies[2].wait()
+    out_ref[...] = jnp.dot(
+        att_ref[...], w_ref[...], preferred_element_type=jnp.float32
+    ).astype(out_ref.dtype)
 
 
 def merge_project(sums, stats, returned, w_out, group):
@@ -262,14 +269,22 @@
     part_width = returned[0].shape[1]
     model = w_out.shape[1]
     full = lambda shape: pl.BlockSpec(shape, lambda i: (0, 0))
+    anywhere = pl.BlockSpec(memory_space=pl.ANY)
     return pl.pallas_call(
-        functools.partial(merge_kernel, group),
+        functools.partial(merge_kernel, group, len(returned)),
         out_shape=jax.ShapeDtypeStruct((rows, model), jnp.bfloat16),
         grid=(1,),
-        in_specs=[full((rows, width)), full((rows, STAT_LANES))]
+        in_specs=[anywhere, anywhere]
         + [full((rows, part_width)) for _ in returned]
-        + [full(w_out.shape)],
+        + [anywhere],
         out_specs=full((rows, model)),
+        scratch_shapes=[
+            pltpu.VMEM(sums.shape, sums.dtype),
+            pltpu.VMEM(stats.shape, stats.dtype),
+            pltpu.VMEM(w_out.shape, w_out.dtype),
+            pltpu.VMEM((rows, width), jnp.bfloat16),
+            pltpu.SemaphoreType.DMA((3,)),
+        ],
         compiler_params=pltpu.CompilerParams(vmem_limit_bytes=48 * 1024 * 1024),
     )(sums, stats, *returned, w_out)
 

time: 106 us -> 105 us (level)
  Pallas kernels: 22.2 us -> 20.8 us
    pallas_call x1, Pallas kernels: 3.11 us -> 1.69 us  [merge_project(): pl.pallas_call(functools.partial(merge_kernel, group, len(returned)), out...]
where the time goes in v10:
time: 105 us; the launch traced here: 104 us
  starting transfers between devices  41.3 us (39%)
  waiting for transfers between devices  30.7 us (29%)
  Pallas kernels  20.8 us (20%)
  local copies, waits for them, and re-layouts  7.98 us (8%)
  other arithmetic  2.48 us (2%)
  between operations  1.06 us (1%)
    ppermute x12, starting transfers between devices, shifted(): return lax.ppermute(value, axis, pairs)  41.3 us
    ppermute x12, waiting for transfers between devices, shifted(): return lax.ppermute(value, axis, pairs)  30.7 us
    pallas_call x2, Pallas kernels, holder_partial(): pl.pallas_call(functools.partial(holder_kernel, page_index, group), out_s...  8.07 us
    pallas_call x1, Pallas kernels, local_partial(): pl.pallas_call(functools.partial(local_kernel, group, page_ids), out_shap...  7.32 us
    unnamed x24, local copies, waits for them, and re-layouts  5.79 us
    pallas_call x1, Pallas kernels, tree_partial(): pl.pallas_call(functools.partial(tree_kernel, group), out_shape=(jax.Shap...  3.7 us
  transfers between devices with their start and end apart: 12, of which 7 were waited for; matrix products, arithmetic and copies ran while one was open for 2% of the time, Pallas kernels for 18%

profile of v10, /device:TPU:62, one launch (start us, length us, event | category | flops | bytes accessed | tf_op | source)
XLA Modules:
  0.0 104.3 jit_solution(3259345240162248782)
XLA Ops:
  0.6 0.0 copy-start.11
  0.6 0.0 copy-start.3
  0.7 1.3 %slice_bitcast_fusion = bf16[8,256,256]{2,1,0:T(8,128)(2,1)S(1)} fusion(bf16[8,4,256,256]{3,2,1,0:T(8,128)(2,1)} %kv_ref.5), kind=kLoop, calls=%fused_computation | loop fusion | bytes 2097152 | tf_op jit(solution)/shard_map/squeeze | solution.py:335
  2.0 2.7 %collective-permute-start = (bf16[8,256,256]{2,1,0:T(8,128)(2,1)S(1)}, bf16[8,256,256]{2,1,0:T(8,128)(2,1)S(1)}, u32[]{:S(2)}, u32[]{:S(2)}) collective-permute-start(bf16[8,256,256]{2,1,0:T(8,128)(2,1)S(1)} %slice_bitcast_fusion), channel_id=1, source_target_pairs={{0,504},{8,0},{16,8},{24,16},{32,24},{40,32},{48,40},{56,48},{64,5... | collective-permute-start | bytes 3145736 | tf_op jit(solution)/shard_map/ppermute | solution.py:25
  4.8 6.2 %collective-permute-start.1 = (bf16[272,256]{1,0:T(8,128)(2,1)S(1)}, bf16[272,256]{1,0:T(8,128)(2,1)S(1)}, u32[]{:S(2)}, u32[]{:S(2)}) collective-permute-start(bf16[272,256]{1,0:T(8,128)(2,1)S(1)} %pad_maximum_fusion), channel_id=1, source_target_pairs={{0,16},{8,24},{16,32},{24,40},{32,48},{40,56},{48,64},{56,72},{64,... | collective-permute-start | bytes 417800 | tf_op jit(solution)/shard_map/ppermute | solution.py:25
  11.0 2.0 %collective-permute-start.3 = (bf16[272,256]{1,0:T(8,128)(2,1)S(1)}, bf16[272,256]{1,0:T(8,128)(2,1)S(1)}, u32[]{:S(2)}, u32[]{:S(2)}) collective-permute-start(bf16[272,256]{1,0:T(8,128)(2,1)S(1)} %pad_maximum_fusion), channel_id=1, source_target_pairs={{0,24},{8,32},{16,40},{24,48},{32,56},{40,64},{48,72},{56,80},{64,... | collective-permute-start | bytes 417800 | tf_op jit(solution)/shard_map/ppermute | solution.py:25
  13.0 0.1 broadcast_add_fusion
  13.1 0.8 reshape.46.parent_ref
  13.9 3.7 %shard_map.112 = (f32[256,384]{1,0:T(8,128)}, bf16[8,8,256]{2,1,0:T(8,128)(2,1)}) custom-call(s32[8]{0:T(128)} %acc_ref.1, bf16[256,256]{1,0:T(8,128)(2,1)} %q_ref.3, bf16[256,256]{1,0:T(8,128)(2,1)} %fresh_ref.1, s32[256,1]{1,0:T(8,128)} %reshape.46.parent_ref), custom_call_target="tpu_custom_call" | custom-call | tf_op jit(solution)/shard_map/pallas_call | solution.py:102
  17.6 0.0 collective-permute-done.1.q_ref
  17.6 0.7 copy-done.8
  18.3 4.0 %shard_map.114 = bf16[256,384]{1,0:T(8,128)(2,1)} custom-call(bf16[272,256]{1,0:T(8,128)(2,1)} %copy-done.8, bf16[8,4,256,256]{3,2,1,0:T(8,128)(2,1)} %kv_ref.5, f32[256,384]{1,0:T(8,128)} %get-tuple-element.7.tree_ref.order_ref), custom_call_target="tpu_custom_call" | custom-call | tf_op jit(solution)/shard_map/pallas_call | solution.py:213
  22.3 3.6 %collective-permute-start.2 = (bf16[256,384]{1,0:T(8,128)(2,1)}, bf16[256,384]{1,0:T(8,128)(2,1)S(1)}, u32[]{:S(2)}, u32[]{:S(2)}) collective-permute-start(bf16[256,384]{1,0:T(8,128)(2,1)} %shard_map.114), channel_id=1, source_target_pairs={{0,496},{8,504},{16,0},{24,8},{32,16},{40,24},{48,32},{56,40},{64,... | collective-permute-start | bytes 589832 | tf_op jit(solution)/shard_map/ppermute | solution.py:25
  25.9 0.0 collective-permute-done.3.q_ref
  26.0 0.0 copy-start.7
  26.0 0.6 copy-done.7
  26.6 4.0 %shard_map.115 = bf16[256,384]{1,0:T(8,128)(2,1)} custom-call(bf16[272,256]{1,0:T(8,128)(2,1)} %copy-done.7, bf16[8,4,256,256]{3,2,1,0:T(8,128)(2,1)} %kv_ref.5, f32[256,384]{1,0:T(8,128)} %get-tuple-element.7.tree_ref.order_ref), custom_call_target="tpu_custom_call" | custom-call | tf_op jit(solution)/shard_map/pallas_call | solution.py:213
  30.7 2.7 %collective-permute-start.4 = (bf16[256,384]{1,0:T(8,128)(2,1)}, bf16[256,384]{1,0:T(8,128)(2,1)S(1)}, u32[]{:S(2)}, u32[]{:S(2)}) collective-permute-start(bf16[256,384]{1,0:T(8,128)(2,1)} %shard_map.115), channel_id=1, source_target_pairs={{0,488},{8,496},{16,504},{24,0},{32,8},{40,16},{48,24},{56,32},{64... | collective-permute-start | bytes 589832 | tf_op jit(solution)/shard_map/ppermute | solution.py:25
  33.4 0.0 collective-permute-done.rest_0_
  33.4 1.0 copy-done.5
  34.4 7.3 %shard_map.113 = (f32[256,256]{1,0:T(8,128)}, f32[256,128]{1,0:T(8,128)}) custom-call(s32[8]{0:T(128)} %lens_ref.1, bf16[256,256]{1,0:T(8,128)(2,1)} %q_ref.3, bf16[8,4,256,256]{3,2,1,0:T(8,128)(2,1)} %kv_ref.5, f32[256,384]{1,0:T(8,128)} %get-tuple-element.7.tree_ref.order_ref, bf16[8,256,256]{2,1,0:T(8,128)(2,1)} %copy-done.5), custom_call_target="tpu_custom_call" | custom-call | tf_op jit(solution)/shard_map/pallas_call | solution.py:159
  41.7 0.0 collective-permute-done.2.rest_0_
  41.7 2.3 %collective-permute-done.4.rest_1_ = bf16[256,384]{1,0:T(8,128)(2,1)S(1)} collective-permute-done((bf16[256,384]{1,0:T(8,128)(2,1)}, bf16[256,384]{1,0:T(8,128)(2,1)S(1)}, u32[]{:S(2)}, u32[]{:S(2)}) %collective-permute-start.4) | collective-permute-done | bytes 196640 | tf_op jit(solution)/shard_map/ppermute | solution.py:25
  44.0 1.6 %copy-done = bf16[256,4096]{1,0:T(8,128)(2,1)S(1)} copy-done((bf16[256,4096]{1,0:T(8,128)(2,1)S(1)}, bf16[256,4096]{1,0:T(8,128)(2,1)}, u32[]{:S(2)}) %copy-start) | copy-done | bytes 2097176
  45.6 0.9 copy-done.1
  46.6 0.9 copy-done.2
  47.5 1.7 %shard_map.116 = bf16[256,4096]{1,0:T(8,128)(2,1)S(1)} custom-call(f32[256,256]{1,0:T(8,128)S(1)} %copy-done.1, f32[256,128]{1,0:T(8,128)S(1)} %copy-done.2, bf16[256,384]{1,0:T(8,128)(2,1)S(1)} %collective-permute-done.2.rest_0_, bf16[256,384]{1,0:T(8,128)(2,1)S(1)} %collective-permute-done.4.rest_1_, bf16[256,4096]{1,0:T(8,128)(2,1)S(1)} %copy-done), custom_call_target="tpu_custom_call" | custom-call | tf_op jit(solution)/shard_map/pallas_call | solution.py:273
  49.2 0.0 copy-start.6
  49.2 2.1 %collective-permute-start.5 = (bf16[32,4096]{1,0:T(8,128)(2,1)S(1)}, bf16[32,4096]{1,0:T(8,128)(2,1)}, u32[]{:S(2)}, u32[]{:S(2)}) collective-permute-start(bf16[32,4096]{1,0:T(8,128)(2,1)S(1)} %get-tuple-element.17), channel_id=1, source_target_pairs={{0,1},{1,2},{2,3},{3,4},{4,5},{5,6},{6,7},{7,0},{8,9},{9,10},{10,1... | collective-permute-start | bytes 786440 | tf_op jit(solution)/shard_map/ppermute | solution.py:25
  51.3 8.4 %collective-permute-start.9 = (bf16[32,4096]{1,0:T(8,128)(2,1)S(1)}, bf16[32,4096]{1,0:T(8,128)(2,1)S(1)}, u32[]{:S(2)}, u32[]{:S(2)}) collective-permute-start(bf16[32,4096]{1,0:T(8,128)(2,1)S(1)} %get-tuple-element.18), channel_id=1, source_target_pairs={{0,7},{1,0},{2,1},{3,2},{4,3},{5,4},{6,5},{7,6},{8,15},{9,8},{10,9... | collective-permute-start | bytes 786440 | tf_op jit(solution)/shard_map/ppermute | solution.py:25
  59.7 3.3 %collective-permute-done.5 = bf16[32,4096]{1,0:T(8,128)(2,1)} collective-permute-done((bf16[32,4096]{1,0:T(8,128)(2,1)S(1)}, bf16[32,4096]{1,0:T(8,128)(2,1)}, u32[]{:S(2)}, u32[]{:S(2)}) %collective-permute-start.5) | collective-permute-done | bytes 262176 | tf_op jit(solution)/shard_map/ppermute | solution.py:25
  63.0 1.0 fusion.7
  64.0 1.9 %collective-permute-start.6 = (bf16[32,4096]{1,0:T(8,128)(2,1)S(1)}, bf16[32,4096]{1,0:T(8,128)(2,1)S(1)}, u32[]{:S(2)}, u32[]{:S(2)}) collective-permute-start(bf16[32,4096]{1,0:T(8,128)(2,1)S(1)} %fusion.7), channel_id=1, source_target_pairs={{0,1},{1,2},{2,3},{3,4},{4,5},{5,6},{6,7},{7,0},{8,9},{9,10},{10,1... | collective-permute-start | bytes 786440 | tf_op jit(solution)/shard_map/ppermute | solution.py:25
  66.0 0.0 copy-start.9
  66.0 0.0 collective-permute-done.9
  66.0 9.5 %collective-permute-done.6 = bf16[32,4096]{1,0:T(8,128)(2,1)S(1)} collective-permute-done((bf16[32,4096]{1,0:T(8,128)(2,1)S(1)}, bf16[32,4096]{1,0:T(8,128)(2,1)S(1)}, u32[]{:S(2)}, u32[]{:S(2)}) %collective-permute-start.6) | collective-permute-done | bytes 262176 | tf_op jit(solution)/shard_map/ppermute | solution.py:25
  75.5 0.1 fusion.6
  75.6 3.1 %collective-permute-start.10 = (bf16[32,4096]{1,0:T(8,128)(2,1)S(1)}, bf16[32,4096]{1,0:T(8,128)(2,1)S(1)}, u32[]{:S(2)}, u32[]{:S(2)}) collective-permute-start(bf16[32,4096]{1,0:T(8,128)(2,1)S(1)} %get-tuple-element.16), channel_id=1, source_target_pairs={{0,7},{1,0},{2,1},{3,2},{4,3},{5,4},{6,5},{7,6},{8,15},{9,8},{10,9... | collective-permute-start | bytes 786440 | tf_op jit(solution)/shard_map/ppermute | solution.py:25
  78.7 2.8 %collective-permute-start.7 = (bf16[32,4096]{1,0:T(8,128)(2,1)S(1)}, bf16[32,4096]{1,0:T(8,128)(2,1)S(1)}, u32[]{:S(2)}, u32[]{:S(2)}) collective-permute-start(bf16[32,4096]{1,0:T(8,128)(2,1)S(1)} %get-tuple-element.15), channel_id=1, source_target_pairs={{0,1},{1,2},{2,3},{3,4},{4,5},{5,6},{6,7},{7,0},{8,9},{9,10},{10,1... | collective-permute-start | bytes 786440 | tf_op jit(solution)/shard_map/ppermute | solution.py:25
  81.5 4.8 %collective-permute-done.10 = bf16[32,4096]{1,0:T(8,128)(2,1)S(1)} collective-permute-done((bf16[32,4096]{1,0:T(8,128)(2,1)S(1)}, bf16[32,4096]{1,0:T(8,128)(2,1)S(1)}, u32[]{:S(2)}, u32[]{:S(2)}) %collective-permute-start.10) | collective-permute-done | bytes 262176 | tf_op jit(solution)/shard_map/ppermute | solution.py:25
  86.4 3.9 %collective-permute-done.7 = bf16[32,4096]{1,0:T(8,128)(2,1)S(1)} collective-permute-done((bf16[32,4096]{1,0:T(8,128)(2,1)S(1)}, bf16[32,4096]{1,0:T(8,128)(2,1)S(1)}, u32[]{:S(2)}, u32[]{:S(2)}) %collective-permute-start.7) | collective-permute-done | bytes 262176 | tf_op jit(solution)/shard_map/ppermute | solution.py:25
  90.3 0.1 fusion.5
  90.4 1.9 %collective-permute-start.11 = (bf16[32,4096]{1,0:T(8,128)(2,1)S(1)}, bf16[32,4096]{1,0:T(8,128)(2,1)S(1)}, u32[]{:S(2)}, u32[]{:S(2)}) collective-permute-start(bf16[32,4096]{1,0:T(8,128)(2,1)S(1)} %get-tuple-element.14), channel_id=1, source_target_pairs={{0,7},{1,0},{2,1},{3,2},{4,3},{5,4},{6,5},{7,6},{8,15},{9,8},{10,9... | collective-permute-start | bytes 786440 | tf_op jit(solution)/shard_map/ppermute | solution.py:25
  92.4 3.9 %collective-permute-start.8 = (bf16[32,4096]{1,0:T(8,128)(2,1)S(1)}, bf16[32,4096]{1,0:T(8,128)(2,1)S(1)}, u32[]{:S(2)}, u32[]{:S(2)}) collective-permute-start(bf16[32,4096]{1,0:T(8,128)(2,1)S(1)} %get-tuple-element.13), channel_id=1, source_target_pairs={{0,1},{1,2},{2,3},{3,4},{4,5},{5,6},{6,7},{7,0},{8,9},{9,10},{10,1... | collective-permute-start | bytes 786440 | tf_op jit(solution)/shard_map/ppermute | solution.py:25
  96.3 3.7 %collective-permute-done.11 = bf16[32,4096]{1,0:T(8,128)(2,1)S(1)} collective-permute-done((bf16[32,4096]{1,0:T(8,128)(2,1)S(1)}, bf16[32,4096]{1,0:T(8,128)(2,1)S(1)}, u32[]{:S(2)}, u32[]{:S(2)}) %collective-permute-start.11) | collective-permute-done | bytes 262176 | tf_op jit(solution)/shard_map/ppermute | solution.py:25
  100.0 3.1 %collective-permute-done.8 = bf16[32,4096]{1,0:T(8,128)(2,1)S(1)} collective-permute-done((bf16[32,4096]{1,0:T(8,128)(2,1)S(1)}, bf16[32,4096]{1,0:T(8,128)(2,1)S(1)}, u32[]{:S(2)}, u32[]{:S(2)}) %collective-permute-start.8) | collective-permute-done | bytes 262176 | tf_op jit(solution)/shard_map/ppermute | solution.py:25
  103.1 0.3 fusion
  103.4 0.8 fusion.2
  (19 shorter events, 0.1 us)
Async XLA Ops:
  0.6 4.1 %copy-start.11 = (s32[8]{0:T(128)S(1)}, s32[8]{0:T(128)}, u32[]{:S(2)}) copy-start(s32[8]{0:T(128)} %lens_ref.1) | copy-start | bytes 100
  0.6 4.1 %copy-start.3 = (bf16[256,256]{1,0:T(8,128)(2,1)S(1)}, bf16[256,256]{1,0:T(8,128)(2,1)}, u32[]{:S(2)}) copy-start(bf16[256,256]{1,0:T(8,128)(2,1)} %q_ref.3) | copy-start | bytes 393220
  0.7 12.4 %copy-start.10 = (s32[8,32]{1,0:T(8,128)S(1)}, s32[8,32]{1,0:T(8,128)}, u32[]{:S(2)}) copy-start(s32[8,32]{1,0:T(8,128)} %param.13) | copy-start | bytes 3076
  2.0 31.4 %collective-permute-start = (bf16[8,256,256]{2,1,0:T(8,128)(2,1)S(1)}, bf16[8,256,256]{2,1,0:T(8,128)(2,1)S(1)}, u32[]{:S(2)}, u32[]{:S(2)}) collective-permute-start(bf16[8,256,256]{2,1,0:T(8,128)(2,1)S(1)} %slice_bitcast_fusion), channel_id=1, source_target_pairs={{0,504},{8,0},{16,8},{24,16},{32,24},{40,32},{48,40},{56,48},{64,5... | collective-permute-start | bytes 3145736 | tf_op jit(solution)/shard_map/ppermute | solution.py:25
  4.8 12.8 %collective-permute-start.1 = (bf16[272,256]{1,0:T(8,128)(2,1)S(1)}, bf16[272,256]{1,0:T(8,128)(2,1)S(1)}, u32[]{:S(2)}, u32[]{:S(2)}) collective-permute-start(bf16[272,256]{1,0:T(8,128)(2,1)S(1)} %pad_maximum_fusion), channel_id=1, source_target_pairs={{0,16},{8,24},{16,32},{24,40},{32,48},{40,56},{48,64},{56,72},{64,... | collective-permute-start | bytes 417800 | tf_op jit(solution)/shard_map/ppermute | solution.py:25
  11.0 15.0 %collective-permute-start.3 = (bf16[272,256]{1,0:T(8,128)(2,1)S(1)}, bf16[272,256]{1,0:T(8,128)(2,1)S(1)}, u32[]{:S(2)}, u32[]{:S(2)}) collective-permute-start(bf16[272,256]{1,0:T(8,128)(2,1)S(1)} %pad_maximum_fusion), channel_id=1, source_target_pairs={{0,24},{8,32},{16,40},{24,48},{32,56},{40,64},{48,72},{56,80},{64,... | collective-permute-start | bytes 417800 | tf_op jit(solution)/shard_map/ppermute | solution.py:25
  17.6 0.7 copy-start.8
  22.3 19.4 %collective-permute-start.2 = (bf16[256,384]{1,0:T(8,128)(2,1)}, bf16[256,384]{1,0:T(8,128)(2,1)S(1)}, u32[]{:S(2)}, u32[]{:S(2)}) collective-permute-start(bf16[256,384]{1,0:T(8,128)(2,1)} %shard_map.114), channel_id=1, source_target_pairs={{0,496},{8,504},{16,0},{24,8},{32,16},{40,24},{48,32},{56,40},{64,... | collective-permute-start | bytes 589832 | tf_op jit(solution)/shard_map/ppermute | solution.py:25
  26.0 0.7 copy-start.7
  30.7 13.4 %collective-permute-start.4 = (bf16[256,384]{1,0:T(8,128)(2,1)}, bf16[256,384]{1,0:T(8,128)(2,1)S(1)}, u32[]{:S(2)}, u32[]{:S(2)}) collective-permute-start(bf16[256,384]{1,0:T(8,128)(2,1)} %shard_map.115), channel_id=1, source_target_pairs={{0,488},{8,496},{16,504},{24,0},{32,8},{40,16},{48,24},{56,32},{64... | collective-permute-start | bytes 589832 | tf_op jit(solution)/shard_map/ppermute | solution.py:25
  33.4 1.0 copy-start.5
  44.0 1.6 %copy-start = (bf16[256,4096]{1,0:T(8,128)(2,1)S(1)}, bf16[256,4096]{1,0:T(8,128)(2,1)}, u32[]{:S(2)}) copy-start(bf16[256,4096]{1,0:T(8,128)(2,1)} %rest_2_.1) | copy-start | bytes 6291460
  45.6 0.9 copy-start.1
  46.6 0.9 copy-start.2
  49.2 53.9 %copy-start.6 = (bf16[32,4096]{1,0:T(8,128)(2,1)S(1)}, bf16[32,4096]{1,0:T(8,128)(2,1)}, u32[]{:S(2)}) copy-start(bf16[32,4096]{1,0:T(8,128)(2,1)} %param.15) | copy-start | bytes 786436
  49.2 13.8 %collective-permute-start.5 = (bf16[32,4096]{1,0:T(8,128)(2,1)S(1)}, bf16[32,4096]{1,0:T(8,128)(2,1)}, u32[]{:S(2)}, u32[]{:S(2)}) collective-permute-start(bf16[32,4096]{1,0:T(8,128)(2,1)S(1)} %get-tuple-element.17), channel_id=1, source_target_pairs={{0,1},{1,2},{2,3},{3,4},{4,5},{5,6},{6,7},{7,0},{8,9},{9,10},{10,1... | collective-permute-start | bytes 786440 | tf_op jit(solution)/shard_map/ppermute | solution.py:25
  51.3 14.7 %collective-permute-start.9 = (bf16[32,4096]{1,0:T(8,128)(2,1)S(1)}, bf16[32,4096]{1,0:T(8,128)(2,1)S(1)}, u32[]{:S(2)}, u32[]{:S(2)}) collective-permute-start(bf16[32,4096]{1,0:T(8,128)(2,1)S(1)} %get-tuple-element.18), channel_id=1, source_target_pairs={{0,7},{1,0},{2,1},{3,2},{4,3},{5,4},{6,5},{7,6},{8,15},{9,8},{10,9... | collective-permute-start | bytes 786440 | tf_op jit(solution)/shard_map/ppermute | solution.py:25
  64.0 11.5 %collective-permute-start.6 = (bf16[32,4096]{1,0:T(8,128)(2,1)S(1)}, bf16[32,4096]{1,0:T(8,128)(2,1)S(1)}, u32[]{:S(2)}, u32[]{:S(2)}) collective-permute-start(bf16[32,4096]{1,0:T(8,128)(2,1)S(1)} %fusion.7), channel_id=1, source_target_pairs={{0,1},{1,2},{2,3},{3,4},{4,5},{5,6},{6,7},{7,0},{8,9},{9,10},{10,1... | collective-permute-start | bytes 786440 | tf_op jit(solution)/shard_map/ppermute | solution.py:25
  66.0 37.4 %copy-start.9 = (f32[4096]{0:T(1024)S(1)}, f32[4096]{0:T(1024)}, u32[]{:S(2)}) copy-start(f32[4096]{0:T(1024)} %param.17) | copy-start | bytes 49156
  75.6 10.7 %collective-permute-start.10 = (bf16[32,4096]{1,0:T(8,128)(2,1)S(1)}, bf16[32,4096]{1,0:T(8,128)(2,1)S(1)}, u32[]{:S(2)}, u32[]{:S(2)}) collective-permute-start(bf16[32,4096]{1,0:T(8,128)(2,1)S(1)} %get-tuple-element.16), channel_id=1, source_target_pairs={{0,7},{1,0},{2,1},{3,2},{4,3},{5,4},{6,5},{7,6},{8,15},{9,8},{10,9... | collective-permute-start | bytes 786440 | tf_op jit(solution)/shard_map/ppermute | solution.py:25
  78.7 11.6 %collective-permute-start.7 = (bf16[32,4096]{1,0:T(8,128)(2,1)S(1)}, bf16[32,4096]{1,0:T(8,128)(2,1)S(1)}, u32[]{:S(2)}, u32[]{:S(2)}) collective-permute-start(bf16[32,4096]{1,0:T(8,128)(2,1)S(1)} %get-tuple-element.15), channel_id=1, source_target_pairs={{0,1},{1,2},{2,3},{3,4},{4,5},{5,6},{6,7},{7,0},{8,9},{9,10},{10,1... | collective-permute-start | bytes 786440 | tf_op jit(solution)/shard_map/ppermute | solution.py:25
  90.4 9.5 %collective-permute-start.11 = (bf16[32,4096]{1,0:T(8,128)(2,1)S(1)}, bf16[32,4096]{1,0:T(8,128)(2,1)S(1)}, u32[]{:S(2)}, u32[]{:S(2)}) collective-permute-start(bf16[32,4096]{1,0:T(8,128)(2,1)S(1)} %get-tuple-element.14), channel_id=1, source_target_pairs={{0,7},{1,0},{2,1},{3,2},{4,3},{5,4},{6,5},{7,6},{8,15},{9,8},{10,9... | collective-permute-start | bytes 786440 | tf_op jit(solution)/shard_map/ppermute | solution.py:25
  92.4 10.8 %collective-permute-start.8 = (bf16[32,4096]{1,0:T(8,128)(2,1)S(1)}, bf16[32,4096]{1,0:T(8,128)(2,1)S(1)}, u32[]{:S(2)}, u32[]{:S(2)}) collective-permute-start(bf16[32,4096]{1,0:T(8,128)(2,1)S(1)} %get-tuple-element.13), channel_id=1, source_target_pairs={{0,1},{1,2},{2,3},{3,4},{4,5},{5,6},{6,7},{7,0},{8,9},{9,10},{10,1... | collective-permute-start | bytes 786440 | tf_op jit(solution)/shard_map/ppermute | solution.py:25
  103.4 0.9 copy-start.4

commit v11 on v10

--- a/solution.py
+++ b/solution.py
@@ -129,10 +129,17 @@
             jnp.concatenate([lane_pick(tree_stats, group + g) for g in range(group)], axis=0),
             stacked_heads(tree_ref, row0, group),
         )]
-        for page_index, page_ref in zip(page_ids, (kv_ref,) + tuple(pages)):
-            positions = lax.broadcasted_iota(jnp.int32, (1, page_size), 1) + page_index * page_size
-            blocks.append(attend(query, page_ref[r, :, 0:HD], page_ref[r, :, HD : 2 * HD],
-                                 positions < length, False))
+        page_refs = (kv_ref,) + tuple(pages)
+        if page_ids == tuple(range(len(page_ids))):
+            keys = jnp.concatenate([ref[r, :, 0:HD] for ref in page_refs], axis=0)
+            values = jnp.concatenate([ref[r, :, HD : 2 * HD] for ref in page_refs], axis=0)
+            positions = lax.broadcasted_iota(jnp.int32, (1, page_size * len(page_refs)), 1)
+            blocks.append(attend(query, keys, values, positions < length, False))
+        else:
+            for page_index, page_ref in zip(page_ids, page_refs):
+                positions = lax.broadcasted_iota(jnp.int32, (1, page_size), 1) + page_index * page_size
+                blocks.append(attend(query, page_ref[r, :, 0:HD], page_ref[r, :, HD : 2 * HD],
+                                     positions < length, False))
         top = blocks[0][0]
         for block in blocks[1:]:
             top = jnp.maximum(top, block[0])

time: 105 us -> 103 us (0.981)
  the two profiles are of different devices: /device:TPU:62 before, /device:TPU:16 now
where the time goes in v11:
time: 103 us
  starting transfers between devices  44.1 us (43%)
  waiting for transfers between devices  28 us (27%)
  Pallas kernels  19.1 us (19%)
  local copies, waits for them, and re-layouts  7.97 us (8%)
  other arithmetic  2.48 us (2%)
  between operations  1.07 us (1%)
    ppermute x12, starting transfers between devices, shifted(): return lax.ppermute(value, axis, pairs)  44.1 us
    ppermute x12, waiting for transfers between devices, shifted(): return lax.ppermute(value, axis, pairs)  28 us
    pallas_call x2, Pallas kernels, holder_partial(): pl.pallas_call(functools.partial(holder_kernel, page_index, group), out_s...  8.07 us
    unnamed x24, local copies, waits for them, and re-layouts  5.79 us
    pallas_call x1, Pallas kernels, local_partial(): pl.pallas_call(functools.partial(local_kernel, group, page_ids), out_shap...  5.63 us
    pallas_call x1, Pallas kernels, tree_partial(): pl.pallas_call(functools.partial(tree_kernel, group), out_shape=(jax.Shap...  3.71 us
  transfers between devices with their start and end apart: 12, of which 6 were waited for; matrix products, arithmetic and copies ran while one was open for 2% of the time, Pallas kernels for 17%

profile of v11, /device:TPU:16, one launch (start us, length us, event | category | flops | bytes accessed | tf_op | source)
XLA Modules:
  0.0 102.8 jit_solution(9633177738536981256)
XLA Ops:
  0.6 0.0 copy-start.11
  0.6 0.0 copy-start.3
  0.7 1.3 %slice_bitcast_fusion = bf16[8,256,256]{2,1,0:T(8,128)(2,1)S(1)} fusion(bf16[8,4,256,256]{3,2,1,0:T(8,128)(2,1)} %kv_ref.5), kind=kLoop, calls=%fused_computation | loop fusion | bytes 2097152 | tf_op jit(solution)/shard_map/squeeze | solution.py:342
  2.0 1.9 %collective-permute-start = (bf16[8,256,256]{2,1,0:T(8,128)(2,1)S(1)}, bf16[8,256,256]{2,1,0:T(8,128)(2,1)S(1)}, u32[]{:S(2)}, u32[]{:S(2)}) collective-permute-start(bf16[8,256,256]{2,1,0:T(8,128)(2,1)S(1)} %slice_bitcast_fusion), channel_id=1, source_target_pairs={{0,504},{8,0},{16,8},{24,16},{32,24},{40,32},{48,40},{56,48},{64,5... | collective-permute-start | bytes 3145736 | tf_op jit(solution)/shard_map/ppermute | solution.py:25
  4.0 3.5 %collective-permute-start.1 = (bf16[272,256]{1,0:T(8,128)(2,1)S(1)}, bf16[272,256]{1,0:T(8,128)(2,1)S(1)}, u32[]{:S(2)}, u32[]{:S(2)}) collective-permute-start(bf16[272,256]{1,0:T(8,128)(2,1)S(1)} %pad_maximum_fusion), channel_id=1, source_target_pairs={{0,16},{8,24},{16,32},{24,40},{32,48},{40,56},{48,64},{56,72},{64,... | collective-permute-start | bytes 417800 | tf_op jit(solution)/shard_map/ppermute | solution.py:25
  7.5 4.5 %collective-permute-start.3 = (bf16[272,256]{1,0:T(8,128)(2,1)S(1)}, bf16[272,256]{1,0:T(8,128)(2,1)S(1)}, u32[]{:S(2)}, u32[]{:S(2)}) collective-permute-start(bf16[272,256]{1,0:T(8,128)(2,1)S(1)} %pad_maximum_fusion), channel_id=1, source_target_pairs={{0,24},{8,32},{16,40},{24,48},{32,56},{40,64},{48,72},{56,80},{64,... | collective-permute-start | bytes 417800 | tf_op jit(solution)/shard_map/ppermute | solution.py:25
  12.1 0.1 broadcast_add_fusion
  12.1 0.8 reshape.46.parent_ref
  12.9 3.7 %shard_map.112 = (f32[256,384]{1,0:T(8,128)}, bf16[8,8,256]{2,1,0:T(8,128)(2,1)}) custom-call(s32[8]{0:T(128)} %acc_ref.1, bf16[256,256]{1,0:T(8,128)(2,1)} %q_ref.3, bf16[256,256]{1,0:T(8,128)(2,1)} %fresh_ref.1, s32[256,1]{1,0:T(8,128)} %reshape.46.parent_ref), custom_call_target="tpu_custom_call" | custom-call | tf_op jit(solution)/shard_map/pallas_call | solution.py:102
  16.6 0.0 collective-permute-done.1.q_ref
  16.6 0.7 copy-done.8
  17.3 4.0 %shard_map.114 = bf16[256,384]{1,0:T(8,128)(2,1)} custom-call(bf16[272,256]{1,0:T(8,128)(2,1)} %copy-done.8, bf16[8,4,256,256]{3,2,1,0:T(8,128)(2,1)} %kv_ref.5, f32[256,384]{1,0:T(8,128)} %get-tuple-element.7.tree_ref.order_ref), custom_call_target="tpu_custom_call" | custom-call | tf_op jit(solution)/shard_map/pallas_call | solution.py:220
  21.3 2.6 %collective-permute-start.2 = (bf16[256,384]{1,0:T(8,128)(2,1)}, bf16[256,384]{1,0:T(8,128)(2,1)S(1)}, u32[]{:S(2)}, u32[]{:S(2)}) collective-permute-start(bf16[256,384]{1,0:T(8,128)(2,1)} %shard_map.114), channel_id=1, source_target_pairs={{0,496},{8,504},{16,0},{24,8},{32,16},{40,24},{48,32},{56,40},{64,... | collective-permute-start | bytes 589832 | tf_op jit(solution)/shard_map/ppermute | solution.py:25
  24.0 0.0 collective-permute-done.3.q_ref
  24.0 0.0 copy-start.7
  24.0 0.6 copy-done.7
  24.6 4.0 %shard_map.115 = bf16[256,384]{1,0:T(8,128)(2,1)} custom-call(bf16[272,256]{1,0:T(8,128)(2,1)} %copy-done.7, bf16[8,4,256,256]{3,2,1,0:T(8,128)(2,1)} %kv_ref.5, f32[256,384]{1,0:T(8,128)} %get-tuple-element.7.tree_ref.order_ref), custom_call_target="tpu_custom_call" | custom-call | tf_op jit(solution)/shard_map/pallas_call | solution.py:220
  28.7 7.6 %collective-permute-start.4 = (bf16[256,384]{1,0:T(8,128)(2,1)}, bf16[256,384]{1,0:T(8,128)(2,1)S(1)}, u32[]{:S(2)}, u32[]{:S(2)}) collective-permute-start(bf16[256,384]{1,0:T(8,128)(2,1)} %shard_map.115), channel_id=1, source_target_pairs={{0,488},{8,496},{16,504},{24,0},{32,8},{40,16},{48,24},{56,32},{64... | collective-permute-start | bytes 589832 | tf_op jit(solution)/shard_map/ppermute | solution.py:25
  36.3 0.0 collective-permute-done.rest_0_
  36.3 1.0 copy-done.5
  37.3 5.6 %shard_map.113 = (f32[256,256]{1,0:T(8,128)}, f32[256,128]{1,0:T(8,128)}) custom-call(s32[8]{0:T(128)} %lens_ref.1, bf16[256,256]{1,0:T(8,128)(2,1)} %q_ref.3, bf16[8,4,256,256]{3,2,1,0:T(8,128)(2,1)} %kv_ref.5, f32[256,384]{1,0:T(8,128)} %get-tuple-element.7.tree_ref.order_ref, bf16[8,256,256]{2,1,0:T(8,128)(2,1)} %copy-done.5), custom_call_target="tpu_custom_call" | custom-call | tf_op jit(solution)/shard_map/pallas_call | solution.py:166
  43.0 0.0 collective-permute-done.2.rest_0_
  43.0 0.0 collective-permute-done.4.rest_1_
  43.0 0.0 copy-start
  43.0 1.6 %copy-done = bf16[256,4096]{1,0:T(8,128)(2,1)S(1)} copy-done((bf16[256,4096]{1,0:T(8,128)(2,1)S(1)}, bf16[256,4096]{1,0:T(8,128)(2,1)}, u32[]{:S(2)}) %copy-start) | copy-done | bytes 2097176
  44.6 0.9 copy-done.1
  45.5 0.9 copy-done.2
  46.4 1.7 %shard_map.116 = bf16[256,4096]{1,0:T(8,128)(2,1)S(1)} custom-call(f32[256,256]{1,0:T(8,128)S(1)} %copy-done.1, f32[256,128]{1,0:T(8,128)S(1)} %copy-done.2, bf16[256,384]{1,0:T(8,128)(2,1)S(1)} %collective-permute-done.2.rest_0_, bf16[256,384]{1,0:T(8,128)(2,1)S(1)} %collective-permute-done.4.rest_1_, bf16[256,4096]{1,0:T(8,128)(2,1)S(1)} %copy-done), custom_call_target="tpu_custom_call" | custom-call | tf_op jit(solution)/shard_map/pallas_call | solution.py:280
  48.2 0.0 copy-start.6
  48.2 2.1 %collective-permute-start.5 = (bf16[32,4096]{1,0:T(8,128)(2,1)S(1)}, bf16[32,4096]{1,0:T(8,128)(2,1)}, u32[]{:S(2)}, u32[]{:S(2)}) collective-permute-start(bf16[32,4096]{1,0:T(8,128)(2,1)S(1)} %get-tuple-element.17), channel_id=1, source_target_pairs={{0,1},{1,2},{2,3},{3,4},{4,5},{5,6},{6,7},{7,0},{8,9},{9,10},{10,1... | collective-permute-start | bytes 786440 | tf_op jit(solution)/shard_map/ppermute | solution.py:25
  50.3 8.3 %collective-permute-start.9 = (bf16[32,4096]{1,0:T(8,128)(2,1)S(1)}, bf16[32,4096]{1,0:T(8,128)(2,1)S(1)}, u32[]{:S(2)}, u32[]{:S(2)}) collective-permute-start(bf16[32,4096]{1,0:T(8,128)(2,1)S(1)} %get-tuple-element.18), channel_id=1, source_target_pairs={{0,7},{1,0},{2,1},{3,2},{4,3},{5,4},{6,5},{7,6},{8,15},{9,8},{10,9... | collective-permute-start | bytes 786440 | tf_op jit(solution)/shard_map/ppermute | solution.py:25
  58.6 4.5 %collective-permute-done.5 = bf16[32,4096]{1,0:T(8,128)(2,1)} collective-permute-done((bf16[32,4096]{1,0:T(8,128)(2,1)S(1)}, bf16[32,4096]{1,0:T(8,128)(2,1)}, u32[]{:S(2)}, u32[]{:S(2)}) %collective-permute-start.5) | collective-permute-done | bytes 262176 | tf_op jit(solution)/shard_map/ppermute | solution.py:25
  63.1 1.0 fusion.7
  64.1 1.9 %collective-permute-start.6 = (bf16[32,4096]{1,0:T(8,128)(2,1)S(1)}, bf16[32,4096]{1,0:T(8,128)(2,1)S(1)}, u32[]{:S(2)}, u32[]{:S(2)}) collective-permute-start(bf16[32,4096]{1,0:T(8,128)(2,1)S(1)} %fusion.7), channel_id=1, source_target_pairs={{0,1},{1,2},{2,3},{3,4},{4,5},{5,6},{6,7},{7,0},{8,9},{9,10},{10,1... | collective-permute-start | bytes 786440 | tf_op jit(solution)/shard_map/ppermute | solution.py:25
  66.1 0.0 copy-start.9
  66.1 9.9 %collective-permute-done.6 = bf16[32,4096]{1,0:T(8,128)(2,1)S(1)} collective-permute-done((bf16[32,4096]{1,0:T(8,128)(2,1)S(1)}, bf16[32,4096]{1,0:T(8,128)(2,1)S(1)}, u32[]{:S(2)}, u32[]{:S(2)}) %collective-permute-start.6) | collective-permute-done | bytes 262176 | tf_op jit(solution)/shard_map/ppermute | solution.py:25
  76.0 0.1 fusion.6
  76.2 2.9 %collective-permute-start.10 = (bf16[32,4096]{1,0:T(8,128)(2,1)S(1)}, bf16[32,4096]{1,0:T(8,128)(2,1)S(1)}, u32[]{:S(2)}, u32[]{:S(2)}) collective-permute-start(bf16[32,4096]{1,0:T(8,128)(2,1)S(1)} %get-tuple-element.16), channel_id=1, source_target_pairs={{0,7},{1,0},{2,1},{3,2},{4,3},{5,4},{6,5},{7,6},{8,15},{9,8},{10,9... | collective-permute-start | bytes 786440 | tf_op jit(solution)/shard_map/ppermute | solution.py:25
  79.1 2.9 %collective-permute-start.7 = (bf16[32,4096]{1,0:T(8,128)(2,1)S(1)}, bf16[32,4096]{1,0:T(8,128)(2,1)S(1)}, u32[]{:S(2)}, u32[]{:S(2)}) collective-permute-start(bf16[32,4096]{1,0:T(8,128)(2,1)S(1)} %get-tuple-element.15), channel_id=1, source_target_pairs={{0,1},{1,2},{2,3},{3,4},{4,5},{5,6},{6,7},{7,0},{8,9},{9,10},{10,1... | collective-permute-start | bytes 786440 | tf_op jit(solution)/shard_map/ppermute | solution.py:25
  82.1 4.0 %collective-permute-done.10 = bf16[32,4096]{1,0:T(8,128)(2,1)S(1)} collective-permute-done((bf16[32,4096]{1,0:T(8,128)(2,1)S(1)}, bf16[32,4096]{1,0:T(8,128)(2,1)S(1)}, u32[]{:S(2)}, u32[]{:S(2)}) %collective-permute-start.10) | collective-permute-done | bytes 262176 | tf_op jit(solution)/shard_map/ppermute | solution.py:25
  86.1 3.7 %collective-permute-done.7 = bf16[32,4096]{1,0:T(8,128)(2,1)S(1)} collective-permute-done((bf16[32,4096]{1,0:T(8,128)(2,1)S(1)}, bf16[32,4096]{1,0:T(8,128)(2,1)S(1)}, u32[]{:S(2)}, u32[]{:S(2)}) %collective-permute-start.7) | collective-permute-done | bytes 262176 | tf_op jit(solution)/shard_map/ppermute | solution.py:25
  89.8 0.1 fusion.5
  89.9 1.9 %collective-permute-start.11 = (bf16[32,4096]{1,0:T(8,128)(2,1)S(1)}, bf16[32,4096]{1,0:T(8,128)(2,1)S(1)}, u32[]{:S(2)}, u32[]{:S(2)}) collective-permute-start(bf16[32,4096]{1,0:T(8,128)(2,1)S(1)} %get-tuple-element.14), channel_id=1, source_target_pairs={{0,7},{1,0},{2,1},{3,2},{4,3},{5,4},{6,5},{7,6},{8,15},{9,8},{10,9... | collective-permute-start | bytes 786440 | tf_op jit(solution)/shard_map/ppermute | solution.py:25
  91.8 3.9 %collective-permute-start.8 = (bf16[32,4096]{1,0:T(8,128)(2,1)S(1)}, bf16[32,4096]{1,0:T(8,128)(2,1)S(1)}, u32[]{:S(2)}, u32[]{:S(2)}) collective-permute-start(bf16[32,4096]{1,0:T(8,128)(2,1)S(1)} %get-tuple-element.13), channel_id=1, source_target_pairs={{0,1},{1,2},{2,3},{3,4},{4,5},{5,6},{6,7},{7,0},{8,9},{9,10},{10,1... | collective-permute-start | bytes 786440 | tf_op jit(solution)/shard_map/ppermute | solution.py:25
  95.8 2.7 %collective-permute-done.11 = bf16[32,4096]{1,0:T(8,128)(2,1)S(1)} collective-permute-done((bf16[32,4096]{1,0:T(8,128)(2,1)S(1)}, bf16[32,4096]{1,0:T(8,128)(2,1)S(1)}, u32[]{:S(2)}, u32[]{:S(2)}) %collective-permute-start.11) | collective-permute-done | bytes 262176 | tf_op jit(solution)/shard_map/ppermute | solution.py:25
  98.5 3.1 %collective-permute-done.8 = bf16[32,4096]{1,0:T(8,128)(2,1)S(1)} collective-permute-done((bf16[32,4096]{1,0:T(8,128)(2,1)S(1)}, bf16[32,4096]{1,0:T(8,128)(2,1)S(1)}, u32[]{:S(2)}, u32[]{:S(2)}) %collective-permute-start.8) | collective-permute-done | bytes 262176 | tf_op jit(solution)/shard_map/ppermute | solution.py:25
  101.6 0.3 fusion
  101.9 0.8 fusion.2
  (19 shorter events, 0.1 us)
Async XLA Ops:
  0.6 3.3 %copy-start.11 = (s32[8]{0:T(128)S(1)}, s32[8]{0:T(128)}, u32[]{:S(2)}) copy-start(s32[8]{0:T(128)} %lens_ref.1) | copy-start | bytes 100
  0.6 3.3 %copy-start.3 = (bf16[256,256]{1,0:T(8,128)(2,1)S(1)}, bf16[256,256]{1,0:T(8,128)(2,1)}, u32[]{:S(2)}) copy-start(bf16[256,256]{1,0:T(8,128)(2,1)} %q_ref.3) | copy-start | bytes 393220
  0.7 11.4 %copy-start.10 = (s32[8,32]{1,0:T(8,128)S(1)}, s32[8,32]{1,0:T(8,128)}, u32[]{:S(2)}) copy-start(s32[8,32]{1,0:T(8,128)} %param.13) | copy-start | bytes 3076
  2.0 34.3 %collective-permute-start = (bf16[8,256,256]{2,1,0:T(8,128)(2,1)S(1)}, bf16[8,256,256]{2,1,0:T(8,128)(2,1)S(1)}, u32[]{:S(2)}, u32[]{:S(2)}) collective-permute-start(bf16[8,256,256]{2,1,0:T(8,128)(2,1)S(1)} %slice_bitcast_fusion), channel_id=1, source_target_pairs={{0,504},{8,0},{16,8},{24,16},{32,24},{40,32},{48,40},{56,48},{64,5... | collective-permute-start | bytes 3145736 | tf_op jit(solution)/shard_map/ppermute | solution.py:25
  4.0 12.6 %collective-permute-start.1 = (bf16[272,256]{1,0:T(8,128)(2,1)S(1)}, bf16[272,256]{1,0:T(8,128)(2,1)S(1)}, u32[]{:S(2)}, u32[]{:S(2)}) collective-permute-start(bf16[272,256]{1,0:T(8,128)(2,1)S(1)} %pad_maximum_fusion), channel_id=1, source_target_pairs={{0,16},{8,24},{16,32},{24,40},{32,48},{40,56},{48,64},{56,72},{64,... | collective-permute-start | bytes 417800 | tf_op jit(solution)/shard_map/ppermute | solution.py:25
  7.5 16.4 %collective-permute-start.3 = (bf16[272,256]{1,0:T(8,128)(2,1)S(1)}, bf16[272,256]{1,0:T(8,128)(2,1)S(1)}, u32[]{:S(2)}, u32[]{:S(2)}) collective-permute-start(bf16[272,256]{1,0:T(8,128)(2,1)S(1)} %pad_maximum_fusion), channel_id=1, source_target_pairs={{0,24},{8,32},{16,40},{24,48},{32,56},{40,64},{48,72},{56,80},{64,... | collective-permute-start | bytes 417800 | tf_op jit(solution)/shard_map/ppermute | solution.py:25
  16.6 0.7 copy-start.8
  21.3 21.6 %collective-permute-start.2 = (bf16[256,384]{1,0:T(8,128)(2,1)}, bf16[256,384]{1,0:T(8,128)(2,1)S(1)}, u32[]{:S(2)}, u32[]{:S(2)}) collective-permute-start(bf16[256,384]{1,0:T(8,128)(2,1)} %shard_map.114), channel_id=1, source_target_pairs={{0,496},{8,504},{16,0},{24,8},{32,16},{40,24},{48,32},{56,40},{64,... | collective-permute-start | bytes 589832 | tf_op jit(solution)/shard_map/ppermute | solution.py:25
  24.0 0.7 copy-start.7
  28.7 14.3 %collective-permute-start.4 = (bf16[256,384]{1,0:T(8,128)(2,1)}, bf16[256,384]{1,0:T(8,128)(2,1)S(1)}, u32[]{:S(2)}, u32[]{:S(2)}) collective-permute-start(bf16[256,384]{1,0:T(8,128)(2,1)} %shard_map.115), channel_id=1, source_target_pairs={{0,488},{8,496},{16,504},{24,0},{32,8},{40,16},{48,24},{56,32},{64... | collective-permute-start | bytes 589832 | tf_op jit(solution)/shard_map/ppermute | solution.py:25
  36.3 1.0 copy-start.5
  43.0 1.6 %copy-start = (bf16[256,4096]{1,0:T(8,128)(2,1)S(1)}, bf16[256,4096]{1,0:T(8,128)(2,1)}, u32[]{:S(2)}) copy-start(bf16[256,4096]{1,0:T(8,128)(2,1)} %rest_2_.1) | copy-start | bytes 6291460
  44.6 0.9 copy-start.1
  45.5 0.9 copy-start.2
  48.2 53.5 %copy-start.6 = (bf16[32,4096]{1,0:T(8,128)(2,1)S(1)}, bf16[32,4096]{1,0:T(8,128)(2,1)}, u32[]{:S(2)}) copy-start(bf16[32,4096]{1,0:T(8,128)(2,1)} %param.15) | copy-start | bytes 786436
  48.2 14.9 %collective-permute-start.5 = (bf16[32,4096]{1,0:T(8,128)(2,1)S(1)}, bf16[32,4096]{1,0:T(8,128)(2,1)}, u32[]{:S(2)}, u32[]{:S(2)}) collective-permute-start(bf16[32,4096]{1,0:T(8,128)(2,1)S(1)} %get-tuple-element.17), channel_id=1, source_target_pairs={{0,1},{1,2},{2,3},{3,4},{4,5},{5,6},{6,7},{7,0},{8,9},{9,10},{10,1... | collective-permute-start | bytes 786440 | tf_op jit(solution)/shard_map/ppermute | solution.py:25
  50.3 15.9 %collective-permute-start.9 = (bf16[32,4096]{1,0:T(8,128)(2,1)S(1)}, bf16[32,4096]{1,0:T(8,128)(2,1)S(1)}, u32[]{:S(2)}, u32[]{:S(2)}) collective-permute-start(bf16[32,4096]{1,0:T(8,128)(2,1)S(1)} %get-tuple-element.18), channel_id=1, source_target_pairs={{0,7},{1,0},{2,1},{3,2},{4,3},{5,4},{6,5},{7,6},{8,15},{9,8},{10,9... | collective-permute-start | bytes 786440 | tf_op jit(solution)/shard_map/ppermute | solution.py:25
  64.1 11.9 %collective-permute-start.6 = (bf16[32,4096]{1,0:T(8,128)(2,1)S(1)}, bf16[32,4096]{1,0:T(8,128)(2,1)S(1)}, u32[]{:S(2)}, u32[]{:S(2)}) collective-permute-start(bf16[32,4096]{1,0:T(8,128)(2,1)S(1)} %fusion.7), channel_id=1, source_target_pairs={{0,1},{1,2},{2,3},{3,4},{4,5},{5,6},{6,7},{7,0},{8,9},{9,10},{10,1... | collective-permute-start | bytes 786440 | tf_op jit(solution)/shard_map/ppermute | solution.py:25
  66.1 35.8 %copy-start.9 = (f32[4096]{0:T(1024)S(1)}, f32[4096]{0:T(1024)}, u32[]{:S(2)}) copy-start(f32[4096]{0:T(1024)} %param.17) | copy-start | bytes 49156
  76.2 9.9 %collective-permute-start.10 = (bf16[32,4096]{1,0:T(8,128)(2,1)S(1)}, bf16[32,4096]{1,0:T(8,128)(2,1)S(1)}, u32[]{:S(2)}, u32[]{:S(2)}) collective-permute-start(bf16[32,4096]{1,0:T(8,128)(2,1)S(1)} %get-tuple-element.16), channel_id=1, source_target_pairs={{0,7},{1,0},{2,1},{3,2},{4,3},{5,4},{6,5},{7,6},{8,15},{9,8},{10,9... | collective-permute-start | bytes 786440 | tf_op jit(solution)/shard_map/ppermute | solution.py:25
  79.1 10.7 %collective-permute-start.7 = (bf16[32,4096]{1,0:T(8,128)(2,1)S(1)}, bf16[32,4096]{1,0:T(8,128)(2,1)S(1)}, u32[]{:S(2)}, u32[]{:S(2)}) collective-permute-start(bf16[32,4096]{1,0:T(8,128)(2,1)S(1)} %get-tuple-element.15), channel_id=1, source_target_pairs={{0,1},{1,2},{2,3},{3,4},{4,5},{5,6},{6,7},{7,0},{8,9},{9,10},{10,1... | collective-permute-start | bytes 786440 | tf_op jit(solution)/shard_map/ppermute | solution.py:25
  89.9 8.6 %collective-permute-start.11 = (bf16[32,4096]{1,0:T(8,128)(2,1)S(1)}, bf16[32,4096]{1,0:T(8,128)(2,1)S(1)}, u32[]{:S(2)}, u32[]{:S(2)}) collective-permute-start(bf16[32,4096]{1,0:T(8,128)(2,1)S(1)} %get-tuple-element.14), channel_id=1, source_target_pairs={{0,7},{1,0},{2,1},{3,2},{4,3},{5,4},{6,5},{7,6},{8,15},{9,8},{10,9... | collective-permute-start | bytes 786440 | tf_op jit(solution)/shard_map/ppermute | solution.py:25
  91.8 9.8 %collective-permute-start.8 = (bf16[32,4096]{1,0:T(8,128)(2,1)S(1)}, bf16[32,4096]{1,0:T(8,128)(2,1)S(1)}, u32[]{:S(2)}, u32[]{:S(2)}) collective-permute-start(bf16[32,4096]{1,0:T(8,128)(2,1)S(1)} %get-tuple-element.13), channel_id=1, source_target_pairs={{0,1},{1,2},{2,3},{3,4},{4,5},{5,6},{6,7},{7,0},{8,9},{9,10},{10,1... | collective-permute-start | bytes 786440 | tf_op jit(solution)/shard_map/ppermute | solution.py:25
  101.9 0.9 copy-start.4

commit v12 on v11

--- a/solution.py
+++ b/solution.py
@@ -190,27 +190,36 @@
     rows = req_count * TREE
     extra = q_ref[rows : rows + EXTRA, :].astype(jnp.float32)
     length_row = extra[0:1, :] * 16.0 + extra[1:2, :]
-    positions = (
-        lax.broadcasted_iota(jnp.int32, (1, page_size), 1) + page_index * page_size
-    ).astype(jnp.float32)
+    pair = 2 if req_count % 2 == 0 else 1
+    q_rows = pair * group * TREE
+    sub = lax.broadcasted_iota(jnp.int32, (q_rows, pair * page_size), 0)
+    lane = lax.broadcasted_iota(jnp.int32, (q_rows, pair * page_size), 1)
+    same_request = (sub // (group * TREE)) == (lane // page_size)
+    positions = ((lane % page_size) + page_index * page_size).astype(jnp.float32)
+    row_owner = lax.broadcasted_iota(jnp.int32, (q_rows, 1), 0) // (group * TREE)
     stat_lanes = lax.broadcasted_iota(jnp.int32, (TREE, STAT_LANES), 1)
-    for r in range(req_count):
-        row0 = r * TREE
-        valid = positions < lane_pick(length_row, r)
-        query = stacked_heads(q_ref, row0, group)
-        largest, totals, weighted = attend(
-            query, kv_ref[r, :, 0:HD], kv_ref[r, :, HD : 2 * HD], valid, True
-        )
+    for r0 in range(0, req_count, pair):
+        members = list(range(r0, r0 + pair))
+        length = jnp.zeros((q_rows, 1), jnp.float32)
+        for k, r in enumerate(members):
+            length = jnp.where(row_owner == k, lane_pick(length_row, r), length)
+        valid = same_request & (positions < length)
+        query = jnp.concatenate([stacked_heads(q_ref, r * TREE, group) for r in members], axis=0)
+        key = jnp.concatenate([kv_ref[r, :, 0:HD] for r in members], axis=0)
+        value = jnp.concatenate([kv_ref[r, :, HD : 2 * HD] for r in members], axis=0)
+        largest, totals, weighted = attend(query, key, value, valid, True)
         total_hi = totals.astype(jnp.bfloat16).astype(jnp.float32)
         total_lo = totals - total_hi
-        stats = jnp.zeros((TREE, STAT_LANES), jnp.float32)
-        for g in range(group):
-            part = slice(g * TREE, (g + 1) * TREE)
-            out_ref[row0 : row0 + TREE, g * HD : (g + 1) * HD] = weighted[part].astype(jnp.bfloat16)
-            stats = jnp.where(stat_lanes == g, largest[part], stats)
-            stats = jnp.where(stat_lanes == group + g, total_hi[part], stats)
-            stats = jnp.where(stat_lanes == 2 * group + g, total_lo[part], stats)
-        out_ref[row0 : row0 + TREE, group * HD : group * HD + STAT_LANES] = stats.astype(jnp.bfloat16)
+        for k, r in enumerate(members):
+            row0 = r * TREE
+            stats = jnp.zeros((TREE, STAT_LANES), jnp.float32)
+            for g in range(group):
+                part = slice((k * group + g) * TREE, (k * group + g + 1) * TREE)
+                out_ref[row0 : row0 + TREE, g * HD : (g + 1) * HD] = weighted[part].astype(jnp.bfloat16)
+                stats = jnp.where(stat_lanes == g, largest[part], stats)
+                stats = jnp.where(stat_lanes == group + g, total_hi[part], stats)
+                stats = jnp.where(stat_lanes == 2 * group + g, total_lo[part], stats)
+            out_ref[row0 : row0 + TREE, group * HD : group * HD + STAT_LANES] = stats.astype(jnp.bfloat16)
 
 
 def holder_partial(packed_queries, kv_pool, page_index, group, order_after):

time: 103 us -> 102 us (level)
  Pallas kernels: 19.1 us -> 17.4 us
    pallas_call x2, Pallas kernels: 8.07 us -> 6.38 us  [holder_partial(): pl.pallas_call(functools.partial(holder_kernel, page_index, group), out_s...]
  transfers between devices with their start and end apart: 12 -> 12, of which waited for: 6 -> 6; matrix products, arithmetic and copies ran while one was open for 2% -> 2% of each run, Pallas kernels for 17% -> 16%
where the time goes in v12:
time: 102 us; the launch traced here: 101 us
  starting transfers between devices  44.1 us (43%)
  waiting for transfers between devices  28 us (27%)
  Pallas kernels  17.4 us (17%)
  local copies, waits for them, and re-layouts  7.97 us (8%)
  other arithmetic  2.48 us (2%)
  between operations  1.07 us (1%)
    ppermute x12, starting transfers between devices, shifted(): return lax.ppermute(value, axis, pairs)  44.1 us
    ppermute x12, waiting for transfers between devices, shifted(): return lax.ppermute(value, axis, pairs)  28 us
    pallas_call x2, Pallas kernels, holder_partial(): pl.pallas_call(functools.partial(holder_kernel, page_index, group), out_s...  6.38 us
    unnamed x24, local copies, waits for them, and re-layouts  5.79 us
    pallas_call x1, Pallas kernels, local_partial(): pl.pallas_call(functools.partial(local_kernel, group, page_ids), out_shap...  5.63 us
    pallas_call x1, Pallas kernels, tree_partial(): pl.pallas_call(functools.partial(tree_kernel, group), out_shape=(jax.Shap...  3.71 us
  transfers between devices with their start and end apart: 12, of which 6 were waited for; matrix products, arithmetic and copies ran while one was open for 2% of the time, Pallas kernels for 16%

profile of v12, /device:TPU:16, one launch (start us, length us, event | category | flops | bytes accessed | tf_op | source)
XLA Modules:
  0.0 101.1 jit_solution(5173279445623191919)
XLA Ops:
  0.6 0.0 copy-start.11
  0.6 0.0 copy-start.3
  0.7 1.3 %slice_bitcast_fusion = bf16[8,256,256]{2,1,0:T(8,128)(2,1)S(1)} fusion(bf16[8,4,256,256]{3,2,1,0:T(8,128)(2,1)} %kv_ref.5), kind=kLoop, calls=%fused_computation | loop fusion | bytes 2097152 | tf_op jit(solution)/shard_map/squeeze | solution.py:351
  2.0 1.9 %collective-permute-start = (bf16[8,256,256]{2,1,0:T(8,128)(2,1)S(1)}, bf16[8,256,256]{2,1,0:T(8,128)(2,1)S(1)}, u32[]{:S(2)}, u32[]{:S(2)}) collective-permute-start(bf16[8,256,256]{2,1,0:T(8,128)(2,1)S(1)} %slice_bitcast_fusion), channel_id=1, source_target_pairs={{0,504},{8,0},{16,8},{24,16},{32,24},{40,32},{48,40},{56,48},{64,5... | collective-permute-start | bytes 3145736 | tf_op jit(solution)/shard_map/ppermute | solution.py:25
  4.0 3.5 %collective-permute-start.1 = (bf16[272,256]{1,0:T(8,128)(2,1)S(1)}, bf16[272,256]{1,0:T(8,128)(2,1)S(1)}, u32[]{:S(2)}, u32[]{:S(2)}) collective-permute-start(bf16[272,256]{1,0:T(8,128)(2,1)S(1)} %pad_maximum_fusion), channel_id=1, source_target_pairs={{0,16},{8,24},{16,32},{24,40},{32,48},{40,56},{48,64},{56,72},{64,... | collective-permute-start | bytes 417800 | tf_op jit(solution)/shard_map/ppermute | solution.py:25
  7.5 4.5 %collective-permute-start.3 = (bf16[272,256]{1,0:T(8,128)(2,1)S(1)}, bf16[272,256]{1,0:T(8,128)(2,1)S(1)}, u32[]{:S(2)}, u32[]{:S(2)}) collective-permute-start(bf16[272,256]{1,0:T(8,128)(2,1)S(1)} %pad_maximum_fusion), channel_id=1, source_target_pairs={{0,24},{8,32},{16,40},{24,48},{32,56},{40,64},{48,72},{56,80},{64,... | collective-permute-start | bytes 417800 | tf_op jit(solution)/shard_map/ppermute | solution.py:25
  12.1 0.1 broadcast_add_fusion
  12.1 0.8 reshape.46.parent_ref
  12.9 3.7 %shard_map.112 = (f32[256,384]{1,0:T(8,128)}, bf16[8,8,256]{2,1,0:T(8,128)(2,1)}) custom-call(s32[8]{0:T(128)} %acc_ref.1, bf16[256,256]{1,0:T(8,128)(2,1)} %q_ref.3, bf16[256,256]{1,0:T(8,128)(2,1)} %fresh_ref.1, s32[256,1]{1,0:T(8,128)} %reshape.46.parent_ref), custom_call_target="tpu_custom_call" | custom-call | tf_op jit(solution)/shard_map/pallas_call | solution.py:102
  16.6 0.0 collective-permute-done.1.q_ref
  16.6 0.7 copy-done.8
  17.3 3.2 %shard_map.114 = bf16[256,384]{1,0:T(8,128)(2,1)} custom-call(bf16[272,256]{1,0:T(8,128)(2,1)} %copy-done.8, bf16[8,4,256,256]{3,2,1,0:T(8,128)(2,1)} %kv_ref.5, f32[256,384]{1,0:T(8,128)} %get-tuple-element.7.tree_ref.order_ref), custom_call_target="tpu_custom_call" | custom-call | tf_op jit(solution)/shard_map/pallas_call | solution.py:229
  20.5 2.6 %collective-permute-start.2 = (bf16[256,384]{1,0:T(8,128)(2,1)}, bf16[256,384]{1,0:T(8,128)(2,1)S(1)}, u32[]{:S(2)}, u32[]{:S(2)}) collective-permute-start(bf16[256,384]{1,0:T(8,128)(2,1)} %shard_map.114), channel_id=1, source_target_pairs={{0,496},{8,504},{16,0},{24,8},{32,16},{40,24},{48,32},{56,40},{64,... | collective-permute-start | bytes 589832 | tf_op jit(solution)/shard_map/ppermute | solution.py:25
  23.1 0.0 copy-start.7
  23.1 0.6 copy-done.7
  23.8 3.2 %shard_map.115 = bf16[256,384]{1,0:T(8,128)(2,1)} custom-call(bf16[272,256]{1,0:T(8,128)(2,1)} %copy-done.7, bf16[8,4,256,256]{3,2,1,0:T(8,128)(2,1)} %kv_ref.5, f32[256,384]{1,0:T(8,128)} %get-tuple-element.7.tree_ref.order_ref), custom_call_target="tpu_custom_call" | custom-call | tf_op jit(solution)/shard_map/pallas_call | solution.py:229
  27.0 7.6 %collective-permute-start.4 = (bf16[256,384]{1,0:T(8,128)(2,1)}, bf16[256,384]{1,0:T(8,128)(2,1)S(1)}, u32[]{:S(2)}, u32[]{:S(2)}) collective-permute-start(bf16[256,384]{1,0:T(8,128)(2,1)} %shard_map.115), channel_id=1, source_target_pairs={{0,488},{8,496},{16,504},{24,0},{32,8},{40,16},{48,24},{56,32},{64... | collective-permute-start | bytes 589832 | tf_op jit(solution)/shard_map/ppermute | solution.py:25
  34.6 0.0 collective-permute-done.rest_0_
  34.6 1.0 copy-done.5
  35.6 5.6 %shard_map.113 = (f32[256,256]{1,0:T(8,128)}, f32[256,128]{1,0:T(8,128)}) custom-call(s32[8]{0:T(128)} %lens_ref.1, bf16[256,256]{1,0:T(8,128)(2,1)} %q_ref.3, bf16[8,4,256,256]{3,2,1,0:T(8,128)(2,1)} %kv_ref.5, f32[256,384]{1,0:T(8,128)} %get-tuple-element.7.tree_ref.order_ref, bf16[8,256,256]{2,1,0:T(8,128)(2,1)} %copy-done.5), custom_call_target="tpu_custom_call" | custom-call | tf_op jit(solution)/shard_map/pallas_call | solution.py:166
  41.3 0.0 collective-permute-done.2.rest_0_
  41.3 0.0 collective-permute-done.4.rest_1_
  41.3 0.0 copy-start
  41.3 1.6 %copy-done = bf16[256,4096]{1,0:T(8,128)(2,1)S(1)} copy-done((bf16[256,4096]{1,0:T(8,128)(2,1)S(1)}, bf16[256,4096]{1,0:T(8,128)(2,1)}, u32[]{:S(2)}) %copy-start) | copy-done | bytes 2097176
  42.9 0.9 copy-done.1
  43.8 0.9 copy-done.2
  44.7 1.7 %shard_map.116 = bf16[256,4096]{1,0:T(8,128)(2,1)S(1)} custom-call(f32[256,256]{1,0:T(8,128)S(1)} %copy-done.1, f32[256,128]{1,0:T(8,128)S(1)} %copy-done.2, bf16[256,384]{1,0:T(8,128)(2,1)S(1)} %collective-permute-done.2.rest_0_, bf16[256,384]{1,0:T(8,128)(2,1)S(1)} %collective-permute-done.4.rest_1_, bf16[256,4096]{1,0:T(8,128)(2,1)S(1)} %copy-done), custom_call_target="tpu_custom_call" | custom-call | tf_op jit(solution)/shard_map/pallas_call | solution.py:289
  46.5 0.0 copy-start.6
  46.5 2.1 %collective-permute-start.5 = (bf16[32,4096]{1,0:T(8,128)(2,1)S(1)}, bf16[32,4096]{1,0:T(8,128)(2,1)}, u32[]{:S(2)}, u32[]{:S(2)}) collective-permute-start(bf16[32,4096]{1,0:T(8,128)(2,1)S(1)} %get-tuple-element.17), channel_id=1, source_target_pairs={{0,1},{1,2},{2,3},{3,4},{4,5},{5,6},{6,7},{7,0},{8,9},{9,10},{10,1... | collective-permute-start | bytes 786440 | tf_op jit(solution)/shard_map/ppermute | solution.py:25
  48.6 8.3 %collective-permute-start.9 = (bf16[32,4096]{1,0:T(8,128)(2,1)S(1)}, bf16[32,4096]{1,0:T(8,128)(2,1)S(1)}, u32[]{:S(2)}, u32[]{:S(2)}) collective-permute-start(bf16[32,4096]{1,0:T(8,128)(2,1)S(1)} %get-tuple-element.18), channel_id=1, source_target_pairs={{0,7},{1,0},{2,1},{3,2},{4,3},{5,4},{6,5},{7,6},{8,15},{9,8},{10,9... | collective-permute-start | bytes 786440 | tf_op jit(solution)/shard_map/ppermute | solution.py:25
  56.9 4.5 %collective-permute-done.5 = bf16[32,4096]{1,0:T(8,128)(2,1)} collective-permute-done((bf16[32,4096]{1,0:T(8,128)(2,1)S(1)}, bf16[32,4096]{1,0:T(8,128)(2,1)}, u32[]{:S(2)}, u32[]{:S(2)}) %collective-permute-start.5) | collective-permute-done | bytes 262176 | tf_op jit(solution)/shard_map/ppermute | solution.py:25
  61.4 1.0 %fusion.7 = bf16[32,4096]{1,0:T(8,128)(2,1)S(1)} fusion(bf16[32,4096]{1,0:T(8,128)(2,1)} %collective-permute-done.5, bf16[8,32,4096]{2,1,0:T(8,128)(2,1)S(1)} %bitcast.33, s32[]{:T(128)S(6)} %select_n.78), kind=kLoop, calls=%fused_computation.15 | loop fusion | flops 524288 | bytes 786436 | tf_op jit(solution)/shard_map/convert_element_type | solution.py:327
  62.4 1.9 %collective-permute-start.6 = (bf16[32,4096]{1,0:T(8,128)(2,1)S(1)}, bf16[32,4096]{1,0:T(8,128)(2,1)S(1)}, u32[]{:S(2)}, u32[]{:S(2)}) collective-permute-start(bf16[32,4096]{1,0:T(8,128)(2,1)S(1)} %fusion.7), channel_id=1, source_target_pairs={{0,1},{1,2},{2,3},{3,4},{4,5},{5,6},{6,7},{7,0},{8,9},{9,10},{10,1... | collective-permute-start | bytes 786440 | tf_op jit(solution)/shard_map/ppermute | solution.py:25
  64.4 0.0 copy-start.9
  64.4 0.0 collective-permute-done.9
  64.4 9.9 %collective-permute-done.6 = bf16[32,4096]{1,0:T(8,128)(2,1)S(1)} collective-permute-done((bf16[32,4096]{1,0:T(8,128)(2,1)S(1)}, bf16[32,4096]{1,0:T(8,128)(2,1)S(1)}, u32[]{:S(2)}, u32[]{:S(2)}) %collective-permute-start.6) | collective-permute-done | bytes 262176 | tf_op jit(solution)/shard_map/ppermute | solution.py:25
  74.4 0.1 fusion.6
  74.5 2.9 %collective-permute-start.10 = (bf16[32,4096]{1,0:T(8,128)(2,1)S(1)}, bf16[32,4096]{1,0:T(8,128)(2,1)S(1)}, u32[]{:S(2)}, u32[]{:S(2)}) collective-permute-start(bf16[32,4096]{1,0:T(8,128)(2,1)S(1)} %get-tuple-element.16), channel_id=1, source_target_pairs={{0,7},{1,0},{2,1},{3,2},{4,3},{5,4},{6,5},{7,6},{8,15},{9,8},{10,9... | collective-permute-start | bytes 786440 | tf_op jit(solution)/shard_map/ppermute | solution.py:25
  77.4 2.9 %collective-permute-start.7 = (bf16[32,4096]{1,0:T(8,128)(2,1)S(1)}, bf16[32,4096]{1,0:T(8,128)(2,1)S(1)}, u32[]{:S(2)}, u32[]{:S(2)}) collective-permute-start(bf16[32,4096]{1,0:T(8,128)(2,1)S(1)} %get-tuple-element.15), channel_id=1, source_target_pairs={{0,1},{1,2},{2,3},{3,4},{4,5},{5,6},{6,7},{7,0},{8,9},{9,10},{10,1... | collective-permute-start | bytes 786440 | tf_op jit(solution)/shard_map/ppermute | solution.py:25
  80.4 4.0 %collective-permute-done.10 = bf16[32,4096]{1,0:T(8,128)(2,1)S(1)} collective-permute-done((bf16[32,4096]{1,0:T(8,128)(2,1)S(1)}, bf16[32,4096]{1,0:T(8,128)(2,1)S(1)}, u32[]{:S(2)}, u32[]{:S(2)}) %collective-permute-start.10) | collective-permute-done | bytes 262176 | tf_op jit(solution)/shard_map/ppermute | solution.py:25
  84.4 3.7 %collective-permute-done.7 = bf16[32,4096]{1,0:T(8,128)(2,1)S(1)} collective-permute-done((bf16[32,4096]{1,0:T(8,128)(2,1)S(1)}, bf16[32,4096]{1,0:T(8,128)(2,1)S(1)}, u32[]{:S(2)}, u32[]{:S(2)}) %collective-permute-start.7) | collective-permute-done | bytes 262176 | tf_op jit(solution)/shard_map/ppermute | solution.py:25
  88.1 0.1 fusion.5
  88.2 1.9 %collective-permute-start.11 = (bf16[32,4096]{1,0:T(8,128)(2,1)S(1)}, bf16[32,4096]{1,0:T(8,128)(2,1)S(1)}, u32[]{:S(2)}, u32[]{:S(2)}) collective-permute-start(bf16[32,4096]{1,0:T(8,128)(2,1)S(1)} %get-tuple-element.14), channel_id=1, source_target_pairs={{0,7},{1,0},{2,1},{3,2},{4,3},{5,4},{6,5},{7,6},{8,15},{9,8},{10,9... | collective-permute-start | bytes 786440 | tf_op jit(solution)/shard_map/ppermute | solution.py:25
  90.2 3.9 %collective-permute-start.8 = (bf16[32,4096]{1,0:T(8,128)(2,1)S(1)}, bf16[32,4096]{1,0:T(8,128)(2,1)S(1)}, u32[]{:S(2)}, u32[]{:S(2)}) collective-permute-start(bf16[32,4096]{1,0:T(8,128)(2,1)S(1)} %get-tuple-element.13), channel_id=1, source_target_pairs={{0,1},{1,2},{2,3},{3,4},{4,5},{5,6},{6,7},{7,0},{8,9},{9,10},{10,1... | collective-permute-start | bytes 786440 | tf_op jit(solution)/shard_map/ppermute | solution.py:25
  94.1 2.7 %collective-permute-done.11 = bf16[32,4096]{1,0:T(8,128)(2,1)S(1)} collective-permute-done((bf16[32,4096]{1,0:T(8,128)(2,1)S(1)}, bf16[32,4096]{1,0:T(8,128)(2,1)S(1)}, u32[]{:S(2)}, u32[]{:S(2)}) %collective-permute-start.11) | collective-permute-done | bytes 262176 | tf_op jit(solution)/shard_map/ppermute | solution.py:25
  96.8 3.1 %collective-permute-done.8 = bf16[32,4096]{1,0:T(8,128)(2,1)S(1)} collective-permute-done((bf16[32,4096]{1,0:T(8,128)(2,1)S(1)}, bf16[32,4096]{1,0:T(8,128)(2,1)S(1)}, u32[]{:S(2)}, u32[]{:S(2)}) %collective-permute-start.8) | collective-permute-done | bytes 262176 | tf_op jit(solution)/shard_map/ppermute | solution.py:25
  99.9 0.3 fusion
  100.2 0.8 fusion.2
  (19 shorter events, 0.1 us)
Async XLA Ops:
  0.6 3.3 %copy-start.11 = (s32[8]{0:T(128)S(1)}, s32[8]{0:T(128)}, u32[]{:S(2)}) copy-start(s32[8]{0:T(128)} %lens_ref.1) | copy-start | bytes 100
  0.6 3.3 %copy-start.3 = (bf16[256,256]{1,0:T(8,128)(2,1)S(1)}, bf16[256,256]{1,0:T(8,128)(2,1)}, u32[]{:S(2)}) copy-start(bf16[256,256]{1,0:T(8,128)(2,1)} %q_ref.3) | copy-start | bytes 393220
  0.7 11.4 %copy-start.10 = (s32[8,32]{1,0:T(8,128)S(1)}, s32[8,32]{1,0:T(8,128)}, u32[]{:S(2)}) copy-start(s32[8,32]{1,0:T(8,128)} %param.13) | copy-start | bytes 3076
  2.0 32.6 %collective-permute-start = (bf16[8,256,256]{2,1,0:T(8,128)(2,1)S(1)}, bf16[8,256,256]{2,1,0:T(8,128)(2,1)S(1)}, u32[]{:S(2)}, u32[]{:S(2)}) collective-permute-start(bf16[8,256,256]{2,1,0:T(8,128)(2,1)S(1)} %slice_bitcast_fusion), channel_id=1, source_target_pairs={{0,504},{8,0},{16,8},{24,16},{32,24},{40,32},{48,40},{56,48},{64,5... | collective-permute-start | bytes 3145736 | tf_op jit(solution)/shard_map/ppermute | solution.py:25
  4.0 12.6 %collective-permute-start.1 = (bf16[272,256]{1,0:T(8,128)(2,1)S(1)}, bf16[272,256]{1,0:T(8,128)(2,1)S(1)}, u32[]{:S(2)}, u32[]{:S(2)}) collective-permute-start(bf16[272,256]{1,0:T(8,128)(2,1)S(1)} %pad_maximum_fusion), channel_id=1, source_target_pairs={{0,16},{8,24},{16,32},{24,40},{32,48},{40,56},{48,64},{56,72},{64,... | collective-permute-start | bytes 417800 | tf_op jit(solution)/shard_map/ppermute | solution.py:25
  7.5 15.6 %collective-permute-start.3 = (bf16[272,256]{1,0:T(8,128)(2,1)S(1)}, bf16[272,256]{1,0:T(8,128)(2,1)S(1)}, u32[]{:S(2)}, u32[]{:S(2)}) collective-permute-start(bf16[272,256]{1,0:T(8,128)(2,1)S(1)} %pad_maximum_fusion), channel_id=1, source_target_pairs={{0,24},{8,32},{16,40},{24,48},{32,56},{40,64},{48,72},{56,80},{64,... | collective-permute-start | bytes 417800 | tf_op jit(solution)/shard_map/ppermute | solution.py:25
  16.6 0.7 copy-start.8
  20.5 20.8 %collective-permute-start.2 = (bf16[256,384]{1,0:T(8,128)(2,1)}, bf16[256,384]{1,0:T(8,128)(2,1)S(1)}, u32[]{:S(2)}, u32[]{:S(2)}) collective-permute-start(bf16[256,384]{1,0:T(8,128)(2,1)} %shard_map.114), channel_id=1, source_target_pairs={{0,496},{8,504},{16,0},{24,8},{32,16},{40,24},{48,32},{56,40},{64,... | collective-permute-start | bytes 589832 | tf_op jit(solution)/shard_map/ppermute | solution.py:25
  23.1 0.7 copy-start.7
  27.0 14.3 %collective-permute-start.4 = (bf16[256,384]{1,0:T(8,128)(2,1)}, bf16[256,384]{1,0:T(8,128)(2,1)S(1)}, u32[]{:S(2)}, u32[]{:S(2)}) collective-permute-start(bf16[256,384]{1,0:T(8,128)(2,1)} %shard_map.115), channel_id=1, source_target_pairs={{0,488},{8,496},{16,504},{24,0},{32,8},{40,16},{48,24},{56,32},{64... | collective-permute-start | bytes 589832 | tf_op jit(solution)/shard_map/ppermute | solution.py:25
  34.6 1.0 %copy-start.5 = (bf16[8,256,256]{2,1,0:T(8,128)(2,1)}, bf16[8,256,256]{2,1,0:T(8,128)(2,1)S(1)}, u32[]{:S(2)}) copy-start(bf16[8,256,256]{2,1,0:T(8,128)(2,1)S(1)} %collective-permute-done.rest_0_) | copy-start | bytes 3145732
  41.3 1.6 %copy-start = (bf16[256,4096]{1,0:T(8,128)(2,1)S(1)}, bf16[256,4096]{1,0:T(8,128)(2,1)}, u32[]{:S(2)}) copy-start(bf16[256,4096]{1,0:T(8,128)(2,1)} %rest_2_.1) | copy-start | bytes 6291460
  42.9 0.9 copy-start.1
  43.8 0.9 copy-start.2
  46.5 53.5 %copy-start.6 = (bf16[32,4096]{1,0:T(8,128)(2,1)S(1)}, bf16[32,4096]{1,0:T(8,128)(2,1)}, u32[]{:S(2)}) copy-start(bf16[32,4096]{1,0:T(8,128)(2,1)} %param.15) | copy-start | bytes 786436
  46.5 15.0 %collective-permute-start.5 = (bf16[32,4096]{1,0:T(8,128)(2,1)S(1)}, bf16[32,4096]{1,0:T(8,128)(2,1)}, u32[]{:S(2)}, u32[]{:S(2)}) collective-permute-start(bf16[32,4096]{1,0:T(8,128)(2,1)S(1)} %get-tuple-element.17), channel_id=1, source_target_pairs={{0,1},{1,2},{2,3},{3,4},{4,5},{5,6},{6,7},{7,0},{8,9},{9,10},{10,1... | collective-permute-start | bytes 786440 | tf_op jit(solution)/shard_map/ppermute | solution.py:25
  48.6 15.9 %collective-permute-start.9 = (bf16[32,4096]{1,0:T(8,128)(2,1)S(1)}, bf16[32,4096]{1,0:T(8,128)(2,1)S(1)}, u32[]{:S(2)}, u32[]{:S(2)}) collective-permute-start(bf16[32,4096]{1,0:T(8,128)(2,1)S(1)} %get-tuple-element.18), channel_id=1, source_target_pairs={{0,7},{1,0},{2,1},{3,2},{4,3},{5,4},{6,5},{7,6},{8,15},{9,8},{10,9... | collective-permute-start | bytes 786440 | tf_op jit(solution)/shard_map/ppermute | solution.py:25
  62.4 11.9 %collective-permute-start.6 = (bf16[32,4096]{1,0:T(8,128)(2,1)S(1)}, bf16[32,4096]{1,0:T(8,128)(2,1)S(1)}, u32[]{:S(2)}, u32[]{:S(2)}) collective-permute-start(bf16[32,4096]{1,0:T(8,128)(2,1)S(1)} %fusion.7), channel_id=1, source_target_pairs={{0,1},{1,2},{2,3},{3,4},{4,5},{5,6},{6,7},{7,0},{8,9},{9,10},{10,1... | collective-permute-start | bytes 786440 | tf_op jit(solution)/shard_map/ppermute | solution.py:25
  64.4 35.8 %copy-start.9 = (f32[4096]{0:T(1024)S(1)}, f32[4096]{0:T(1024)}, u32[]{:S(2)}) copy-start(f32[4096]{0:T(1024)} %param.17) | copy-start | bytes 49156
  74.5 9.9 %collective-permute-start.10 = (bf16[32,4096]{1,0:T(8,128)(2,1)S(1)}, bf16[32,4096]{1,0:T(8,128)(2,1)S(1)}, u32[]{:S(2)}, u32[]{:S(2)}) collective-permute-start(bf16[32,4096]{1,0:T(8,128)(2,1)S(1)} %get-tuple-element.16), channel_id=1, source_target_pairs={{0,7},{1,0},{2,1},{3,2},{4,3},{5,4},{6,5},{7,6},{8,15},{9,8},{10,9... | collective-permute-start | bytes 786440 | tf_op jit(solution)/shard_map/ppermute | solution.py:25
  77.4 10.7 %collective-permute-start.7 = (bf16[32,4096]{1,0:T(8,128)(2,1)S(1)}, bf16[32,4096]{1,0:T(8,128)(2,1)S(1)}, u32[]{:S(2)}, u32[]{:S(2)}) collective-permute-start(bf16[32,4096]{1,0:T(8,128)(2,1)S(1)} %get-tuple-element.15), channel_id=1, source_target_pairs={{0,1},{1,2},{2,3},{3,4},{4,5},{5,6},{6,7},{7,0},{8,9},{9,10},{10,1... | collective-permute-start | bytes 786440 | tf_op jit(solution)/shard_map/ppermute | solution.py:25
  88.2 8.6 %collective-permute-start.11 = (bf16[32,4096]{1,0:T(8,128)(2,1)S(1)}, bf16[32,4096]{1,0:T(8,128)(2,1)S(1)}, u32[]{:S(2)}, u32[]{:S(2)}) collective-permute-start(bf16[32,4096]{1,0:T(8,128)(2,1)S(1)} %get-tuple-element.14), channel_id=1, source_target_pairs={{0,7},{1,0},{2,1},{3,2},{4,3},{5,4},{6,5},{7,6},{8,15},{9,8},{10,9... | collective-permute-start | bytes 786440 | tf_op jit(solution)/shard_map/ppermute | solution.py:25
  90.2 9.8 %collective-permute-start.8 = (bf16[32,4096]{1,0:T(8,128)(2,1)S(1)}, bf16[32,4096]{1,0:T(8,128)(2,1)S(1)}, u32[]{:S(2)}, u32[]{:S(2)}) collective-permute-start(bf16[32,4096]{1,0:T(8,128)(2,1)S(1)} %get-tuple-element.13), channel_id=1, source_target_pairs={{0,1},{1,2},{2,3},{3,4},{4,5},{5,6},{6,7},{7,0},{8,9},{9,10},{10,1... | collective-permute-start | bytes 786440 | tf_op jit(solution)/shard_map/ppermute | solution.py:25
  100.2 0.9 copy-start.4

commit v13 on v12

--- a/solution.py
+++ b/solution.py
@@ -118,24 +118,36 @@
     pages = rest[: len(page_ids) - 1]
     sum_ref, stat_ref = rest[-2:]
     req_count, page_size = kv_ref.shape[0], kv_ref.shape[1]
+    page_refs = (kv_ref,) + tuple(pages)
+    joined = page_ids == tuple(range(len(page_ids)))
+    pair = 2 if (joined and req_count % 2 == 0) else 1
+    span = page_size * len(page_refs)
+    q_rows = pair * group * TREE
     stat_lanes = lax.broadcasted_iota(jnp.int32, (TREE, STAT_LANES), 1)
-    for r in range(req_count):
-        row0 = r * TREE
-        query = stacked_heads(q_ref, row0, group)
-        length = lens_ref[r]
-        tree_stats = tree_ref[row0 : row0 + TREE, group * HD : group * HD + STAT_LANES]
-        blocks = [(
-            jnp.concatenate([lane_pick(tree_stats, g) for g in range(group)], axis=0),
-            jnp.concatenate([lane_pick(tree_stats, group + g) for g in range(group)], axis=0),
-            stacked_heads(tree_ref, row0, group),
-        )]
-        page_refs = (kv_ref,) + tuple(pages)
-        if page_ids == tuple(range(len(page_ids))):
-            keys = jnp.concatenate([ref[r, :, 0:HD] for ref in page_refs], axis=0)
-            values = jnp.concatenate([ref[r, :, HD : 2 * HD] for ref in page_refs], axis=0)
-            positions = lax.broadcasted_iota(jnp.int32, (1, page_size * len(page_refs)), 1)
-            blocks.append(attend(query, keys, values, positions < length, False))
+    row_owner = lax.broadcasted_iota(jnp.int32, (q_rows, 1), 0) // (group * TREE)
+    for r0 in range(0, req_count, pair):
+        members = list(range(r0, r0 + pair))
+        query = jnp.concatenate([stacked_heads(q_ref, r * TREE, group) for r in members], axis=0)
+        tree_rows = []
+        for r in members:
+            tree_rows.append(tree_ref[r * TREE : (r + 1) * TREE, group * HD : group * HD + STAT_LANES])
+        m1 = jnp.concatenate([lane_pick(t, g) for t in tree_rows for g in range(group)], axis=0)
+        l1 = jnp.concatenate([lane_pick(t, group + g) for t in tree_rows for g in range(group)], axis=0)
+        a1 = jnp.concatenate([stacked_heads(tree_ref, r * TREE, group) for r in members], axis=0)
+        blocks = [(m1, l1, a1)]
+        if joined:
+            length = jnp.zeros((q_rows, 1), jnp.int32)
+            for k, r in enumerate(members):
+                length = jnp.where(row_owner == k, lens_ref[r], length)
+            sub = lax.broadcasted_iota(jnp.int32, (q_rows, pair * span), 0)
+            lane = lax.broadcasted_iota(jnp.int32, (q_rows, pair * span), 1)
+            valid = ((sub // (group * TREE)) == (lane // span)) & ((lane % span) < length)
+            keys = jnp.concatenate([ref[r, :, 0:HD] for r in members for ref in page_refs], axis=0)
+            values = jnp.concatenate([ref[r, :, HD : 2 * HD] for r in members for ref in page_refs], axis=0)
+            blocks.append(attend(query, keys, values, valid, False))
         else:
+            r = r0
+            length = lens_ref[r]
             for page_index, page_ref in zip(page_ids, page_refs):
                 positions = lax.broadcasted_iota(jnp.int32, (1, page_size), 1) + page_index * page_size
                 blocks.append(attend(query, page_ref[r, :, 0:HD], page_ref[r, :, HD : 2 * HD],
@@ -149,13 +161,15 @@
             factor = jnp.exp(largest - top)
             totals = totals + factor * part_totals
             weighted = weighted + factor * part_weighted
-        stats = jnp.zeros((TREE, STAT_LANES), jnp.float32)
-        for g in range(group):
-            rows = slice(g * TREE, (g + 1) * TREE)
-            sum_ref[row0 : row0 + TREE, g * HD : (g + 1) * HD] = weighted[rows]
-            stats = jnp.where(stat_lanes == g, top[rows], stats)
-            stats = jnp.where(stat_lanes == group + g, totals[rows], stats)
-        stat_ref[row0 : row0 + TREE, :] = stats
+        for k, r in enumerate(members):
+            row0 = r * TREE
+            stats = jnp.zeros((TREE, STAT_LANES), jnp.float32)
+            for g in range(group):
+                part = slice((k * group + g) * TREE, (k * group + g + 1) * TREE)
+                sum_ref[row0 : row0 + TREE, g * HD : (g + 1) * HD] = weighted[part]
+                stats = jnp.where(stat_lanes == g, top[part], stats)
+                stats = jnp.where(stat_lanes == group + g, totals[part], stats)
+            stat_ref[row0 : row0 + TREE, :] = stats
 
 
 def local_partial(cache_lens, queries, kv_pool, tree_part, shipped, group):

time: 102 us -> 102 us (level)
  transfers between devices with their start and end apart: 12 -> 12, of which waited for: 6 -> 7; matrix products, arithmetic and copies ran while one was open for 2% -> 2% of each run, Pallas kernels for 16% -> 15%
where the time goes in v13:
time: 102 us; the launch traced here: 101 us
  starting transfers between devices  44.2 us (43%)
  waiting for transfers between devices  28.5 us (28%)
  Pallas kernels  16.9 us (17%)
  local copies, waits for them, and re-layouts  7.98 us (8%)
  other arithmetic  2.48 us (2%)
  between operations  1.06 us (1%)
    ppermute x12, starting transfers between devices, shifted(): return lax.ppermute(value, axis, pairs)  44.2 us
    ppermute x12, waiting for transfers between devices, shifted(): return lax.ppermute(value, axis, pairs)  28.5 us
    pallas_call x2, Pallas kernels, holder_partial(): pl.pallas_call(functools.partial(holder_kernel, page_index, group), out_s...  6.38 us
    unnamed x24, local copies, waits for them, and re-layouts  5.79 us
    pallas_call x1, Pallas kernels, local_partial(): pl.pallas_call(functools.partial(local_kernel, group, page_ids), out_shap...  5.15 us
    pallas_call x1, Pallas kernels, tree_partial(): pl.pallas_call(functools.partial(tree_kernel, group), out_shape=(jax.Shap...  3.71 us
  transfers between devices with their start and end apart: 12, of which 7 were waited for; matrix products, arithmetic and copies ran while one was open for 2% of the time, Pallas kernels for 15%

profile of v13, /device:TPU:16, one launch (start us, length us, event | category | flops | bytes accessed | tf_op | source)
XLA Modules:
  0.0 101.1 jit_solution(4102094610747119523)
XLA Ops:
  0.6 0.0 copy-start.11
  0.6 0.0 copy-start.3
  0.7 1.3 %slice_bitcast_fusion = bf16[8,256,256]{2,1,0:T(8,128)(2,1)S(1)} fusion(bf16[8,4,256,256]{3,2,1,0:T(8,128)(2,1)} %kv_ref.5), kind=kLoop, calls=%fused_computation | loop fusion | bytes 2097152 | tf_op jit(solution)/shard_map/squeeze | solution.py:365
  2.0 1.9 %collective-permute-start = (bf16[8,256,256]{2,1,0:T(8,128)(2,1)S(1)}, bf16[8,256,256]{2,1,0:T(8,128)(2,1)S(1)}, u32[]{:S(2)}, u32[]{:S(2)}) collective-permute-start(bf16[8,256,256]{2,1,0:T(8,128)(2,1)S(1)} %slice_bitcast_fusion), channel_id=1, source_target_pairs={{0,504},{8,0},{16,8},{24,16},{32,24},{40,32},{48,40},{56,48},{64,5... | collective-permute-start | bytes 3145736 | tf_op jit(solution)/shard_map/ppermute | solution.py:25
  4.0 3.5 %collective-permute-start.1 = (bf16[272,256]{1,0:T(8,128)(2,1)S(1)}, bf16[272,256]{1,0:T(8,128)(2,1)S(1)}, u32[]{:S(2)}, u32[]{:S(2)}) collective-permute-start(bf16[272,256]{1,0:T(8,128)(2,1)S(1)} %pad_maximum_fusion), channel_id=1, source_target_pairs={{0,16},{8,24},{16,32},{24,40},{32,48},{40,56},{48,64},{56,72},{64,... | collective-permute-start | bytes 417800 | tf_op jit(solution)/shard_map/ppermute | solution.py:25
  7.5 4.5 %collective-permute-start.3 = (bf16[272,256]{1,0:T(8,128)(2,1)S(1)}, bf16[272,256]{1,0:T(8,128)(2,1)S(1)}, u32[]{:S(2)}, u32[]{:S(2)}) collective-permute-start(bf16[272,256]{1,0:T(8,128)(2,1)S(1)} %pad_maximum_fusion), channel_id=1, source_target_pairs={{0,24},{8,32},{16,40},{24,48},{32,56},{40,64},{48,72},{56,80},{64,... | collective-permute-start | bytes 417800 | tf_op jit(solution)/shard_map/ppermute | solution.py:25
  12.1 0.1 broadcast_add_fusion
  12.1 0.8 reshape.46.parent_ref
  12.9 3.7 %shard_map.112 = (f32[256,384]{1,0:T(8,128)}, bf16[8,8,256]{2,1,0:T(8,128)(2,1)}) custom-call(s32[8]{0:T(128)} %acc_ref.1, bf16[256,256]{1,0:T(8,128)(2,1)} %q_ref.3, bf16[256,256]{1,0:T(8,128)(2,1)} %fresh_ref.1, s32[256,1]{1,0:T(8,128)} %reshape.46.parent_ref), custom_call_target="tpu_custom_call" | custom-call | tf_op jit(solution)/shard_map/pallas_call | solution.py:102
  16.6 0.0 collective-permute-done.1.q_ref
  16.6 0.7 copy-done.8
  17.3 3.2 %shard_map.114 = bf16[256,384]{1,0:T(8,128)(2,1)} custom-call(bf16[272,256]{1,0:T(8,128)(2,1)} %copy-done.8, bf16[8,4,256,256]{3,2,1,0:T(8,128)(2,1)} %kv_ref.5, f32[256,384]{1,0:T(8,128)} %get-tuple-element.7.tree_ref.order_ref), custom_call_target="tpu_custom_call" | custom-call | tf_op jit(solution)/shard_map/pallas_call | solution.py:243
  20.5 2.6 %collective-permute-start.2 = (bf16[256,384]{1,0:T(8,128)(2,1)}, bf16[256,384]{1,0:T(8,128)(2,1)S(1)}, u32[]{:S(2)}, u32[]{:S(2)}) collective-permute-start(bf16[256,384]{1,0:T(8,128)(2,1)} %shard_map.114), channel_id=1, source_target_pairs={{0,496},{8,504},{16,0},{24,8},{32,16},{40,24},{48,32},{56,40},{64,... | collective-permute-start | bytes 589832 | tf_op jit(solution)/shard_map/ppermute | solution.py:25
  23.1 0.0 collective-permute-done.3.q_ref
  23.1 0.0 copy-start.7
  23.1 0.6 copy-done.7
  23.8 3.2 %shard_map.115 = bf16[256,384]{1,0:T(8,128)(2,1)} custom-call(bf16[272,256]{1,0:T(8,128)(2,1)} %copy-done.7, bf16[8,4,256,256]{3,2,1,0:T(8,128)(2,1)} %kv_ref.5, f32[256,384]{1,0:T(8,128)} %get-tuple-element.7.tree_ref.order_ref), custom_call_target="tpu_custom_call" | custom-call | tf_op jit(solution)/shard_map/pallas_call | solution.py:243
  27.0 7.6 %collective-permute-start.4 = (bf16[256,384]{1,0:T(8,128)(2,1)}, bf16[256,384]{1,0:T(8,128)(2,1)S(1)}, u32[]{:S(2)}, u32[]{:S(2)}) collective-permute-start(bf16[256,384]{1,0:T(8,128)(2,1)} %shard_map.115), channel_id=1, source_target_pairs={{0,488},{8,496},{16,504},{24,0},{32,8},{40,16},{48,24},{56,32},{64... | collective-permute-start | bytes 589832 | tf_op jit(solution)/shard_map/ppermute | solution.py:25
  34.6 0.0 collective-permute-done.rest_0_
  34.6 1.0 copy-done.5
  35.6 5.2 %shard_map.113 = (f32[256,256]{1,0:T(8,128)}, f32[256,128]{1,0:T(8,128)}) custom-call(s32[8]{0:T(128)} %lens_ref.1, bf16[256,256]{1,0:T(8,128)(2,1)} %q_ref.3, bf16[8,4,256,256]{3,2,1,0:T(8,128)(2,1)} %kv_ref.5, f32[256,384]{1,0:T(8,128)} %get-tuple-element.7.tree_ref.order_ref, bf16[8,256,256]{2,1,0:T(8,128)(2,1)} %copy-done.5), custom_call_target="tpu_custom_call" | custom-call | tf_op jit(solution)/shard_map/pallas_call | solution.py:180
  40.8 0.0 collective-permute-done.2.rest_0_
  40.8 0.5 collective-permute-done.4.rest_1_
  41.2 1.6 %copy-done = bf16[256,4096]{1,0:T(8,128)(2,1)S(1)} copy-done((bf16[256,4096]{1,0:T(8,128)(2,1)S(1)}, bf16[256,4096]{1,0:T(8,128)(2,1)}, u32[]{:S(2)}) %copy-start) | copy-done | bytes 2097176
  42.8 0.9 copy-done.1
  43.8 0.9 copy-done.2
  44.7 1.7 %shard_map.116 = bf16[256,4096]{1,0:T(8,128)(2,1)S(1)} custom-call(f32[256,256]{1,0:T(8,128)S(1)} %copy-done.1, f32[256,128]{1,0:T(8,128)S(1)} %copy-done.2, bf16[256,384]{1,0:T(8,128)(2,1)S(1)} %collective-permute-done.2.rest_0_, bf16[256,384]{1,0:T(8,128)(2,1)S(1)} %collective-permute-done.4.rest_1_, bf16[256,4096]{1,0:T(8,128)(2,1)S(1)} %copy-done), custom_call_target="tpu_custom_call" | custom-call | tf_op jit(solution)/shard_map/pallas_call | solution.py:303
  46.4 0.0 copy-start.6
  46.4 2.1 %collective-permute-start.5 = (bf16[32,4096]{1,0:T(8,128)(2,1)S(1)}, bf16[32,4096]{1,0:T(8,128)(2,1)}, u32[]{:S(2)}, u32[]{:S(2)}) collective-permute-start(bf16[32,4096]{1,0:T(8,128)(2,1)S(1)} %get-tuple-element.17), channel_id=1, source_target_pairs={{0,1},{1,2},{2,3},{3,4},{4,5},{5,6},{6,7},{7,0},{8,9},{9,10},{10,1... | collective-permute-start | bytes 786440 | tf_op jit(solution)/shard_map/ppermute | solution.py:25
  48.5 8.4 %collective-permute-start.9 = (bf16[32,4096]{1,0:T(8,128)(2,1)S(1)}, bf16[32,4096]{1,0:T(8,128)(2,1)S(1)}, u32[]{:S(2)}, u32[]{:S(2)}) collective-permute-start(bf16[32,4096]{1,0:T(8,128)(2,1)S(1)} %get-tuple-element.18), channel_id=1, source_target_pairs={{0,7},{1,0},{2,1},{3,2},{4,3},{5,4},{6,5},{7,6},{8,15},{9,8},{10,9... | collective-permute-start | bytes 786440 | tf_op jit(solution)/shard_map/ppermute | solution.py:25
  56.9 4.5 %collective-permute-done.5 = bf16[32,4096]{1,0:T(8,128)(2,1)} collective-permute-done((bf16[32,4096]{1,0:T(8,128)(2,1)S(1)}, bf16[32,4096]{1,0:T(8,128)(2,1)}, u32[]{:S(2)}, u32[]{:S(2)}) %collective-permute-start.5) | collective-permute-done | bytes 262176 | tf_op jit(solution)/shard_map/ppermute | solution.py:25
  61.4 1.0 %fusion.7 = bf16[32,4096]{1,0:T(8,128)(2,1)S(1)} fusion(bf16[32,4096]{1,0:T(8,128)(2,1)} %collective-permute-done.5, bf16[8,32,4096]{2,1,0:T(8,128)(2,1)S(1)} %bitcast.33, s32[]{:T(128)S(6)} %select_n.78), kind=kLoop, calls=%fused_computation.15 | loop fusion | flops 524288 | bytes 786436 | tf_op jit(solution)/shard_map/convert_element_type | solution.py:341
  62.4 1.9 %collective-permute-start.6 = (bf16[32,4096]{1,0:T(8,128)(2,1)S(1)}, bf16[32,4096]{1,0:T(8,128)(2,1)S(1)}, u32[]{:S(2)}, u32[]{:S(2)}) collective-permute-start(bf16[32,4096]{1,0:T(8,128)(2,1)S(1)} %fusion.7), channel_id=1, source_target_pairs={{0,1},{1,2},{2,3},{3,4},{4,5},{5,6},{6,7},{7,0},{8,9},{9,10},{10,1... | collective-permute-start | bytes 786440 | tf_op jit(solution)/shard_map/ppermute | solution.py:25
  64.4 0.0 copy-start.9
  64.4 0.0 collective-permute-done.9
  64.4 9.9 %collective-permute-done.6 = bf16[32,4096]{1,0:T(8,128)(2,1)S(1)} collective-permute-done((bf16[32,4096]{1,0:T(8,128)(2,1)S(1)}, bf16[32,4096]{1,0:T(8,128)(2,1)S(1)}, u32[]{:S(2)}, u32[]{:S(2)}) %collective-permute-start.6) | collective-permute-done | bytes 262176 | tf_op jit(solution)/shard_map/ppermute | solution.py:25
  74.4 0.1 fusion.6
  74.5 2.9 %collective-permute-start.10 = (bf16[32,4096]{1,0:T(8,128)(2,1)S(1)}, bf16[32,4096]{1,0:T(8,128)(2,1)S(1)}, u32[]{:S(2)}, u32[]{:S(2)}) collective-permute-start(bf16[32,4096]{1,0:T(8,128)(2,1)S(1)} %get-tuple-element.16), channel_id=1, source_target_pairs={{0,7},{1,0},{2,1},{3,2},{4,3},{5,4},{6,5},{7,6},{8,15},{9,8},{10,9... | collective-permute-start | bytes 786440 | tf_op jit(solution)/shard_map/ppermute | solution.py:25
  77.4 2.9 %collective-permute-start.7 = (bf16[32,4096]{1,0:T(8,128)(2,1)S(1)}, bf16[32,4096]{1,0:T(8,128)(2,1)S(1)}, u32[]{:S(2)}, u32[]{:S(2)}) collective-permute-start(bf16[32,4096]{1,0:T(8,128)(2,1)S(1)} %get-tuple-element.15), channel_id=1, source_target_pairs={{0,1},{1,2},{2,3},{3,4},{4,5},{5,6},{6,7},{7,0},{8,9},{9,10},{10,1... | collective-permute-start | bytes 786440 | tf_op jit(solution)/shard_map/ppermute | solution.py:25
  80.4 4.0 %collective-permute-done.10 = bf16[32,4096]{1,0:T(8,128)(2,1)S(1)} collective-permute-done((bf16[32,4096]{1,0:T(8,128)(2,1)S(1)}, bf16[32,4096]{1,0:T(8,128)(2,1)S(1)}, u32[]{:S(2)}, u32[]{:S(2)}) %collective-permute-start.10) | collective-permute-done | bytes 262176 | tf_op jit(solution)/shard_map/ppermute | solution.py:25
  84.4 3.7 %collective-permute-done.7 = bf16[32,4096]{1,0:T(8,128)(2,1)S(1)} collective-permute-done((bf16[32,4096]{1,0:T(8,128)(2,1)S(1)}, bf16[32,4096]{1,0:T(8,128)(2,1)S(1)}, u32[]{:S(2)}, u32[]{:S(2)}) %collective-permute-start.7) | collective-permute-done | bytes 262176 | tf_op jit(solution)/shard_map/ppermute | solution.py:25
  88.1 0.1 fusion.5
  88.2 1.9 %collective-permute-start.11 = (bf16[32,4096]{1,0:T(8,128)(2,1)S(1)}, bf16[32,4096]{1,0:T(8,128)(2,1)S(1)}, u32[]{:S(2)}, u32[]{:S(2)}) collective-permute-start(bf16[32,4096]{1,0:T(8,128)(2,1)S(1)} %get-tuple-element.14), channel_id=1, source_target_pairs={{0,7},{1,0},{2,1},{3,2},{4,3},{5,4},{6,5},{7,6},{8,15},{9,8},{10,9... | collective-permute-start | bytes 786440 | tf_op jit(solution)/shard_map/ppermute | solution.py:25
  90.2 3.9 %collective-permute-start.8 = (bf16[32,4096]{1,0:T(8,128)(2,1)S(1)}, bf16[32,4096]{1,0:T(8,128)(2,1)S(1)}, u32[]{:S(2)}, u32[]{:S(2)}) collective-permute-start(bf16[32,4096]{1,0:T(8,128)(2,1)S(1)} %get-tuple-element.13), channel_id=1, source_target_pairs={{0,1},{1,2},{2,3},{3,4},{4,5},{5,6},{6,7},{7,0},{8,9},{9,10},{10,1... | collective-permute-start | bytes 786440 | tf_op jit(solution)/shard_map/ppermute | solution.py:25
  94.1 2.7 %collective-permute-done.11 = bf16[32,4096]{1,0:T(8,128)(2,1)S(1)} collective-permute-done((bf16[32,4096]{1,0:T(8,128)(2,1)S(1)}, bf16[32,4096]{1,0:T(8,128)(2,1)S(1)}, u32[]{:S(2)}, u32[]{:S(2)}) %collective-permute-start.11) | collective-permute-done | bytes 262176 | tf_op jit(solution)/shard_map/ppermute | solution.py:25
  96.8 3.1 %collective-permute-done.8 = bf16[32,4096]{1,0:T(8,128)(2,1)S(1)} collective-permute-done((bf16[32,4096]{1,0:T(8,128)(2,1)S(1)}, bf16[32,4096]{1,0:T(8,128)(2,1)S(1)}, u32[]{:S(2)}, u32[]{:S(2)}) %collective-permute-start.8) | collective-permute-done | bytes 262176 | tf_op jit(solution)/shard_map/ppermute | solution.py:25
  99.9 0.3 fusion
  100.2 0.8 fusion.2
  (19 shorter events, 0.1 us)
Async XLA Ops:
  0.6 3.3 %copy-start.11 = (s32[8]{0:T(128)S(1)}, s32[8]{0:T(128)}, u32[]{:S(2)}) copy-start(s32[8]{0:T(128)} %lens_ref.1) | copy-start | bytes 100
  0.6 3.3 %copy-start.3 = (bf16[256,256]{1,0:T(8,128)(2,1)S(1)}, bf16[256,256]{1,0:T(8,128)(2,1)}, u32[]{:S(2)}) copy-start(bf16[256,256]{1,0:T(8,128)(2,1)} %q_ref.3) | copy-start | bytes 393220
  0.7 11.4 %copy-start.10 = (s32[8,32]{1,0:T(8,128)S(1)}, s32[8,32]{1,0:T(8,128)}, u32[]{:S(2)}) copy-start(s32[8,32]{1,0:T(8,128)} %param.13) | copy-start | bytes 3076
  2.0 32.6 %collective-permute-start = (bf16[8,256,256]{2,1,0:T(8,128)(2,1)S(1)}, bf16[8,256,256]{2,1,0:T(8,128)(2,1)S(1)}, u32[]{:S(2)}, u32[]{:S(2)}) collective-permute-start(bf16[8,256,256]{2,1,0:T(8,128)(2,1)S(1)} %slice_bitcast_fusion), channel_id=1, source_target_pairs={{0,504},{8,0},{16,8},{24,16},{32,24},{40,32},{48,40},{56,48},{64,5... | collective-permute-start | bytes 3145736 | tf_op jit(solution)/shard_map/ppermute | solution.py:25
  4.0 12.6 %collective-permute-start.1 = (bf16[272,256]{1,0:T(8,128)(2,1)S(1)}, bf16[272,256]{1,0:T(8,128)(2,1)S(1)}, u32[]{:S(2)}, u32[]{:S(2)}) collective-permute-start(bf16[272,256]{1,0:T(8,128)(2,1)S(1)} %pad_maximum_fusion), channel_id=1, source_target_pairs={{0,16},{8,24},{16,32},{24,40},{32,48},{40,56},{48,64},{56,72},{64,... | collective-permute-start | bytes 417800 | tf_op jit(solution)/shard_map/ppermute | solution.py:25
  7.5 15.6 %collective-permute-start.3 = (bf16[272,256]{1,0:T(8,128)(2,1)S(1)}, bf16[272,256]{1,0:T(8,128)(2,1)S(1)}, u32[]{:S(2)}, u32[]{:S(2)}) collective-permute-start(bf16[272,256]{1,0:T(8,128)(2,1)S(1)} %pad_maximum_fusion), channel_id=1, source_target_pairs={{0,24},{8,32},{16,40},{24,48},{32,56},{40,64},{48,72},{56,80},{64,... | collective-permute-start | bytes 417800 | tf_op jit(solution)/shard_map/ppermute | solution.py:25
  16.6 0.7 copy-start.8
  20.5 20.3 %collective-permute-start.2 = (bf16[256,384]{1,0:T(8,128)(2,1)}, bf16[256,384]{1,0:T(8,128)(2,1)S(1)}, u32[]{:S(2)}, u32[]{:S(2)}) collective-permute-start(bf16[256,384]{1,0:T(8,128)(2,1)} %shard_map.114), channel_id=1, source_target_pairs={{0,496},{8,504},{16,0},{24,8},{32,16},{40,24},{48,32},{56,40},{64,... | collective-permute-start | bytes 589832 | tf_op jit(solution)/shard_map/ppermute | solution.py:25
  23.1 0.7 copy-start.7
  27.0 14.3 %collective-permute-start.4 = (bf16[256,384]{1,0:T(8,128)(2,1)}, bf16[256,384]{1,0:T(8,128)(2,1)S(1)}, u32[]{:S(2)}, u32[]{:S(2)}) collective-permute-start(bf16[256,384]{1,0:T(8,128)(2,1)} %shard_map.115), channel_id=1, source_target_pairs={{0,488},{8,496},{16,504},{24,0},{32,8},{40,16},{48,24},{56,32},{64... | collective-permute-start | bytes 589832 | tf_op jit(solution)/shard_map/ppermute | solution.py:25
  34.6 1.0 %copy-start.5 = (bf16[8,256,256]{2,1,0:T(8,128)(2,1)}, bf16[8,256,256]{2,1,0:T(8,128)(2,1)S(1)}, u32[]{:S(2)}) copy-start(bf16[8,256,256]{2,1,0:T(8,128)(2,1)S(1)} %collective-permute-done.rest_0_) | copy-start | bytes 3145732
  41.2 1.6 %copy-start = (bf16[256,4096]{1,0:T(8,128)(2,1)S(1)}, bf16[256,4096]{1,0:T(8,128)(2,1)}, u32[]{:S(2)}) copy-start(bf16[256,4096]{1,0:T(8,128)(2,1)} %rest_2_.1) | copy-start | bytes 6291460
  42.8 0.9 copy-start.1
  43.8 0.9 copy-start.2
  46.4 53.5 %copy-start.6 = (bf16[32,4096]{1,0:T(8,128)(2,1)S(1)}, bf16[32,4096]{1,0:T(8,128)(2,1)}, u32[]{:S(2)}) copy-start(bf16[32,4096]{1,0:T(8,128)(2,1)} %param.15) | copy-start | bytes 786436
  46.4 15.0 %collective-permute-start.5 = (bf16[32,4096]{1,0:T(8,128)(2,1)S(1)}, bf16[32,4096]{1,0:T(8,128)(2,1)}, u32[]{:S(2)}, u32[]{:S(2)}) collective-permute-start(bf16[32,4096]{1,0:T(8,128)(2,1)S(1)} %get-tuple-element.17), channel_id=1, source_target_pairs={{0,1},{1,2},{2,3},{3,4},{4,5},{5,6},{6,7},{7,0},{8,9},{9,10},{10,1... | collective-permute-start | bytes 786440 | tf_op jit(solution)/shard_map/ppermute | solution.py:25
  48.5 15.9 %collective-permute-start.9 = (bf16[32,4096]{1,0:T(8,128)(2,1)S(1)}, bf16[32,4096]{1,0:T(8,128)(2,1)S(1)}, u32[]{:S(2)}, u32[]{:S(2)}) collective-permute-start(bf16[32,4096]{1,0:T(8,128)(2,1)S(1)} %get-tuple-element.18), channel_id=1, source_target_pairs={{0,7},{1,0},{2,1},{3,2},{4,3},{5,4},{6,5},{7,6},{8,15},{9,8},{10,9... | collective-permute-start | bytes 786440 | tf_op jit(solution)/shard_map/ppermute | solution.py:25
  62.4 11.9 %collective-permute-start.6 = (bf16[32,4096]{1,0:T(8,128)(2,1)S(1)}, bf16[32,4096]{1,0:T(8,128)(2,1)S(1)}, u32[]{:S(2)}, u32[]{:S(2)}) collective-permute-start(bf16[32,4096]{1,0:T(8,128)(2,1)S(1)} %fusion.7), channel_id=1, source_target_pairs={{0,1},{1,2},{2,3},{3,4},{4,5},{5,6},{6,7},{7,0},{8,9},{9,10},{10,1... | collective-permute-start | bytes 786440 | tf_op jit(solution)/shard_map/ppermute | solution.py:25
  64.4 35.8 %copy-start.9 = (f32[4096]{0:T(1024)S(1)}, f32[4096]{0:T(1024)}, u32[]{:S(2)}) copy-start(f32[4096]{0:T(1024)} %param.17) | copy-start | bytes 49156
  74.5 9.9 %collective-permute-start.10 = (bf16[32,4096]{1,0:T(8,128)(2,1)S(1)}, bf16[32,4096]{1,0:T(8,128)(2,1)S(1)}, u32[]{:S(2)}, u32[]{:S(2)}) collective-permute-start(bf16[32,4096]{1,0:T(8,128)(2,1)S(1)} %get-tuple-element.16), channel_id=1, source_target_pairs={{0,7},{1,0},{2,1},{3,2},{4,3},{5,4},{6,5},{7,6},{8,15},{9,8},{10,9... | collective-permute-start | bytes 786440 | tf_op jit(solution)/shard_map/ppermute | solution.py:25
  77.4 10.7 %collective-permute-start.7 = (bf16[32,4096]{1,0:T(8,128)(2,1)S(1)}, bf16[32,4096]{1,0:T(8,128)(2,1)S(1)}, u32[]{:S(2)}, u32[]{:S(2)}) collective-permute-start(bf16[32,4096]{1,0:T(8,128)(2,1)S(1)} %get-tuple-element.15), channel_id=1, source_target_pairs={{0,1},{1,2},{2,3},{3,4},{4,5},{5,6},{6,7},{7,0},{8,9},{9,10},{10,1... | collective-permute-start | bytes 786440 | tf_op jit(solution)/shard_map/ppermute | solution.py:25
  88.2 8.6 %collective-permute-start.11 = (bf16[32,4096]{1,0:T(8,128)(2,1)S(1)}, bf16[32,4096]{1,0:T(8,128)(2,1)S(1)}, u32[]{:S(2)}, u32[]{:S(2)}) collective-permute-start(bf16[32,4096]{1,0:T(8,128)(2,1)S(1)} %get-tuple-element.14), channel_id=1, source_target_pairs={{0,7},{1,0},{2,1},{3,2},{4,3},{5,4},{6,5},{7,6},{8,15},{9,8},{10,9... | collective-permute-start | bytes 786440 | tf_op jit(solution)/shard_map/ppermute | solution.py:25
  90.2 9.8 %collective-permute-start.8 = (bf16[32,4096]{1,0:T(8,128)(2,1)S(1)}, bf16[32,4096]{1,0:T(8,128)(2,1)S(1)}, u32[]{:S(2)}, u32[]{:S(2)}) collective-permute-start(bf16[32,4096]{1,0:T(8,128)(2,1)S(1)} %get-tuple-element.13), channel_id=1, source_target_pairs={{0,1},{1,2},{2,3},{3,4},{4,5},{5,6},{6,7},{7,0},{8,9},{9,10},{10,1... | collective-permute-start | bytes 786440 | tf_op jit(solution)/shard_map/ppermute | solution.py:25
  100.2 0.9 copy-start.4

commit v14 on v13

--- a/solution.py
+++ b/solution.py
@@ -204,7 +204,7 @@
     rows = req_count * TREE
     extra = q_ref[rows : rows + EXTRA, :].astype(jnp.float32)
     length_row = extra[0:1, :] * 16.0 + extra[1:2, :]
-    pair = 2 if req_count % 2 == 0 else 1
+    pair = 4 if req_count % 4 == 0 else 1
     q_rows = pair * group * TREE
     sub = lax.broadcasted_iota(jnp.int32, (q_rows, pair * page_size), 0)
     lane = lax.broadcasted_iota(jnp.int32, (q_rows, pair * page_size), 1)

time: 102 us -> 102 us (level)
  no operation moved by 1% of the time
where the time goes in v14:
time: 102 us; the launch traced here: 101 us
  starting transfers between devices  44.2 us (43%)
  waiting for transfers between devices  28.5 us (28%)
  Pallas kernels  16.7 us (16%)
  local copies, waits for them, and re-layouts  7.98 us (8%)
  other arithmetic  2.48 us (2%)
  between operations  1.06 us (1%)
    ppermute x12, starting transfers between devices, shifted(): return lax.ppermute(value, axis, pairs)  44.2 us
    ppermute x12, waiting for transfers between devices, shifted(): return lax.ppermute(value, axis, pairs)  28.5 us
    pallas_call x2, Pallas kernels, holder_partial(): pl.pallas_call(functools.partial(holder_kernel, page_index, group), out_s...  6.14 us
    unnamed x24, local copies, waits for them, and re-layouts  5.79 us
    pallas_call x1, Pallas kernels, local_partial(): pl.pallas_call(functools.partial(local_kernel, group, page_ids), out_shap...  5.16 us
    pallas_call x1, Pallas kernels, tree_partial(): pl.pallas_call(functools.partial(tree_kernel, group), out_shape=(jax.Shap...  3.71 us
  transfers between devices with their start and end apart: 12, of which 7 were waited for; matrix products, arithmetic and copies ran while one was open for 2% of the time, Pallas kernels for 15%

profile of v14, /device:TPU:16, one launch (start us, length us, event | category | flops | bytes accessed | tf_op | source)
XLA Modules:
  0.0 100.8 jit_solution(6399081243426969229)
XLA Ops:
  0.6 0.0 copy-start.11
  0.6 0.0 copy-start.3
  0.7 1.3 %slice_bitcast_fusion = bf16[8,256,256]{2,1,0:T(8,128)(2,1)S(1)} fusion(bf16[8,4,256,256]{3,2,1,0:T(8,128)(2,1)} %kv_ref.5), kind=kLoop, calls=%fused_computation | loop fusion | bytes 2097152 | tf_op jit(solution)/shard_map/squeeze | solution.py:365
  2.0 1.9 %collective-permute-start = (bf16[8,256,256]{2,1,0:T(8,128)(2,1)S(1)}, bf16[8,256,256]{2,1,0:T(8,128)(2,1)S(1)}, u32[]{:S(2)}, u32[]{:S(2)}) collective-permute-start(bf16[8,256,256]{2,1,0:T(8,128)(2,1)S(1)} %slice_bitcast_fusion), channel_id=1, source_target_pairs={{0,504},{8,0},{16,8},{24,16},{32,24},{40,32},{48,40},{56,48},{64,5... | collective-permute-start | bytes 3145736 | tf_op jit(solution)/shard_map/ppermute | solution.py:25
  4.0 3.5 %collective-permute-start.1 = (bf16[272,256]{1,0:T(8,128)(2,1)S(1)}, bf16[272,256]{1,0:T(8,128)(2,1)S(1)}, u32[]{:S(2)}, u32[]{:S(2)}) collective-permute-start(bf16[272,256]{1,0:T(8,128)(2,1)S(1)} %pad_maximum_fusion), channel_id=1, source_target_pairs={{0,16},{8,24},{16,32},{24,40},{32,48},{40,56},{48,64},{56,72},{64,... | collective-permute-start | bytes 417800 | tf_op jit(solution)/shard_map/ppermute | solution.py:25
  7.5 4.5 %collective-permute-start.3 = (bf16[272,256]{1,0:T(8,128)(2,1)S(1)}, bf16[272,256]{1,0:T(8,128)(2,1)S(1)}, u32[]{:S(2)}, u32[]{:S(2)}) collective-permute-start(bf16[272,256]{1,0:T(8,128)(2,1)S(1)} %pad_maximum_fusion), channel_id=1, source_target_pairs={{0,24},{8,32},{16,40},{24,48},{32,56},{40,64},{48,72},{56,80},{64,... | collective-permute-start | bytes 417800 | tf_op jit(solution)/shard_map/ppermute | solution.py:25
  12.1 0.1 broadcast_add_fusion
  12.1 0.8 reshape.46.parent_ref
  12.9 3.7 %shard_map.112 = (f32[256,384]{1,0:T(8,128)}, bf16[8,8,256]{2,1,0:T(8,128)(2,1)}) custom-call(s32[8]{0:T(128)} %acc_ref.1, bf16[256,256]{1,0:T(8,128)(2,1)} %q_ref.3, bf16[256,256]{1,0:T(8,128)(2,1)} %fresh_ref.1, s32[256,1]{1,0:T(8,128)} %reshape.46.parent_ref), custom_call_target="tpu_custom_call" | custom-call | tf_op jit(solution)/shard_map/pallas_call | solution.py:102
  16.6 0.0 collective-permute-done.1.q_ref
  16.6 0.7 copy-done.8
  17.3 3.1 %shard_map.114 = bf16[256,384]{1,0:T(8,128)(2,1)} custom-call(bf16[272,256]{1,0:T(8,128)(2,1)} %copy-done.8, bf16[8,4,256,256]{3,2,1,0:T(8,128)(2,1)} %kv_ref.5, f32[256,384]{1,0:T(8,128)} %get-tuple-element.7.tree_ref.order_ref), custom_call_target="tpu_custom_call" | custom-call | tf_op jit(solution)/shard_map/pallas_call | solution.py:243
  20.4 2.6 %collective-permute-start.2 = (bf16[256,384]{1,0:T(8,128)(2,1)}, bf16[256,384]{1,0:T(8,128)(2,1)S(1)}, u32[]{:S(2)}, u32[]{:S(2)}) collective-permute-start(bf16[256,384]{1,0:T(8,128)(2,1)} %shard_map.114), channel_id=1, source_target_pairs={{0,496},{8,504},{16,0},{24,8},{32,16},{40,24},{48,32},{56,40},{64,... | collective-permute-start | bytes 589832 | tf_op jit(solution)/shard_map/ppermute | solution.py:25
  23.0 0.0 collective-permute-done.3.q_ref
  23.0 0.0 copy-start.7
  23.0 0.6 copy-done.7
  23.7 3.1 %shard_map.115 = bf16[256,384]{1,0:T(8,128)(2,1)} custom-call(bf16[272,256]{1,0:T(8,128)(2,1)} %copy-done.7, bf16[8,4,256,256]{3,2,1,0:T(8,128)(2,1)} %kv_ref.5, f32[256,384]{1,0:T(8,128)} %get-tuple-element.7.tree_ref.order_ref), custom_call_target="tpu_custom_call" | custom-call | tf_op jit(solution)/shard_map/pallas_call | solution.py:243
  26.7 7.6 %collective-permute-start.4 = (bf16[256,384]{1,0:T(8,128)(2,1)}, bf16[256,384]{1,0:T(8,128)(2,1)S(1)}, u32[]{:S(2)}, u32[]{:S(2)}) collective-permute-start(bf16[256,384]{1,0:T(8,128)(2,1)} %shard_map.115), channel_id=1, source_target_pairs={{0,488},{8,496},{16,504},{24,0},{32,8},{40,16},{48,24},{56,32},{64... | collective-permute-start | bytes 589832 | tf_op jit(solution)/shard_map/ppermute | solution.py:25
  34.4 0.0 collective-permute-done.rest_0_
  34.4 1.0 copy-done.5
  35.4 5.2 %shard_map.113 = (f32[256,256]{1,0:T(8,128)}, f32[256,128]{1,0:T(8,128)}) custom-call(s32[8]{0:T(128)} %lens_ref.1, bf16[256,256]{1,0:T(8,128)(2,1)} %q_ref.3, bf16[8,4,256,256]{3,2,1,0:T(8,128)(2,1)} %kv_ref.5, f32[256,384]{1,0:T(8,128)} %get-tuple-element.7.tree_ref.order_ref, bf16[8,256,256]{2,1,0:T(8,128)(2,1)} %copy-done.5), custom_call_target="tpu_custom_call" | custom-call | tf_op jit(solution)/shard_map/pallas_call | solution.py:180
  40.5 0.0 collective-permute-done.2.rest_0_
  40.6 0.4 collective-permute-done.4.rest_1_
  41.0 1.6 %copy-done = bf16[256,4096]{1,0:T(8,128)(2,1)S(1)} copy-done((bf16[256,4096]{1,0:T(8,128)(2,1)S(1)}, bf16[256,4096]{1,0:T(8,128)(2,1)}, u32[]{:S(2)}) %copy-start) | copy-done | bytes 2097176
  42.6 0.9 copy-done.1
  43.5 0.9 copy-done.2
  44.4 1.7 %shard_map.116 = bf16[256,4096]{1,0:T(8,128)(2,1)S(1)} custom-call(f32[256,256]{1,0:T(8,128)S(1)} %copy-done.1, f32[256,128]{1,0:T(8,128)S(1)} %copy-done.2, bf16[256,384]{1,0:T(8,128)(2,1)S(1)} %collective-permute-done.2.rest_0_, bf16[256,384]{1,0:T(8,128)(2,1)S(1)} %collective-permute-done.4.rest_1_, bf16[256,4096]{1,0:T(8,128)(2,1)S(1)} %copy-done), custom_call_target="tpu_custom_call" | custom-call | tf_op jit(solution)/shard_map/pallas_call | solution.py:303
  46.2 0.0 copy-start.6
  46.2 2.1 %collective-permute-start.5 = (bf16[32,4096]{1,0:T(8,128)(2,1)S(1)}, bf16[32,4096]{1,0:T(8,128)(2,1)}, u32[]{:S(2)}, u32[]{:S(2)}) collective-permute-start(bf16[32,4096]{1,0:T(8,128)(2,1)S(1)} %get-tuple-element.17), channel_id=1, source_target_pairs={{0,1},{1,2},{2,3},{3,4},{4,5},{5,6},{6,7},{7,0},{8,9},{9,10},{10,1... | collective-permute-start | bytes 786440 | tf_op jit(solution)/shard_map/ppermute | solution.py:25
  48.3 8.4 %collective-permute-start.9 = (bf16[32,4096]{1,0:T(8,128)(2,1)S(1)}, bf16[32,4096]{1,0:T(8,128)(2,1)S(1)}, u32[]{:S(2)}, u32[]{:S(2)}) collective-permute-start(bf16[32,4096]{1,0:T(8,128)(2,1)S(1)} %get-tuple-element.18), channel_id=1, source_target_pairs={{0,7},{1,0},{2,1},{3,2},{4,3},{5,4},{6,5},{7,6},{8,15},{9,8},{10,9... | collective-permute-start | bytes 786440 | tf_op jit(solution)/shard_map/ppermute | solution.py:25
  56.7 4.5 %collective-permute-done.5 = bf16[32,4096]{1,0:T(8,128)(2,1)} collective-permute-done((bf16[32,4096]{1,0:T(8,128)(2,1)S(1)}, bf16[32,4096]{1,0:T(8,128)(2,1)}, u32[]{:S(2)}, u32[]{:S(2)}) %collective-permute-start.5) | collective-permute-done | bytes 262176 | tf_op jit(solution)/shard_map/ppermute | solution.py:25
  61.2 1.0 %fusion.7 = bf16[32,4096]{1,0:T(8,128)(2,1)S(1)} fusion(bf16[32,4096]{1,0:T(8,128)(2,1)} %collective-permute-done.5, bf16[8,32,4096]{2,1,0:T(8,128)(2,1)S(1)} %bitcast.33, s32[]{:T(128)S(6)} %select_n.78), kind=kLoop, calls=%fused_computation.15 | loop fusion | flops 524288 | bytes 786436 | tf_op jit(solution)/shard_map/convert_element_type | solution.py:341
  62.2 1.9 %collective-permute-start.6 = (bf16[32,4096]{1,0:T(8,128)(2,1)S(1)}, bf16[32,4096]{1,0:T(8,128)(2,1)S(1)}, u32[]{:S(2)}, u32[]{:S(2)}) collective-permute-start(bf16[32,4096]{1,0:T(8,128)(2,1)S(1)} %fusion.7), channel_id=1, source_target_pairs={{0,1},{1,2},{2,3},{3,4},{4,5},{5,6},{6,7},{7,0},{8,9},{9,10},{10,1... | collective-permute-start | bytes 786440 | tf_op jit(solution)/shard_map/ppermute | solution.py:25
  64.2 0.0 copy-start.9
  64.2 0.0 collective-permute-done.9
  64.2 9.9 %collective-permute-done.6 = bf16[32,4096]{1,0:T(8,128)(2,1)S(1)} collective-permute-done((bf16[32,4096]{1,0:T(8,128)(2,1)S(1)}, bf16[32,4096]{1,0:T(8,128)(2,1)S(1)}, u32[]{:S(2)}, u32[]{:S(2)}) %collective-permute-start.6) | collective-permute-done | bytes 262176 | tf_op jit(solution)/shard_map/ppermute | solution.py:25
  74.1 0.1 fusion.6
  74.2 2.9 %collective-permute-start.10 = (bf16[32,4096]{1,0:T(8,128)(2,1)S(1)}, bf16[32,4096]{1,0:T(8,128)(2,1)S(1)}, u32[]{:S(2)}, u32[]{:S(2)}) collective-permute-start(bf16[32,4096]{1,0:T(8,128)(2,1)S(1)} %get-tuple-element.16), channel_id=1, source_target_pairs={{0,7},{1,0},{2,1},{3,2},{4,3},{5,4},{6,5},{7,6},{8,15},{9,8},{10,9... | collective-permute-start | bytes 786440 | tf_op jit(solution)/shard_map/ppermute | solution.py:25
  77.2 2.9 %collective-permute-start.7 = (bf16[32,4096]{1,0:T(8,128)(2,1)S(1)}, bf16[32,4096]{1,0:T(8,128)(2,1)S(1)}, u32[]{:S(2)}, u32[]{:S(2)}) collective-permute-start(bf16[32,4096]{1,0:T(8,128)(2,1)S(1)} %get-tuple-element.15), channel_id=1, source_target_pairs={{0,1},{1,2},{2,3},{3,4},{4,5},{5,6},{6,7},{7,0},{8,9},{9,10},{10,1... | collective-permute-start | bytes 786440 | tf_op jit(solution)/shard_map/ppermute | solution.py:25
  80.1 4.0 %collective-permute-done.10 = bf16[32,4096]{1,0:T(8,128)(2,1)S(1)} collective-permute-done((bf16[32,4096]{1,0:T(8,128)(2,1)S(1)}, bf16[32,4096]{1,0:T(8,128)(2,1)S(1)}, u32[]{:S(2)}, u32[]{:S(2)}) %collective-permute-start.10) | collective-permute-done | bytes 262176 | tf_op jit(solution)/shard_map/ppermute | solution.py:25
  84.2 3.7 %collective-permute-done.7 = bf16[32,4096]{1,0:T(8,128)(2,1)S(1)} collective-permute-done((bf16[32,4096]{1,0:T(8,128)(2,1)S(1)}, bf16[32,4096]{1,0:T(8,128)(2,1)S(1)}, u32[]{:S(2)}, u32[]{:S(2)}) %collective-permute-start.7) | collective-permute-done | bytes 262176 | tf_op jit(solution)/shard_map/ppermute | solution.py:25
  87.9 0.1 fusion.5
  88.0 1.9 %collective-permute-start.11 = (bf16[32,4096]{1,0:T(8,128)(2,1)S(1)}, bf16[32,4096]{1,0:T(8,128)(2,1)S(1)}, u32[]{:S(2)}, u32[]{:S(2)}) collective-permute-start(bf16[32,4096]{1,0:T(8,128)(2,1)S(1)} %get-tuple-element.14), channel_id=1, source_target_pairs={{0,7},{1,0},{2,1},{3,2},{4,3},{5,4},{6,5},{7,6},{8,15},{9,8},{10,9... | collective-permute-start | bytes 786440 | tf_op jit(solution)/shard_map/ppermute | solution.py:25
  89.9 3.9 %collective-permute-start.8 = (bf16[32,4096]{1,0:T(8,128)(2,1)S(1)}, bf16[32,4096]{1,0:T(8,128)(2,1)S(1)}, u32[]{:S(2)}, u32[]{:S(2)}) collective-permute-start(bf16[32,4096]{1,0:T(8,128)(2,1)S(1)} %get-tuple-element.13), channel_id=1, source_target_pairs={{0,1},{1,2},{2,3},{3,4},{4,5},{5,6},{6,7},{7,0},{8,9},{9,10},{10,1... | collective-permute-start | bytes 786440 | tf_op jit(solution)/shard_map/ppermute | solution.py:25
  93.9 2.7 %collective-permute-done.11 = bf16[32,4096]{1,0:T(8,128)(2,1)S(1)} collective-permute-done((bf16[32,4096]{1,0:T(8,128)(2,1)S(1)}, bf16[32,4096]{1,0:T(8,128)(2,1)S(1)}, u32[]{:S(2)}, u32[]{:S(2)}) %collective-permute-start.11) | collective-permute-done | bytes 262176 | tf_op jit(solution)/shard_map/ppermute | solution.py:25
  96.6 3.1 %collective-permute-done.8 = bf16[32,4096]{1,0:T(8,128)(2,1)S(1)} collective-permute-done((bf16[32,4096]{1,0:T(8,128)(2,1)S(1)}, bf16[32,4096]{1,0:T(8,128)(2,1)S(1)}, u32[]{:S(2)}, u32[]{:S(2)}) %collective-permute-start.8) | collective-permute-done | bytes 262176 | tf_op jit(solution)/shard_map/ppermute | solution.py:25
  99.7 0.3 fusion
  100.0 0.8 fusion.2
  (19 shorter events, 0.1 us)
Async XLA Ops:
  0.6 3.3 %copy-start.11 = (s32[8]{0:T(128)S(1)}, s32[8]{0:T(128)}, u32[]{:S(2)}) copy-start(s32[8]{0:T(128)} %lens_ref.1) | copy-start | bytes 100
  0.6 3.3 %copy-start.3 = (bf16[256,256]{1,0:T(8,128)(2,1)S(1)}, bf16[256,256]{1,0:T(8,128)(2,1)}, u32[]{:S(2)}) copy-start(bf16[256,256]{1,0:T(8,128)(2,1)} %q_ref.3) | copy-start | bytes 393220
  0.7 11.4 %copy-start.10 = (s32[8,32]{1,0:T(8,128)S(1)}, s32[8,32]{1,0:T(8,128)}, u32[]{:S(2)}) copy-start(s32[8,32]{1,0:T(8,128)} %param.13) | copy-start | bytes 3076
  2.0 32.4 %collective-permute-start = (bf16[8,256,256]{2,1,0:T(8,128)(2,1)S(1)}, bf16[8,256,256]{2,1,0:T(8,128)(2,1)S(1)}, u32[]{:S(2)}, u32[]{:S(2)}) collective-permute-start(bf16[8,256,256]{2,1,0:T(8,128)(2,1)S(1)} %slice_bitcast_fusion), channel_id=1, source_target_pairs={{0,504},{8,0},{16,8},{24,16},{32,24},{40,32},{48,40},{56,48},{64,5... | collective-permute-start | bytes 3145736 | tf_op jit(solution)/shard_map/ppermute | solution.py:25
  4.0 12.6 %collective-permute-start.1 = (bf16[272,256]{1,0:T(8,128)(2,1)S(1)}, bf16[272,256]{1,0:T(8,128)(2,1)S(1)}, u32[]{:S(2)}, u32[]{:S(2)}) collective-permute-start(bf16[272,256]{1,0:T(8,128)(2,1)S(1)} %pad_maximum_fusion), channel_id=1, source_target_pairs={{0,16},{8,24},{16,32},{24,40},{32,48},{40,56},{48,64},{56,72},{64,... | collective-permute-start | bytes 417800 | tf_op jit(solution)/shard_map/ppermute | solution.py:25
  7.5 15.5 %collective-permute-start.3 = (bf16[272,256]{1,0:T(8,128)(2,1)S(1)}, bf16[272,256]{1,0:T(8,128)(2,1)S(1)}, u32[]{:S(2)}, u32[]{:S(2)}) collective-permute-start(bf16[272,256]{1,0:T(8,128)(2,1)S(1)} %pad_maximum_fusion), channel_id=1, source_target_pairs={{0,24},{8,32},{16,40},{24,48},{32,56},{40,64},{48,72},{56,80},{64,... | collective-permute-start | bytes 417800 | tf_op jit(solution)/shard_map/ppermute | solution.py:25
  16.6 0.7 copy-start.8
  20.4 20.2 %collective-permute-start.2 = (bf16[256,384]{1,0:T(8,128)(2,1)}, bf16[256,384]{1,0:T(8,128)(2,1)S(1)}, u32[]{:S(2)}, u32[]{:S(2)}) collective-permute-start(bf16[256,384]{1,0:T(8,128)(2,1)} %shard_map.114), channel_id=1, source_target_pairs={{0,496},{8,504},{16,0},{24,8},{32,16},{40,24},{48,32},{56,40},{64,... | collective-permute-start | bytes 589832 | tf_op jit(solution)/shard_map/ppermute | solution.py:25
  23.0 0.7 copy-start.7
  26.7 14.3 %collective-permute-start.4 = (bf16[256,384]{1,0:T(8,128)(2,1)}, bf16[256,384]{1,0:T(8,128)(2,1)S(1)}, u32[]{:S(2)}, u32[]{:S(2)}) collective-permute-start(bf16[256,384]{1,0:T(8,128)(2,1)} %shard_map.115), channel_id=1, source_target_pairs={{0,488},{8,496},{16,504},{24,0},{32,8},{40,16},{48,24},{56,32},{64... | collective-permute-start | bytes 589832 | tf_op jit(solution)/shard_map/ppermute | solution.py:25
  34.4 1.0 %copy-start.5 = (bf16[8,256,256]{2,1,0:T(8,128)(2,1)}, bf16[8,256,256]{2,1,0:T(8,128)(2,1)S(1)}, u32[]{:S(2)}) copy-start(bf16[8,256,256]{2,1,0:T(8,128)(2,1)S(1)} %collective-permute-done.rest_0_) | copy-start | bytes 3145732
  41.0 1.6 %copy-start = (bf16[256,4096]{1,0:T(8,128)(2,1)S(1)}, bf16[256,4096]{1,0:T(8,128)(2,1)}, u32[]{:S(2)}) copy-start(bf16[256,4096]{1,0:T(8,128)(2,1)} %rest_2_.1) | copy-start | bytes 6291460
  42.6 0.9 copy-start.1
  43.5 0.9 copy-start.2
  46.2 53.5 %copy-start.6 = (bf16[32,4096]{1,0:T(8,128)(2,1)S(1)}, bf16[32,4096]{1,0:T(8,128)(2,1)}, u32[]{:S(2)}) copy-start(bf16[32,4096]{1,0:T(8,128)(2,1)} %param.15) | copy-start | bytes 786436
  46.2 15.0 %collective-permute-start.5 = (bf16[32,4096]{1,0:T(8,128)(2,1)S(1)}, bf16[32,4096]{1,0:T(8,128)(2,1)}, u32[]{:S(2)}, u32[]{:S(2)}) collective-permute-start(bf16[32,4096]{1,0:T(8,128)(2,1)S(1)} %get-tuple-element.17), channel_id=1, source_target_pairs={{0,1},{1,2},{2,3},{3,4},{4,5},{5,6},{6,7},{7,0},{8,9},{9,10},{10,1... | collective-permute-start | bytes 786440 | tf_op jit(solution)/shard_map/ppermute | solution.py:25
  48.3 15.9 %collective-permute-start.9 = (bf16[32,4096]{1,0:T(8,128)(2,1)S(1)}, bf16[32,4096]{1,0:T(8,128)(2,1)S(1)}, u32[]{:S(2)}, u32[]{:S(2)}) collective-permute-start(bf16[32,4096]{1,0:T(8,128)(2,1)S(1)} %get-tuple-element.18), channel_id=1, source_target_pairs={{0,7},{1,0},{2,1},{3,2},{4,3},{5,4},{6,5},{7,6},{8,15},{9,8},{10,9... | collective-permute-start | bytes 786440 | tf_op jit(solution)/shard_map/ppermute | solution.py:25
  62.2 11.9 %collective-permute-start.6 = (bf16[32,4096]{1,0:T(8,128)(2,1)S(1)}, bf16[32,4096]{1,0:T(8,128)(2,1)S(1)}, u32[]{:S(2)}, u32[]{:S(2)}) collective-permute-start(bf16[32,4096]{1,0:T(8,128)(2,1)S(1)} %fusion.7), channel_id=1, source_target_pairs={{0,1},{1,2},{2,3},{3,4},{4,5},{5,6},{6,7},{7,0},{8,9},{9,10},{10,1... | collective-permute-start | bytes 786440 | tf_op jit(solution)/shard_map/ppermute | solution.py:25
  64.2 35.8 %copy-start.9 = (f32[4096]{0:T(1024)S(1)}, f32[4096]{0:T(1024)}, u32[]{:S(2)}) copy-start(f32[4096]{0:T(1024)} %param.17) | copy-start | bytes 49156
  74.2 9.9 %collective-permute-start.10 = (bf16[32,4096]{1,0:T(8,128)(2,1)S(1)}, bf16[32,4096]{1,0:T(8,128)(2,1)S(1)}, u32[]{:S(2)}, u32[]{:S(2)}) collective-permute-start(bf16[32,4096]{1,0:T(8,128)(2,1)S(1)} %get-tuple-element.16), channel_id=1, source_target_pairs={{0,7},{1,0},{2,1},{3,2},{4,3},{5,4},{6,5},{7,6},{8,15},{9,8},{10,9... | collective-permute-start | bytes 786440 | tf_op jit(solution)/shard_map/ppermute | solution.py:25
  77.2 10.7 %collective-permute-start.7 = (bf16[32,4096]{1,0:T(8,128)(2,1)S(1)}, bf16[32,4096]{1,0:T(8,128)(2,1)S(1)}, u32[]{:S(2)}, u32[]{:S(2)}) collective-permute-start(bf16[32,4096]{1,0:T(8,128)(2,1)S(1)} %get-tuple-element.15), channel_id=1, source_target_pairs={{0,1},{1,2},{2,3},{3,4},{4,5},{5,6},{6,7},{7,0},{8,9},{9,10},{10,1... | collective-permute-start | bytes 786440 | tf_op jit(solution)/shard_map/ppermute | solution.py:25
  88.0 8.6 %collective-permute-start.11 = (bf16[32,4096]{1,0:T(8,128)(2,1)S(1)}, bf16[32,4096]{1,0:T(8,128)(2,1)S(1)}, u32[]{:S(2)}, u32[]{:S(2)}) collective-permute-start(bf16[32,4096]{1,0:T(8,128)(2,1)S(1)} %get-tuple-element.14), channel_id=1, source_target_pairs={{0,7},{1,0},{2,1},{3,2},{4,3},{5,4},{6,5},{7,6},{8,15},{9,8},{10,9... | collective-permute-start | bytes 786440 | tf_op jit(solution)/shard_map/ppermute | solution.py:25
  89.9 9.8 %collective-permute-start.8 = (bf16[32,4096]{1,0:T(8,128)(2,1)S(1)}, bf16[32,4096]{1,0:T(8,128)(2,1)S(1)}, u32[]{:S(2)}, u32[]{:S(2)}) collective-permute-start(bf16[32,4096]{1,0:T(8,128)(2,1)S(1)} %get-tuple-element.13), channel_id=1, source_target_pairs={{0,1},{1,2},{2,3},{3,4},{4,5},{5,6},{6,7},{7,0},{8,9},{9,10},{10,1... | collective-permute-start | bytes 786440 | tf_op jit(solution)/shard_map/ppermute | solution.py:25
  100.0 0.9 copy-start.4

commit v15 on v13

--- a/solution.py
+++ b/solution.py
@@ -325,8 +325,11 @@
     chunk = product.shape[0] // count
     pieces = product.reshape(count, chunk, product.shape[1])
 
+    doubled = jnp.concatenate([pieces, pieces], axis=0)
+    rotated = lax.dynamic_slice_in_dim(doubled, me, count, 0)
+
     def piece(offset):
-        return lax.dynamic_index_in_dim(pieces, (me + offset) % count, 0, keepdims=False)
+        return rotated[offset % count]
 
     forward_hops = count // 2
     backward_hops = count - 1 - forward_hops

time: 102 us -> 106 us (1.039)
  the two profiles are of different devices: /device:TPU:16 before, /device:TPU:6 now
where the time goes in v15:
time: 106 us; the launch traced here: 105 us
  waiting for transfers between devices  39.9 us (38%)
  starting transfers between devices  38 us (36%)
  Pallas kernels  17.1 us (16%)
  local copies, waits for them, and re-layouts  6.35 us (6%)
  other arithmetic  2.32 us (2%)
    ppermute x12, waiting for transfers between devices, shifted(): return lax.ppermute(value, axis, pairs)  39.9 us
    ppermute x12, starting transfers between devices, shifted(): return lax.ppermute(value, axis, pairs)  38 us
    pallas_call x2, Pallas kernels, holder_partial(): pl.pallas_call(functools.partial(holder_kernel, page_index, group), out_s...  6.39 us
    pallas_call x1, Pallas kernels, local_partial(): pl.pallas_call(functools.partial(local_kernel, group, page_ids), out_shap...  5.26 us
    pallas_call x1, Pallas kernels, tree_partial(): pl.pallas_call(functools.partial(tree_kernel, group), out_shape=(jax.Shap...  3.71 us
    unnamed x22, local copies, waits for them, and re-layouts  3.2 us
    squeeze x1, local copies, waits for them, and re-layouts, per_device(): shipped = [(p, shifted(kv_pool[:, p], 'req', -p)) for p in SHIPPED_PAGES]  2.32 us
  transfers between devices with their start and end apart: 12, of which 7 were waited for; matrix products, arithmetic and copies ran while one was open for 1% of the time, Pallas kernels for 15%

profile of v15, /device:TPU:6, one launch (start us, length us, event | category | flops | bytes accessed | tf_op | source)
XLA Modules:
  0.0 104.5 jit_solution(14264450349663827865)
XLA Ops:
  0.6 0.0 copy-start.10
  0.6 0.0 copy-start.3
  0.7 2.3 %slice_bitcast_fusion = bf16[8,256,256]{2,1,0:T(8,128)(2,1)} fusion(bf16[8,4,256,256]{3,2,1,0:T(8,128)(2,1)} %kv_ref.5), kind=kLoop, calls=%fused_computation.3 | loop fusion | bytes 2097152 | tf_op jit(solution)/shard_map/squeeze | solution.py:368
  3.0 5.1 %collective-permute-start = (bf16[8,256,256]{2,1,0:T(8,128)(2,1)}, bf16[8,256,256]{2,1,0:T(8,128)(2,1)}, u32[]{:S(2)}, u32[]{:S(2)}) collective-permute-start(bf16[8,256,256]{2,1,0:T(8,128)(2,1)} %slice_bitcast_fusion), channel_id=1, source_target_pairs={{0,504},{8,0},{16,8},{24,16},{32,24},{40,32},{48,40},{56,48},{64,5... | collective-permute-start | bytes 3145736 | tf_op jit(solution)/shard_map/ppermute | solution.py:25
  8.1 1.9 %collective-permute-start.3 = (bf16[272,256]{1,0:T(8,128)(2,1)S(1)}, bf16[272,256]{1,0:T(8,128)(2,1)S(1)}, u32[]{:S(2)}, u32[]{:S(2)}) collective-permute-start(bf16[272,256]{1,0:T(8,128)(2,1)S(1)} %pad_maximum_fusion), channel_id=1, source_target_pairs={{0,24},{8,32},{16,40},{24,48},{32,56},{40,64},{48,72},{56,80},{64,... | collective-permute-start | bytes 417800 | tf_op jit(solution)/shard_map/ppermute | solution.py:25
  10.1 2.0 %collective-permute-start.1 = (bf16[272,256]{1,0:T(8,128)(2,1)S(1)}, bf16[272,256]{1,0:T(8,128)(2,1)S(1)}, u32[]{:S(2)}, u32[]{:S(2)}) collective-permute-start(bf16[272,256]{1,0:T(8,128)(2,1)S(1)} %pad_maximum_fusion), channel_id=1, source_target_pairs={{0,16},{8,24},{16,32},{24,40},{32,48},{40,56},{48,64},{56,72},{64,... | collective-permute-start | bytes 417800 | tf_op jit(solution)/shard_map/ppermute | solution.py:25
  12.1 0.1 broadcast_add_fusion
  12.2 0.8 reshape.46.parent_ref
  13.0 3.7 %shard_map.112 = (f32[256,384]{1,0:T(8,128)}, bf16[8,8,256]{2,1,0:T(8,128)(2,1)}) custom-call(s32[8]{0:T(128)} %acc_ref.1, bf16[256,256]{1,0:T(8,128)(2,1)} %q_ref.3, bf16[256,256]{1,0:T(8,128)(2,1)} %fresh_ref.1, s32[256,1]{1,0:T(8,128)} %reshape.46.parent_ref), custom_call_target="tpu_custom_call" | custom-call | tf_op jit(solution)/shard_map/pallas_call | solution.py:102
  16.7 3.9 %collective-permute-done.1.q_ref = bf16[272,256]{1,0:T(8,128)(2,1)S(1)} collective-permute-done((bf16[272,256]{1,0:T(8,128)(2,1)S(1)}, bf16[272,256]{1,0:T(8,128)(2,1)S(1)}, u32[]{:S(2)}, u32[]{:S(2)}) %collective-permute-start.1) | collective-permute-done | bytes 139296 | tf_op jit(solution)/shard_map/ppermute | solution.py:25
  20.5 0.7 copy-done.7
  21.2 3.2 %shard_map.114 = bf16[256,384]{1,0:T(8,128)(2,1)} custom-call(bf16[272,256]{1,0:T(8,128)(2,1)} %copy-done.7, bf16[8,4,256,256]{3,2,1,0:T(8,128)(2,1)} %kv_ref.5, f32[256,384]{1,0:T(8,128)} %get-tuple-element.7.tree_ref.order_ref), custom_call_target="tpu_custom_call" | custom-call | tf_op jit(solution)/shard_map/pallas_call | solution.py:243
  24.4 2.1 %collective-permute-start.2 = (bf16[256,384]{1,0:T(8,128)(2,1)}, bf16[256,384]{1,0:T(8,128)(2,1)S(1)}, u32[]{:S(2)}, u32[]{:S(2)}) collective-permute-start(bf16[256,384]{1,0:T(8,128)(2,1)} %shard_map.114), channel_id=1, source_target_pairs={{0,496},{8,504},{16,0},{24,8},{32,16},{40,24},{48,32},{56,40},{64,... | collective-permute-start | bytes 589832 | tf_op jit(solution)/shard_map/ppermute | solution.py:25
  26.5 0.0 collective-permute-done.3.q_ref
  26.5 0.0 copy-start.6
  26.5 0.6 copy-done.6
  27.2 3.2 %shard_map.115 = bf16[256,384]{1,0:T(8,128)(2,1)} custom-call(bf16[272,256]{1,0:T(8,128)(2,1)} %copy-done.6, bf16[8,4,256,256]{3,2,1,0:T(8,128)(2,1)} %kv_ref.5, f32[256,384]{1,0:T(8,128)} %get-tuple-element.7.tree_ref.order_ref), custom_call_target="tpu_custom_call" | custom-call | tf_op jit(solution)/shard_map/pallas_call | solution.py:243
  30.4 4.2 %collective-permute-start.4 = (bf16[256,384]{1,0:T(8,128)(2,1)}, bf16[256,384]{1,0:T(8,128)(2,1)S(1)}, u32[]{:S(2)}, u32[]{:S(2)}) collective-permute-start(bf16[256,384]{1,0:T(8,128)(2,1)} %shard_map.115), channel_id=1, source_target_pairs={{0,488},{8,496},{16,504},{24,0},{32,8},{40,16},{48,24},{56,32},{64... | collective-permute-start | bytes 589832 | tf_op jit(solution)/shard_map/ppermute | solution.py:25
  34.6 0.0 copy-start
  34.6 0.0 collective-permute-done.rest_0_
  34.6 5.3 %shard_map.113 = (f32[256,256]{1,0:T(8,128)}, f32[256,128]{1,0:T(8,128)}) custom-call(s32[8]{0:T(128)} %lens_ref.1, bf16[256,256]{1,0:T(8,128)(2,1)} %q_ref.3, bf16[8,4,256,256]{3,2,1,0:T(8,128)(2,1)} %kv_ref.5, f32[256,384]{1,0:T(8,128)} %get-tuple-element.7.tree_ref.order_ref, bf16[8,256,256]{2,1,0:T(8,128)(2,1)} %collective-permute-done.rest_0_), custom_call_target="tpu_custom_call" | custom-call | tf_op jit(solution)/shard_map/pallas_call | solution.py:180
  39.9 0.0 collective-permute-done.2.rest_0_
  39.9 1.6 %collective-permute-done.4.rest_1_ = bf16[256,384]{1,0:T(8,128)(2,1)S(1)} collective-permute-done((bf16[256,384]{1,0:T(8,128)(2,1)}, bf16[256,384]{1,0:T(8,128)(2,1)S(1)}, u32[]{:S(2)}, u32[]{:S(2)}) %collective-permute-start.4) | collective-permute-done | bytes 196640 | tf_op jit(solution)/shard_map/ppermute | solution.py:25
  41.5 0.9 copy-done.1
  42.5 0.9 copy-done.2
  43.4 1.7 %shard_map.116 = bf16[256,4096]{1,0:T(8,128)(2,1)S(1)} custom-call(f32[256,256]{1,0:T(8,128)S(1)} %copy-done.1, f32[256,128]{1,0:T(8,128)S(1)} %copy-done.2, bf16[256,384]{1,0:T(8,128)(2,1)S(1)} %collective-permute-done.2.rest_0_, bf16[256,384]{1,0:T(8,128)(2,1)S(1)} %collective-permute-done.4.rest_1_, bf16[256,4096]{1,0:T(8,128)(2,1)S(1)} %copy-done), custom_call_target="tpu_custom_call" | custom-call | tf_op jit(solution)/shard_map/pallas_call | solution.py:303
  45.1 0.8 fusion
  45.9 0.0 copy-start.5
  45.9 4.4 %collective-permute-start.5 = (bf16[32,4096]{1,0:T(8,128)(2,1)S(1)}, bf16[32,4096]{1,0:T(8,128)(2,1)S(1)}, u32[]{:S(2)}, u32[]{:S(2)}) collective-permute-start(bf16[32,4096]{1,0:T(8,128)(2,1)S(1)} %get-tuple-element.15), channel_id=1, source_target_pairs={{0,1},{1,2},{2,3},{3,4},{4,5},{5,6},{6,7},{7,0},{8,9},{9,10},{10,1... | collective-permute-start | bytes 786440 | tf_op jit(solution)/shard_map/ppermute | solution.py:25
  50.3 13.3 %collective-permute-done.5 = bf16[32,4096]{1,0:T(8,128)(2,1)S(1)} collective-permute-done((bf16[32,4096]{1,0:T(8,128)(2,1)S(1)}, bf16[32,4096]{1,0:T(8,128)(2,1)S(1)}, u32[]{:S(2)}, u32[]{:S(2)}) %collective-permute-start.5) | collective-permute-done | bytes 262176 | tf_op jit(solution)/shard_map/ppermute | solution.py:25
  63.7 0.1 fusion.8
  63.7 1.9 %collective-permute-start.6 = (bf16[32,4096]{1,0:T(8,128)(2,1)S(1)}, bf16[32,4096]{1,0:T(8,128)(2,1)S(1)}, u32[]{:S(2)}, u32[]{:S(2)}) collective-permute-start(bf16[32,4096]{1,0:T(8,128)(2,1)S(1)} %fusion.8), channel_id=1, source_target_pairs={{0,1},{1,2},{2,3},{3,4},{4,5},{5,6},{6,7},{7,0},{8,9},{9,10},{10,1... | collective-permute-start | bytes 786440 | tf_op jit(solution)/shard_map/ppermute | solution.py:25
  65.7 0.0 copy-start.8
  65.7 5.1 %collective-permute-start.9 = (bf16[32,4096]{1,0:T(8,128)(2,1)S(1)}, bf16[32,4096]{1,0:T(8,128)(2,1)S(1)}, u32[]{:S(2)}, u32[]{:S(2)}) collective-permute-start(bf16[32,4096]{1,0:T(8,128)(2,1)S(1)} %get-tuple-element.16), channel_id=1, source_target_pairs={{0,7},{1,0},{2,1},{3,2},{4,3},{5,4},{6,5},{7,6},{8,15},{9,8},{10,9... | collective-permute-start | bytes 786440 | tf_op jit(solution)/shard_map/ppermute | solution.py:25
  70.8 4.5 %collective-permute-done.6 = bf16[32,4096]{1,0:T(8,128)(2,1)S(1)} collective-permute-done((bf16[32,4096]{1,0:T(8,128)(2,1)S(1)}, bf16[32,4096]{1,0:T(8,128)(2,1)S(1)}, u32[]{:S(2)}, u32[]{:S(2)}) %collective-permute-start.6) | collective-permute-done | bytes 262176 | tf_op jit(solution)/shard_map/ppermute | solution.py:25
  75.4 0.1 fusion.7
  75.4 1.9 %collective-permute-start.7 = (bf16[32,4096]{1,0:T(8,128)(2,1)S(1)}, bf16[32,4096]{1,0:T(8,128)(2,1)S(1)}, u32[]{:S(2)}, u32[]{:S(2)}) collective-permute-start(bf16[32,4096]{1,0:T(8,128)(2,1)S(1)} %fusion.7), channel_id=1, source_target_pairs={{0,1},{1,2},{2,3},{3,4},{4,5},{5,6},{6,7},{7,0},{8,9},{9,10},{10,1... | collective-permute-start | bytes 786440 | tf_op jit(solution)/shard_map/ppermute | solution.py:25
  77.4 0.0 collective-permute-done.9
  77.4 8.9 %collective-permute-done.7 = bf16[32,4096]{1,0:T(8,128)(2,1)S(1)} collective-permute-done((bf16[32,4096]{1,0:T(8,128)(2,1)S(1)}, bf16[32,4096]{1,0:T(8,128)(2,1)S(1)}, u32[]{:S(2)}, u32[]{:S(2)}) %collective-permute-start.7) | collective-permute-done | bytes 262176 | tf_op jit(solution)/shard_map/ppermute | solution.py:25
  86.2 0.1 fusion.6
  86.4 1.9 %collective-permute-start.10 = (bf16[32,4096]{1,0:T(8,128)(2,1)S(1)}, bf16[32,4096]{1,0:T(8,128)(2,1)S(1)}, u32[]{:S(2)}, u32[]{:S(2)}) collective-permute-start(bf16[32,4096]{1,0:T(8,128)(2,1)S(1)} %get-tuple-element.14), channel_id=1, source_target_pairs={{0,7},{1,0},{2,1},{3,2},{4,3},{5,4},{6,5},{7,6},{8,15},{9,8},{10,9... | collective-permute-start | bytes 786440 | tf_op jit(solution)/shard_map/ppermute | solution.py:25
  88.3 3.9 %collective-permute-start.8 = (bf16[32,4096]{1,0:T(8,128)(2,1)S(1)}, bf16[32,4096]{1,0:T(8,128)(2,1)S(1)}, u32[]{:S(2)}, u32[]{:S(2)}) collective-permute-start(bf16[32,4096]{1,0:T(8,128)(2,1)S(1)} %get-tuple-element.13), channel_id=1, source_target_pairs={{0,1},{1,2},{2,3},{3,4},{4,5},{5,6},{6,7},{7,0},{8,9},{9,10},{10,1... | collective-permute-start | bytes 786440 | tf_op jit(solution)/shard_map/ppermute | solution.py:25
  92.2 2.8 %collective-permute-done.10 = bf16[32,4096]{1,0:T(8,128)(2,1)S(1)} collective-permute-done((bf16[32,4096]{1,0:T(8,128)(2,1)S(1)}, bf16[32,4096]{1,0:T(8,128)(2,1)S(1)}, u32[]{:S(2)}, u32[]{:S(2)}) %collective-permute-start.10) | collective-permute-done | bytes 262176 | tf_op jit(solution)/shard_map/ppermute | solution.py:25
  95.0 0.1 fusion.4
  95.1 3.4 %collective-permute-start.11 = (bf16[32,4096]{1,0:T(8,128)(2,1)S(1)}, bf16[32,4096]{1,0:T(8,128)(2,1)S(1)}, u32[]{:S(2)}, u32[]{:S(2)}) collective-permute-start(bf16[32,4096]{1,0:T(8,128)(2,1)S(1)} %fusion.4), channel_id=1, source_target_pairs={{0,7},{1,0},{2,1},{3,2},{4,3},{5,4},{6,5},{7,6},{8,15},{9,8},{10,9... | collective-permute-start | bytes 786440 | tf_op jit(solution)/shard_map/ppermute | solution.py:25
  98.5 4.8 %collective-permute-done.11 = bf16[32,4096]{1,0:T(8,128)(2,1)S(1)} collective-permute-done((bf16[32,4096]{1,0:T(8,128)(2,1)S(1)}, bf16[32,4096]{1,0:T(8,128)(2,1)S(1)}, u32[]{:S(2)}, u32[]{:S(2)}) %collective-permute-start.11) | collective-permute-done | bytes 262176 | tf_op jit(solution)/shard_map/ppermute | solution.py:25
  103.4 0.3 fusion.1
  103.7 0.8 fusion.3
  (19 shorter events, 0.1 us)
Async XLA Ops:
  0.6 7.4 %copy-start.10 = (s32[8]{0:T(128)S(1)}, s32[8]{0:T(128)}, u32[]{:S(2)}) copy-start(s32[8]{0:T(128)} %lens_ref.1) | copy-start | bytes 100
  0.6 7.5 %copy-start.3 = (bf16[256,256]{1,0:T(8,128)(2,1)S(1)}, bf16[256,256]{1,0:T(8,128)(2,1)}, u32[]{:S(2)}) copy-start(bf16[256,256]{1,0:T(8,128)(2,1)} %q_ref.3) | copy-start | bytes 393220
  0.7 11.4 %copy-start.9 = (s32[8,32]{1,0:T(8,128)S(1)}, s32[8,32]{1,0:T(8,128)}, u32[]{:S(2)}) copy-start(s32[8,32]{1,0:T(8,128)} %param.13) | copy-start | bytes 3076
  3.0 31.7 %collective-permute-start = (bf16[8,256,256]{2,1,0:T(8,128)(2,1)}, bf16[8,256,256]{2,1,0:T(8,128)(2,1)}, u32[]{:S(2)}, u32[]{:S(2)}) collective-permute-start(bf16[8,256,256]{2,1,0:T(8,128)(2,1)} %slice_bitcast_fusion), channel_id=1, source_target_pairs={{0,504},{8,0},{16,8},{24,16},{32,24},{40,32},{48,40},{56,48},{64,5... | collective-permute-start | bytes 3145736 | tf_op jit(solution)/shard_map/ppermute | solution.py:25
  8.1 18.4 %collective-permute-start.3 = (bf16[272,256]{1,0:T(8,128)(2,1)S(1)}, bf16[272,256]{1,0:T(8,128)(2,1)S(1)}, u32[]{:S(2)}, u32[]{:S(2)}) collective-permute-start(bf16[272,256]{1,0:T(8,128)(2,1)S(1)} %pad_maximum_fusion), channel_id=1, source_target_pairs={{0,24},{8,32},{16,40},{24,48},{32,56},{40,64},{48,72},{56,80},{64,... | collective-permute-start | bytes 417800 | tf_op jit(solution)/shard_map/ppermute | solution.py:25
  10.1 10.5 %collective-permute-start.1 = (bf16[272,256]{1,0:T(8,128)(2,1)S(1)}, bf16[272,256]{1,0:T(8,128)(2,1)S(1)}, u32[]{:S(2)}, u32[]{:S(2)}) collective-permute-start(bf16[272,256]{1,0:T(8,128)(2,1)S(1)} %pad_maximum_fusion), channel_id=1, source_target_pairs={{0,16},{8,24},{16,32},{24,40},{32,48},{40,56},{48,64},{56,72},{64,... | collective-permute-start | bytes 417800 | tf_op jit(solution)/shard_map/ppermute | solution.py:25
  20.5 0.7 copy-start.7
  24.4 15.5 %collective-permute-start.2 = (bf16[256,384]{1,0:T(8,128)(2,1)}, bf16[256,384]{1,0:T(8,128)(2,1)S(1)}, u32[]{:S(2)}, u32[]{:S(2)}) collective-permute-start(bf16[256,384]{1,0:T(8,128)(2,1)} %shard_map.114), channel_id=1, source_target_pairs={{0,496},{8,504},{16,0},{24,8},{32,16},{40,24},{48,32},{56,40},{64,... | collective-permute-start | bytes 589832 | tf_op jit(solution)/shard_map/ppermute | solution.py:25
  26.5 0.7 copy-start.6
  30.4 11.2 %collective-permute-start.4 = (bf16[256,384]{1,0:T(8,128)(2,1)}, bf16[256,384]{1,0:T(8,128)(2,1)S(1)}, u32[]{:S(2)}, u32[]{:S(2)}) collective-permute-start(bf16[256,384]{1,0:T(8,128)(2,1)} %shard_map.115), channel_id=1, source_target_pairs={{0,488},{8,496},{16,504},{24,0},{32,8},{40,16},{48,24},{56,32},{64... | collective-permute-start | bytes 589832 | tf_op jit(solution)/shard_map/ppermute | solution.py:25
  34.6 6.9 %copy-start = (bf16[256,4096]{1,0:T(8,128)(2,1)S(1)}, bf16[256,4096]{1,0:T(8,128)(2,1)}, u32[]{:S(2)}) copy-start(bf16[256,4096]{1,0:T(8,128)(2,1)} %rest_2_.1) | copy-start | bytes 6291460
  41.5 1.0 copy-start.1
  42.5 0.9 copy-start.2
  45.9 57.5 %copy-start.5 = (bf16[32,4096]{1,0:T(8,128)(2,1)S(1)}, bf16[32,4096]{1,0:T(8,128)(2,1)}, u32[]{:S(2)}) copy-start(bf16[32,4096]{1,0:T(8,128)(2,1)} %param.15) | copy-start | bytes 786436
  45.9 17.7 %collective-permute-start.5 = (bf16[32,4096]{1,0:T(8,128)(2,1)S(1)}, bf16[32,4096]{1,0:T(8,128)(2,1)S(1)}, u32[]{:S(2)}, u32[]{:S(2)}) collective-permute-start(bf16[32,4096]{1,0:T(8,128)(2,1)S(1)} %get-tuple-element.15), channel_id=1, source_target_pairs={{0,1},{1,2},{2,3},{3,4},{4,5},{5,6},{6,7},{7,0},{8,9},{9,10},{10,1... | collective-permute-start | bytes 786440 | tf_op jit(solution)/shard_map/ppermute | solution.py:25
  63.7 11.6 %collective-permute-start.6 = (bf16[32,4096]{1,0:T(8,128)(2,1)S(1)}, bf16[32,4096]{1,0:T(8,128)(2,1)S(1)}, u32[]{:S(2)}, u32[]{:S(2)}) collective-permute-start(bf16[32,4096]{1,0:T(8,128)(2,1)S(1)} %fusion.8), channel_id=1, source_target_pairs={{0,1},{1,2},{2,3},{3,4},{4,5},{5,6},{6,7},{7,0},{8,9},{9,10},{10,1... | collective-permute-start | bytes 786440 | tf_op jit(solution)/shard_map/ppermute | solution.py:25
  65.7 38.0 %copy-start.8 = (f32[4096]{0:T(1024)S(1)}, f32[4096]{0:T(1024)}, u32[]{:S(2)}) copy-start(f32[4096]{0:T(1024)} %param.17) | copy-start | bytes 49156
  65.7 11.7 %collective-permute-start.9 = (bf16[32,4096]{1,0:T(8,128)(2,1)S(1)}, bf16[32,4096]{1,0:T(8,128)(2,1)S(1)}, u32[]{:S(2)}, u32[]{:S(2)}) collective-permute-start(bf16[32,4096]{1,0:T(8,128)(2,1)S(1)} %get-tuple-element.16), channel_id=1, source_target_pairs={{0,7},{1,0},{2,1},{3,2},{4,3},{5,4},{6,5},{7,6},{8,15},{9,8},{10,9... | collective-permute-start | bytes 786440 | tf_op jit(solution)/shard_map/ppermute | solution.py:25
  75.4 10.8 %collective-permute-start.7 = (bf16[32,4096]{1,0:T(8,128)(2,1)S(1)}, bf16[32,4096]{1,0:T(8,128)(2,1)S(1)}, u32[]{:S(2)}, u32[]{:S(2)}) collective-permute-start(bf16[32,4096]{1,0:T(8,128)(2,1)S(1)} %fusion.7), channel_id=1, source_target_pairs={{0,1},{1,2},{2,3},{3,4},{4,5},{5,6},{6,7},{7,0},{8,9},{9,10},{10,1... | collective-permute-start | bytes 786440 | tf_op jit(solution)/shard_map/ppermute | solution.py:25
  86.4 8.7 %collective-permute-start.10 = (bf16[32,4096]{1,0:T(8,128)(2,1)S(1)}, bf16[32,4096]{1,0:T(8,128)(2,1)S(1)}, u32[]{:S(2)}, u32[]{:S(2)}) collective-permute-start(bf16[32,4096]{1,0:T(8,128)(2,1)S(1)} %get-tuple-element.14), channel_id=1, source_target_pairs={{0,7},{1,0},{2,1},{3,2},{4,3},{5,4},{6,5},{7,6},{8,15},{9,8},{10,9... | collective-permute-start | bytes 786440 | tf_op jit(solution)/shard_map/ppermute | solution.py:25
  88.3 10.2 %collective-permute-start.8 = (bf16[32,4096]{1,0:T(8,128)(2,1)S(1)}, bf16[32,4096]{1,0:T(8,128)(2,1)S(1)}, u32[]{:S(2)}, u32[]{:S(2)}) collective-permute-start(bf16[32,4096]{1,0:T(8,128)(2,1)S(1)} %get-tuple-element.13), channel_id=1, source_target_pairs={{0,1},{1,2},{2,3},{3,4},{4,5},{5,6},{6,7},{7,0},{8,9},{9,10},{10,1... | collective-permute-start | bytes 786440 | tf_op jit(solution)/shard_map/ppermute | solution.py:25
  95.1 8.3 %collective-permute-start.11 = (bf16[32,4096]{1,0:T(8,128)(2,1)S(1)}, bf16[32,4096]{1,0:T(8,128)(2,1)S(1)}, u32[]{:S(2)}, u32[]{:S(2)}) collective-permute-start(bf16[32,4096]{1,0:T(8,128)(2,1)S(1)} %fusion.4), channel_id=1, source_target_pairs={{0,7},{1,0},{2,1},{3,2},{4,3},{5,4},{6,5},{7,6},{8,15},{9,8},{10,9... | collective-permute-start | bytes 786440 | tf_op jit(solution)/shard_map/ppermute | solution.py:25
  103.7 0.9 copy-start.4
